TPU v7x, 128 devices: a whole 4x4x4 slice. The times are simulated.
128 devices in a mesh: section: 8 (over y, core), seq: 16 (over z, x).
Axes of the slice: x: 4, y: 4, z: 4, core: 2. Of those that a mesh axis runs over, the one named last changes fastest.
Arguments:
- hidden: bfloat16 [2, 2048, 4096], P(None, 'seq'), may hold values from -6 to 6
- queries: bfloat16 [8, 2, 2048, 4096], P('section', None, 'seq'), may hold values from -6 to 6
- gain: float32 [8, 4096], P('section'), may hold values from 0.5 to 2
- key_weight: bfloat16 [8, 4096, 512], P('section'), may hold values from -1 to 1
- value_weight: bfloat16 [8, 4096, 512], P('section'), may hold values from -0.09375 to 0.09375
- tree_ids: int32 [2, 2048], replicated, may hold values from 0 to 7, as said below
- branch_ids: int32 [2, 2048], replicated, may hold values from 0 to 2, as said below
- span_order: int32 [2, 32], replicated, may hold values from 0 to 31, each once within a row
Outputs:
- layer_out: bfloat16 [8, 2, 2048, 4096], P('section', None, 'seq')
Inputs may be any that keep to these rules, and one draw needn't show every extreme that they name: `tree_ids`: in each microbatch nondecreasing along the packed positions, every value of 0 to 7 present, each tree a multiple of 16 positions long. `branch_ids`: within each tree the prompt, chosen and rejected positions come in that order, each branch one position or more. `span_order`: each row is a permutation of 0 to 31.
All inputs are finite; a program needn't handle non-finite values.
Results may differ from a plain program's by a relative error of at most 0.02.
Values may be sent and summed in bfloat16 or wider, within the bound.
No kernel may reach another device: no remote copies, remote signals or barrier semaphores. Data moves between devices by JAX's collectives and lax.ppermute only.
A program may use at most 128 MiB of HBM per device.

v0:
```python
import math

import jax
import jax.numpy as jnp
from jax import lax
from jax.sharding import PartitionSpec as P

HQ = 32
HK = 4
HD = 128
SPAN = 64


rope_base = 500000.0


def from_behind(value, axis, by):
    size = lax.axis_size(axis)
    pairs = [(i, i + by) for i in range(size) if 0 <= i + by < size]
    return lax.ppermute(value, axis, pairs)


def frequencies():
    exponent = jnp.arange(HD // 2, dtype=jnp.float32) * (2.0 / HD)
    return jnp.power(jnp.float32(rope_base), -exponent)


def rotate(vectors, angles):
    half_dim = vectors.shape[-1] // 2
    cosine = jnp.cos(angles)[..., None, :]
    sine_part = jnp.sin(angles)[..., None, :]
    lower_half = vectors[..., :half_dim]
    upper_half = vectors[..., half_dim:]
    return jnp.concatenate(
        [
            lower_half * cosine - upper_half * sine_part,
            upper_half * cosine + lower_half * sine_part,
        ],
        axis=-1,
    )


def tree_positions(tree_ids, branch_ids):
    positions = jnp.arange(tree_ids.shape[1], dtype=jnp.int32)[None, :]
    opening = jnp.concatenate(
        [jnp.ones_like(tree_ids[:, :1]), (tree_ids[:, 1:] != tree_ids[:, :-1]).astype(jnp.int32)],
        axis=1,
    )
    starts = lax.cummax(jnp.where(opening > 0, positions, 0), axis=1)
    chosen = (branch_ids == 1).astype(jnp.int32)
    counted = jnp.cumsum(chosen, axis=1, dtype=jnp.int32)
    before = jnp.take_along_axis(counted - chosen, starts, axis=1)
    skipped = jnp.where(branch_ids == 2, counted - before, 0)
    return positions - starts - skipped


def local(hidden, queries, gain, key_weight, value_weight, tree_ids, branch_ids, span_order):
    section_id = lax.axis_index("section")
    shard_id = lax.axis_index("seq")
    section_count = lax.axis_size("section")
    micro_count, row_count, model_width = hidden.shape
    seq_len = tree_ids.shape[1]
    per_pass = 1
    ratio = HQ // HK
    scale = 1.0 / math.sqrt(HD)
    rotary_all = tree_positions(tree_ids, branch_ids)
    stored_ids = jnp.arange(seq_len, dtype=jnp.int32)
    packed_all = jnp.take(span_order, stored_ids // SPAN, axis=1) * SPAN + stored_ids % SPAN
    inverse = frequencies()
    gain_row = gain[0]
    key_mat = key_weight[0]
    value_mat = value_weight[0]

    def run_layer(current, first_mb, active):
        packed = lax.dynamic_slice_in_dim(packed_all, first_mb, per_pass, 0)
        trees = lax.dynamic_slice_in_dim(tree_ids, first_mb, per_pass, 0)
        branches = lax.dynamic_slice_in_dim(branch_ids, first_mb, per_pass, 0)
        rotary = lax.dynamic_slice_in_dim(rotary_all, first_mb, per_pass, 0)
        own_packed = lax.dynamic_slice_in_dim(packed, shard_id * row_count, row_count, 1)
        own_tree = jnp.take_along_axis(trees, own_packed, axis=1)
        own_branch = jnp.take_along_axis(branches, own_packed, axis=1)
        own_angles = (
            jnp.take_along_axis(rotary, own_packed, axis=1).astype(jnp.float32)[..., None] * inverse
        )
        widened = current.astype(jnp.float32)
        norm_scale = lax.rsqrt(jnp.mean(widened * widened, axis=-1, keepdims=True) + 1e-05)
        normed = (widened * norm_scale * gain_row).astype(jnp.bfloat16)
        flat = normed.reshape(per_pass * row_count, model_width)
        key_proj = jnp.dot(flat, key_mat, preferred_element_type=jnp.float32).reshape(
            per_pass, row_count, HK, HD
        )
        key_rows = (
            rotate(key_proj, own_angles).astype(jnp.bfloat16).reshape(per_pass, row_count, HK * HD)
        )
        value_rows = (
            jnp.dot(flat, value_mat, preferred_element_type=jnp.float32)
            .astype(jnp.bfloat16)
            .reshape(per_pass, row_count, HK * HD)
        )
        query_local = lax.dynamic_slice_in_dim(queries[0], first_mb, per_pass, 0)
        turned = rotate(
            query_local.astype(jnp.float32).reshape(per_pass, row_count, HQ, HD), own_angles
        ).astype(jnp.bfloat16)
        grouped = turned.reshape(per_pass, row_count, HK, ratio, HD)
        start_top = jnp.full((per_pass, HK, ratio, row_count), -jnp.inf, jnp.float32)
        start_sum = jnp.zeros((per_pass, HK, ratio, row_count), jnp.float32)
        start_acc = jnp.zeros((per_pass, HK, ratio, row_count, HD), jnp.float32)
        key_piece = lax.all_gather(key_rows, "seq", axis=1, tiled=True)
        value_piece = lax.all_gather(value_rows, "seq", axis=1, tiled=True)
        piece_len = key_piece.shape[1]
        block_len = math.gcd(piece_len, 512)

        def update(inner, operands):
            row_top, denominator, accum = inner
            key_blk, value_blk, allowed = operands
            scores = (
                jnp.einsum(
                    "grkhd,gskd->gkhrs",
                    grouped,
                    key_blk.reshape(per_pass, block_len, HK, HD),
                    preferred_element_type=jnp.float32,
                )
                * scale
            )
            masked = jnp.where(allowed[:, None, None], scores, -jnp.inf)
            new_top = jnp.maximum(row_top, jnp.max(masked, axis=-1))
            safe_top = jnp.where(jnp.isfinite(new_top), new_top, 0.0)
            weights = jnp.exp(masked - safe_top[..., None])
            rescale = jnp.exp(row_top - safe_top)
            denominator = denominator * rescale + jnp.sum(weights, axis=-1)
            accum = accum * rescale[..., None] + jnp.einsum(
                "gkhrs,gskd->gkhrd",
                weights.astype(jnp.bfloat16),
                value_blk.reshape(per_pass, block_len, HK, HD),
                preferred_element_type=jnp.float32,
            )
            return (new_top, denominator, accum)

        def step(block_id, inner):
            begin = block_id * block_len
            key_blk = lax.dynamic_slice_in_dim(key_piece, begin, block_len, 1)
            value_blk = lax.dynamic_slice_in_dim(value_piece, begin, block_len, 1)
            key_packed = lax.dynamic_slice_in_dim(packed, begin, block_len, 1)
            key_tree = jnp.take_along_axis(trees, key_packed, axis=1)
            key_branch = jnp.take_along_axis(branches, key_packed, axis=1)
            allowed = (
                (own_tree[:, :, None] == key_tree[:, None, :])
                & (key_packed[:, None, :] <= own_packed[:, :, None])
                & (
                    (key_branch[:, None, :] == 0)
                    | (key_branch[:, None, :] == own_branch[:, :, None])
                )
            )
            operands = (key_blk, value_blk, allowed)
            return update(inner, operands)

        def sweep(inner):
            return lax.fori_loop(0, piece_len // block_len, step, inner)

        row_top, denominator, accum = lax.cond(
            active, sweep, lambda inner: inner, (start_top, start_sum, start_acc)
        )
        safe_sum = jnp.where(denominator > 0.0, denominator, 1.0)
        attended = (
            (accum / safe_sum[..., None])
            .transpose(0, 3, 1, 2, 4)
            .reshape(per_pass, row_count, HQ * HD)
            .astype(jnp.bfloat16)
        )
        return (widened + attended.astype(jnp.float32)).astype(jnp.bfloat16)

    tick_count = section_count + micro_count // per_pass - 1

    def advance(step_id, state_pair):
        previous, outputs = state_pair
        incoming = from_behind(previous, "section", 1)
        first_mb = (step_id - section_id) * per_pass
        active = (first_mb >= 0) & (first_mb < micro_count)
        start_at = jnp.clip(first_mb, 0, micro_count - per_pass)
        entering = lax.dynamic_slice_in_dim(hidden, start_at, per_pass, 0)
        current = jnp.where(section_id == 0, entering, incoming)
        computed = run_layer(current, start_at, active)
        result = jnp.where(active, computed, jnp.zeros_like(computed))
        stored = lax.dynamic_update_slice_in_dim(outputs, result, start_at, 0)
        outputs = jnp.where(active, stored, outputs)
        return (result, outputs)

    empty_pass = jnp.zeros((per_pass, row_count, model_width), jnp.bfloat16)
    empty_out = jnp.zeros((micro_count, row_count, model_width), jnp.bfloat16)
    final_pass, outputs = lax.fori_loop(0, tick_count, advance, (empty_pass, empty_out))
    return outputs[None]


def solution(mesh):
    placed = (
        P(None, "seq", None),
        P("section", None, "seq", None),
        P("section", None),
        P("section", None, None),
        P("section", None, None),
        P(),
        P(),
        P(),
    )
    return jax.shard_map(
        local,
        mesh=mesh,
        in_specs=placed,
        out_specs=P("section", None, "seq", None),
        check_vma=False,
    )
```

profile of v0, /device:TPU:25, one launch (start us, length us, event | category | flops | bytes accessed | tf_op | source)
XLA Modules:
  0.0 2184.3 jit_solution(5759646535908856767)
XLA Ops:
  6.5 6.4 copy.28
  15.4 34.9 %gather_fusion.6 = s32[4096]{0:T(1024)S(1)} fusion(s32[2,2048]{1,0:T(2,128)S(1)} %bitcast_subtract_fusion, s32[4096]{0:T(1024)S(1)} %bitcast.243), kind=kCustom, calls=%fused_computation.6 | custom fusion | bytes 65536 | tf_op jit(solution)/shard_map/jit(take_along_axis)/gather | solution.py:52
  50.5 5.5 gather_fusion.5
  58.6 2118.9 %while.41 = (s32[]{:T(128)}, bf16[1,128,4096]{2,1,0:T(8,128)(2,1)}, bf16[2,128,4096]{2,1,0:T(8,128)(2,1)}, s32[]{:T(128)}, pred[]{:T(512)}, /*index=5*/bf16[2,12...) while((s32[]{:T(128)}, bf16[1,128,4096]{2,1,0:T(8,128)(2,1)}, ...), condition=%wide.region_12.15_spmd.clone, body=%wide.region_4.14_spmd.clone.sunk | while | flops 2188912640 | bytes 114081576 | solution.py:190
  80.2 49.8 %all-gather.7.cloned.1.call-done = bf16[1,2048,512]{1,2,0:T(8,128)(2,1)} async-done(((bf16[1,128,512]{1,2,0:T(8,128)(2,1)}), bf16[1,2048,512]{1,2,0:T(8,128)(2,1)}) %all-gather.7.cloned.1.call-update) | async-done | bytes 2097168 | tf_op jit(solution)/shard_map/while/body/eval_jaxpr/all_gather | solution.py:108
  130.0 46.5 %all-gather.9.cloned.1.call-done = bf16[2048,512]{1,0:T(8,128)(2,1)} async-done(((bf16[128,512]{1,0:T(8,128)(2,1)}), bf16[2048,512]{1,0:T(8,128)(2,1)}) %all-gather.9.cloned.1.call-update) | async-done | bytes 2097168 | tf_op jit(solution)/shard_map/while/body/eval_jaxpr/all_gather | solution.py:109
  212.5 140.5 %all-gather.7.cloned.1.call-done = bf16[1,2048,512]{1,2,0:T(8,128)(2,1)} async-done(((bf16[1,128,512]{1,2,0:T(8,128)(2,1)}), bf16[1,2048,512]{1,2,0:T(8,128)(2,1)}) %all-gather.7.cloned.1.call-update) | async-done | bytes 2097168 | tf_op jit(solution)/shard_map/while/body/eval_jaxpr/all_gather | solution.py:108
  353.0 46.4 %all-gather.9.cloned.1.call-done = bf16[2048,512]{1,0:T(8,128)(2,1)} async-done(((bf16[128,512]{1,0:T(8,128)(2,1)}), bf16[2048,512]{1,0:T(8,128)(2,1)}) %all-gather.9.cloned.1.call-update) | async-done | bytes 2097168 | tf_op jit(solution)/shard_map/while/body/eval_jaxpr/all_gather | solution.py:109
  435.4 151.1 %all-gather.7.cloned.1.call-done = bf16[1,2048,512]{1,2,0:T(8,128)(2,1)} async-done(((bf16[1,128,512]{1,2,0:T(8,128)(2,1)}), bf16[1,2048,512]{1,2,0:T(8,128)(2,1)}) %all-gather.7.cloned.1.call-update) | async-done | bytes 2097168 | tf_op jit(solution)/shard_map/while/body/eval_jaxpr/all_gather | solution.py:108
  586.6 46.4 %all-gather.9.cloned.1.call-done = bf16[2048,512]{1,0:T(8,128)(2,1)} async-done(((bf16[128,512]{1,0:T(8,128)(2,1)}), bf16[2048,512]{1,0:T(8,128)(2,1)}) %all-gather.9.cloned.1.call-update) | async-done | bytes 2097168 | tf_op jit(solution)/shard_map/while/body/eval_jaxpr/all_gather | solution.py:109
  669.0 154.0 %all-gather.7.cloned.1.call-done = bf16[1,2048,512]{1,2,0:T(8,128)(2,1)} async-done(((bf16[1,128,512]{1,2,0:T(8,128)(2,1)}), bf16[1,2048,512]{1,2,0:T(8,128)(2,1)}) %all-gather.7.cloned.1.call-update) | async-done | bytes 2097168 | tf_op jit(solution)/shard_map/while/body/eval_jaxpr/all_gather | solution.py:108
  822.9 46.5 %all-gather.9.cloned.1.call-done = bf16[2048,512]{1,0:T(8,128)(2,1)} async-done(((bf16[128,512]{1,0:T(8,128)(2,1)}), bf16[2048,512]{1,0:T(8,128)(2,1)}) %all-gather.9.cloned.1.call-update) | async-done | bytes 2097168 | tf_op jit(solution)/shard_map/while/body/eval_jaxpr/all_gather | solution.py:109
  905.4 154.0 %all-gather.7.cloned.1.call-done = bf16[1,2048,512]{1,2,0:T(8,128)(2,1)} async-done(((bf16[1,128,512]{1,2,0:T(8,128)(2,1)}), bf16[1,2048,512]{1,2,0:T(8,128)(2,1)}) %all-gather.7.cloned.1.call-update) | async-done | bytes 2097168 | tf_op jit(solution)/shard_map/while/body/eval_jaxpr/all_gather | solution.py:108
  1059.4 46.4 %all-gather.9.cloned.1.call-done = bf16[2048,512]{1,0:T(8,128)(2,1)} async-done(((bf16[128,512]{1,0:T(8,128)(2,1)}), bf16[2048,512]{1,0:T(8,128)(2,1)}) %all-gather.9.cloned.1.call-update) | async-done | bytes 2097168 | tf_op jit(solution)/shard_map/while/body/eval_jaxpr/all_gather | solution.py:109
  1141.8 155.5 %all-gather.7.cloned.1.call-done = bf16[1,2048,512]{1,2,0:T(8,128)(2,1)} async-done(((bf16[1,128,512]{1,2,0:T(8,128)(2,1)}), bf16[1,2048,512]{1,2,0:T(8,128)(2,1)}) %all-gather.7.cloned.1.call-update) | async-done | bytes 2097168 | tf_op jit(solution)/shard_map/while/body/eval_jaxpr/all_gather | solution.py:108
  1297.3 46.4 %all-gather.9.cloned.1.call-done = bf16[2048,512]{1,0:T(8,128)(2,1)} async-done(((bf16[128,512]{1,0:T(8,128)(2,1)}), bf16[2048,512]{1,0:T(8,128)(2,1)}) %all-gather.9.cloned.1.call-update) | async-done | bytes 2097168 | tf_op jit(solution)/shard_map/while/body/eval_jaxpr/all_gather | solution.py:109
  1379.7 155.5 %all-gather.7.cloned.1.call-done = bf16[1,2048,512]{1,2,0:T(8,128)(2,1)} async-done(((bf16[1,128,512]{1,2,0:T(8,128)(2,1)}), bf16[1,2048,512]{1,2,0:T(8,128)(2,1)}) %all-gather.7.cloned.1.call-update) | async-done | bytes 2097168 | tf_op jit(solution)/shard_map/while/body/eval_jaxpr/all_gather | solution.py:108
  1535.2 46.4 %all-gather.9.cloned.1.call-done = bf16[2048,512]{1,0:T(8,128)(2,1)} async-done(((bf16[128,512]{1,0:T(8,128)(2,1)}), bf16[2048,512]{1,0:T(8,128)(2,1)}) %all-gather.9.cloned.1.call-update) | async-done | bytes 2097168 | tf_op jit(solution)/shard_map/while/body/eval_jaxpr/all_gather | solution.py:109
  1597.8 111.5 %collective-permute-done = bf16[1,128,4096]{2,1,0:T(8,128)(2,1)S(1)} collective-permute-done((bf16[1,128,4096]{2,1,0:T(8,128)(2,1)S(1)}, bf16[1,128,4096]{2,1,0:T(8,128)(2,1)S(1)}, u32[]{:S(2)}, u32[]{:S(2)}) %collective-permute-start) | collective-permute-done | bytes 1048608 | tf_op jit(solution)/shard_map/while/body/eval_jaxpr/ppermute | solution.py:20
  1726.1 46.7 %all-gather.7.cloned.1.call-done = bf16[1,2048,512]{1,2,0:T(8,128)(2,1)} async-done(((bf16[1,128,512]{1,2,0:T(8,128)(2,1)}), bf16[1,2048,512]{1,2,0:T(8,128)(2,1)}) %all-gather.7.cloned.1.call-update) | async-done | bytes 2097168 | tf_op jit(solution)/shard_map/while/body/eval_jaxpr/all_gather | solution.py:108
  1772.8 46.4 %all-gather.9.cloned.1.call-done = bf16[2048,512]{1,0:T(8,128)(2,1)} async-done(((bf16[128,512]{1,0:T(8,128)(2,1)}), bf16[2048,512]{1,0:T(8,128)(2,1)}) %all-gather.9.cloned.1.call-update) | async-done | bytes 2097168 | tf_op jit(solution)/shard_map/while/body/eval_jaxpr/all_gather | solution.py:109
  1819.1 110.7 %conditional.3 = (f32[1,4,8,128]{3,2,1,0:T(8,128)}, f32[1,4,8,128,128]{4,3,2,1,0:T(8,128)}) conditional(s32[]{:T(128)} %convert_element_type.273, () %tuple.129, (s32[2,2048]{1,0:T(2,128)S(1)}, s32[]{:T(128)}, pred[1,128]{1,0:T(4,128)(4,1)S(1)}, s32[1,2048]{1,0:T(1,128)S(1)}, s32[1,128]{1,0:T(1,128)S(1)}, /*index=5*/s32[1,2048]{1,0:T(1,128)S(1)}, ...), branch_computations={%region_6.7_spmd, %region_7.13_spmd.clone} | conditional | flops 1098833152 | bytes 35224720 | solution.py:160
  1819.2 110.7 %while.40 = (s32[]{:T(128)}, f32[1,4,8,128]{3,2,1,0:T(8,128)S(1)}, f32[1,4,8,128]{3,2,1,0:T(8,128)}, f32[1,4,8,128,128]{4,3,2,1,0:T(8,128)}, s32[1,128]{1,0:T(1,...) while((s32[]{:T(128)}, f32[1,4,8,128]{3,2,1,0:T(8,128)S(1)}, ...), condition=%wide.region_11.12_spmd.clone, body=%wide.region_8.11_spmd.clone.sunk | while | flops 1098832896 | bytes 35205864 | solution.py:158
  1827.0 4.6 fusion.86
  1831.6 5.1 fusion.89
  1838.6 7.3 bitcast_add_fusion.5
  1853.6 4.6 fusion.86
  1858.3 5.1 fusion.89
  1866.0 7.9 bitcast_add_fusion.5
  1881.6 4.6 fusion.86
  1886.3 5.1 fusion.89
  1894.0 7.9 bitcast_add_fusion.5
  1909.6 4.6 fusion.86
  1914.3 5.1 fusion.89
  1922.0 7.9 bitcast_add_fusion.5
  1963.7 46.7 %all-gather.7.cloned.1.call-done = bf16[1,2048,512]{1,2,0:T(8,128)(2,1)} async-done(((bf16[1,128,512]{1,2,0:T(8,128)(2,1)}), bf16[1,2048,512]{1,2,0:T(8,128)(2,1)}) %all-gather.7.cloned.1.call-update) | async-done | bytes 2097168 | tf_op jit(solution)/shard_map/while/body/eval_jaxpr/all_gather | solution.py:108
  2010.4 46.4 %all-gather.9.cloned.1.call-done = bf16[2048,512]{1,0:T(8,128)(2,1)} async-done(((bf16[128,512]{1,0:T(8,128)(2,1)}), bf16[2048,512]{1,0:T(8,128)(2,1)}) %all-gather.9.cloned.1.call-update) | async-done | bytes 2097168 | tf_op jit(solution)/shard_map/while/body/eval_jaxpr/all_gather | solution.py:109
  2056.7 110.7 %conditional.3 = (f32[1,4,8,128]{3,2,1,0:T(8,128)}, f32[1,4,8,128,128]{4,3,2,1,0:T(8,128)}) conditional(s32[]{:T(128)} %convert_element_type.273, () %tuple.129, (s32[2,2048]{1,0:T(2,128)S(1)}, s32[]{:T(128)}, pred[1,128]{1,0:T(4,128)(4,1)S(1)}, s32[1,2048]{1,0:T(1,128)S(1)}, s32[1,128]{1,0:T(1,128)S(1)}, /*index=5*/s32[1,2048]{1,0:T(1,128)S(1)}, ...), branch_computations={%region_6.7_spmd, %region_7.13_spmd.clone} | conditional | flops 1098833152 | bytes 35224720 | solution.py:160
  2056.8 110.7 %while.40 = (s32[]{:T(128)}, f32[1,4,8,128]{3,2,1,0:T(8,128)S(1)}, f32[1,4,8,128]{3,2,1,0:T(8,128)}, f32[1,4,8,128,128]{4,3,2,1,0:T(8,128)}, s32[1,128]{1,0:T(1,...) while((s32[]{:T(128)}, f32[1,4,8,128]{3,2,1,0:T(8,128)S(1)}, ...), condition=%wide.region_11.12_spmd.clone, body=%wide.region_8.11_spmd.clone.sunk | while | flops 1098832896 | bytes 35205864 | solution.py:158
  2064.6 4.6 fusion.86
  2069.2 5.1 fusion.89
  2076.2 7.3 bitcast_add_fusion.5
  2095.9 5.1 fusion.89
  2103.6 7.9 bitcast_add_fusion.5
  2123.9 5.1 fusion.89
  2131.6 7.9 bitcast_add_fusion.5
  2151.9 5.1 fusion.89
  2159.6 7.9 bitcast_add_fusion.5
  (515 shorter events, 428.6 us)
Async XLA Ops:
  6.5 6.4 copy-start.1
  6.5 7.5 copy-start.2
  15.4 35.0 %copy-start.3 = (s32[2,32]{1,0:T(2,128)S(1)}, s32[2,32]{1,0:T(2,128)}, u32[]{:S(2)}) copy-start(s32[2,32]{1,0:T(2,128)} %param.25) | copy-start | bytes 772
  56.7 1.9 copy-start.4
  58.6 71.3 %all-gather.7.cloned.1.call-start = ((), (), s32[]{:S(2)}) async-start(), calls=%async_computation | async-start | bytes 2228224 | tf_op jit(solution)/shard_map/while/body/eval_jaxpr/all_gather | solution.py:108
  58.7 4.7 collective-permute-start
  69.4 107.1 %all-gather.9.cloned.1.call-start = ((), (), s32[]{:S(2)}) async-start(), calls=%async_computation.1 | async-start | bytes 2228224 | tf_op jit(solution)/shard_map/while/body/eval_jaxpr/all_gather | solution.py:109
  69.4 4.0 copy-start
  188.7 164.3 %all-gather.7.cloned.1.call-start = ((), (), s32[]{:S(2)}) async-start(), calls=%async_computation | async-start | bytes 2228224 | tf_op jit(solution)/shard_map/while/body/eval_jaxpr/all_gather | solution.py:108
  190.0 5.8 collective-permute-start
  201.7 197.6 %all-gather.9.cloned.1.call-start = ((), (), s32[]{:S(2)}) async-start(), calls=%async_computation.1 | async-start | bytes 2228224 | tf_op jit(solution)/shard_map/while/body/eval_jaxpr/all_gather | solution.py:109
  201.8 4.0 copy-start
  411.6 174.9 %all-gather.7.cloned.1.call-start = ((), (), s32[]{:S(2)}) async-start(), calls=%async_computation | async-start | bytes 2228224 | tf_op jit(solution)/shard_map/while/body/eval_jaxpr/all_gather | solution.py:108
  412.9 5.8 collective-permute-start
  424.6 208.3 %all-gather.9.cloned.1.call-start = ((), (), s32[]{:S(2)}) async-start(), calls=%async_computation.1 | async-start | bytes 2228224 | tf_op jit(solution)/shard_map/while/body/eval_jaxpr/all_gather | solution.py:109
  424.7 4.0 copy-start
  645.1 177.8 %all-gather.7.cloned.1.call-start = ((), (), s32[]{:S(2)}) async-start(), calls=%async_computation | async-start | bytes 2228224 | tf_op jit(solution)/shard_map/while/body/eval_jaxpr/all_gather | solution.py:108
  646.4 5.8 collective-permute-start
  658.2 211.2 %all-gather.9.cloned.1.call-start = ((), (), s32[]{:S(2)}) async-start(), calls=%async_computation.1 | async-start | bytes 2228224 | tf_op jit(solution)/shard_map/while/body/eval_jaxpr/all_gather | solution.py:109
  658.2 4.0 copy-start
  881.6 177.8 %all-gather.7.cloned.1.call-start = ((), (), s32[]{:S(2)}) async-start(), calls=%async_computation | async-start | bytes 2228224 | tf_op jit(solution)/shard_map/while/body/eval_jaxpr/all_gather | solution.py:108
  882.9 5.8 collective-permute-start
  894.7 211.1 %all-gather.9.cloned.1.call-start = ((), (), s32[]{:S(2)}) async-start(), calls=%async_computation.1 | async-start | bytes 2228224 | tf_op jit(solution)/shard_map/while/body/eval_jaxpr/all_gather | solution.py:109
  894.7 4.0 copy-start
  1118.0 179.3 %all-gather.7.cloned.1.call-start = ((), (), s32[]{:S(2)}) async-start(), calls=%async_computation | async-start | bytes 2228224 | tf_op jit(solution)/shard_map/while/body/eval_jaxpr/all_gather | solution.py:108
  1119.3 5.8 collective-permute-start
  1131.0 212.6 %all-gather.9.cloned.1.call-start = ((), (), s32[]{:S(2)}) async-start(), calls=%async_computation.1 | async-start | bytes 2228224 | tf_op jit(solution)/shard_map/while/body/eval_jaxpr/all_gather | solution.py:109
  1131.1 4.0 copy-start
  1355.9 179.3 %all-gather.7.cloned.1.call-start = ((), (), s32[]{:S(2)}) async-start(), calls=%async_computation | async-start | bytes 2228224 | tf_op jit(solution)/shard_map/while/body/eval_jaxpr/all_gather | solution.py:108
  1357.2 5.8 collective-permute-start
  1368.9 212.6 %all-gather.9.cloned.1.call-start = ((), (), s32[]{:S(2)}) async-start(), calls=%async_computation.1 | async-start | bytes 2228224 | tf_op jit(solution)/shard_map/while/body/eval_jaxpr/all_gather | solution.py:109
  1369.0 4.0 copy-start
  1593.7 179.0 %all-gather.7.cloned.1.call-start = ((), (), s32[]{:S(2)}) async-start(), calls=%async_computation | async-start | bytes 2228224 | tf_op jit(solution)/shard_map/while/body/eval_jaxpr/all_gather | solution.py:108
  1595.0 114.3 %collective-permute-start = (bf16[1,128,4096]{2,1,0:T(8,128)(2,1)S(1)}, bf16[1,128,4096]{2,1,0:T(8,128)(2,1)S(1)}, u32[]{:S(2)}, u32[]{:S(2)}) collective-permute-start(bf16[1,128,4096]{2,1,0:T(8,128)(2,1)S(1)} %broadcast_select_fusion.7), channel_id=1, source_target_pairs={{0,16},{16,32},{32,48},{48,64},{64,80},{80,96},{96,112},{1,17},{17... | collective-permute-start | bytes 3145736 | tf_op jit(solution)/shard_map/while/body/eval_jaxpr/ppermute | solution.py:20
  1715.3 103.8 %all-gather.9.cloned.1.call-start = ((), (), s32[]{:S(2)}) async-start(), calls=%async_computation.1 | async-start | bytes 2228224 | tf_op jit(solution)/shard_map/while/body/eval_jaxpr/all_gather | solution.py:109
  1715.4 4.0 copy-start
  1939.9 70.5 %all-gather.7.cloned.1.call-start = ((), (), s32[]{:S(2)}) async-start(), calls=%async_computation | async-start | bytes 2228224 | tf_op jit(solution)/shard_map/while/body/eval_jaxpr/all_gather | solution.py:108
  1941.2 5.8 collective-permute-start
  1952.9 103.8 %all-gather.9.cloned.1.call-start = ((), (), s32[]{:S(2)}) async-start(), calls=%async_computation.1 | async-start | bytes 2228224 | tf_op jit(solution)/shard_map/while/body/eval_jaxpr/all_gather | solution.py:109
  1953.0 4.0 copy-start
Sparse Core Ops, SparseCore 0:
  69.5 60.4 all-gather.6
  132.1 44.3 all-gather.8
  201.9 151.1 all-gather.6
  355.0 44.3 all-gather.8
  424.8 161.7 all-gather.6
  588.5 44.3 all-gather.8
  658.3 164.5 all-gather.6
  825.0 44.3 all-gather.8
  894.8 164.5 all-gather.6
  1061.4 44.3 all-gather.8
  1131.1 166.0 all-gather.6
  1299.3 44.3 all-gather.8
  1369.0 166.0 all-gather.6
  1537.1 44.3 all-gather.8
  1715.4 57.2 all-gather.6
  1774.8 44.3 all-gather.8
  1953.0 57.2 all-gather.6
  2012.4 44.3 all-gather.8
where the time goes:
time: 2190 us; the launch traced here: 2180 us
  waiting for transfers between devices  1610 us (74%)
  local copies, waits for them, and re-layouts  215 us (10%)
  other arithmetic  171 us (8%)
  matrix products  164 us (7%)
    all_gather x9, waiting for transfers between devices, run_layer(): key_piece = lax.all_gather(key_rows, 'seq', axis=1, tiled=True)  1050 us
    all_gather x9, waiting for transfers between devices, run_layer(): value_piece = lax.all_gather(value_rows, 'seq', axis=1, tiled=True)  418 us
    ppermute x9, waiting for transfers between devices, from_behind(): return lax.ppermute(value, axis, pairs)  134 us
    dot_general x8, matrix products, update(): jnp.einsum('gkhrs,gskd->gkhrd', weights.astype(jnp.bfloat16), value_blk.r...  61.6 us
  transfers between devices with their start and end apart: 27, of which 27 were waited for; matrix products, arithmetic and copies ran while one was open for 5% of the time, Pallas kernels for 0%

commit v1 on v0

v1 whole, which is shorter than its diff:
```python
import math

import jax
import jax.numpy as jnp
from jax import lax
from jax.experimental import pallas as pl
from jax.experimental.pallas import tpu as pltpu
from jax.sharding import PartitionSpec as P

HQ = 32
HK = 4
HD = 128
SPAN = 64


rope_base = 500000.0


def from_behind(value, axis, by):
    size = lax.axis_size(axis)
    pairs = [(i, i + by) for i in range(size) if 0 <= i + by < size]
    return lax.ppermute(value, axis, pairs)


def frequencies():
    exponent = jnp.arange(HD // 2, dtype=jnp.float32) * (2.0 / HD)
    return jnp.power(jnp.float32(rope_base), -exponent)


def rotate(vectors, cosine, sine_part):
    half_dim = vectors.shape[-1] // 2
    lower_half = vectors[..., :half_dim]
    upper_half = vectors[..., half_dim:]
    return jnp.concatenate(
        [
            lower_half * cosine - upper_half * sine_part,
            upper_half * cosine + lower_half * sine_part,
        ],
        axis=-1,
    )


def tree_positions(tree_ids, branch_ids):
    positions = jnp.arange(tree_ids.shape[1], dtype=jnp.int32)[None, :]
    opening = jnp.concatenate(
        [jnp.ones_like(tree_ids[:, :1]), (tree_ids[:, 1:] != tree_ids[:, :-1]).astype(jnp.int32)],
        axis=1,
    )
    starts = lax.cummax(jnp.where(opening > 0, positions, 0), axis=1)
    chosen = (branch_ids == 1).astype(jnp.int32)
    counted = jnp.cumsum(chosen, axis=1, dtype=jnp.int32)
    before = jnp.take_along_axis(counted - chosen, starts, axis=1)
    skipped = jnp.where(branch_ids == 2, counted - before, 0)
    return positions - starts - skipped


def attention_kernel(q_ref, k_ref, v_ref, bias_ref, res_ref, o_ref):
    ratio = HQ // HK
    scale = 1.0 / math.sqrt(HD)
    keys = k_ref[...]
    values = v_ref[...]
    bias = bias_ref[...]
    for g in range(ratio):
        cols = slice(g * HD, (g + 1) * HD)
        scores = lax.dot_general(
            q_ref[:, cols],
            keys,
            (((1,), (1,)), ((), ())),
            preferred_element_type=jnp.float32,
        )
        masked = scores * scale + bias
        row_top = jnp.max(masked, axis=-1, keepdims=True)
        weights = jnp.exp(masked - row_top)
        denominator = jnp.sum(weights, axis=-1, keepdims=True)
        summed = jnp.dot(
            weights.astype(jnp.bfloat16), values, preferred_element_type=jnp.float32
        )
        attended = (summed / denominator).astype(jnp.bfloat16)
        o_ref[:, cols] = (
            res_ref[:, cols].astype(jnp.float32) + attended.astype(jnp.float32)
        ).astype(o_ref.dtype)


def attention(turned, kv_all, bias, residual):
    rows, width = turned.shape
    keys_len = kv_all.shape[0]
    group = width // HK
    return pl.pallas_call(
        attention_kernel,
        grid=(HK,),
        in_specs=[
            pl.BlockSpec((rows, group), lambda k: (0, k)),
            pl.BlockSpec((keys_len, HD), lambda k: (0, k)),
            pl.BlockSpec((keys_len, HD), lambda k: (0, HK + k)),
            pl.BlockSpec((rows, keys_len), lambda k: (0, 0)),
            pl.BlockSpec((rows, group), lambda k: (0, k)),
        ],
        out_specs=pl.BlockSpec((rows, group), lambda k: (0, k)),
        out_shape=jax.ShapeDtypeStruct((rows, width), jnp.bfloat16),
    )(turned, kv_all, kv_all, bias, residual)


def local(hidden, queries, gain, key_weight, value_weight, tree_ids, branch_ids, span_order):
    section_id = lax.axis_index("section")
    shard_id = lax.axis_index("seq")
    section_count = lax.axis_size("section")
    micro_count, row_count, model_width = hidden.shape
    seq_len = tree_ids.shape[1]
    rotary_all = tree_positions(tree_ids, branch_ids)
    stored_ids = jnp.arange(seq_len, dtype=jnp.int32)
    packed_all = jnp.take(span_order, stored_ids // SPAN, axis=1) * SPAN + stored_ids % SPAN
    key_tree = jnp.take_along_axis(tree_ids, packed_all, axis=1)
    key_branch = jnp.take_along_axis(branch_ids, packed_all, axis=1)
    key_rotary = jnp.take_along_axis(rotary_all, packed_all, axis=1)
    first_row = shard_id * row_count
    own_packed = lax.dynamic_slice_in_dim(packed_all, first_row, row_count, 1)
    own_tree = lax.dynamic_slice_in_dim(key_tree, first_row, row_count, 1)
    own_branch = lax.dynamic_slice_in_dim(key_branch, first_row, row_count, 1)
    own_rotary = lax.dynamic_slice_in_dim(key_rotary, first_row, row_count, 1)
    allowed = (
        (own_tree[:, :, None] == key_tree[:, None, :])
        & (packed_all[:, None, :] <= own_packed[:, :, None])
        & ((key_branch[:, None, :] == 0) | (key_branch[:, None, :] == own_branch[:, :, None]))
    )
    bias_all = jnp.where(allowed, 0.0, -jnp.inf).astype(jnp.float32)
    angles = own_rotary.astype(jnp.float32)[..., None] * frequencies()
    cos_all = jnp.cos(angles)
    sin_all = jnp.sin(angles)
    gain_row = gain[0]
    key_mat = key_weight[0]
    value_mat = value_weight[0]
    kv_mat = jnp.concatenate([key_mat, value_mat], axis=1)

    def run_layer(current, mb):
        cosine = lax.dynamic_index_in_dim(cos_all, mb, 0, keepdims=False)
        sine_part = lax.dynamic_index_in_dim(sin_all, mb, 0, keepdims=False)
        bias = lax.dynamic_index_in_dim(bias_all, mb, 0, keepdims=False)
        widened = current.astype(jnp.float32)
        norm_scale = lax.rsqrt(jnp.mean(widened * widened, axis=-1, keepdims=True) + 1e-05)
        normed = (widened * norm_scale * gain_row).astype(jnp.bfloat16)
        kv_proj = jnp.dot(normed, kv_mat, preferred_element_type=jnp.float32)
        key_proj = kv_proj[:, : HK * HD].reshape(row_count, HK, HD)
        key_rows = (
            rotate(key_proj, cosine[:, None, :], sine_part[:, None, :])
            .astype(jnp.bfloat16)
            .reshape(row_count, HK * HD)
        )
        value_rows = kv_proj[:, HK * HD :].astype(jnp.bfloat16)
        kv_rows = jnp.concatenate([key_rows, value_rows], axis=1)
        kv_all = lax.all_gather(kv_rows, "seq", axis=0, tiled=True)
        query_local = lax.dynamic_index_in_dim(queries[0], mb, 0, keepdims=False)
        turned = (
            rotate(
                query_local.astype(jnp.float32).reshape(row_count, HQ, HD),
                cosine[:, None, :],
                sine_part[:, None, :],
            )
            .astype(jnp.bfloat16)
            .reshape(row_count, HQ * HD)
        )
        return attention(turned, kv_all, bias, current)

    tick_count = section_count + micro_count - 1

    def advance(step_id, state_pair):
        previous, outputs = state_pair
        incoming = from_behind(previous, "section", 1)
        first_mb = step_id - section_id
        active = (first_mb >= 0) & (first_mb < micro_count)
        start_at = jnp.clip(first_mb, 0, micro_count - 1)
        entering = lax.dynamic_index_in_dim(hidden, start_at, 0, keepdims=False)
        current = jnp.where(section_id == 0, entering, incoming)
        computed = run_layer(current, start_at)
        result = jnp.where(active, computed, jnp.zeros_like(computed))
        stored = lax.dynamic_update_index_in_dim(outputs, result, start_at, 0)
        outputs = jnp.where(active, stored, outputs)
        return (result, outputs)

    empty_pass = jnp.zeros((row_count, model_width), jnp.bfloat16)
    empty_out = jnp.zeros((micro_count, row_count, model_width), jnp.bfloat16)
    final_pass, outputs = lax.fori_loop(0, tick_count, advance, (empty_pass, empty_out))
    return outputs[None]


def solution(mesh):
    placed = (
        P(None, "seq", None),
        P("section", None, "seq", None),
        P("section", None),
        P("section", None, None),
        P("section", None, None),
        P(),
        P(),
        P(),
    )
    return jax.shard_map(
        local,
        mesh=mesh,
        in_specs=placed,
        out_specs=P("section", None, "seq", None),
        check_vma=False,
    )
```

time: 2190 us -> 1060 us (0.48)
  waiting for transfers between devices: 1610 us -> 560 us
  Pallas kernels: 0 us -> 178 us
  matrix products: 164 us -> 46 us
  other arithmetic: 171 us -> 62.6 us
  local copies, waits for them, and re-layouts: 215 us -> 188 us
    all_gather x18 -> x9, waiting for transfers between devices: 1470 us -> 528 us  [run_layer(): kv_all = lax.all_gather(kv_rows, 'seq', axis=0, tiled=True)]
    pallas_call x0 -> x9, Pallas kernels: none -> 178 us  [attention(): pl.pallas_call(attention_kernel, grid=(HK,), in_specs=[pl.BlockSpec((rows...]
    dot_general x34 -> x9, matrix products: 164 us -> 46 us  [run_layer(): kv_proj = jnp.dot(normed, kv_mat, preferred_element_type=jnp.float32)]
    ppermute x9, waiting for transfers between devices: 134 us -> 31.8 us  [from_behind(): return lax.ppermute(value, axis, pairs)]
    reduce_sum x8 -> x0, other arithmetic: 40.5 us -> none  [update(): denominator = denominator * rescale + jnp.sum(weights, axis=-1)]
    convert_element_type x18 -> x0, local copies, waits for them, and re-layouts: 38.7 us -> none  [run_layer(): return (widened + attended.astype(jnp.float32)).astype(jnp.bfloat16)]
    while x35 -> x117, local copies, waits for them, and re-layouts: 3.38 us -> 29.7 us
    gather x43 -> x6, local copies, waits for them, and re-layouts: 81.3 us -> 105 us  [the longest x2 34.9 us: local(): key_rotary = jnp.take_along_axis(rotary_all, packed_all, axis=1)]
  transfers between devices with their start and end apart: 27 -> 18, of which waited for: 27 -> 18; matrix products, arithmetic and copies ran while one was open for 5% -> 4% of each run, Pallas kernels for 0% -> 0%
where the time goes in v1:
time: 1060 us
  waiting for transfers between devices  560 us (53%)
  local copies, waits for them, and re-layouts  188 us (18%)
  Pallas kernels  178 us (17%)
  other arithmetic  62.6 us (6%)
  matrix products  46 us (4%)
  between operations  13.3 us (1%)
  starting transfers between devices  11.6 us (1%)
    all_gather x9, waiting for transfers between devices, run_layer(): kv_all = lax.all_gather(kv_rows, 'seq', axis=0, tiled=True)  528 us
    pallas_call x9, Pallas kernels, attention(): pl.pallas_call(attention_kernel, grid=(HK,), in_specs=[pl.BlockSpec((rows...  178 us
    dot_general x9, matrix products, run_layer(): kv_proj = jnp.dot(normed, kv_mat, preferred_element_type=jnp.float32)  46 us
    gather x2, local copies, waits for them, and re-layouts, local(): key_rotary = jnp.take_along_axis(rotary_all, packed_all, axis=1)  34.9 us
    gather x2, local copies, waits for them, and re-layouts, tree_positions(): before = jnp.take_along_axis(counted - chosen, starts, axis=1)  34.9 us
    gather x2, local copies, waits for them, and re-layouts, local(): key_branch = jnp.take_along_axis(branch_ids, packed_all, axis=1)  34.9 us
    gather x2, local copies, waits for them, and re-layouts, local(): key_tree = jnp.take_along_axis(tree_ids, packed_all, axis=1)  34.9 us
    ppermute x9, waiting for transfers between devices, from_behind(): return lax.ppermute(value, axis, pairs)  31.8 us
  transfers between devices with their start and end apart: 18, of which 18 were waited for; matrix products, arithmetic and copies ran while one was open for 4% of the time, Pallas kernels for 0%

profile of v1, /device:TPU:25, one launch (start us, length us, event | category | flops | bytes accessed | tf_op | source)
XLA Modules:
  0.0 1061.4 jit_solution(17062808416191552556)
XLA Ops:
  11.1 34.9 %gather_fusion.1 = s32[4096]{0:T(1024)S(1)} fusion(s32[2,2048]{1,0:T(2,128)S(1)} %bitcast_subtract_fusion, s32[4096]{0:T(1024)S(1)} %bitcast.110), kind=kCustom, calls=%fused_computation.clone | custom fusion | bytes 65536 | tf_op jit(solution)/shard_map/jit(take_along_axis)/gather | solution.py:52
  46.2 5.5 gather_fusion
  52.1 34.9 %gather_fusion.2 = s32[4096]{0:T(1024)S(1)} fusion(s32[2,2048]{1,0:T(2,128)S(1)} %fusion.9, s32[4096]{0:T(1024)S(1)} %bitcast.106), kind=kCustom, calls=%fused_computation.1.clone | custom fusion | bytes 65536 | tf_op jit(solution)/shard_map/jit(take_along_axis)/gather | solution.py:114
  86.9 34.9 %gather_fusion.4 = s32[4096]{0:T(1024)S(1)} fusion(s32[2,2048]{1,0:T(2,128)S(1)} %copy-done, s32[4096]{0:T(1024)S(1)} %bitcast.107), kind=kCustom, calls=%fused_computation.3.clone | custom fusion | bytes 65536 | tf_op jit(solution)/shard_map/jit(take_along_axis)/gather | solution.py:113
  122.4 7.9 pad_maximum_fusion.3
  130.3 34.9 %gather_fusion.3 = s32[4096]{0:T(1024)S(1)} fusion(s32[2,2048]{1,0:T(2,128)S(1)} %copy-done.1, s32[4096]{0:T(1024)S(1)} %bitcast.108), kind=kCustom, calls=%fused_computation.2.clone | custom fusion | bytes 65536 | tf_op jit(solution)/shard_map/jit(take_along_axis)/gather | solution.py:112
  165.3 2.3 and_select_fusion
  169.1 885.7 %while.17 = (s32[]{:T(128)}, bf16[128,4096]{1,0:T(8,128)(2,1)S(1)}, bf16[2,128,4096]{2,1,0:T(8,128)(2,1)}, s32[]{:T(128)}, bf16[1,2,128,4096]{3,2,1,0:T(8,128)(2...) while((s32[]{:T(128)}, bf16[128,4096]{1,0:T(8,128)(2,1)S(1)}, ...), condition=%wide.region_6.8_spmd.clone, body=%wide.region_4.7_spmd.clone.sunk | while | flops 1085276288 | bytes 94523320 | solution.py:181
  170.5 3.4 collective-permute-done
  173.9 1.7 fusion.34
  175.7 5.1 fusion.35
  186.8 60.7 %all-gather.2.cloned.1.call-done.k_ref.v_ref = bf16[2048,1024]{1,0:T(8,128)(2,1)} async-done(((bf16[128,1024]{1,0:T(8,128)(2,1)}), bf16[2048,1024]{1,0:T(8,128)(2,1)}) %all-gather.2.cloned.1.call-update) | async-done | bytes 4194320 | tf_op jit(solution)/shard_map/while/body/eval_jaxpr/all_gather | solution.py:150
  247.5 19.8 %eval_jaxpr.6 = bf16[128,4096]{1,0:T(8,128)(2,1)} custom-call(bf16[128,4096]{1,0:T(8,128)(2,1)} %bitcast.111, bf16[2048,1024]{1,0:T(8,128)(2,1)} %all-gather.2.cloned.1.call-done.k_ref.v_ref, bf16[2048,1024]{1,0:T(8,128)(2,1)} %all-gather.2.cloned.1.call-done.k_ref.v_ref, f32[128,2048]{1,0:T(8,128)} %dynamic-slice_bitcast_fusion.6.bias_ref, ...), custom_call_target="tpu_custom_call" | custom-call | tf_op jit(solution)/shard_map/while/body/eval_jaxpr/pallas_call | solution.py:88
  270.6 3.4 collective-permute-done
  274.0 1.7 fusion.34
  275.7 5.1 fusion.35
  286.9 58.2 %all-gather.2.cloned.1.call-done.k_ref.v_ref = bf16[2048,1024]{1,0:T(8,128)(2,1)} async-done(((bf16[128,1024]{1,0:T(8,128)(2,1)}), bf16[2048,1024]{1,0:T(8,128)(2,1)}) %all-gather.2.cloned.1.call-update) | async-done | bytes 4194320 | tf_op jit(solution)/shard_map/while/body/eval_jaxpr/all_gather | solution.py:150
  345.0 19.8 %eval_jaxpr.6 = bf16[128,4096]{1,0:T(8,128)(2,1)} custom-call(bf16[128,4096]{1,0:T(8,128)(2,1)} %bitcast.111, bf16[2048,1024]{1,0:T(8,128)(2,1)} %all-gather.2.cloned.1.call-done.k_ref.v_ref, bf16[2048,1024]{1,0:T(8,128)(2,1)} %all-gather.2.cloned.1.call-done.k_ref.v_ref, f32[128,2048]{1,0:T(8,128)} %dynamic-slice_bitcast_fusion.6.bias_ref, ...), custom_call_target="tpu_custom_call" | custom-call | tf_op jit(solution)/shard_map/while/body/eval_jaxpr/pallas_call | solution.py:88
  368.1 3.4 collective-permute-done
  373.2 5.1 fusion.35
  384.4 58.2 %all-gather.2.cloned.1.call-done.k_ref.v_ref = bf16[2048,1024]{1,0:T(8,128)(2,1)} async-done(((bf16[128,1024]{1,0:T(8,128)(2,1)}), bf16[2048,1024]{1,0:T(8,128)(2,1)}) %all-gather.2.cloned.1.call-update) | async-done | bytes 4194320 | tf_op jit(solution)/shard_map/while/body/eval_jaxpr/all_gather | solution.py:150
  442.6 19.8 %eval_jaxpr.6 = bf16[128,4096]{1,0:T(8,128)(2,1)} custom-call(bf16[128,4096]{1,0:T(8,128)(2,1)} %bitcast.111, bf16[2048,1024]{1,0:T(8,128)(2,1)} %all-gather.2.cloned.1.call-done.k_ref.v_ref, bf16[2048,1024]{1,0:T(8,128)(2,1)} %all-gather.2.cloned.1.call-done.k_ref.v_ref, f32[128,2048]{1,0:T(8,128)} %dynamic-slice_bitcast_fusion.6.bias_ref, ...), custom_call_target="tpu_custom_call" | custom-call | tf_op jit(solution)/shard_map/while/body/eval_jaxpr/pallas_call | solution.py:88
  465.6 3.4 collective-permute-done
  470.7 5.1 fusion.35
  481.9 58.2 %all-gather.2.cloned.1.call-done.k_ref.v_ref = bf16[2048,1024]{1,0:T(8,128)(2,1)} async-done(((bf16[128,1024]{1,0:T(8,128)(2,1)}), bf16[2048,1024]{1,0:T(8,128)(2,1)}) %all-gather.2.cloned.1.call-update) | async-done | bytes 4194320 | tf_op jit(solution)/shard_map/while/body/eval_jaxpr/all_gather | solution.py:150
  540.1 19.8 %eval_jaxpr.6 = bf16[128,4096]{1,0:T(8,128)(2,1)} custom-call(bf16[128,4096]{1,0:T(8,128)(2,1)} %bitcast.111, bf16[2048,1024]{1,0:T(8,128)(2,1)} %all-gather.2.cloned.1.call-done.k_ref.v_ref, bf16[2048,1024]{1,0:T(8,128)(2,1)} %all-gather.2.cloned.1.call-done.k_ref.v_ref, f32[128,2048]{1,0:T(8,128)} %dynamic-slice_bitcast_fusion.6.bias_ref, ...), custom_call_target="tpu_custom_call" | custom-call | tf_op jit(solution)/shard_map/while/body/eval_jaxpr/pallas_call | solution.py:88
  563.1 3.4 collective-permute-done
  568.2 5.1 fusion.35
  579.4 58.2 %all-gather.2.cloned.1.call-done.k_ref.v_ref = bf16[2048,1024]{1,0:T(8,128)(2,1)} async-done(((bf16[128,1024]{1,0:T(8,128)(2,1)}), bf16[2048,1024]{1,0:T(8,128)(2,1)}) %all-gather.2.cloned.1.call-update) | async-done | bytes 4194320 | tf_op jit(solution)/shard_map/while/body/eval_jaxpr/all_gather | solution.py:150
  637.6 19.8 %eval_jaxpr.6 = bf16[128,4096]{1,0:T(8,128)(2,1)} custom-call(bf16[128,4096]{1,0:T(8,128)(2,1)} %bitcast.111, bf16[2048,1024]{1,0:T(8,128)(2,1)} %all-gather.2.cloned.1.call-done.k_ref.v_ref, bf16[2048,1024]{1,0:T(8,128)(2,1)} %all-gather.2.cloned.1.call-done.k_ref.v_ref, f32[128,2048]{1,0:T(8,128)} %dynamic-slice_bitcast_fusion.6.bias_ref, ...), custom_call_target="tpu_custom_call" | custom-call | tf_op jit(solution)/shard_map/while/body/eval_jaxpr/pallas_call | solution.py:88
  660.6 3.4 collective-permute-done
  665.8 5.1 fusion.35
  676.9 59.4 %all-gather.2.cloned.1.call-done.k_ref.v_ref = bf16[2048,1024]{1,0:T(8,128)(2,1)} async-done(((bf16[128,1024]{1,0:T(8,128)(2,1)}), bf16[2048,1024]{1,0:T(8,128)(2,1)}) %all-gather.2.cloned.1.call-update) | async-done | bytes 4194320 | tf_op jit(solution)/shard_map/while/body/eval_jaxpr/all_gather | solution.py:150
  736.3 19.8 %eval_jaxpr.6 = bf16[128,4096]{1,0:T(8,128)(2,1)} custom-call(bf16[128,4096]{1,0:T(8,128)(2,1)} %bitcast.111, bf16[2048,1024]{1,0:T(8,128)(2,1)} %all-gather.2.cloned.1.call-done.k_ref.v_ref, bf16[2048,1024]{1,0:T(8,128)(2,1)} %all-gather.2.cloned.1.call-done.k_ref.v_ref, f32[128,2048]{1,0:T(8,128)} %dynamic-slice_bitcast_fusion.6.bias_ref, ...), custom_call_target="tpu_custom_call" | custom-call | tf_op jit(solution)/shard_map/while/body/eval_jaxpr/pallas_call | solution.py:88
  759.4 3.4 collective-permute-done
  764.5 5.1 fusion.35
  775.7 59.4 %all-gather.2.cloned.1.call-done.k_ref.v_ref = bf16[2048,1024]{1,0:T(8,128)(2,1)} async-done(((bf16[128,1024]{1,0:T(8,128)(2,1)}), bf16[2048,1024]{1,0:T(8,128)(2,1)}) %all-gather.2.cloned.1.call-update) | async-done | bytes 4194320 | tf_op jit(solution)/shard_map/while/body/eval_jaxpr/all_gather | solution.py:150
  835.1 19.8 %eval_jaxpr.6 = bf16[128,4096]{1,0:T(8,128)(2,1)} custom-call(bf16[128,4096]{1,0:T(8,128)(2,1)} %bitcast.111, bf16[2048,1024]{1,0:T(8,128)(2,1)} %all-gather.2.cloned.1.call-done.k_ref.v_ref, bf16[2048,1024]{1,0:T(8,128)(2,1)} %all-gather.2.cloned.1.call-done.k_ref.v_ref, f32[128,2048]{1,0:T(8,128)} %dynamic-slice_bitcast_fusion.6.bias_ref, ...), custom_call_target="tpu_custom_call" | custom-call | tf_op jit(solution)/shard_map/while/body/eval_jaxpr/pallas_call | solution.py:88
  858.1 4.6 collective-permute-done
  864.4 5.1 fusion.35
  875.6 57.9 %all-gather.2.cloned.1.call-done.k_ref.v_ref = bf16[2048,1024]{1,0:T(8,128)(2,1)} async-done(((bf16[128,1024]{1,0:T(8,128)(2,1)}), bf16[2048,1024]{1,0:T(8,128)(2,1)}) %all-gather.2.cloned.1.call-update) | async-done | bytes 4194320 | tf_op jit(solution)/shard_map/while/body/eval_jaxpr/all_gather | solution.py:150
  933.5 19.8 %eval_jaxpr.6 = bf16[128,4096]{1,0:T(8,128)(2,1)} custom-call(bf16[128,4096]{1,0:T(8,128)(2,1)} %bitcast.111, bf16[2048,1024]{1,0:T(8,128)(2,1)} %all-gather.2.cloned.1.call-done.k_ref.v_ref, bf16[2048,1024]{1,0:T(8,128)(2,1)} %all-gather.2.cloned.1.call-done.k_ref.v_ref, f32[128,2048]{1,0:T(8,128)} %dynamic-slice_bitcast_fusion.6.bias_ref, ...), custom_call_target="tpu_custom_call" | custom-call | tf_op jit(solution)/shard_map/while/body/eval_jaxpr/pallas_call | solution.py:88
  953.4 1.7 fusion.36
  957.8 3.4 collective-permute-done
  962.9 5.1 fusion.35
  974.1 57.9 %all-gather.2.cloned.1.call-done.k_ref.v_ref = bf16[2048,1024]{1,0:T(8,128)(2,1)} async-done(((bf16[128,1024]{1,0:T(8,128)(2,1)}), bf16[2048,1024]{1,0:T(8,128)(2,1)}) %all-gather.2.cloned.1.call-update) | async-done | bytes 4194320 | tf_op jit(solution)/shard_map/while/body/eval_jaxpr/all_gather | solution.py:150
  1032.0 19.8 %eval_jaxpr.6 = bf16[128,4096]{1,0:T(8,128)(2,1)} custom-call(bf16[128,4096]{1,0:T(8,128)(2,1)} %bitcast.111, bf16[2048,1024]{1,0:T(8,128)(2,1)} %all-gather.2.cloned.1.call-done.k_ref.v_ref, bf16[2048,1024]{1,0:T(8,128)(2,1)} %all-gather.2.cloned.1.call-done.k_ref.v_ref, f32[128,2048]{1,0:T(8,128)} %dynamic-slice_bitcast_fusion.6.bias_ref, ...), custom_call_target="tpu_custom_call" | custom-call | tf_op jit(solution)/shard_map/while/body/eval_jaxpr/pallas_call | solution.py:88
  1051.8 1.7 fusion.36
  (320 shorter events, 100.3 us)
Async XLA Ops:
  11.1 34.9 %copy-start = (s32[2,2048]{1,0:T(2,128)S(1)}, s32[2,2048]{1,0:T(2,128)}, u32[]{:S(2)}) copy-start(s32[2,2048]{1,0:T(2,128)} %param.18) | copy-start | bytes 49156
  11.1 35.0 %copy-start.8 = (s32[2,32]{1,0:T(2,128)S(1)}, s32[2,32]{1,0:T(2,128)}, u32[]{:S(2)}) copy-start(s32[2,32]{1,0:T(2,128)} %param.19) | copy-start | bytes 772
  122.4 7.9 copy-start.1
  165.3 3.9 copy-start.7
  169.1 78.4 %all-gather.2.cloned.1.call-start = ((), (), s32[]{:S(2)}) async-start(), calls=%async_computation | async-start | bytes 4456448 | tf_op jit(solution)/shard_map/while/body/eval_jaxpr/all_gather | solution.py:150
  169.2 4.7 collective-permute-start
  175.6 5.1 copy-start.2
  183.7 2.0 copy-start.3
  247.5 19.8 %copy-start.4 = (bf16[2,128,4096]{2,1,0:T(8,128)(2,1)S(1)}, bf16[2,128,4096]{2,1,0:T(8,128)(2,1)}, u32[]{:S(2)}) copy-start(bf16[2,128,4096]{2,1,0:T(8,128)(2,1)} %get-tuple-element.434) | copy-start | bytes 6291460 | tf_op jit(solution)/shard_map/while
  269.2 75.9 %all-gather.2.cloned.1.call-start = ((), (), s32[]{:S(2)}) async-start(), calls=%async_computation | async-start | bytes 4456448 | tf_op jit(solution)/shard_map/while/body/eval_jaxpr/all_gather | solution.py:150
  269.3 4.7 collective-permute-start
  275.7 5.1 copy-start.2
  283.8 2.0 copy-start.3
  345.0 19.8 %copy-start.4 = (bf16[2,128,4096]{2,1,0:T(8,128)(2,1)S(1)}, bf16[2,128,4096]{2,1,0:T(8,128)(2,1)}, u32[]{:S(2)}) copy-start(bf16[2,128,4096]{2,1,0:T(8,128)(2,1)} %get-tuple-element.434) | copy-start | bytes 6291460 | tf_op jit(solution)/shard_map/while
  366.7 75.9 %all-gather.2.cloned.1.call-start = ((), (), s32[]{:S(2)}) async-start(), calls=%async_computation | async-start | bytes 4456448 | tf_op jit(solution)/shard_map/while/body/eval_jaxpr/all_gather | solution.py:150
  366.8 4.7 collective-permute-start
  373.2 5.1 copy-start.2
  381.3 2.0 copy-start.3
  442.6 19.8 %copy-start.4 = (bf16[2,128,4096]{2,1,0:T(8,128)(2,1)S(1)}, bf16[2,128,4096]{2,1,0:T(8,128)(2,1)}, u32[]{:S(2)}) copy-start(bf16[2,128,4096]{2,1,0:T(8,128)(2,1)} %get-tuple-element.434) | copy-start | bytes 6291460 | tf_op jit(solution)/shard_map/while
  464.2 75.9 %all-gather.2.cloned.1.call-start = ((), (), s32[]{:S(2)}) async-start(), calls=%async_computation | async-start | bytes 4456448 | tf_op jit(solution)/shard_map/while/body/eval_jaxpr/all_gather | solution.py:150
  464.3 4.7 collective-permute-start
  470.7 5.1 copy-start.2
  478.8 2.0 copy-start.3
  540.1 19.8 %copy-start.4 = (bf16[2,128,4096]{2,1,0:T(8,128)(2,1)S(1)}, bf16[2,128,4096]{2,1,0:T(8,128)(2,1)}, u32[]{:S(2)}) copy-start(bf16[2,128,4096]{2,1,0:T(8,128)(2,1)} %get-tuple-element.434) | copy-start | bytes 6291460 | tf_op jit(solution)/shard_map/while
  561.7 75.9 %all-gather.2.cloned.1.call-start = ((), (), s32[]{:S(2)}) async-start(), calls=%async_computation | async-start | bytes 4456448 | tf_op jit(solution)/shard_map/while/body/eval_jaxpr/all_gather | solution.py:150
  561.8 4.7 collective-permute-start
  568.2 5.1 copy-start.2
  576.3 2.0 copy-start.3
  637.6 19.8 %copy-start.4 = (bf16[2,128,4096]{2,1,0:T(8,128)(2,1)S(1)}, bf16[2,128,4096]{2,1,0:T(8,128)(2,1)}, u32[]{:S(2)}) copy-start(bf16[2,128,4096]{2,1,0:T(8,128)(2,1)} %get-tuple-element.434) | copy-start | bytes 6291460 | tf_op jit(solution)/shard_map/while
  659.2 77.1 %all-gather.2.cloned.1.call-start = ((), (), s32[]{:S(2)}) async-start(), calls=%async_computation | async-start | bytes 4456448 | tf_op jit(solution)/shard_map/while/body/eval_jaxpr/all_gather | solution.py:150
  659.3 4.7 collective-permute-start
  665.7 5.1 copy-start.2
  673.9 2.0 copy-start.3
  736.3 19.8 %copy-start.4 = (bf16[2,128,4096]{2,1,0:T(8,128)(2,1)S(1)}, bf16[2,128,4096]{2,1,0:T(8,128)(2,1)}, u32[]{:S(2)}) copy-start(bf16[2,128,4096]{2,1,0:T(8,128)(2,1)} %get-tuple-element.434) | copy-start | bytes 6291460 | tf_op jit(solution)/shard_map/while
  758.0 77.1 %all-gather.2.cloned.1.call-start = ((), (), s32[]{:S(2)}) async-start(), calls=%async_computation | async-start | bytes 4456448 | tf_op jit(solution)/shard_map/while/body/eval_jaxpr/all_gather | solution.py:150
  758.1 4.7 collective-permute-start
  764.5 5.1 copy-start.2
  772.6 2.0 copy-start.3
  835.1 19.8 %copy-start.4 = (bf16[2,128,4096]{2,1,0:T(8,128)(2,1)S(1)}, bf16[2,128,4096]{2,1,0:T(8,128)(2,1)}, u32[]{:S(2)}) copy-start(bf16[2,128,4096]{2,1,0:T(8,128)(2,1)} %get-tuple-element.434) | copy-start | bytes 6291460 | tf_op jit(solution)/shard_map/while
  856.7 76.8 %all-gather.2.cloned.1.call-start = ((), (), s32[]{:S(2)}) async-start(), calls=%async_computation | async-start | bytes 4456448 | tf_op jit(solution)/shard_map/while/body/eval_jaxpr/all_gather | solution.py:150
  856.8 6.0 collective-permute-start
  864.4 5.1 copy-start.2
  933.5 19.8 %copy-start.4 = (bf16[2,128,4096]{2,1,0:T(8,128)(2,1)S(1)}, bf16[2,128,4096]{2,1,0:T(8,128)(2,1)}, u32[]{:S(2)}) copy-start(bf16[2,128,4096]{2,1,0:T(8,128)(2,1)} %get-tuple-element.434) | copy-start | bytes 6291460 | tf_op jit(solution)/shard_map/while
  956.4 75.6 %all-gather.2.cloned.1.call-start = ((), (), s32[]{:S(2)}) async-start(), calls=%async_computation | async-start | bytes 4456448 | tf_op jit(solution)/shard_map/while/body/eval_jaxpr/all_gather | solution.py:150
  956.5 4.7 collective-permute-start
  962.9 5.1 copy-start.2
  971.0 2.0 copy-start.3
  1032.0 19.8 %copy-start.4 = (bf16[2,128,4096]{2,1,0:T(8,128)(2,1)S(1)}, bf16[2,128,4096]{2,1,0:T(8,128)(2,1)}, u32[]{:S(2)}) copy-start(bf16[2,128,4096]{2,1,0:T(8,128)(2,1)} %get-tuple-element.434) | copy-start | bytes 6291460 | tf_op jit(solution)/shard_map/while
  (19 other events, 28.3 us)
Sparse Core Ops, SparseCore 0:
  182.3 65.1 all-gather.1
  282.4 62.6 all-gather.1
  379.9 62.6 all-gather.1
  477.4 62.6 all-gather.1
  574.9 62.6 all-gather.1
  672.4 63.8 all-gather.1
  771.2 63.8 all-gather.1
  871.1 62.3 all-gather.1
  969.6 62.3 all-gather.1

commit v2 on v1

--- a/solution.py
+++ b/solution.py
@@ -41,17 +41,24 @@
 
 
 def tree_positions(tree_ids, branch_ids):
+    trees = jnp.arange(8, dtype=jnp.int32)[None, :, None]
     positions = jnp.arange(tree_ids.shape[1], dtype=jnp.int32)[None, :]
-    opening = jnp.concatenate(
-        [jnp.ones_like(tree_ids[:, :1]), (tree_ids[:, 1:] != tree_ids[:, :-1]).astype(jnp.int32)],
-        axis=1,
-    )
-    starts = lax.cummax(jnp.where(opening > 0, positions, 0), axis=1)
-    chosen = (branch_ids == 1).astype(jnp.int32)
-    counted = jnp.cumsum(chosen, axis=1, dtype=jnp.int32)
-    before = jnp.take_along_axis(counted - chosen, starts, axis=1)
-    skipped = jnp.where(branch_ids == 2, counted - before, 0)
-    return positions - starts - skipped
+    same = tree_ids[:, None, :] == trees
+    starts = jnp.sum((tree_ids[:, None, :] < trees).astype(jnp.int32), axis=2)
+    chosen = jnp.sum((same & (branch_ids[:, None, :] == 1)).astype(jnp.int32), axis=2)
+    own_start = jnp.sum(jnp.where(same, starts[:, :, None], 0), axis=1)
+    own_chosen = jnp.sum(jnp.where(same, chosen[:, :, None], 0), axis=1)
+    skipped = jnp.where(branch_ids == 2, own_chosen, 0)
+    return positions - own_start - skipped
+
+
+def by_span(values, span_order):
+    micro_count, seq_len = values.shape
+    spans = seq_len // SPAN
+    blocks = values.reshape(micro_count, 1, spans, SPAN)
+    picks = span_order[:, :, None] == jnp.arange(spans, dtype=jnp.int32)[None, None, :]
+    chosen = jnp.where(picks[..., None], blocks, 0)
+    return jnp.sum(chosen, axis=2).reshape(micro_count, seq_len)
 
 
 def attention_kernel(q_ref, k_ref, v_ref, bias_ref, res_ref, o_ref):
@@ -108,10 +115,10 @@
     seq_len = tree_ids.shape[1]
     rotary_all = tree_positions(tree_ids, branch_ids)
     stored_ids = jnp.arange(seq_len, dtype=jnp.int32)
-    packed_all = jnp.take(span_order, stored_ids // SPAN, axis=1) * SPAN + stored_ids % SPAN
-    key_tree = jnp.take_along_axis(tree_ids, packed_all, axis=1)
-    key_branch = jnp.take_along_axis(branch_ids, packed_all, axis=1)
-    key_rotary = jnp.take_along_axis(rotary_all, packed_all, axis=1)
+    packed_all = jnp.repeat(span_order, SPAN, axis=1) * SPAN + stored_ids % SPAN
+    key_tree = by_span(tree_ids, span_order)
+    key_branch = by_span(branch_ids, span_order)
+    key_rotary = by_span(rotary_all, span_order)
     first_row = shard_id * row_count
     own_packed = lax.dynamic_slice_in_dim(packed_all, first_row, row_count, 1)
     own_tree = lax.dynamic_slice_in_dim(key_tree, first_row, row_count, 1)

time: 1060 us -> 921 us (0.87)
  local copies, waits for them, and re-layouts: 188 us -> 44.3 us
    gather x10 -> x0, local copies, waits for them, and re-layouts: 145 us -> none  [the longest x2 34.9 us: local(): key_rotary = jnp.take_along_axis(rotary_all, packed_all, axis=1)]
where the time goes in v2:
time: 921 us; the launch traced here: 919 us
  waiting for transfers between devices  560 us (61%)
  Pallas kernels  179 us (19%)
  other arithmetic  63.9 us (7%)
  matrix products  45.9 us (5%)
  local copies, waits for them, and re-layouts  44.3 us (5%)
  between operations  13.2 us (1%)
  starting transfers between devices  11.6 us (1%)
    all_gather x9, waiting for transfers between devices, run_layer(): kv_all = lax.all_gather(kv_rows, 'seq', axis=0, tiled=True)  528 us
    pallas_call x9, Pallas kernels, attention(): pl.pallas_call(attention_kernel, grid=(HK,), in_specs=[pl.BlockSpec((rows...  179 us
    dot_general x9, matrix products, run_layer(): kv_proj = jnp.dot(normed, kv_mat, preferred_element_type=jnp.float32)  45.9 us
    ppermute x9, waiting for transfers between devices, from_behind(): return lax.ppermute(value, axis, pairs)  31.8 us
    while x117, local copies, waits for them, and re-layouts  29.7 us
  transfers between devices with their start and end apart: 18, of which 18 were waited for; matrix products, arithmetic and copies ran while one was open for 4% of the time, Pallas kernels for 0%

profile of v2, /device:TPU:25, one launch (start us, length us, event | category | flops | bytes accessed | tf_op | source)
XLA Modules:
  0.0 918.9 jit_solution(17026684552167302790)
XLA Ops:
  14.5 7.9 pad_maximum_fusion.3
  22.6 2.3 and_select_fusion
  26.5 885.9 %while.17 = (s32[]{:T(128)}, bf16[128,4096]{1,0:T(8,128)(2,1)S(1)}, bf16[2,128,4096]{2,1,0:T(8,128)(2,1)}, s32[]{:T(128)}, bf16[1,2,128,4096]{3,2,1,0:T(8,128)(2...) while((s32[]{:T(128)}, bf16[128,4096]{1,0:T(8,128)(2,1)S(1)}, ...), condition=%wide.region_9.10_spmd.clone, body=%wide.region_7.9_spmd.clone.sunk | while | flops 1085276288 | bytes 94523320 | solution.py:188
  27.9 3.4 collective-permute-done
  31.3 1.7 fusion.21
  33.0 5.1 fusion.22
  44.2 60.7 %all-gather.2.cloned.1.call-done.k_ref.v_ref = bf16[2048,1024]{1,0:T(8,128)(2,1)} async-done(((bf16[128,1024]{1,0:T(8,128)(2,1)}), bf16[2048,1024]{1,0:T(8,128)(2,1)}) %all-gather.2.cloned.1.call-update) | async-done | bytes 4194320 | tf_op jit(solution)/shard_map/while/body/eval_jaxpr/all_gather | solution.py:157
  104.9 19.8 %eval_jaxpr.6 = bf16[128,4096]{1,0:T(8,128)(2,1)} custom-call(bf16[128,4096]{1,0:T(8,128)(2,1)} %bitcast.54, bf16[2048,1024]{1,0:T(8,128)(2,1)} %all-gather.2.cloned.1.call-done.k_ref.v_ref, bf16[2048,1024]{1,0:T(8,128)(2,1)} %all-gather.2.cloned.1.call-done.k_ref.v_ref, f32[128,2048]{1,0:T(8,128)} %dynamic-slice_bitcast_fusion.6.bias_ref, ...), custom_call_target="tpu_custom_call" | custom-call | tf_op jit(solution)/shard_map/while/body/eval_jaxpr/pallas_call | solution.py:95
  128.0 3.4 collective-permute-done
  131.4 1.7 fusion.21
  133.1 5.1 fusion.22
  144.3 58.2 %all-gather.2.cloned.1.call-done.k_ref.v_ref = bf16[2048,1024]{1,0:T(8,128)(2,1)} async-done(((bf16[128,1024]{1,0:T(8,128)(2,1)}), bf16[2048,1024]{1,0:T(8,128)(2,1)}) %all-gather.2.cloned.1.call-update) | async-done | bytes 4194320 | tf_op jit(solution)/shard_map/while/body/eval_jaxpr/all_gather | solution.py:157
  202.4 19.8 %eval_jaxpr.6 = bf16[128,4096]{1,0:T(8,128)(2,1)} custom-call(bf16[128,4096]{1,0:T(8,128)(2,1)} %bitcast.54, bf16[2048,1024]{1,0:T(8,128)(2,1)} %all-gather.2.cloned.1.call-done.k_ref.v_ref, bf16[2048,1024]{1,0:T(8,128)(2,1)} %all-gather.2.cloned.1.call-done.k_ref.v_ref, f32[128,2048]{1,0:T(8,128)} %dynamic-slice_bitcast_fusion.6.bias_ref, ...), custom_call_target="tpu_custom_call" | custom-call | tf_op jit(solution)/shard_map/while/body/eval_jaxpr/pallas_call | solution.py:95
  225.5 3.4 collective-permute-done
  228.9 1.7 fusion.21
  230.6 5.1 fusion.22
  241.8 58.2 %all-gather.2.cloned.1.call-done.k_ref.v_ref = bf16[2048,1024]{1,0:T(8,128)(2,1)} async-done(((bf16[128,1024]{1,0:T(8,128)(2,1)}), bf16[2048,1024]{1,0:T(8,128)(2,1)}) %all-gather.2.cloned.1.call-update) | async-done | bytes 4194320 | tf_op jit(solution)/shard_map/while/body/eval_jaxpr/all_gather | solution.py:157
  300.0 19.8 %eval_jaxpr.6 = bf16[128,4096]{1,0:T(8,128)(2,1)} custom-call(bf16[128,4096]{1,0:T(8,128)(2,1)} %bitcast.54, bf16[2048,1024]{1,0:T(8,128)(2,1)} %all-gather.2.cloned.1.call-done.k_ref.v_ref, bf16[2048,1024]{1,0:T(8,128)(2,1)} %all-gather.2.cloned.1.call-done.k_ref.v_ref, f32[128,2048]{1,0:T(8,128)} %dynamic-slice_bitcast_fusion.6.bias_ref, ...), custom_call_target="tpu_custom_call" | custom-call | tf_op jit(solution)/shard_map/while/body/eval_jaxpr/pallas_call | solution.py:95
  323.0 3.4 collective-permute-done
  326.4 1.7 fusion.21
  328.1 5.1 fusion.22
  339.4 58.1 %all-gather.2.cloned.1.call-done.k_ref.v_ref = bf16[2048,1024]{1,0:T(8,128)(2,1)} async-done(((bf16[128,1024]{1,0:T(8,128)(2,1)}), bf16[2048,1024]{1,0:T(8,128)(2,1)}) %all-gather.2.cloned.1.call-update) | async-done | bytes 4194320 | tf_op jit(solution)/shard_map/while/body/eval_jaxpr/all_gather | solution.py:157
  397.5 19.8 %eval_jaxpr.6 = bf16[128,4096]{1,0:T(8,128)(2,1)} custom-call(bf16[128,4096]{1,0:T(8,128)(2,1)} %bitcast.54, bf16[2048,1024]{1,0:T(8,128)(2,1)} %all-gather.2.cloned.1.call-done.k_ref.v_ref, bf16[2048,1024]{1,0:T(8,128)(2,1)} %all-gather.2.cloned.1.call-done.k_ref.v_ref, f32[128,2048]{1,0:T(8,128)} %dynamic-slice_bitcast_fusion.6.bias_ref, ...), custom_call_target="tpu_custom_call" | custom-call | tf_op jit(solution)/shard_map/while/body/eval_jaxpr/pallas_call | solution.py:95
  420.6 3.4 collective-permute-done
  424.0 1.7 fusion.21
  425.7 5.1 fusion.22
  436.9 58.2 %all-gather.2.cloned.1.call-done.k_ref.v_ref = bf16[2048,1024]{1,0:T(8,128)(2,1)} async-done(((bf16[128,1024]{1,0:T(8,128)(2,1)}), bf16[2048,1024]{1,0:T(8,128)(2,1)}) %all-gather.2.cloned.1.call-update) | async-done | bytes 4194320 | tf_op jit(solution)/shard_map/while/body/eval_jaxpr/all_gather | solution.py:157
  495.0 19.8 %eval_jaxpr.6 = bf16[128,4096]{1,0:T(8,128)(2,1)} custom-call(bf16[128,4096]{1,0:T(8,128)(2,1)} %bitcast.54, bf16[2048,1024]{1,0:T(8,128)(2,1)} %all-gather.2.cloned.1.call-done.k_ref.v_ref, bf16[2048,1024]{1,0:T(8,128)(2,1)} %all-gather.2.cloned.1.call-done.k_ref.v_ref, f32[128,2048]{1,0:T(8,128)} %dynamic-slice_bitcast_fusion.6.bias_ref, ...), custom_call_target="tpu_custom_call" | custom-call | tf_op jit(solution)/shard_map/while/body/eval_jaxpr/pallas_call | solution.py:95
  518.1 3.4 collective-permute-done
  521.5 1.7 fusion.21
  523.2 5.1 fusion.22
  534.4 59.4 %all-gather.2.cloned.1.call-done.k_ref.v_ref = bf16[2048,1024]{1,0:T(8,128)(2,1)} async-done(((bf16[128,1024]{1,0:T(8,128)(2,1)}), bf16[2048,1024]{1,0:T(8,128)(2,1)}) %all-gather.2.cloned.1.call-update) | async-done | bytes 4194320 | tf_op jit(solution)/shard_map/while/body/eval_jaxpr/all_gather | solution.py:157
  593.8 19.8 %eval_jaxpr.6 = bf16[128,4096]{1,0:T(8,128)(2,1)} custom-call(bf16[128,4096]{1,0:T(8,128)(2,1)} %bitcast.54, bf16[2048,1024]{1,0:T(8,128)(2,1)} %all-gather.2.cloned.1.call-done.k_ref.v_ref, bf16[2048,1024]{1,0:T(8,128)(2,1)} %all-gather.2.cloned.1.call-done.k_ref.v_ref, f32[128,2048]{1,0:T(8,128)} %dynamic-slice_bitcast_fusion.6.bias_ref, ...), custom_call_target="tpu_custom_call" | custom-call | tf_op jit(solution)/shard_map/while/body/eval_jaxpr/pallas_call | solution.py:95
  616.9 3.4 collective-permute-done
  620.3 1.7 fusion.21
  622.0 5.1 fusion.22
  633.2 59.4 %all-gather.2.cloned.1.call-done.k_ref.v_ref = bf16[2048,1024]{1,0:T(8,128)(2,1)} async-done(((bf16[128,1024]{1,0:T(8,128)(2,1)}), bf16[2048,1024]{1,0:T(8,128)(2,1)}) %all-gather.2.cloned.1.call-update) | async-done | bytes 4194320 | tf_op jit(solution)/shard_map/while/body/eval_jaxpr/all_gather | solution.py:157
  692.5 19.8 %eval_jaxpr.6 = bf16[128,4096]{1,0:T(8,128)(2,1)} custom-call(bf16[128,4096]{1,0:T(8,128)(2,1)} %bitcast.54, bf16[2048,1024]{1,0:T(8,128)(2,1)} %all-gather.2.cloned.1.call-done.k_ref.v_ref, bf16[2048,1024]{1,0:T(8,128)(2,1)} %all-gather.2.cloned.1.call-done.k_ref.v_ref, f32[128,2048]{1,0:T(8,128)} %dynamic-slice_bitcast_fusion.6.bias_ref, ...), custom_call_target="tpu_custom_call" | custom-call | tf_op jit(solution)/shard_map/while/body/eval_jaxpr/pallas_call | solution.py:95
  715.6 4.6 collective-permute-done
  721.9 5.1 fusion.22
  733.1 57.9 %all-gather.2.cloned.1.call-done.k_ref.v_ref = bf16[2048,1024]{1,0:T(8,128)(2,1)} async-done(((bf16[128,1024]{1,0:T(8,128)(2,1)}), bf16[2048,1024]{1,0:T(8,128)(2,1)}) %all-gather.2.cloned.1.call-update) | async-done | bytes 4194320 | tf_op jit(solution)/shard_map/while/body/eval_jaxpr/all_gather | solution.py:157
  791.0 19.8 %eval_jaxpr.6 = bf16[128,4096]{1,0:T(8,128)(2,1)} custom-call(bf16[128,4096]{1,0:T(8,128)(2,1)} %bitcast.54, bf16[2048,1024]{1,0:T(8,128)(2,1)} %all-gather.2.cloned.1.call-done.k_ref.v_ref, bf16[2048,1024]{1,0:T(8,128)(2,1)} %all-gather.2.cloned.1.call-done.k_ref.v_ref, f32[128,2048]{1,0:T(8,128)} %dynamic-slice_bitcast_fusion.6.bias_ref, ...), custom_call_target="tpu_custom_call" | custom-call | tf_op jit(solution)/shard_map/while/body/eval_jaxpr/pallas_call | solution.py:95
  810.9 1.7 fusion.23
  815.3 3.4 collective-permute-done
  820.4 5.1 fusion.22
  831.6 57.9 %all-gather.2.cloned.1.call-done.k_ref.v_ref = bf16[2048,1024]{1,0:T(8,128)(2,1)} async-done(((bf16[128,1024]{1,0:T(8,128)(2,1)}), bf16[2048,1024]{1,0:T(8,128)(2,1)}) %all-gather.2.cloned.1.call-update) | async-done | bytes 4194320 | tf_op jit(solution)/shard_map/while/body/eval_jaxpr/all_gather | solution.py:157
  889.5 19.8 %eval_jaxpr.6 = bf16[128,4096]{1,0:T(8,128)(2,1)} custom-call(bf16[128,4096]{1,0:T(8,128)(2,1)} %bitcast.54, bf16[2048,1024]{1,0:T(8,128)(2,1)} %all-gather.2.cloned.1.call-done.k_ref.v_ref, bf16[2048,1024]{1,0:T(8,128)(2,1)} %all-gather.2.cloned.1.call-done.k_ref.v_ref, f32[128,2048]{1,0:T(8,128)} %dynamic-slice_bitcast_fusion.6.bias_ref, ...), custom_call_target="tpu_custom_call" | custom-call | tf_op jit(solution)/shard_map/while/body/eval_jaxpr/pallas_call | solution.py:95
  909.3 1.7 fusion.23
  (296 shorter events, 94.6 us)
Async XLA Ops:
  22.6 3.9 copy-start.5
  26.5 78.4 %all-gather.2.cloned.1.call-start = ((), (), s32[]{:S(2)}) async-start(), calls=%async_computation | async-start | bytes 4456448 | tf_op jit(solution)/shard_map/while/body/eval_jaxpr/all_gather | solution.py:157
  26.6 4.7 collective-permute-start
  33.0 5.1 copy-start
  38.1 1.6 copy-start.4
  41.1 2.0 copy-start.1
  104.9 19.8 %copy-start.2 = (bf16[2,128,4096]{2,1,0:T(8,128)(2,1)S(1)}, bf16[2,128,4096]{2,1,0:T(8,128)(2,1)}, u32[]{:S(2)}) copy-start(bf16[2,128,4096]{2,1,0:T(8,128)(2,1)} %get-tuple-element.435) | copy-start | bytes 6291460 | tf_op jit(solution)/shard_map/while
  126.6 75.9 %all-gather.2.cloned.1.call-start = ((), (), s32[]{:S(2)}) async-start(), calls=%async_computation | async-start | bytes 4456448 | tf_op jit(solution)/shard_map/while/body/eval_jaxpr/all_gather | solution.py:157
  126.6 4.7 collective-permute-start
  133.1 5.1 copy-start
  141.2 2.0 copy-start.1
  202.4 19.8 %copy-start.2 = (bf16[2,128,4096]{2,1,0:T(8,128)(2,1)S(1)}, bf16[2,128,4096]{2,1,0:T(8,128)(2,1)}, u32[]{:S(2)}) copy-start(bf16[2,128,4096]{2,1,0:T(8,128)(2,1)} %get-tuple-element.435) | copy-start | bytes 6291460 | tf_op jit(solution)/shard_map/while
  224.1 75.9 %all-gather.2.cloned.1.call-start = ((), (), s32[]{:S(2)}) async-start(), calls=%async_computation | async-start | bytes 4456448 | tf_op jit(solution)/shard_map/while/body/eval_jaxpr/all_gather | solution.py:157
  224.2 4.7 collective-permute-start
  230.6 5.1 copy-start
  235.7 1.6 copy-start.4
  238.7 2.0 copy-start.1
  300.0 19.8 %copy-start.2 = (bf16[2,128,4096]{2,1,0:T(8,128)(2,1)S(1)}, bf16[2,128,4096]{2,1,0:T(8,128)(2,1)}, u32[]{:S(2)}) copy-start(bf16[2,128,4096]{2,1,0:T(8,128)(2,1)} %get-tuple-element.435) | copy-start | bytes 6291460 | tf_op jit(solution)/shard_map/while
  321.6 75.9 %all-gather.2.cloned.1.call-start = ((), (), s32[]{:S(2)}) async-start(), calls=%async_computation | async-start | bytes 4456448 | tf_op jit(solution)/shard_map/while/body/eval_jaxpr/all_gather | solution.py:157
  321.7 4.7 collective-permute-start
  328.1 5.1 copy-start
  336.2 2.0 copy-start.1
  397.5 19.8 %copy-start.2 = (bf16[2,128,4096]{2,1,0:T(8,128)(2,1)S(1)}, bf16[2,128,4096]{2,1,0:T(8,128)(2,1)}, u32[]{:S(2)}) copy-start(bf16[2,128,4096]{2,1,0:T(8,128)(2,1)} %get-tuple-element.435) | copy-start | bytes 6291460 | tf_op jit(solution)/shard_map/while
  419.2 75.9 %all-gather.2.cloned.1.call-start = ((), (), s32[]{:S(2)}) async-start(), calls=%async_computation | async-start | bytes 4456448 | tf_op jit(solution)/shard_map/while/body/eval_jaxpr/all_gather | solution.py:157
  419.2 4.7 collective-permute-start
  425.7 5.1 copy-start
  433.8 2.0 copy-start.1
  495.0 19.8 %copy-start.2 = (bf16[2,128,4096]{2,1,0:T(8,128)(2,1)S(1)}, bf16[2,128,4096]{2,1,0:T(8,128)(2,1)}, u32[]{:S(2)}) copy-start(bf16[2,128,4096]{2,1,0:T(8,128)(2,1)} %get-tuple-element.435) | copy-start | bytes 6291460 | tf_op jit(solution)/shard_map/while
  516.7 77.1 %all-gather.2.cloned.1.call-start = ((), (), s32[]{:S(2)}) async-start(), calls=%async_computation | async-start | bytes 4456448 | tf_op jit(solution)/shard_map/while/body/eval_jaxpr/all_gather | solution.py:157
  516.8 4.7 collective-permute-start
  523.2 5.1 copy-start
  531.3 2.0 copy-start.1
  593.8 19.8 %copy-start.2 = (bf16[2,128,4096]{2,1,0:T(8,128)(2,1)S(1)}, bf16[2,128,4096]{2,1,0:T(8,128)(2,1)}, u32[]{:S(2)}) copy-start(bf16[2,128,4096]{2,1,0:T(8,128)(2,1)} %get-tuple-element.435) | copy-start | bytes 6291460 | tf_op jit(solution)/shard_map/while
  615.4 77.1 %all-gather.2.cloned.1.call-start = ((), (), s32[]{:S(2)}) async-start(), calls=%async_computation | async-start | bytes 4456448 | tf_op jit(solution)/shard_map/while/body/eval_jaxpr/all_gather | solution.py:157
  615.5 4.7 collective-permute-start
  621.9 5.1 copy-start
  630.1 2.0 copy-start.1
  692.5 19.8 %copy-start.2 = (bf16[2,128,4096]{2,1,0:T(8,128)(2,1)S(1)}, bf16[2,128,4096]{2,1,0:T(8,128)(2,1)}, u32[]{:S(2)}) copy-start(bf16[2,128,4096]{2,1,0:T(8,128)(2,1)} %get-tuple-element.435) | copy-start | bytes 6291460 | tf_op jit(solution)/shard_map/while
  714.2 76.8 %all-gather.2.cloned.1.call-start = ((), (), s32[]{:S(2)}) async-start(), calls=%async_computation | async-start | bytes 4456448 | tf_op jit(solution)/shard_map/while/body/eval_jaxpr/all_gather | solution.py:157
  714.3 6.0 collective-permute-start
  721.9 5.1 copy-start
  730.0 2.0 copy-start.1
  791.0 19.8 %copy-start.2 = (bf16[2,128,4096]{2,1,0:T(8,128)(2,1)S(1)}, bf16[2,128,4096]{2,1,0:T(8,128)(2,1)}, u32[]{:S(2)}) copy-start(bf16[2,128,4096]{2,1,0:T(8,128)(2,1)} %get-tuple-element.435) | copy-start | bytes 6291460 | tf_op jit(solution)/shard_map/while
  813.9 75.6 %all-gather.2.cloned.1.call-start = ((), (), s32[]{:S(2)}) async-start(), calls=%async_computation | async-start | bytes 4456448 | tf_op jit(solution)/shard_map/while/body/eval_jaxpr/all_gather | solution.py:157
  814.0 4.7 collective-permute-start
  820.4 5.1 copy-start
  828.5 2.0 copy-start.1
  889.5 19.8 %copy-start.2 = (bf16[2,128,4096]{2,1,0:T(8,128)(2,1)S(1)}, bf16[2,128,4096]{2,1,0:T(8,128)(2,1)}, u32[]{:S(2)}) copy-start(bf16[2,128,4096]{2,1,0:T(8,128)(2,1)} %get-tuple-element.435) | copy-start | bytes 6291460 | tf_op jit(solution)/shard_map/while
  (16 other events, 23.1 us)
Sparse Core Ops, SparseCore 0:
  39.7 65.1 all-gather.1
  139.8 62.6 all-gather.1
  237.3 62.6 all-gather.1
  334.8 62.6 all-gather.1
  432.4 62.6 all-gather.1
  529.9 63.8 all-gather.1
  628.6 63.8 all-gather.1
  728.6 62.3 all-gather.1
  827.1 62.3 all-gather.1

commit v3 on v2

--- a/solution.py
+++ b/solution.py
@@ -61,7 +61,8 @@
     return jnp.sum(chosen, axis=2).reshape(micro_count, seq_len)
 
 
-def attention_kernel(q_ref, k_ref, v_ref, bias_ref, res_ref, o_ref):
+def attention_kernel(q_ref, k_ref, v_ref, bias_ref, res_ref, *rest):
+    o_ref = rest[-1]
     ratio = HQ // HK
     scale = 1.0 / math.sqrt(HD)
     keys = k_ref[...]
@@ -88,23 +89,32 @@
         ).astype(o_ref.dtype)
 
 
-def attention(turned, kv_all, bias, residual):
+def attention(turned, kv_part, bias, residual, first, base=None):
     rows, width = turned.shape
-    keys_len = kv_all.shape[0]
+    keys_len = kv_part.shape[0]
     group = width // HK
+    heads = kv_part.shape[1] // (2 * HD)
+    in_specs = [
+        pl.BlockSpec((rows, group), lambda k: (0, first + k)),
+        pl.BlockSpec((keys_len, HD), lambda k: (0, k)),
+        pl.BlockSpec((keys_len, HD), lambda k: (0, heads + k)),
+        pl.BlockSpec((rows, keys_len), lambda k: (0, 0)),
+        pl.BlockSpec((rows, group), lambda k: (0, first + k)),
+    ]
+    operands = [turned, kv_part, kv_part, bias, residual]
+    aliases = {}
+    if base is not None:
+        in_specs.append(pl.BlockSpec(memory_space=pl.ANY))
+        operands.append(base)
+        aliases = {len(operands) - 1: 0}
     return pl.pallas_call(
         attention_kernel,
-        grid=(HK,),
-        in_specs=[
-            pl.BlockSpec((rows, group), lambda k: (0, k)),
-            pl.BlockSpec((keys_len, HD), lambda k: (0, k)),
-            pl.BlockSpec((keys_len, HD), lambda k: (0, HK + k)),
-            pl.BlockSpec((rows, keys_len), lambda k: (0, 0)),
-            pl.BlockSpec((rows, group), lambda k: (0, k)),
-        ],
-        out_specs=pl.BlockSpec((rows, group), lambda k: (0, k)),
+        grid=(heads,),
+        in_specs=in_specs,
+        out_specs=pl.BlockSpec((rows, group), lambda k: (0, first + k)),
         out_shape=jax.ShapeDtypeStruct((rows, width), jnp.bfloat16),
-    )(turned, kv_all, kv_all, bias, residual)
+        input_output_aliases=aliases,
+    )(*operands)
 
 
 def local(hidden, queries, gain, key_weight, value_weight, tree_ids, branch_ids, span_order):
@@ -153,8 +163,11 @@
             .reshape(row_count, HK * HD)
         )
         value_rows = kv_proj[:, HK * HD :].astype(jnp.bfloat16)
-        kv_rows = jnp.concatenate([key_rows, value_rows], axis=1)
-        kv_all = lax.all_gather(kv_rows, "seq", axis=0, tiled=True)
+        half = HK // 2 * HD
+        kv_front = jnp.concatenate([key_rows[:, :half], value_rows[:, :half]], axis=1)
+        kv_back = jnp.concatenate([key_rows[:, half:], value_rows[:, half:]], axis=1)
+        front_all = lax.all_gather(kv_front, "seq", axis=0, tiled=True)
+        back_all = lax.all_gather(kv_back, "seq", axis=0, tiled=True)
         query_local = lax.dynamic_index_in_dim(queries[0], mb, 0, keepdims=False)
         turned = (
             rotate(
@@ -165,7 +178,8 @@
             .astype(jnp.bfloat16)
             .reshape(row_count, HQ * HD)
         )
-        return attention(turned, kv_all, bias, current)
+        partial = attention(turned, front_all, bias, current, 0)
+        return attention(turned, back_all, bias, current, HK // 2, partial)
 
     tick_count = section_count + micro_count - 1
 

time: 921 us -> 1200 us (1.30)
  waiting for transfers between devices: 560 us -> 813 us
  Pallas kernels: 179 us -> 200 us
    all_gather x9 -> x18, waiting for transfers between devices: 528 us -> 772 us  [the longest x9 453 us: run_layer(): front_all = lax.all_gather(kv_front, 'seq', axis=0, tiled=True)]
    pallas_call x9 -> x18, Pallas kernels: 179 us -> 200 us  [attention(): pl.pallas_call(attention_kernel, grid=(heads,), in_specs=in_specs, out_sp...]
    while x117 -> x153, local copies, waits for them, and re-layouts: 29.7 us -> 28.4 us
  transfers between devices with their start and end apart: 18 -> 27, of which waited for: 18 -> 27; matrix products, arithmetic and copies ran while one was open for 4% -> 4% of each run, Pallas kernels for 0% -> 8%
where the time goes in v3:
time: 1200 us
  waiting for transfers between devices  813 us (68%)
  Pallas kernels  200 us (17%)
  other arithmetic  69.4 us (6%)
  matrix products  45.9 us (4%)
  local copies, waits for them, and re-layouts  42.9 us (4%)
  between operations  13.5 us (1%)
  starting transfers between devices  12 us (1%)
    all_gather x9, waiting for transfers between devices, run_layer(): front_all = lax.all_gather(kv_front, 'seq', axis=0, tiled=True)  453 us
    all_gather x9, waiting for transfers between devices, run_layer(): back_all = lax.all_gather(kv_back, 'seq', axis=0, tiled=True)  319 us
    pallas_call x18, Pallas kernels, attention(): pl.pallas_call(attention_kernel, grid=(heads,), in_specs=in_specs, out_sp...  200 us
    dot_general x9, matrix products, run_layer(): kv_proj = jnp.dot(normed, kv_mat, preferred_element_type=jnp.float32)  45.9 us
    ppermute x9, waiting for transfers between devices, from_behind(): return lax.ppermute(value, axis, pairs)  40.3 us
    while x153, local copies, waits for them, and re-layouts  28.4 us
  transfers between devices with their start and end apart: 27, of which 27 were waited for; matrix products, arithmetic and copies ran while one was open for 4% of the time, Pallas kernels for 8%

profile of v3, /device:TPU:25, one launch (start us, length us, event | category | flops | bytes accessed | tf_op | source)
XLA Modules:
  0.0 1199.0 jit_solution(12289523679891820959)
XLA Ops:
  17.1 7.9 pad_maximum_fusion.4
  26.5 1165.7 %while.17 = (s32[]{:T(128)}, bf16[128,4096]{1,0:T(8,128)(2,1)S(1)}, bf16[2,128,4096]{2,1,0:T(8,128)(2,1)}, s32[]{:T(128)}, bf16[1,2,128,4096]{3,2,1,0:T(8,128)(2...) while((s32[]{:T(128)}, bf16[128,4096]{1,0:T(8,128)(2,1)S(1)}, ...), condition=%wide.region_9.10_spmd.clone, body=%wide.region_7.9_spmd.clone.sunk | while | flops 1085407360 | bytes 95571992 | solution.py:202
  33.0 5.1 fusion.25
  44.8 52.6 %all-gather.5.cloned.1.call-done.k_ref.v_ref = bf16[2048,512]{1,0:T(8,128)(2,1)} async-done(((bf16[128,512]{1,0:T(8,128)(2,1)}), bf16[2048,512]{1,0:T(8,128)(2,1)}) %all-gather.5.cloned.1.call-update) | async-done | bytes 2097168 | tf_op jit(solution)/shard_map/while/body/eval_jaxpr/all_gather | solution.py:169
  97.4 11.1 eval_jaxpr.7.rest_0_
  108.5 35.6 %all-gather.3.cloned.1.call-done.k_ref.v_ref = bf16[2048,512]{1,0:T(8,128)(2,1)} async-done(((bf16[128,512]{1,0:T(8,128)(2,1)}), bf16[2048,512]{1,0:T(8,128)(2,1)}) %all-gather.3.cloned.1.call-update) | async-done | bytes 2097168 | tf_op jit(solution)/shard_map/while/body/eval_jaxpr/all_gather | solution.py:170
  144.1 11.1 eval_jaxpr.8
  164.7 5.1 fusion.25
  176.4 49.8 %all-gather.5.cloned.1.call-done.k_ref.v_ref = bf16[2048,512]{1,0:T(8,128)(2,1)} async-done(((bf16[128,512]{1,0:T(8,128)(2,1)}), bf16[2048,512]{1,0:T(8,128)(2,1)}) %all-gather.5.cloned.1.call-update) | async-done | bytes 2097168 | tf_op jit(solution)/shard_map/while/body/eval_jaxpr/all_gather | solution.py:169
  226.2 11.1 eval_jaxpr.7.rest_0_
  237.3 35.4 %all-gather.3.cloned.1.call-done.k_ref.v_ref = bf16[2048,512]{1,0:T(8,128)(2,1)} async-done(((bf16[128,512]{1,0:T(8,128)(2,1)}), bf16[2048,512]{1,0:T(8,128)(2,1)}) %all-gather.3.cloned.1.call-update) | async-done | bytes 2097168 | tf_op jit(solution)/shard_map/while/body/eval_jaxpr/all_gather | solution.py:170
  272.8 11.1 eval_jaxpr.8
  293.3 5.1 fusion.25
  305.0 49.8 %all-gather.5.cloned.1.call-done.k_ref.v_ref = bf16[2048,512]{1,0:T(8,128)(2,1)} async-done(((bf16[128,512]{1,0:T(8,128)(2,1)}), bf16[2048,512]{1,0:T(8,128)(2,1)}) %all-gather.5.cloned.1.call-update) | async-done | bytes 2097168 | tf_op jit(solution)/shard_map/while/body/eval_jaxpr/all_gather | solution.py:169
  354.8 11.1 eval_jaxpr.7.rest_0_
  366.0 35.4 %all-gather.3.cloned.1.call-done.k_ref.v_ref = bf16[2048,512]{1,0:T(8,128)(2,1)} async-done(((bf16[128,512]{1,0:T(8,128)(2,1)}), bf16[2048,512]{1,0:T(8,128)(2,1)}) %all-gather.3.cloned.1.call-update) | async-done | bytes 2097168 | tf_op jit(solution)/shard_map/while/body/eval_jaxpr/all_gather | solution.py:170
  401.4 11.1 eval_jaxpr.8
  422.0 5.1 fusion.25
  433.7 49.8 %all-gather.5.cloned.1.call-done.k_ref.v_ref = bf16[2048,512]{1,0:T(8,128)(2,1)} async-done(((bf16[128,512]{1,0:T(8,128)(2,1)}), bf16[2048,512]{1,0:T(8,128)(2,1)}) %all-gather.5.cloned.1.call-update) | async-done | bytes 2097168 | tf_op jit(solution)/shard_map/while/body/eval_jaxpr/all_gather | solution.py:169
  483.5 11.1 eval_jaxpr.7.rest_0_
  494.6 35.6 %all-gather.3.cloned.1.call-done.k_ref.v_ref = bf16[2048,512]{1,0:T(8,128)(2,1)} async-done(((bf16[128,512]{1,0:T(8,128)(2,1)}), bf16[2048,512]{1,0:T(8,128)(2,1)}) %all-gather.3.cloned.1.call-update) | async-done | bytes 2097168 | tf_op jit(solution)/shard_map/while/body/eval_jaxpr/all_gather | solution.py:170
  530.2 11.1 eval_jaxpr.8
  550.8 5.1 fusion.25
  562.5 49.8 %all-gather.5.cloned.1.call-done.k_ref.v_ref = bf16[2048,512]{1,0:T(8,128)(2,1)} async-done(((bf16[128,512]{1,0:T(8,128)(2,1)}), bf16[2048,512]{1,0:T(8,128)(2,1)}) %all-gather.5.cloned.1.call-update) | async-done | bytes 2097168 | tf_op jit(solution)/shard_map/while/body/eval_jaxpr/all_gather | solution.py:169
  612.3 11.1 eval_jaxpr.7.rest_0_
  623.4 35.4 %all-gather.3.cloned.1.call-done.k_ref.v_ref = bf16[2048,512]{1,0:T(8,128)(2,1)} async-done(((bf16[128,512]{1,0:T(8,128)(2,1)}), bf16[2048,512]{1,0:T(8,128)(2,1)}) %all-gather.3.cloned.1.call-update) | async-done | bytes 2097168 | tf_op jit(solution)/shard_map/while/body/eval_jaxpr/all_gather | solution.py:170
  658.8 11.1 eval_jaxpr.8
  679.4 5.1 fusion.25
  691.1 51.1 %all-gather.5.cloned.1.call-done.k_ref.v_ref = bf16[2048,512]{1,0:T(8,128)(2,1)} async-done(((bf16[128,512]{1,0:T(8,128)(2,1)}), bf16[2048,512]{1,0:T(8,128)(2,1)}) %all-gather.5.cloned.1.call-update) | async-done | bytes 2097168 | tf_op jit(solution)/shard_map/while/body/eval_jaxpr/all_gather | solution.py:169
  742.2 11.1 eval_jaxpr.7.rest_0_
  753.3 35.4 %all-gather.3.cloned.1.call-done.k_ref.v_ref = bf16[2048,512]{1,0:T(8,128)(2,1)} async-done(((bf16[128,512]{1,0:T(8,128)(2,1)}), bf16[2048,512]{1,0:T(8,128)(2,1)}) %all-gather.3.cloned.1.call-update) | async-done | bytes 2097168 | tf_op jit(solution)/shard_map/while/body/eval_jaxpr/all_gather | solution.py:170
  788.7 11.1 eval_jaxpr.8
  809.3 5.1 fusion.25
  821.0 51.1 %all-gather.5.cloned.1.call-done.k_ref.v_ref = bf16[2048,512]{1,0:T(8,128)(2,1)} async-done(((bf16[128,512]{1,0:T(8,128)(2,1)}), bf16[2048,512]{1,0:T(8,128)(2,1)}) %all-gather.5.cloned.1.call-update) | async-done | bytes 2097168 | tf_op jit(solution)/shard_map/while/body/eval_jaxpr/all_gather | solution.py:169
  872.1 11.1 eval_jaxpr.7.rest_0_
  883.2 35.4 %all-gather.3.cloned.1.call-done.k_ref.v_ref = bf16[2048,512]{1,0:T(8,128)(2,1)} async-done(((bf16[128,512]{1,0:T(8,128)(2,1)}), bf16[2048,512]{1,0:T(8,128)(2,1)}) %all-gather.3.cloned.1.call-update) | async-done | bytes 2097168 | tf_op jit(solution)/shard_map/while/body/eval_jaxpr/all_gather | solution.py:170
  918.6 11.1 eval_jaxpr.8
  933.0 5.7 collective-permute-done
  940.5 5.1 fusion.25
  952.2 49.5 %all-gather.5.cloned.1.call-done.k_ref.v_ref = bf16[2048,512]{1,0:T(8,128)(2,1)} async-done(((bf16[128,512]{1,0:T(8,128)(2,1)}), bf16[2048,512]{1,0:T(8,128)(2,1)}) %all-gather.5.cloned.1.call-update) | async-done | bytes 2097168 | tf_op jit(solution)/shard_map/while/body/eval_jaxpr/all_gather | solution.py:169
  1001.7 11.1 eval_jaxpr.7.rest_0_
  1012.9 35.4 %all-gather.3.cloned.1.call-done.k_ref.v_ref = bf16[2048,512]{1,0:T(8,128)(2,1)} async-done(((bf16[128,512]{1,0:T(8,128)(2,1)}), bf16[2048,512]{1,0:T(8,128)(2,1)}) %all-gather.3.cloned.1.call-update) | async-done | bytes 2097168 | tf_op jit(solution)/shard_map/while/body/eval_jaxpr/all_gather | solution.py:170
  1048.3 11.1 eval_jaxpr.8
  1070.1 5.1 fusion.25
  1081.8 49.5 %all-gather.5.cloned.1.call-done.k_ref.v_ref = bf16[2048,512]{1,0:T(8,128)(2,1)} async-done(((bf16[128,512]{1,0:T(8,128)(2,1)}), bf16[2048,512]{1,0:T(8,128)(2,1)}) %all-gather.5.cloned.1.call-update) | async-done | bytes 2097168 | tf_op jit(solution)/shard_map/while/body/eval_jaxpr/all_gather | solution.py:169
  1131.3 11.1 eval_jaxpr.7.rest_0_
  1142.5 35.4 %all-gather.3.cloned.1.call-done.k_ref.v_ref = bf16[2048,512]{1,0:T(8,128)(2,1)} async-done(((bf16[128,512]{1,0:T(8,128)(2,1)}), bf16[2048,512]{1,0:T(8,128)(2,1)}) %all-gather.3.cloned.1.call-update) | async-done | bytes 2097168 | tf_op jit(solution)/shard_map/while/body/eval_jaxpr/all_gather | solution.py:170
  1177.9 11.1 eval_jaxpr.8
  (386 shorter events, 151.3 us)
Async XLA Ops:
  26.5 6.5 copy-start.6
  26.5 70.9 %all-gather.5.cloned.1.call-start = ((), (), s32[]{:S(2)}) async-start(), calls=%async_computation.1 | async-start | bytes 2228224 | tf_op jit(solution)/shard_map/while/body/eval_jaxpr/all_gather | solution.py:169
  26.6 4.7 collective-permute-start
  33.0 5.2 copy-start
  39.6 104.5 %all-gather.3.cloned.1.call-start = ((), (), s32[]{:S(2)}) async-start(), calls=%async_computation | async-start | bytes 2228224 | tf_op jit(solution)/shard_map/while/body/eval_jaxpr/all_gather | solution.py:170
  108.5 46.7 %copy-start.2 = (bf16[2,128,4096]{2,1,0:T(8,128)(2,1)S(1)}, bf16[2,128,4096]{2,1,0:T(8,128)(2,1)}, u32[]{:S(2)}) copy-start(bf16[2,128,4096]{2,1,0:T(8,128)(2,1)} %get-tuple-element.453) | copy-start | bytes 6291460 | tf_op jit(solution)/shard_map/while
  157.1 7.6 copy-start.6
  157.1 69.1 %all-gather.5.cloned.1.call-start = ((), (), s32[]{:S(2)}) async-start(), calls=%async_computation.1 | async-start | bytes 2228224 | tf_op jit(solution)/shard_map/while/body/eval_jaxpr/all_gather | solution.py:169
  157.2 5.8 collective-permute-start
  164.6 5.1 copy-start
  171.2 101.6 %all-gather.3.cloned.1.call-start = ((), (), s32[]{:S(2)}) async-start(), calls=%async_computation | async-start | bytes 2228224 | tf_op jit(solution)/shard_map/while/body/eval_jaxpr/all_gather | solution.py:170
  237.3 46.6 %copy-start.2 = (bf16[2,128,4096]{2,1,0:T(8,128)(2,1)S(1)}, bf16[2,128,4096]{2,1,0:T(8,128)(2,1)}, u32[]{:S(2)}) copy-start(bf16[2,128,4096]{2,1,0:T(8,128)(2,1)} %get-tuple-element.453) | copy-start | bytes 6291460 | tf_op jit(solution)/shard_map/while
  285.7 7.6 copy-start.6
  285.7 69.1 %all-gather.5.cloned.1.call-start = ((), (), s32[]{:S(2)}) async-start(), calls=%async_computation.1 | async-start | bytes 2228224 | tf_op jit(solution)/shard_map/while/body/eval_jaxpr/all_gather | solution.py:169
  285.8 5.8 collective-permute-start
  293.3 5.1 copy-start
  299.8 101.6 %all-gather.3.cloned.1.call-start = ((), (), s32[]{:S(2)}) async-start(), calls=%async_computation | async-start | bytes 2228224 | tf_op jit(solution)/shard_map/while/body/eval_jaxpr/all_gather | solution.py:170
  366.0 46.6 %copy-start.2 = (bf16[2,128,4096]{2,1,0:T(8,128)(2,1)S(1)}, bf16[2,128,4096]{2,1,0:T(8,128)(2,1)}, u32[]{:S(2)}) copy-start(bf16[2,128,4096]{2,1,0:T(8,128)(2,1)} %get-tuple-element.453) | copy-start | bytes 6291460 | tf_op jit(solution)/shard_map/while
  414.4 7.6 copy-start.6
  414.4 69.1 %all-gather.5.cloned.1.call-start = ((), (), s32[]{:S(2)}) async-start(), calls=%async_computation.1 | async-start | bytes 2228224 | tf_op jit(solution)/shard_map/while/body/eval_jaxpr/all_gather | solution.py:169
  414.5 5.8 collective-permute-start
  428.5 101.7 %all-gather.3.cloned.1.call-start = ((), (), s32[]{:S(2)}) async-start(), calls=%async_computation | async-start | bytes 2228224 | tf_op jit(solution)/shard_map/while/body/eval_jaxpr/all_gather | solution.py:170
  494.6 46.7 %copy-start.2 = (bf16[2,128,4096]{2,1,0:T(8,128)(2,1)S(1)}, bf16[2,128,4096]{2,1,0:T(8,128)(2,1)}, u32[]{:S(2)}) copy-start(bf16[2,128,4096]{2,1,0:T(8,128)(2,1)} %get-tuple-element.453) | copy-start | bytes 6291460 | tf_op jit(solution)/shard_map/while
  543.2 7.6 copy-start.6
  543.2 69.1 %all-gather.5.cloned.1.call-start = ((), (), s32[]{:S(2)}) async-start(), calls=%async_computation.1 | async-start | bytes 2228224 | tf_op jit(solution)/shard_map/while/body/eval_jaxpr/all_gather | solution.py:169
  543.3 5.8 collective-permute-start
  557.3 101.6 %all-gather.3.cloned.1.call-start = ((), (), s32[]{:S(2)}) async-start(), calls=%async_computation | async-start | bytes 2228224 | tf_op jit(solution)/shard_map/while/body/eval_jaxpr/all_gather | solution.py:170
  623.4 46.6 %copy-start.2 = (bf16[2,128,4096]{2,1,0:T(8,128)(2,1)S(1)}, bf16[2,128,4096]{2,1,0:T(8,128)(2,1)}, u32[]{:S(2)}) copy-start(bf16[2,128,4096]{2,1,0:T(8,128)(2,1)} %get-tuple-element.453) | copy-start | bytes 6291460 | tf_op jit(solution)/shard_map/while
  671.8 7.6 copy-start.6
  671.8 70.4 %all-gather.5.cloned.1.call-start = ((), (), s32[]{:S(2)}) async-start(), calls=%async_computation.1 | async-start | bytes 2228224 | tf_op jit(solution)/shard_map/while/body/eval_jaxpr/all_gather | solution.py:169
  671.9 5.8 collective-permute-start
  685.9 102.8 %all-gather.3.cloned.1.call-start = ((), (), s32[]{:S(2)}) async-start(), calls=%async_computation | async-start | bytes 2228224 | tf_op jit(solution)/shard_map/while/body/eval_jaxpr/all_gather | solution.py:170
  753.3 46.6 %copy-start.2 = (bf16[2,128,4096]{2,1,0:T(8,128)(2,1)S(1)}, bf16[2,128,4096]{2,1,0:T(8,128)(2,1)}, u32[]{:S(2)}) copy-start(bf16[2,128,4096]{2,1,0:T(8,128)(2,1)} %get-tuple-element.453) | copy-start | bytes 6291460 | tf_op jit(solution)/shard_map/while
  801.7 7.6 copy-start.6
  801.7 70.4 %all-gather.5.cloned.1.call-start = ((), (), s32[]{:S(2)}) async-start(), calls=%async_computation.1 | async-start | bytes 2228224 | tf_op jit(solution)/shard_map/while/body/eval_jaxpr/all_gather | solution.py:169
  801.8 5.8 collective-permute-start
  815.8 102.8 %all-gather.3.cloned.1.call-start = ((), (), s32[]{:S(2)}) async-start(), calls=%async_computation | async-start | bytes 2228224 | tf_op jit(solution)/shard_map/while/body/eval_jaxpr/all_gather | solution.py:170
  883.2 46.6 %copy-start.2 = (bf16[2,128,4096]{2,1,0:T(8,128)(2,1)S(1)}, bf16[2,128,4096]{2,1,0:T(8,128)(2,1)}, u32[]{:S(2)}) copy-start(bf16[2,128,4096]{2,1,0:T(8,128)(2,1)} %get-tuple-element.453) | copy-start | bytes 6291460 | tf_op jit(solution)/shard_map/while
  931.6 8.8 copy-start.6
  931.6 70.1 %all-gather.5.cloned.1.call-start = ((), (), s32[]{:S(2)}) async-start(), calls=%async_computation.1 | async-start | bytes 2228224 | tf_op jit(solution)/shard_map/while/body/eval_jaxpr/all_gather | solution.py:169
  931.7 7.0 collective-permute-start
  947.0 101.3 %all-gather.3.cloned.1.call-start = ((), (), s32[]{:S(2)}) async-start(), calls=%async_computation | async-start | bytes 2228224 | tf_op jit(solution)/shard_map/while/body/eval_jaxpr/all_gather | solution.py:170
  1012.8 46.6 %copy-start.2 = (bf16[2,128,4096]{2,1,0:T(8,128)(2,1)S(1)}, bf16[2,128,4096]{2,1,0:T(8,128)(2,1)}, u32[]{:S(2)}) copy-start(bf16[2,128,4096]{2,1,0:T(8,128)(2,1)} %get-tuple-element.453) | copy-start | bytes 6291460 | tf_op jit(solution)/shard_map/while
  1062.5 7.6 copy-start.6
  1062.5 68.8 %all-gather.5.cloned.1.call-start = ((), (), s32[]{:S(2)}) async-start(), calls=%async_computation.1 | async-start | bytes 2228224 | tf_op jit(solution)/shard_map/while/body/eval_jaxpr/all_gather | solution.py:169
  1062.6 5.8 collective-permute-start
  1076.6 101.3 %all-gather.3.cloned.1.call-start = ((), (), s32[]{:S(2)}) async-start(), calls=%async_computation | async-start | bytes 2228224 | tf_op jit(solution)/shard_map/while/body/eval_jaxpr/all_gather | solution.py:170
  1142.5 46.6 %copy-start.2 = (bf16[2,128,4096]{2,1,0:T(8,128)(2,1)S(1)}, bf16[2,128,4096]{2,1,0:T(8,128)(2,1)}, u32[]{:S(2)}) copy-start(bf16[2,128,4096]{2,1,0:T(8,128)(2,1)} %get-tuple-element.453) | copy-start | bytes 6291460 | tf_op jit(solution)/shard_map/while
  (43 other events, 100.6 us)
Sparse Core Ops, SparseCore 0:
  39.7 57.6 all-gather.4
  99.5 44.5 all-gather.2
  171.3 54.8 all-gather.4
  228.2 44.5 all-gather.2
  299.9 54.8 all-gather.4
  356.8 44.5 all-gather.2
  428.6 54.8 all-gather.4
  485.6 44.5 all-gather.2
  557.4 54.8 all-gather.4
  614.3 44.5 all-gather.2
  686.0 56.1 all-gather.4
  744.2 44.5 all-gather.2
  815.9 56.1 all-gather.4
  874.1 44.5 all-gather.2
  947.1 54.5 all-gather.4
  1003.7 44.5 all-gather.2
  1076.7 54.5 all-gather.4
  1133.3 44.5 all-gather.2

commit v4 on v2

--- a/solution.py
+++ b/solution.py
@@ -59,6 +59,59 @@
     picks = span_order[:, :, None] == jnp.arange(spans, dtype=jnp.int32)[None, None, :]
     chosen = jnp.where(picks[..., None], blocks, 0)
     return jnp.sum(chosen, axis=2).reshape(micro_count, seq_len)
+
+
+def ring_gather(value, shift):
+    ahead = shift(value, 1)
+    behind = shift(value, -1)
+    width = value.shape[1] // 2
+    far = jnp.concatenate(
+        [shift(ahead[:, :width], 1), shift(behind[:, width:], -1)], axis=1
+    )
+    return [value, ahead, behind, far]
+
+
+RING_OFFSETS = (0, -1, 1, 2)
+
+
+def torus_gather(value, side):
+    def shifter(along_z):
+        def shift(piece, by):
+            pairs = []
+            for z in range(side):
+                for x in range(side):
+                    if along_z:
+                        pairs.append((z * side + x, ((z + by) % side) * side + x))
+                    else:
+                        pairs.append((z * side + x, z * side + (x + by) % side))
+            return lax.ppermute(piece, "seq", pairs)
+
+        return shift
+
+    shift_z = shifter(True)
+    shift_x = shifter(False)
+    rows = value.shape[0]
+    width = value.shape[1] // 2
+    row_a = jnp.concatenate(ring_gather(value[:, :width], shift_x), axis=0)
+    full_a = jnp.concatenate(ring_gather(row_a, shift_z), axis=0)
+    col_b = jnp.concatenate(ring_gather(value[:, width:], shift_z), axis=0)
+    pieces_b = ring_gather(col_b, shift_x)
+    full_b = jnp.stack(pieces_b, axis=0).reshape(side, side, rows, width)
+    full_b = full_b.transpose(1, 0, 2, 3).reshape(side * side * rows, width)
+    return jnp.concatenate([full_a, full_b], axis=1)
+
+
+def torus_order(values, shard_id, side, rows):
+    micro_count = values.shape[0]
+    z = shard_id // side
+    x = shard_id % side
+    blocks = values.reshape(micro_count, side, side, rows)
+    blocks = jnp.roll(blocks, -z, axis=1)
+    blocks = jnp.roll(blocks, -x, axis=2)
+    picks = [o % side for o in RING_OFFSETS]
+    blocks = jnp.stack([blocks[:, p] for p in picks], axis=1)
+    blocks = jnp.stack([blocks[:, :, q] for q in picks], axis=2)
+    return blocks.reshape(micro_count, side * side * rows)
 
 
 def attention_kernel(q_ref, k_ref, v_ref, bias_ref, res_ref, o_ref):
@@ -124,10 +177,15 @@
     own_tree = lax.dynamic_slice_in_dim(key_tree, first_row, row_count, 1)
     own_branch = lax.dynamic_slice_in_dim(key_branch, first_row, row_count, 1)
     own_rotary = lax.dynamic_slice_in_dim(key_rotary, first_row, row_count, 1)
+    seq_count = lax.axis_size("seq")
+    side = math.isqrt(seq_count)
+    order_tree = torus_order(key_tree, shard_id, side, row_count)
+    order_branch = torus_order(key_branch, shard_id, side, row_count)
+    order_packed = torus_order(packed_all, shard_id, side, row_count)
     allowed = (
-        (own_tree[:, :, None] == key_tree[:, None, :])
-        & (packed_all[:, None, :] <= own_packed[:, :, None])
-        & ((key_branch[:, None, :] == 0) | (key_branch[:, None, :] == own_branch[:, :, None]))
+        (own_tree[:, :, None] == order_tree[:, None, :])
+        & (order_packed[:, None, :] <= own_packed[:, :, None])
+        & ((order_branch[:, None, :] == 0) | (order_branch[:, None, :] == own_branch[:, :, None]))
     )
     bias_all = jnp.where(allowed, 0.0, -jnp.inf).astype(jnp.float32)
     angles = own_rotary.astype(jnp.float32)[..., None] * frequencies()
@@ -154,7 +212,7 @@
         )
         value_rows = kv_proj[:, HK * HD :].astype(jnp.bfloat16)
         kv_rows = jnp.concatenate([key_rows, value_rows], axis=1)
-        kv_all = lax.all_gather(kv_rows, "seq", axis=0, tiled=True)
+        kv_all = torus_gather(kv_rows, side)
         query_local = lax.dynamic_index_in_dim(queries[0], mb, 0, keepdims=False)
         turned = (
             rotate(

time: 921 us -> 871 us (0.946)
  the two profiles are of different devices: /device:TPU:25 before, /device:TPU:14 now
where the time goes in v4:
time: 871 us; the launch traced here: 867 us
  waiting for transfers between devices  223 us (26%)
  starting transfers between devices  207 us (24%)
  Pallas kernels  179 us (21%)
  local copies, waits for them, and re-layouts  128 us (15%)
  other arithmetic  115 us (13%)
  matrix products  12.1 us (1%)
    ppermute x144, starting transfers between devices, shift(): return lax.ppermute(piece, 'seq', pairs)  189 us
    pallas_call x9, Pallas kernels, attention(): pl.pallas_call(attention_kernel, grid=(HK,), in_specs=[pl.BlockSpec((rows...  179 us
    ppermute x144, waiting for transfers between devices, shift(): return lax.ppermute(piece, 'seq', pairs)  128 us
    ppermute x9, waiting for transfers between devices, from_behind(): return lax.ppermute(value, axis, pairs)  95.4 us
    while x252, local copies, waits for them, and re-layouts  52.5 us
    concatenate x9, other arithmetic, torus_gather(): return jnp.concatenate([full_a, full_b], axis=1)  23.9 us
    squeeze x9, local copies, waits for them, and re-layouts, run_layer(): bias = lax.dynamic_index_in_dim(bias_all, mb, 0, keepdims=False)  20.7 us
  transfers between devices with their start and end apart: 153, of which 55 were waited for; matrix products, arithmetic and copies ran while one was open for 17% of the time, Pallas kernels for 0%

profile of v4, /device:TPU:14, one launch (start us, length us, event | category | flops | bytes accessed | tf_op | source)
XLA Modules:
  0.0 866.9 jit_solution(4051903202023601972)
XLA Ops:
  12.0 7.9 pad_maximum_fusion.5
  21.4 845.5 %while.17 = (s32[]{:T(128)}, bf16[128,4096]{1,0:T(8,128)(2,1)S(1)}, bf16[2,128,4096]{2,1,0:T(8,128)(2,1)}, s32[]{:T(128)}, bf16[1,2,128,4096]{3,2,1,0:T(8,128)(2...) while((s32[]{:T(128)}, bf16[128,4096]{1,0:T(8,128)(2,1)S(1)}, ...), condition=%wide.region_9.12_spmd.clone, body=%wide.region_7.11_spmd.clone.sunk | while | flops 1103626368 | bytes 138826384 | solution.py:246
  27.1 10.6 %collective-permute-done = bf16[128,4096]{1,0:T(8,128)(2,1)} collective-permute-done((bf16[128,4096]{1,0:T(8,128)(2,1)S(1)}, bf16[128,4096]{1,0:T(8,128)(2,1)}, u32[]{:S(2)}, u32[]{:S(2)}) %collective-permute-start) | collective-permute-done | bytes 1048608 | tf_op jit(solution)/shard_map/while/body/eval_jaxpr/ppermute | solution.py:22
  48.3 4.0 collective-permute-start.1
  58.6 3.2 collective-permute-start.2
  63.7 3.3 collective-permute-start.14
  74.2 7.9 collective-permute-done.5
  96.9 19.8 %eval_jaxpr.6 = bf16[128,4096]{1,0:T(8,128)(2,1)} custom-call(bf16[128,4096]{1,0:T(8,128)(2,1)} %bitcast.89, bf16[2048,1024]{1,0:T(8,128)(2,1)} %pad_maximum_fusion.15.k_ref.v_ref, bf16[2048,1024]{1,0:T(8,128)(2,1)} %pad_maximum_fusion.15.k_ref.v_ref, f32[128,2048]{1,0:T(8,128)} %dynamic-slice_bitcast_fusion.6.bias_ref, bf16[128,4096]{1,0:T(8,128)(2,1)} %copy-done), custom_call_target="tpu_custom_call" | custom-call | tf_op jit(solution)/shard_map/while/body/eval_jaxpr/pallas_call | solution.py:148
  124.3 10.6 %collective-permute-done = bf16[128,4096]{1,0:T(8,128)(2,1)} collective-permute-done((bf16[128,4096]{1,0:T(8,128)(2,1)S(1)}, bf16[128,4096]{1,0:T(8,128)(2,1)}, u32[]{:S(2)}, u32[]{:S(2)}) %collective-permute-start) | collective-permute-done | bytes 1048608 | tf_op jit(solution)/shard_map/while/body/eval_jaxpr/ppermute | solution.py:22
  163.9 3.3 collective-permute-start.7
  168.1 7.8 collective-permute-done.5
  176.0 3.3 collective-permute-start.8
  190.7 19.8 %eval_jaxpr.6 = bf16[128,4096]{1,0:T(8,128)(2,1)} custom-call(bf16[128,4096]{1,0:T(8,128)(2,1)} %bitcast.89, bf16[2048,1024]{1,0:T(8,128)(2,1)} %pad_maximum_fusion.15.k_ref.v_ref, bf16[2048,1024]{1,0:T(8,128)(2,1)} %pad_maximum_fusion.15.k_ref.v_ref, f32[128,2048]{1,0:T(8,128)} %dynamic-slice_bitcast_fusion.6.bias_ref, bf16[128,4096]{1,0:T(8,128)(2,1)} %copy-done), custom_call_target="tpu_custom_call" | custom-call | tf_op jit(solution)/shard_map/while/body/eval_jaxpr/pallas_call | solution.py:148
  218.0 10.6 %collective-permute-done = bf16[128,4096]{1,0:T(8,128)(2,1)} collective-permute-done((bf16[128,4096]{1,0:T(8,128)(2,1)S(1)}, bf16[128,4096]{1,0:T(8,128)(2,1)}, u32[]{:S(2)}, u32[]{:S(2)}) %collective-permute-start) | collective-permute-done | bytes 1048608 | tf_op jit(solution)/shard_map/while/body/eval_jaxpr/ppermute | solution.py:22
  258.1 3.3 collective-permute-start.7
  262.3 7.8 collective-permute-done.5
  270.2 3.3 collective-permute-start.8
  284.9 19.8 %eval_jaxpr.6 = bf16[128,4096]{1,0:T(8,128)(2,1)} custom-call(bf16[128,4096]{1,0:T(8,128)(2,1)} %bitcast.89, bf16[2048,1024]{1,0:T(8,128)(2,1)} %pad_maximum_fusion.15.k_ref.v_ref, bf16[2048,1024]{1,0:T(8,128)(2,1)} %pad_maximum_fusion.15.k_ref.v_ref, f32[128,2048]{1,0:T(8,128)} %dynamic-slice_bitcast_fusion.6.bias_ref, bf16[128,4096]{1,0:T(8,128)(2,1)} %copy-done), custom_call_target="tpu_custom_call" | custom-call | tf_op jit(solution)/shard_map/while/body/eval_jaxpr/pallas_call | solution.py:148
  313.4 10.6 %collective-permute-done = bf16[128,4096]{1,0:T(8,128)(2,1)} collective-permute-done((bf16[128,4096]{1,0:T(8,128)(2,1)S(1)}, bf16[128,4096]{1,0:T(8,128)(2,1)}, u32[]{:S(2)}, u32[]{:S(2)}) %collective-permute-start) | collective-permute-done | bytes 1048608 | tf_op jit(solution)/shard_map/while/body/eval_jaxpr/ppermute | solution.py:22
  353.5 3.3 collective-permute-start.7
  357.7 9.0 %collective-permute-done.5 = bf16[512,512]{1,0:T(8,128)(2,1)S(1)} collective-permute-done((bf16[512,512]{1,0:T(8,128)(2,1)S(1)}, bf16[512,512]{1,0:T(8,128)(2,1)S(1)}, u32[]{:S(2)}, u32[]{:S(2)}) %collective-permute-start.5) | collective-permute-done | bytes 524320 | tf_op jit(solution)/shard_map/while/body/eval_jaxpr/ppermute | solution.py:87
  366.8 3.3 collective-permute-start.8
  381.5 19.8 %eval_jaxpr.6 = bf16[128,4096]{1,0:T(8,128)(2,1)} custom-call(bf16[128,4096]{1,0:T(8,128)(2,1)} %bitcast.89, bf16[2048,1024]{1,0:T(8,128)(2,1)} %pad_maximum_fusion.15.k_ref.v_ref, bf16[2048,1024]{1,0:T(8,128)(2,1)} %pad_maximum_fusion.15.k_ref.v_ref, f32[128,2048]{1,0:T(8,128)} %dynamic-slice_bitcast_fusion.6.bias_ref, bf16[128,4096]{1,0:T(8,128)(2,1)} %copy-done), custom_call_target="tpu_custom_call" | custom-call | tf_op jit(solution)/shard_map/while/body/eval_jaxpr/pallas_call | solution.py:148
  410.0 10.6 %collective-permute-done = bf16[128,4096]{1,0:T(8,128)(2,1)} collective-permute-done((bf16[128,4096]{1,0:T(8,128)(2,1)S(1)}, bf16[128,4096]{1,0:T(8,128)(2,1)}, u32[]{:S(2)}, u32[]{:S(2)}) %collective-permute-start) | collective-permute-done | bytes 1048608 | tf_op jit(solution)/shard_map/while/body/eval_jaxpr/ppermute | solution.py:22
  448.2 3.3 collective-permute-start.7
  452.4 8.9 %collective-permute-done.5 = bf16[512,512]{1,0:T(8,128)(2,1)S(1)} collective-permute-done((bf16[512,512]{1,0:T(8,128)(2,1)S(1)}, bf16[512,512]{1,0:T(8,128)(2,1)S(1)}, u32[]{:S(2)}, u32[]{:S(2)}) %collective-permute-start.5) | collective-permute-done | bytes 524320 | tf_op jit(solution)/shard_map/while/body/eval_jaxpr/ppermute | solution.py:87
  461.5 3.3 collective-permute-start.8
  476.6 19.8 %eval_jaxpr.6 = bf16[128,4096]{1,0:T(8,128)(2,1)} custom-call(bf16[128,4096]{1,0:T(8,128)(2,1)} %bitcast.89, bf16[2048,1024]{1,0:T(8,128)(2,1)} %pad_maximum_fusion.15.k_ref.v_ref, bf16[2048,1024]{1,0:T(8,128)(2,1)} %pad_maximum_fusion.15.k_ref.v_ref, f32[128,2048]{1,0:T(8,128)} %dynamic-slice_bitcast_fusion.6.bias_ref, bf16[128,4096]{1,0:T(8,128)(2,1)} %copy-done), custom_call_target="tpu_custom_call" | custom-call | tf_op jit(solution)/shard_map/while/body/eval_jaxpr/pallas_call | solution.py:148
  504.0 10.6 %collective-permute-done = bf16[128,4096]{1,0:T(8,128)(2,1)} collective-permute-done((bf16[128,4096]{1,0:T(8,128)(2,1)S(1)}, bf16[128,4096]{1,0:T(8,128)(2,1)}, u32[]{:S(2)}, u32[]{:S(2)}) %collective-permute-start) | collective-permute-done | bytes 1048608 | tf_op jit(solution)/shard_map/while/body/eval_jaxpr/ppermute | solution.py:22
  542.1 3.2 collective-permute-start.7
  546.2 8.5 collective-permute-done.5
  554.9 3.3 collective-permute-start.8
  569.5 19.8 %eval_jaxpr.6 = bf16[128,4096]{1,0:T(8,128)(2,1)} custom-call(bf16[128,4096]{1,0:T(8,128)(2,1)} %bitcast.89, bf16[2048,1024]{1,0:T(8,128)(2,1)} %pad_maximum_fusion.15.k_ref.v_ref, bf16[2048,1024]{1,0:T(8,128)(2,1)} %pad_maximum_fusion.15.k_ref.v_ref, f32[128,2048]{1,0:T(8,128)} %dynamic-slice_bitcast_fusion.6.bias_ref, bf16[128,4096]{1,0:T(8,128)(2,1)} %copy-done), custom_call_target="tpu_custom_call" | custom-call | tf_op jit(solution)/shard_map/while/body/eval_jaxpr/pallas_call | solution.py:148
  596.9 10.6 %collective-permute-done = bf16[128,4096]{1,0:T(8,128)(2,1)} collective-permute-done((bf16[128,4096]{1,0:T(8,128)(2,1)S(1)}, bf16[128,4096]{1,0:T(8,128)(2,1)}, u32[]{:S(2)}, u32[]{:S(2)}) %collective-permute-start) | collective-permute-done | bytes 1048608 | tf_op jit(solution)/shard_map/while/body/eval_jaxpr/ppermute | solution.py:22
  635.0 3.2 collective-permute-start.7
  639.1 7.7 collective-permute-done.5
  647.0 3.3 collective-permute-start.8
  662.1 19.8 %eval_jaxpr.6 = bf16[128,4096]{1,0:T(8,128)(2,1)} custom-call(bf16[128,4096]{1,0:T(8,128)(2,1)} %bitcast.89, bf16[2048,1024]{1,0:T(8,128)(2,1)} %pad_maximum_fusion.15.k_ref.v_ref, bf16[2048,1024]{1,0:T(8,128)(2,1)} %pad_maximum_fusion.15.k_ref.v_ref, f32[128,2048]{1,0:T(8,128)} %dynamic-slice_bitcast_fusion.6.bias_ref, bf16[128,4096]{1,0:T(8,128)(2,1)} %copy-done), custom_call_target="tpu_custom_call" | custom-call | tf_op jit(solution)/shard_map/while/body/eval_jaxpr/pallas_call | solution.py:148
  689.4 10.6 %collective-permute-done = bf16[128,4096]{1,0:T(8,128)(2,1)} collective-permute-done((bf16[128,4096]{1,0:T(8,128)(2,1)S(1)}, bf16[128,4096]{1,0:T(8,128)(2,1)}, u32[]{:S(2)}, u32[]{:S(2)}) %collective-permute-start) | collective-permute-done | bytes 1048608 | tf_op jit(solution)/shard_map/while/body/eval_jaxpr/ppermute | solution.py:22
  727.6 3.2 collective-permute-start.7
  731.7 7.2 collective-permute-done.5
  739.0 3.3 collective-permute-start.8
  753.9 19.8 %eval_jaxpr.6 = bf16[128,4096]{1,0:T(8,128)(2,1)} custom-call(bf16[128,4096]{1,0:T(8,128)(2,1)} %bitcast.89, bf16[2048,1024]{1,0:T(8,128)(2,1)} %pad_maximum_fusion.15.k_ref.v_ref, bf16[2048,1024]{1,0:T(8,128)(2,1)} %pad_maximum_fusion.15.k_ref.v_ref, f32[128,2048]{1,0:T(8,128)} %dynamic-slice_bitcast_fusion.6.bias_ref, bf16[128,4096]{1,0:T(8,128)(2,1)} %copy-done), custom_call_target="tpu_custom_call" | custom-call | tf_op jit(solution)/shard_map/while/body/eval_jaxpr/pallas_call | solution.py:148
  781.3 10.6 %collective-permute-done = bf16[128,4096]{1,0:T(8,128)(2,1)} collective-permute-done((bf16[128,4096]{1,0:T(8,128)(2,1)S(1)}, bf16[128,4096]{1,0:T(8,128)(2,1)}, u32[]{:S(2)}, u32[]{:S(2)}) %collective-permute-start) | collective-permute-done | bytes 1048608 | tf_op jit(solution)/shard_map/while/body/eval_jaxpr/ppermute | solution.py:22
  819.4 3.2 collective-permute-start.7
  823.5 6.8 collective-permute-done.5
  830.4 3.3 collective-permute-start.8
  845.3 19.8 %eval_jaxpr.6 = bf16[128,4096]{1,0:T(8,128)(2,1)} custom-call(bf16[128,4096]{1,0:T(8,128)(2,1)} %bitcast.89, bf16[2048,1024]{1,0:T(8,128)(2,1)} %pad_maximum_fusion.15.k_ref.v_ref, bf16[2048,1024]{1,0:T(8,128)(2,1)} %pad_maximum_fusion.15.k_ref.v_ref, f32[128,2048]{1,0:T(8,128)} %dynamic-slice_bitcast_fusion.6.bias_ref, bf16[128,4096]{1,0:T(8,128)(2,1)} %copy-done), custom_call_target="tpu_custom_call" | custom-call | tf_op jit(solution)/shard_map/while/body/eval_jaxpr/pallas_call | solution.py:148
  (846 shorter events, 447.3 us)
Async XLA Ops:
  21.5 16.2 %collective-permute-start = (bf16[128,4096]{1,0:T(8,128)(2,1)S(1)}, bf16[128,4096]{1,0:T(8,128)(2,1)}, u32[]{:S(2)}, u32[]{:S(2)}) collective-permute-start(bf16[128,4096]{1,0:T(8,128)(2,1)S(1)} %broadcast_select_fusion.4), channel_id=1, source_target_pairs={{0,16},{16,32},{32,48},{48,64},{64,80},{80,96},{96,112},{1,17},{17... | collective-permute-start | bytes 3145736 | tf_op jit(solution)/shard_map/while/body/eval_jaxpr/ppermute | solution.py:22
  42.9 11.8 %collective-permute-start.10 = (bf16[128,512]{1,0:T(8,128)(2,1)S(1)}, bf16[128,512]{1,0:T(8,128)(2,1)S(1)}, u32[]{:S(2)}, u32[]{:S(2)}) collective-permute-start(bf16[128,512]{1,0:T(8,128)(2,1)S(1)} %bitcast.98), channel_id=1, source_target_pairs={{0,3},{1,0},{2,1},{3,2},{4,7},{5,4},{6,5},{7,6},{8,11},{9,8},{10,9... | collective-permute-start | bytes 393224 | tf_op jit(solution)/shard_map/while/body/eval_jaxpr/ppermute | solution.py:87
  63.6 23.0 %collective-permute-start.13 = (bf16[512,512]{1,0:T(8,128)(2,1)S(1)}, bf16[512,512]{1,0:T(8,128)(2,1)S(1)}, u32[]{:S(2)}, u32[]{:S(2)}) collective-permute-start(bf16[512,512]{1,0:T(8,128)(2,1)S(1)} %maximum_maximum_fusion.5), channel_id=1, source_target_pairs={{0,4},{1,5},{2,6},{3,7},{4,8},{5,9},{6,10},{7,11},{8,12},{9,13},{1... | collective-permute-start | bytes 1572872 | tf_op jit(solution)/shard_map/while/body/eval_jaxpr/ppermute | solution.py:87
  63.7 22.8 %collective-permute-start.14 = (bf16[512,512]{1,0:T(8,128)(2,1)S(1)}, bf16[512,512]{1,0:T(8,128)(2,1)S(1)}, u32[]{:S(2)}, u32[]{:S(2)}) collective-permute-start(bf16[512,512]{1,0:T(8,128)(2,1)S(1)} %maximum_maximum_fusion.5), channel_id=1, source_target_pairs={{0,12},{1,13},{2,14},{3,15},{4,0},{5,1},{6,2},{7,3},{8,4},{9,5},{1... | collective-permute-start | bytes 1572872 | tf_op jit(solution)/shard_map/while/body/eval_jaxpr/ppermute | solution.py:87
  70.0 12.1 %collective-permute-start.5 = (bf16[512,512]{1,0:T(8,128)(2,1)S(1)}, bf16[512,512]{1,0:T(8,128)(2,1)S(1)}, u32[]{:S(2)}, u32[]{:S(2)}) collective-permute-start(bf16[512,512]{1,0:T(8,128)(2,1)S(1)} %maximum_maximum_fusion.4), channel_id=1, source_target_pairs={{0,3},{1,0},{2,1},{3,2},{4,7},{5,4},{6,5},{7,6},{8,11},{9,8},{10,9... | collective-permute-start | bytes 1572872 | tf_op jit(solution)/shard_map/while/body/eval_jaxpr/ppermute | solution.py:87
  70.9 11.6 %collective-permute-start.7 = (bf16[512,512]{1,0:T(8,128)(2,1)S(1)}, bf16[512,512]{1,0:T(8,128)(2,1)S(1)}, u32[]{:S(2)}, u32[]{:S(2)}) collective-permute-start(bf16[512,512]{1,0:T(8,128)(2,1)S(1)} %maximum_maximum_fusion.4), channel_id=1, source_target_pairs={{0,1},{1,2},{2,3},{3,0},{4,5},{5,6},{6,7},{7,4},{8,9},{9,10},{10,1... | collective-permute-start | bytes 1572872 | tf_op jit(solution)/shard_map/while/body/eval_jaxpr/ppermute | solution.py:87
  118.7 16.2 %collective-permute-start = (bf16[128,4096]{1,0:T(8,128)(2,1)S(1)}, bf16[128,4096]{1,0:T(8,128)(2,1)}, u32[]{:S(2)}, u32[]{:S(2)}) collective-permute-start(bf16[128,4096]{1,0:T(8,128)(2,1)S(1)} %broadcast_select_fusion.4), channel_id=1, source_target_pairs={{0,16},{16,32},{32,48},{48,64},{64,80},{80,96},{96,112},{1,17},{17... | collective-permute-start | bytes 3145736 | tf_op jit(solution)/shard_map/while/body/eval_jaxpr/ppermute | solution.py:22
  158.3 22.0 %collective-permute-start.13 = (bf16[512,512]{1,0:T(8,128)(2,1)S(1)}, bf16[512,512]{1,0:T(8,128)(2,1)S(1)}, u32[]{:S(2)}, u32[]{:S(2)}) collective-permute-start(bf16[512,512]{1,0:T(8,128)(2,1)S(1)} %maximum_maximum_fusion.5), channel_id=1, source_target_pairs={{0,4},{1,5},{2,6},{3,7},{4,8},{5,9},{6,10},{7,11},{8,12},{9,13},{1... | collective-permute-start | bytes 1572872 | tf_op jit(solution)/shard_map/while/body/eval_jaxpr/ppermute | solution.py:87
  159.1 21.1 %collective-permute-start.14 = (bf16[512,512]{1,0:T(8,128)(2,1)S(1)}, bf16[512,512]{1,0:T(8,128)(2,1)S(1)}, u32[]{:S(2)}, u32[]{:S(2)}) collective-permute-start(bf16[512,512]{1,0:T(8,128)(2,1)S(1)} %maximum_maximum_fusion.5), channel_id=1, source_target_pairs={{0,12},{1,13},{2,14},{3,15},{4,0},{5,1},{6,2},{7,3},{8,4},{9,5},{1... | collective-permute-start | bytes 1572872 | tf_op jit(solution)/shard_map/while/body/eval_jaxpr/ppermute | solution.py:87
  163.8 12.1 %collective-permute-start.5 = (bf16[512,512]{1,0:T(8,128)(2,1)S(1)}, bf16[512,512]{1,0:T(8,128)(2,1)S(1)}, u32[]{:S(2)}, u32[]{:S(2)}) collective-permute-start(bf16[512,512]{1,0:T(8,128)(2,1)S(1)} %maximum_maximum_fusion.4), channel_id=1, source_target_pairs={{0,3},{1,0},{2,1},{3,2},{4,7},{5,4},{6,5},{7,6},{8,11},{9,8},{10,9... | collective-permute-start | bytes 1572872 | tf_op jit(solution)/shard_map/while/body/eval_jaxpr/ppermute | solution.py:87
  163.9 12.1 %collective-permute-start.7 = (bf16[512,512]{1,0:T(8,128)(2,1)S(1)}, bf16[512,512]{1,0:T(8,128)(2,1)S(1)}, u32[]{:S(2)}, u32[]{:S(2)}) collective-permute-start(bf16[512,512]{1,0:T(8,128)(2,1)S(1)} %maximum_maximum_fusion.4), channel_id=1, source_target_pairs={{0,1},{1,2},{2,3},{3,0},{4,5},{5,6},{6,7},{7,4},{8,9},{9,10},{10,1... | collective-permute-start | bytes 1572872 | tf_op jit(solution)/shard_map/while/body/eval_jaxpr/ppermute | solution.py:87
  212.4 16.2 %collective-permute-start = (bf16[128,4096]{1,0:T(8,128)(2,1)S(1)}, bf16[128,4096]{1,0:T(8,128)(2,1)}, u32[]{:S(2)}, u32[]{:S(2)}) collective-permute-start(bf16[128,4096]{1,0:T(8,128)(2,1)S(1)} %broadcast_select_fusion.4), channel_id=1, source_target_pairs={{0,16},{16,32},{32,48},{48,64},{64,80},{80,96},{96,112},{1,17},{17... | collective-permute-start | bytes 3145736 | tf_op jit(solution)/shard_map/while/body/eval_jaxpr/ppermute | solution.py:22
  239.3 10.6 %collective-permute-start.3 = (bf16[128,512]{1,0:T(8,128)(2,1)}, bf16[128,512]{1,0:T(8,128)(2,1)}, u32[]{:S(2)}, u32[]{:S(2)}) collective-permute-start(bf16[128,512]{1,0:T(8,128)(2,1)} %slice.268), channel_id=1, source_target_pairs={{0,4},{1,5},{2,6},{3,7},{4,8},{5,9},{6,10},{7,11},{8,12},{9,13},{1... | collective-permute-start | bytes 393224 | tf_op jit(solution)/shard_map/while/body/eval_jaxpr/ppermute | solution.py:87
  252.5 22.0 %collective-permute-start.13 = (bf16[512,512]{1,0:T(8,128)(2,1)S(1)}, bf16[512,512]{1,0:T(8,128)(2,1)S(1)}, u32[]{:S(2)}, u32[]{:S(2)}) collective-permute-start(bf16[512,512]{1,0:T(8,128)(2,1)S(1)} %maximum_maximum_fusion.5), channel_id=1, source_target_pairs={{0,4},{1,5},{2,6},{3,7},{4,8},{5,9},{6,10},{7,11},{8,12},{9,13},{1... | collective-permute-start | bytes 1572872 | tf_op jit(solution)/shard_map/while/body/eval_jaxpr/ppermute | solution.py:87
  253.3 21.1 %collective-permute-start.14 = (bf16[512,512]{1,0:T(8,128)(2,1)S(1)}, bf16[512,512]{1,0:T(8,128)(2,1)S(1)}, u32[]{:S(2)}, u32[]{:S(2)}) collective-permute-start(bf16[512,512]{1,0:T(8,128)(2,1)S(1)} %maximum_maximum_fusion.5), channel_id=1, source_target_pairs={{0,12},{1,13},{2,14},{3,15},{4,0},{5,1},{6,2},{7,3},{8,4},{9,5},{1... | collective-permute-start | bytes 1572872 | tf_op jit(solution)/shard_map/while/body/eval_jaxpr/ppermute | solution.py:87
  258.0 12.1 %collective-permute-start.5 = (bf16[512,512]{1,0:T(8,128)(2,1)S(1)}, bf16[512,512]{1,0:T(8,128)(2,1)S(1)}, u32[]{:S(2)}, u32[]{:S(2)}) collective-permute-start(bf16[512,512]{1,0:T(8,128)(2,1)S(1)} %maximum_maximum_fusion.4), channel_id=1, source_target_pairs={{0,3},{1,0},{2,1},{3,2},{4,7},{5,4},{6,5},{7,6},{8,11},{9,8},{10,9... | collective-permute-start | bytes 1572872 | tf_op jit(solution)/shard_map/while/body/eval_jaxpr/ppermute | solution.py:87
  258.1 12.1 %collective-permute-start.7 = (bf16[512,512]{1,0:T(8,128)(2,1)S(1)}, bf16[512,512]{1,0:T(8,128)(2,1)S(1)}, u32[]{:S(2)}, u32[]{:S(2)}) collective-permute-start(bf16[512,512]{1,0:T(8,128)(2,1)S(1)} %maximum_maximum_fusion.4), channel_id=1, source_target_pairs={{0,1},{1,2},{2,3},{3,0},{4,5},{5,6},{6,7},{7,4},{8,9},{9,10},{10,1... | collective-permute-start | bytes 1572872 | tf_op jit(solution)/shard_map/while/body/eval_jaxpr/ppermute | solution.py:87
  307.8 16.2 %collective-permute-start = (bf16[128,4096]{1,0:T(8,128)(2,1)S(1)}, bf16[128,4096]{1,0:T(8,128)(2,1)}, u32[]{:S(2)}, u32[]{:S(2)}) collective-permute-start(bf16[128,4096]{1,0:T(8,128)(2,1)S(1)} %broadcast_select_fusion.4), channel_id=1, source_target_pairs={{0,16},{16,32},{32,48},{48,64},{64,80},{80,96},{96,112},{1,17},{17... | collective-permute-start | bytes 3145736 | tf_op jit(solution)/shard_map/while/body/eval_jaxpr/ppermute | solution.py:22
  334.7 10.6 %collective-permute-start.3 = (bf16[128,512]{1,0:T(8,128)(2,1)}, bf16[128,512]{1,0:T(8,128)(2,1)}, u32[]{:S(2)}, u32[]{:S(2)}) collective-permute-start(bf16[128,512]{1,0:T(8,128)(2,1)} %slice.268), channel_id=1, source_target_pairs={{0,4},{1,5},{2,6},{3,7},{4,8},{5,9},{6,10},{7,11},{8,12},{9,13},{1... | collective-permute-start | bytes 393224 | tf_op jit(solution)/shard_map/while/body/eval_jaxpr/ppermute | solution.py:87
  347.9 23.2 %collective-permute-start.13 = (bf16[512,512]{1,0:T(8,128)(2,1)S(1)}, bf16[512,512]{1,0:T(8,128)(2,1)S(1)}, u32[]{:S(2)}, u32[]{:S(2)}) collective-permute-start(bf16[512,512]{1,0:T(8,128)(2,1)S(1)} %maximum_maximum_fusion.5), channel_id=1, source_target_pairs={{0,4},{1,5},{2,6},{3,7},{4,8},{5,9},{6,10},{7,11},{8,12},{9,13},{1... | collective-permute-start | bytes 1572872 | tf_op jit(solution)/shard_map/while/body/eval_jaxpr/ppermute | solution.py:87
  348.7 22.2 %collective-permute-start.14 = (bf16[512,512]{1,0:T(8,128)(2,1)S(1)}, bf16[512,512]{1,0:T(8,128)(2,1)S(1)}, u32[]{:S(2)}, u32[]{:S(2)}) collective-permute-start(bf16[512,512]{1,0:T(8,128)(2,1)S(1)} %maximum_maximum_fusion.5), channel_id=1, source_target_pairs={{0,12},{1,13},{2,14},{3,15},{4,0},{5,1},{6,2},{7,3},{8,4},{9,5},{1... | collective-permute-start | bytes 1572872 | tf_op jit(solution)/shard_map/while/body/eval_jaxpr/ppermute | solution.py:87
  353.4 13.3 %collective-permute-start.5 = (bf16[512,512]{1,0:T(8,128)(2,1)S(1)}, bf16[512,512]{1,0:T(8,128)(2,1)S(1)}, u32[]{:S(2)}, u32[]{:S(2)}) collective-permute-start(bf16[512,512]{1,0:T(8,128)(2,1)S(1)} %maximum_maximum_fusion.4), channel_id=1, source_target_pairs={{0,3},{1,0},{2,1},{3,2},{4,7},{5,4},{6,5},{7,6},{8,11},{9,8},{10,9... | collective-permute-start | bytes 1572872 | tf_op jit(solution)/shard_map/while/body/eval_jaxpr/ppermute | solution.py:87
  353.5 13.3 %collective-permute-start.7 = (bf16[512,512]{1,0:T(8,128)(2,1)S(1)}, bf16[512,512]{1,0:T(8,128)(2,1)S(1)}, u32[]{:S(2)}, u32[]{:S(2)}) collective-permute-start(bf16[512,512]{1,0:T(8,128)(2,1)S(1)} %maximum_maximum_fusion.4), channel_id=1, source_target_pairs={{0,1},{1,2},{2,3},{3,0},{4,5},{5,6},{6,7},{7,4},{8,9},{9,10},{10,1... | collective-permute-start | bytes 1572872 | tf_op jit(solution)/shard_map/while/body/eval_jaxpr/ppermute | solution.py:87
  404.4 16.2 %collective-permute-start = (bf16[128,4096]{1,0:T(8,128)(2,1)S(1)}, bf16[128,4096]{1,0:T(8,128)(2,1)}, u32[]{:S(2)}, u32[]{:S(2)}) collective-permute-start(bf16[128,4096]{1,0:T(8,128)(2,1)S(1)} %broadcast_select_fusion.4), channel_id=1, source_target_pairs={{0,16},{16,32},{32,48},{48,64},{64,80},{80,96},{96,112},{1,17},{17... | collective-permute-start | bytes 3145736 | tf_op jit(solution)/shard_map/while/body/eval_jaxpr/ppermute | solution.py:22
  443.3 23.0 %collective-permute-start.13 = (bf16[512,512]{1,0:T(8,128)(2,1)S(1)}, bf16[512,512]{1,0:T(8,128)(2,1)S(1)}, u32[]{:S(2)}, u32[]{:S(2)}) collective-permute-start(bf16[512,512]{1,0:T(8,128)(2,1)S(1)} %maximum_maximum_fusion.5), channel_id=1, source_target_pairs={{0,4},{1,5},{2,6},{3,7},{4,8},{5,9},{6,10},{7,11},{8,12},{9,13},{1... | collective-permute-start | bytes 1572872 | tf_op jit(solution)/shard_map/while/body/eval_jaxpr/ppermute | solution.py:87
  444.1 21.4 %collective-permute-start.14 = (bf16[512,512]{1,0:T(8,128)(2,1)S(1)}, bf16[512,512]{1,0:T(8,128)(2,1)S(1)}, u32[]{:S(2)}, u32[]{:S(2)}) collective-permute-start(bf16[512,512]{1,0:T(8,128)(2,1)S(1)} %maximum_maximum_fusion.5), channel_id=1, source_target_pairs={{0,12},{1,13},{2,14},{3,15},{4,0},{5,1},{6,2},{7,3},{8,4},{9,5},{1... | collective-permute-start | bytes 1572872 | tf_op jit(solution)/shard_map/while/body/eval_jaxpr/ppermute | solution.py:87
  448.1 13.2 %collective-permute-start.5 = (bf16[512,512]{1,0:T(8,128)(2,1)S(1)}, bf16[512,512]{1,0:T(8,128)(2,1)S(1)}, u32[]{:S(2)}, u32[]{:S(2)}) collective-permute-start(bf16[512,512]{1,0:T(8,128)(2,1)S(1)} %maximum_maximum_fusion.4), channel_id=1, source_target_pairs={{0,3},{1,0},{2,1},{3,2},{4,7},{5,4},{6,5},{7,6},{8,11},{9,8},{10,9... | collective-permute-start | bytes 1572872 | tf_op jit(solution)/shard_map/while/body/eval_jaxpr/ppermute | solution.py:87
  448.2 13.3 %collective-permute-start.7 = (bf16[512,512]{1,0:T(8,128)(2,1)S(1)}, bf16[512,512]{1,0:T(8,128)(2,1)S(1)}, u32[]{:S(2)}, u32[]{:S(2)}) collective-permute-start(bf16[512,512]{1,0:T(8,128)(2,1)S(1)} %maximum_maximum_fusion.4), channel_id=1, source_target_pairs={{0,1},{1,2},{2,3},{3,0},{4,5},{5,6},{6,7},{7,4},{8,9},{9,10},{10,1... | collective-permute-start | bytes 1572872 | tf_op jit(solution)/shard_map/while/body/eval_jaxpr/ppermute | solution.py:87
  498.4 16.2 %collective-permute-start = (bf16[128,4096]{1,0:T(8,128)(2,1)S(1)}, bf16[128,4096]{1,0:T(8,128)(2,1)}, u32[]{:S(2)}, u32[]{:S(2)}) collective-permute-start(bf16[128,4096]{1,0:T(8,128)(2,1)S(1)} %broadcast_select_fusion.4), channel_id=1, source_target_pairs={{0,16},{16,32},{32,48},{48,64},{64,80},{80,96},{96,112},{1,17},{17... | collective-permute-start | bytes 3145736 | tf_op jit(solution)/shard_map/while/body/eval_jaxpr/ppermute | solution.py:22
  537.2 21.9 %collective-permute-start.13 = (bf16[512,512]{1,0:T(8,128)(2,1)S(1)}, bf16[512,512]{1,0:T(8,128)(2,1)S(1)}, u32[]{:S(2)}, u32[]{:S(2)}) collective-permute-start(bf16[512,512]{1,0:T(8,128)(2,1)S(1)} %maximum_maximum_fusion.5), channel_id=1, source_target_pairs={{0,4},{1,5},{2,6},{3,7},{4,8},{5,9},{6,10},{7,11},{8,12},{9,13},{1... | collective-permute-start | bytes 1572872 | tf_op jit(solution)/shard_map/while/body/eval_jaxpr/ppermute | solution.py:87
  537.5 21.5 %collective-permute-start.14 = (bf16[512,512]{1,0:T(8,128)(2,1)S(1)}, bf16[512,512]{1,0:T(8,128)(2,1)S(1)}, u32[]{:S(2)}, u32[]{:S(2)}) collective-permute-start(bf16[512,512]{1,0:T(8,128)(2,1)S(1)} %maximum_maximum_fusion.5), channel_id=1, source_target_pairs={{0,12},{1,13},{2,14},{3,15},{4,0},{5,1},{6,2},{7,3},{8,4},{9,5},{1... | collective-permute-start | bytes 1572872 | tf_op jit(solution)/shard_map/while/body/eval_jaxpr/ppermute | solution.py:87
  542.0 12.7 %collective-permute-start.5 = (bf16[512,512]{1,0:T(8,128)(2,1)S(1)}, bf16[512,512]{1,0:T(8,128)(2,1)S(1)}, u32[]{:S(2)}, u32[]{:S(2)}) collective-permute-start(bf16[512,512]{1,0:T(8,128)(2,1)S(1)} %maximum_maximum_fusion.4), channel_id=1, source_target_pairs={{0,3},{1,0},{2,1},{3,2},{4,7},{5,4},{6,5},{7,6},{8,11},{9,8},{10,9... | collective-permute-start | bytes 1572872 | tf_op jit(solution)/shard_map/while/body/eval_jaxpr/ppermute | solution.py:87
  542.1 12.8 %collective-permute-start.7 = (bf16[512,512]{1,0:T(8,128)(2,1)S(1)}, bf16[512,512]{1,0:T(8,128)(2,1)S(1)}, u32[]{:S(2)}, u32[]{:S(2)}) collective-permute-start(bf16[512,512]{1,0:T(8,128)(2,1)S(1)} %maximum_maximum_fusion.4), channel_id=1, source_target_pairs={{0,1},{1,2},{2,3},{3,0},{4,5},{5,6},{6,7},{7,4},{8,9},{9,10},{10,1... | collective-permute-start | bytes 1572872 | tf_op jit(solution)/shard_map/while/body/eval_jaxpr/ppermute | solution.py:87
  591.3 16.2 %collective-permute-start = (bf16[128,4096]{1,0:T(8,128)(2,1)S(1)}, bf16[128,4096]{1,0:T(8,128)(2,1)}, u32[]{:S(2)}, u32[]{:S(2)}) collective-permute-start(bf16[128,4096]{1,0:T(8,128)(2,1)S(1)} %broadcast_select_fusion.4), channel_id=1, source_target_pairs={{0,16},{16,32},{32,48},{48,64},{64,80},{80,96},{96,112},{1,17},{17... | collective-permute-start | bytes 3145736 | tf_op jit(solution)/shard_map/while/body/eval_jaxpr/ppermute | solution.py:22
  630.1 21.6 %collective-permute-start.13 = (bf16[512,512]{1,0:T(8,128)(2,1)S(1)}, bf16[512,512]{1,0:T(8,128)(2,1)S(1)}, u32[]{:S(2)}, u32[]{:S(2)}) collective-permute-start(bf16[512,512]{1,0:T(8,128)(2,1)S(1)} %maximum_maximum_fusion.5), channel_id=1, source_target_pairs={{0,4},{1,5},{2,6},{3,7},{4,8},{5,9},{6,10},{7,11},{8,12},{9,13},{1... | collective-permute-start | bytes 1572872 | tf_op jit(solution)/shard_map/while/body/eval_jaxpr/ppermute | solution.py:87
  631.0 20.1 %collective-permute-start.14 = (bf16[512,512]{1,0:T(8,128)(2,1)S(1)}, bf16[512,512]{1,0:T(8,128)(2,1)S(1)}, u32[]{:S(2)}, u32[]{:S(2)}) collective-permute-start(bf16[512,512]{1,0:T(8,128)(2,1)S(1)} %maximum_maximum_fusion.5), channel_id=1, source_target_pairs={{0,12},{1,13},{2,14},{3,15},{4,0},{5,1},{6,2},{7,3},{8,4},{9,5},{1... | collective-permute-start | bytes 1572872 | tf_op jit(solution)/shard_map/while/body/eval_jaxpr/ppermute | solution.py:87
  634.9 11.9 %collective-permute-start.5 = (bf16[512,512]{1,0:T(8,128)(2,1)S(1)}, bf16[512,512]{1,0:T(8,128)(2,1)S(1)}, u32[]{:S(2)}, u32[]{:S(2)}) collective-permute-start(bf16[512,512]{1,0:T(8,128)(2,1)S(1)} %maximum_maximum_fusion.4), channel_id=1, source_target_pairs={{0,3},{1,0},{2,1},{3,2},{4,7},{5,4},{6,5},{7,6},{8,11},{9,8},{10,9... | collective-permute-start | bytes 1572872 | tf_op jit(solution)/shard_map/while/body/eval_jaxpr/ppermute | solution.py:87
  635.0 11.9 %collective-permute-start.7 = (bf16[512,512]{1,0:T(8,128)(2,1)S(1)}, bf16[512,512]{1,0:T(8,128)(2,1)S(1)}, u32[]{:S(2)}, u32[]{:S(2)}) collective-permute-start(bf16[512,512]{1,0:T(8,128)(2,1)S(1)} %maximum_maximum_fusion.4), channel_id=1, source_target_pairs={{0,1},{1,2},{2,3},{3,0},{4,5},{5,6},{6,7},{7,4},{8,9},{9,10},{10,1... | collective-permute-start | bytes 1572872 | tf_op jit(solution)/shard_map/while/body/eval_jaxpr/ppermute | solution.py:87
  683.8 16.2 %collective-permute-start = (bf16[128,4096]{1,0:T(8,128)(2,1)S(1)}, bf16[128,4096]{1,0:T(8,128)(2,1)}, u32[]{:S(2)}, u32[]{:S(2)}) collective-permute-start(bf16[128,4096]{1,0:T(8,128)(2,1)S(1)} %broadcast_select_fusion.4), channel_id=1, source_target_pairs={{0,16},{16,32},{32,48},{48,64},{64,80},{80,96},{96,112},{1,17},{17... | collective-permute-start | bytes 3145736 | tf_op jit(solution)/shard_map/while/body/eval_jaxpr/ppermute | solution.py:22
  722.7 20.9 %collective-permute-start.13 = (bf16[512,512]{1,0:T(8,128)(2,1)S(1)}, bf16[512,512]{1,0:T(8,128)(2,1)S(1)}, u32[]{:S(2)}, u32[]{:S(2)}) collective-permute-start(bf16[512,512]{1,0:T(8,128)(2,1)S(1)} %maximum_maximum_fusion.5), channel_id=1, source_target_pairs={{0,4},{1,5},{2,6},{3,7},{4,8},{5,9},{6,10},{7,11},{8,12},{9,13},{1... | collective-permute-start | bytes 1572872 | tf_op jit(solution)/shard_map/while/body/eval_jaxpr/ppermute | solution.py:87
  723.0 20.1 %collective-permute-start.14 = (bf16[512,512]{1,0:T(8,128)(2,1)S(1)}, bf16[512,512]{1,0:T(8,128)(2,1)S(1)}, u32[]{:S(2)}, u32[]{:S(2)}) collective-permute-start(bf16[512,512]{1,0:T(8,128)(2,1)S(1)} %maximum_maximum_fusion.5), channel_id=1, source_target_pairs={{0,12},{1,13},{2,14},{3,15},{4,0},{5,1},{6,2},{7,3},{8,4},{9,5},{1... | collective-permute-start | bytes 1572872 | tf_op jit(solution)/shard_map/while/body/eval_jaxpr/ppermute | solution.py:87
  727.5 11.4 %collective-permute-start.5 = (bf16[512,512]{1,0:T(8,128)(2,1)S(1)}, bf16[512,512]{1,0:T(8,128)(2,1)S(1)}, u32[]{:S(2)}, u32[]{:S(2)}) collective-permute-start(bf16[512,512]{1,0:T(8,128)(2,1)S(1)} %maximum_maximum_fusion.4), channel_id=1, source_target_pairs={{0,3},{1,0},{2,1},{3,2},{4,7},{5,4},{6,5},{7,6},{8,11},{9,8},{10,9... | collective-permute-start | bytes 1572872 | tf_op jit(solution)/shard_map/while/body/eval_jaxpr/ppermute | solution.py:87
  727.6 11.4 %collective-permute-start.7 = (bf16[512,512]{1,0:T(8,128)(2,1)S(1)}, bf16[512,512]{1,0:T(8,128)(2,1)S(1)}, u32[]{:S(2)}, u32[]{:S(2)}) collective-permute-start(bf16[512,512]{1,0:T(8,128)(2,1)S(1)} %maximum_maximum_fusion.4), channel_id=1, source_target_pairs={{0,1},{1,2},{2,3},{3,0},{4,5},{5,6},{6,7},{7,4},{8,9},{9,10},{10,1... | collective-permute-start | bytes 1572872 | tf_op jit(solution)/shard_map/while/body/eval_jaxpr/ppermute | solution.py:87
  775.6 16.2 %collective-permute-start = (bf16[128,4096]{1,0:T(8,128)(2,1)S(1)}, bf16[128,4096]{1,0:T(8,128)(2,1)}, u32[]{:S(2)}, u32[]{:S(2)}) collective-permute-start(bf16[128,4096]{1,0:T(8,128)(2,1)S(1)} %broadcast_select_fusion.4), channel_id=1, source_target_pairs={{0,16},{16,32},{32,48},{48,64},{64,80},{80,96},{96,112},{1,17},{17... | collective-permute-start | bytes 3145736 | tf_op jit(solution)/shard_map/while/body/eval_jaxpr/ppermute | solution.py:22
  814.5 20.4 %collective-permute-start.13 = (bf16[512,512]{1,0:T(8,128)(2,1)S(1)}, bf16[512,512]{1,0:T(8,128)(2,1)S(1)}, u32[]{:S(2)}, u32[]{:S(2)}) collective-permute-start(bf16[512,512]{1,0:T(8,128)(2,1)S(1)} %maximum_maximum_fusion.5), channel_id=1, source_target_pairs={{0,4},{1,5},{2,6},{3,7},{4,8},{5,9},{6,10},{7,11},{8,12},{9,13},{1... | collective-permute-start | bytes 1572872 | tf_op jit(solution)/shard_map/while/body/eval_jaxpr/ppermute | solution.py:87
  815.1 19.5 %collective-permute-start.14 = (bf16[512,512]{1,0:T(8,128)(2,1)S(1)}, bf16[512,512]{1,0:T(8,128)(2,1)S(1)}, u32[]{:S(2)}, u32[]{:S(2)}) collective-permute-start(bf16[512,512]{1,0:T(8,128)(2,1)S(1)} %maximum_maximum_fusion.5), channel_id=1, source_target_pairs={{0,12},{1,13},{2,14},{3,15},{4,0},{5,1},{6,2},{7,3},{8,4},{9,5},{1... | collective-permute-start | bytes 1572872 | tf_op jit(solution)/shard_map/while/body/eval_jaxpr/ppermute | solution.py:87
  819.3 11.0 %collective-permute-start.5 = (bf16[512,512]{1,0:T(8,128)(2,1)S(1)}, bf16[512,512]{1,0:T(8,128)(2,1)S(1)}, u32[]{:S(2)}, u32[]{:S(2)}) collective-permute-start(bf16[512,512]{1,0:T(8,128)(2,1)S(1)} %maximum_maximum_fusion.4), channel_id=1, source_target_pairs={{0,3},{1,0},{2,1},{3,2},{4,7},{5,4},{6,5},{7,6},{8,11},{9,8},{10,9... | collective-permute-start | bytes 1572872 | tf_op jit(solution)/shard_map/while/body/eval_jaxpr/ppermute | solution.py:87
  819.4 11.0 %collective-permute-start.7 = (bf16[512,512]{1,0:T(8,128)(2,1)S(1)}, bf16[512,512]{1,0:T(8,128)(2,1)S(1)}, u32[]{:S(2)}, u32[]{:S(2)}) collective-permute-start(bf16[512,512]{1,0:T(8,128)(2,1)S(1)} %maximum_maximum_fusion.4), channel_id=1, source_target_pairs={{0,1},{1,2},{2,3},{3,0},{4,5},{5,6},{6,7},{7,4},{8,9},{9,10},{10,1... | collective-permute-start | bytes 1572872 | tf_op jit(solution)/shard_map/while/body/eval_jaxpr/ppermute | solution.py:87
  (187 other events, 1541.7 us)

commit v5 on v4

--- a/solution.py
+++ b/solution.py
@@ -114,50 +114,87 @@
     return blocks.reshape(micro_count, side * side * rows)
 
 
-def attention_kernel(q_ref, k_ref, v_ref, bias_ref, res_ref, o_ref):
+CHUNK = 128
+
+
+def attention_kernel(need_ref, q_ref, k_ref, v_ref, bias_ref, res_ref, o_ref, s_scr, m_scr, l_scr, acc_scr):
     ratio = HQ // HK
     scale = 1.0 / math.sqrt(HD)
-    keys = k_ref[...]
-    values = v_ref[...]
-    bias = bias_ref[...]
+    chunks = k_ref.shape[0] // CHUNK
+    m_scr[...] = jnp.full(m_scr.shape, -jnp.inf, jnp.float32)
+    l_scr[...] = jnp.zeros(l_scr.shape, jnp.float32)
+    acc_scr[...] = jnp.zeros(acc_scr.shape, jnp.float32)
+
+    def score_pass(c, carry):
+        @pl.when(need_ref[c] > 0)
+        def _():
+            keys = k_ref[pl.ds(c * CHUNK, CHUNK), :]
+            bias = bias_ref[:, pl.ds(c * CHUNK, CHUNK)]
+            for g in range(ratio):
+                scores = lax.dot_general(
+                    q_ref[:, g * HD : (g + 1) * HD],
+                    keys,
+                    (((1,), (1,)), ((), ())),
+                    preferred_element_type=jnp.float32,
+                )
+                masked = scores * scale + bias
+                s_scr[g, :, pl.ds(c * CHUNK, CHUNK)] = masked
+                m_scr[g] = jnp.maximum(m_scr[g], jnp.max(masked, axis=-1, keepdims=True))
+
+        return carry
+
+    lax.fori_loop(0, chunks, score_pass, 0)
+
+    def weight_pass(c, carry):
+        @pl.when(need_ref[c] > 0)
+        def _():
+            values = v_ref[pl.ds(c * CHUNK, CHUNK), :]
+            for g in range(ratio):
+                weights = jnp.exp(s_scr[g, :, pl.ds(c * CHUNK, CHUNK)] - m_scr[g])
+                l_scr[g] = l_scr[g] + jnp.sum(weights, axis=-1, keepdims=True)
+                acc_scr[g] = acc_scr[g] + jnp.dot(
+                    weights.astype(jnp.bfloat16), values, preferred_element_type=jnp.float32
+                )
+
+        return carry
+
+    lax.fori_loop(0, chunks, weight_pass, 0)
     for g in range(ratio):
         cols = slice(g * HD, (g + 1) * HD)
-        scores = lax.dot_general(
-            q_ref[:, cols],
-            keys,
-            (((1,), (1,)), ((), ())),
-            preferred_element_type=jnp.float32,
-        )
-        masked = scores * scale + bias
-        row_top = jnp.max(masked, axis=-1, keepdims=True)
-        weights = jnp.exp(masked - row_top)
-        denominator = jnp.sum(weights, axis=-1, keepdims=True)
-        summed = jnp.dot(
-            weights.astype(jnp.bfloat16), values, preferred_element_type=jnp.float32
-        )
-        attended = (summed / denominator).astype(jnp.bfloat16)
+        attended = (acc_scr[g] / l_scr[g]).astype(jnp.bfloat16)
         o_ref[:, cols] = (
             res_ref[:, cols].astype(jnp.float32) + attended.astype(jnp.float32)
         ).astype(o_ref.dtype)
 
 
-def attention(turned, kv_all, bias, residual):
+def attention(need, turned, kv_all, bias, residual):
     rows, width = turned.shape
     keys_len = kv_all.shape[0]
     group = width // HK
+    ratio = HQ // HK
+    grid_spec = pltpu.PrefetchScalarGridSpec(
+        num_scalar_prefetch=1,
+        grid=(HK,),
+        in_specs=[
+            pl.BlockSpec((rows, group), lambda k, n: (0, k)),
+            pl.BlockSpec((keys_len, HD), lambda k, n: (0, k)),
+            pl.BlockSpec((keys_len, HD), lambda k, n: (0, HK + k)),
+            pl.BlockSpec((rows, keys_len), lambda k, n: (0, 0)),
+            pl.BlockSpec((rows, group), lambda k, n: (0, k)),
+        ],
+        out_specs=pl.BlockSpec((rows, group), lambda k, n: (0, k)),
+        scratch_shapes=[
+            pltpu.VMEM((ratio, rows, keys_len), jnp.float32),
+            pltpu.VMEM((ratio, rows, 1), jnp.float32),
+            pltpu.VMEM((ratio, rows, 1), jnp.float32),
+            pltpu.VMEM((ratio, rows, HD), jnp.float32),
+        ],
+    )
     return pl.pallas_call(
         attention_kernel,
-        grid=(HK,),
-        in_specs=[
-            pl.BlockSpec((rows, group), lambda k: (0, k)),
-            pl.BlockSpec((keys_len, HD), lambda k: (0, k)),
-            pl.BlockSpec((keys_len, HD), lambda k: (0, HK + k)),
-            pl.BlockSpec((rows, keys_len), lambda k: (0, 0)),
-            pl.BlockSpec((rows, group), lambda k: (0, k)),
-        ],
-        out_specs=pl.BlockSpec((rows, group), lambda k: (0, k)),
+        grid_spec=grid_spec,
         out_shape=jax.ShapeDtypeStruct((rows, width), jnp.bfloat16),
-    )(turned, kv_all, kv_all, bias, residual)
+    )(need, turned, kv_all, kv_all, bias, residual)
 
 
 def local(hidden, queries, gain, key_weight, value_weight, tree_ids, branch_ids, span_order):
@@ -188,6 +225,9 @@
         & ((order_branch[:, None, :] == 0) | (order_branch[:, None, :] == own_branch[:, :, None]))
     )
     bias_all = jnp.where(allowed, 0.0, -jnp.inf).astype(jnp.float32)
+    need_all = jnp.any(
+        allowed.reshape(micro_count, row_count, seq_len // CHUNK, CHUNK), axis=(1, 3)
+    ).astype(jnp.int32)
     angles = own_rotary.astype(jnp.float32)[..., None] * frequencies()
     cos_all = jnp.cos(angles)
     sin_all = jnp.sin(angles)
@@ -200,6 +240,7 @@
         cosine = lax.dynamic_index_in_dim(cos_all, mb, 0, keepdims=False)
         sine_part = lax.dynamic_index_in_dim(sin_all, mb, 0, keepdims=False)
         bias = lax.dynamic_index_in_dim(bias_all, mb, 0, keepdims=False)
+        need = lax.dynamic_index_in_dim(need_all, mb, 0, keepdims=False)
         widened = current.astype(jnp.float32)
         norm_scale = lax.rsqrt(jnp.mean(widened * widened, axis=-1, keepdims=True) + 1e-05)
         normed = (widened * norm_scale * gain_row).astype(jnp.bfloat16)
@@ -223,7 +264,7 @@
             .astype(jnp.bfloat16)
             .reshape(row_count, HQ * HD)
         )
-        return attention(turned, kv_all, bias, current)
+        return attention(need, turned, kv_all, bias, current)
 
     tick_count = section_count + micro_count - 1
 

time: 871 us -> 1250 us (1.44)
  the two profiles are of different devices: /device:TPU:14 before, /device:TPU:8 now
where the time goes in v5:
time: 1250 us; the launch traced here: 1230 us
  Pallas kernels  499 us (40%)
  starting transfers between devices  252 us (20%)
  waiting for transfers between devices  243 us (19%)
  other arithmetic  117 us (9%)
  local copies, waits for them, and re-layouts  103 us (8%)
    pallas_call x9, Pallas kernels, attention(): pl.pallas_call(attention_kernel, grid_spec=grid_spec, out_shape=jax.Shape...  499 us
    ppermute x144, starting transfers between devices, shift(): return lax.ppermute(piece, 'seq', pairs)  234 us
    ppermute x144, waiting for transfers between devices, shift(): return lax.ppermute(piece, 'seq', pairs)  159 us
    ppermute x9, waiting for transfers between devices, from_behind(): return lax.ppermute(value, axis, pairs)  83.5 us
    while x252, local copies, waits for them, and re-layouts  42.8 us
  transfers between devices with their start and end apart: 153, of which 60 were waited for; matrix products, arithmetic and copies ran while one was open for 10% of the time, Pallas kernels for 0%

profile of v5, /device:TPU:8, one launch (start us, length us, event | category | flops | bytes accessed | tf_op | source)
XLA Modules:
  0.0 1229.6 jit_solution(4516551432220336388)
XLA Ops:
  14.3 7.9 pad_maximum_fusion.5
  23.7 1205.8 %while.17 = (s32[]{:T(128)}, bf16[128,4096]{1,0:T(8,128)(2,1)S(1)}, bf16[2,128,4096]{2,1,0:T(8,128)(2,1)}, s32[]{:T(128)}, s32[2,16]{1,0:T(2,128)}, /*index=5*/b...) while((s32[]{:T(128)}, bf16[128,4096]{1,0:T(8,128)(2,1)S(1)}, ...), condition=%wide.region_10.13_spmd.clone, body=%wide.region_8.12_spmd.clone.sunk | while | flops 1103626368 | bytes 146167056 | solution.py:287
  30.7 9.4 collective-permute-done
  50.1 4.0 collective-permute-start.1
  66.1 3.3 collective-permute-start.14
  74.6 9.9 collective-permute-done.5
  97.2 63.0 %eval_jaxpr.6 = bf16[128,4096]{1,0:T(8,128)(2,1)} custom-call(s32[16]{0:T(128)} %fusion.34.need_ref, bf16[128,4096]{1,0:T(8,128)(2,1)} %bitcast.96, bf16[2048,1024]{1,0:T(8,128)(2,1)} %pad_maximum_fusion.15.k_ref.v_ref, bf16[2048,1024]{1,0:T(8,128)(2,1)} %pad_maximum_fusion.15.k_ref.v_ref, f32[128,2048]{1,0:T(8,128)} %dynamic-slice_bitcast_fusion.6.bias_ref, ...), custom_call_target="tpu_custom_call" | custom-call | tf_op jit(solution)/shard_map/while/body/eval_jaxpr/pallas_call | solution.py:193
  168.9 9.4 collective-permute-done
  192.5 3.3 collective-permute-start.12
  197.2 5.0 collective-permute-start.2
  212.5 9.9 collective-permute-done.5
  235.9 63.0 %eval_jaxpr.6 = bf16[128,4096]{1,0:T(8,128)(2,1)} custom-call(s32[16]{0:T(128)} %fusion.34.need_ref, bf16[128,4096]{1,0:T(8,128)(2,1)} %bitcast.96, bf16[2048,1024]{1,0:T(8,128)(2,1)} %pad_maximum_fusion.15.k_ref.v_ref, bf16[2048,1024]{1,0:T(8,128)(2,1)} %pad_maximum_fusion.15.k_ref.v_ref, f32[128,2048]{1,0:T(8,128)} %dynamic-slice_bitcast_fusion.6.bias_ref, ...), custom_call_target="tpu_custom_call" | custom-call | tf_op jit(solution)/shard_map/while/body/eval_jaxpr/pallas_call | solution.py:193
  307.7 9.4 collective-permute-done
  331.3 3.3 collective-permute-start.12
  336.0 4.2 collective-permute-start.2
  350.5 9.9 collective-permute-done.5
  373.9 63.0 %eval_jaxpr.6 = bf16[128,4096]{1,0:T(8,128)(2,1)} custom-call(s32[16]{0:T(128)} %fusion.34.need_ref, bf16[128,4096]{1,0:T(8,128)(2,1)} %bitcast.96, bf16[2048,1024]{1,0:T(8,128)(2,1)} %pad_maximum_fusion.15.k_ref.v_ref, bf16[2048,1024]{1,0:T(8,128)(2,1)} %pad_maximum_fusion.15.k_ref.v_ref, f32[128,2048]{1,0:T(8,128)} %dynamic-slice_bitcast_fusion.6.bias_ref, ...), custom_call_target="tpu_custom_call" | custom-call | tf_op jit(solution)/shard_map/while/body/eval_jaxpr/pallas_call | solution.py:193
  446.9 9.4 collective-permute-done
  470.5 3.3 collective-permute-start.12
  475.2 4.2 collective-permute-start.2
  489.1 9.9 collective-permute-done.5
  513.1 51.7 %eval_jaxpr.6 = bf16[128,4096]{1,0:T(8,128)(2,1)} custom-call(s32[16]{0:T(128)} %fusion.34.need_ref, bf16[128,4096]{1,0:T(8,128)(2,1)} %bitcast.96, bf16[2048,1024]{1,0:T(8,128)(2,1)} %pad_maximum_fusion.15.k_ref.v_ref, bf16[2048,1024]{1,0:T(8,128)(2,1)} %pad_maximum_fusion.15.k_ref.v_ref, f32[128,2048]{1,0:T(8,128)} %dynamic-slice_bitcast_fusion.6.bias_ref, ...), custom_call_target="tpu_custom_call" | custom-call | tf_op jit(solution)/shard_map/while/body/eval_jaxpr/pallas_call | solution.py:193
  575.5 8.6 collective-permute-done
  594.2 8.0 collective-permute-start.1
  614.2 3.3 collective-permute-start.14
  622.6 9.9 collective-permute-done.5
  645.2 51.7 %eval_jaxpr.6 = bf16[128,4096]{1,0:T(8,128)(2,1)} custom-call(s32[16]{0:T(128)} %fusion.34.need_ref, bf16[128,4096]{1,0:T(8,128)(2,1)} %bitcast.96, bf16[2048,1024]{1,0:T(8,128)(2,1)} %pad_maximum_fusion.15.k_ref.v_ref, bf16[2048,1024]{1,0:T(8,128)(2,1)} %pad_maximum_fusion.15.k_ref.v_ref, f32[128,2048]{1,0:T(8,128)} %dynamic-slice_bitcast_fusion.6.bias_ref, ...), custom_call_target="tpu_custom_call" | custom-call | tf_op jit(solution)/shard_map/while/body/eval_jaxpr/pallas_call | solution.py:193
  705.7 9.4 collective-permute-done
  725.1 8.7 collective-permute-start.1
  745.8 3.3 collective-permute-start.14
  753.5 10.9 collective-permute-done.5
  769.5 4.7 collective-permute-done.6
  780.8 51.7 %eval_jaxpr.6 = bf16[128,4096]{1,0:T(8,128)(2,1)} custom-call(s32[16]{0:T(128)} %fusion.34.need_ref, bf16[128,4096]{1,0:T(8,128)(2,1)} %bitcast.96, bf16[2048,1024]{1,0:T(8,128)(2,1)} %pad_maximum_fusion.15.k_ref.v_ref, bf16[2048,1024]{1,0:T(8,128)(2,1)} %pad_maximum_fusion.15.k_ref.v_ref, f32[128,2048]{1,0:T(8,128)} %dynamic-slice_bitcast_fusion.6.bias_ref, ...), custom_call_target="tpu_custom_call" | custom-call | tf_op jit(solution)/shard_map/while/body/eval_jaxpr/pallas_call | solution.py:193
  841.3 9.4 collective-permute-done
  860.7 9.0 collective-permute-start.1
  881.7 3.3 collective-permute-start.14
  890.1 9.9 collective-permute-done.5
  912.7 51.7 %eval_jaxpr.6 = bf16[128,4096]{1,0:T(8,128)(2,1)} custom-call(s32[16]{0:T(128)} %fusion.34.need_ref, bf16[128,4096]{1,0:T(8,128)(2,1)} %bitcast.96, bf16[2048,1024]{1,0:T(8,128)(2,1)} %pad_maximum_fusion.15.k_ref.v_ref, bf16[2048,1024]{1,0:T(8,128)(2,1)} %pad_maximum_fusion.15.k_ref.v_ref, f32[128,2048]{1,0:T(8,128)} %dynamic-slice_bitcast_fusion.6.bias_ref, ...), custom_call_target="tpu_custom_call" | custom-call | tf_op jit(solution)/shard_map/while/body/eval_jaxpr/pallas_call | solution.py:193
  973.2 9.4 collective-permute-done
  992.6 8.8 collective-permute-start.1
  1013.3 3.3 collective-permute-start.14
  1021.3 9.9 collective-permute-done.5
  1044.4 51.7 %eval_jaxpr.6 = bf16[128,4096]{1,0:T(8,128)(2,1)} custom-call(s32[16]{0:T(128)} %fusion.34.need_ref, bf16[128,4096]{1,0:T(8,128)(2,1)} %bitcast.96, bf16[2048,1024]{1,0:T(8,128)(2,1)} %pad_maximum_fusion.15.k_ref.v_ref, bf16[2048,1024]{1,0:T(8,128)(2,1)} %pad_maximum_fusion.15.k_ref.v_ref, f32[128,2048]{1,0:T(8,128)} %dynamic-slice_bitcast_fusion.6.bias_ref, ...), custom_call_target="tpu_custom_call" | custom-call | tf_op jit(solution)/shard_map/while/body/eval_jaxpr/pallas_call | solution.py:193
  1104.8 9.4 collective-permute-done
  1124.3 8.8 collective-permute-start.1
  1145.0 3.3 collective-permute-start.14
  1152.7 9.9 collective-permute-done.5
  1176.0 51.7 %eval_jaxpr.6 = bf16[128,4096]{1,0:T(8,128)(2,1)} custom-call(s32[16]{0:T(128)} %fusion.34.need_ref, bf16[128,4096]{1,0:T(8,128)(2,1)} %bitcast.96, bf16[2048,1024]{1,0:T(8,128)(2,1)} %pad_maximum_fusion.15.k_ref.v_ref, bf16[2048,1024]{1,0:T(8,128)(2,1)} %pad_maximum_fusion.15.k_ref.v_ref, f32[128,2048]{1,0:T(8,128)} %dynamic-slice_bitcast_fusion.6.bias_ref, ...), custom_call_target="tpu_custom_call" | custom-call | tf_op jit(solution)/shard_map/while/body/eval_jaxpr/pallas_call | solution.py:193
  (858 shorter events, 450.6 us)
Async XLA Ops:
  23.8 16.2 %collective-permute-start = (bf16[128,4096]{1,0:T(8,128)(2,1)S(1)}, bf16[128,4096]{1,0:T(8,128)(2,1)}, u32[]{:S(2)}, u32[]{:S(2)}) collective-permute-start(bf16[128,4096]{1,0:T(8,128)(2,1)S(1)} %broadcast_select_fusion.4), channel_id=1, source_target_pairs={{0,16},{16,32},{32,48},{48,64},{64,80},{80,96},{96,112},{1,17},{17... | collective-permute-start | bytes 3145736 | tf_op jit(solution)/shard_map/while/body/eval_jaxpr/ppermute | solution.py:22
  66.0 20.8 %collective-permute-start.13 = (bf16[512,512]{1,0:T(8,128)(2,1)S(1)}, bf16[512,512]{1,0:T(8,128)(2,1)S(1)}, u32[]{:S(2)}, u32[]{:S(2)}) collective-permute-start(bf16[512,512]{1,0:T(8,128)(2,1)S(1)} %maximum_maximum_fusion.5), channel_id=1, source_target_pairs={{0,4},{1,5},{2,6},{3,7},{4,8},{5,9},{6,10},{7,11},{8,12},{9,13},{1... | collective-permute-start | bytes 1572872 | tf_op jit(solution)/shard_map/while/body/eval_jaxpr/ppermute | solution.py:87
  66.1 20.5 %collective-permute-start.14 = (bf16[512,512]{1,0:T(8,128)(2,1)S(1)}, bf16[512,512]{1,0:T(8,128)(2,1)S(1)}, u32[]{:S(2)}, u32[]{:S(2)}) collective-permute-start(bf16[512,512]{1,0:T(8,128)(2,1)S(1)} %maximum_maximum_fusion.5), channel_id=1, source_target_pairs={{0,12},{1,13},{2,14},{3,15},{4,0},{5,1},{6,2},{7,3},{8,4},{9,5},{1... | collective-permute-start | bytes 1572872 | tf_op jit(solution)/shard_map/while/body/eval_jaxpr/ppermute | solution.py:87
  162.1 16.2 %collective-permute-start = (bf16[128,4096]{1,0:T(8,128)(2,1)S(1)}, bf16[128,4096]{1,0:T(8,128)(2,1)}, u32[]{:S(2)}, u32[]{:S(2)}) collective-permute-start(bf16[128,4096]{1,0:T(8,128)(2,1)S(1)} %broadcast_select_fusion.4), channel_id=1, source_target_pairs={{0,16},{16,32},{32,48},{48,64},{64,80},{80,96},{96,112},{1,17},{17... | collective-permute-start | bytes 3145736 | tf_op jit(solution)/shard_map/while/body/eval_jaxpr/ppermute | solution.py:22
  188.4 13.8 %collective-permute-start.3 = (bf16[128,512]{1,0:T(8,128)(2,1)}, bf16[128,512]{1,0:T(8,128)(2,1)}, u32[]{:S(2)}, u32[]{:S(2)}) collective-permute-start(bf16[128,512]{1,0:T(8,128)(2,1)} %slice.268), channel_id=1, source_target_pairs={{0,4},{1,5},{2,6},{3,7},{4,8},{5,9},{6,10},{7,11},{8,12},{9,13},{1... | collective-permute-start | bytes 393224 | tf_op jit(solution)/shard_map/while/body/eval_jaxpr/ppermute | solution.py:87
  204.0 21.6 %collective-permute-start.13 = (bf16[512,512]{1,0:T(8,128)(2,1)S(1)}, bf16[512,512]{1,0:T(8,128)(2,1)S(1)}, u32[]{:S(2)}, u32[]{:S(2)}) collective-permute-start(bf16[512,512]{1,0:T(8,128)(2,1)S(1)} %maximum_maximum_fusion.5), channel_id=1, source_target_pairs={{0,4},{1,5},{2,6},{3,7},{4,8},{5,9},{6,10},{7,11},{8,12},{9,13},{1... | collective-permute-start | bytes 1572872 | tf_op jit(solution)/shard_map/while/body/eval_jaxpr/ppermute | solution.py:87
  205.5 19.2 %collective-permute-start.14 = (bf16[512,512]{1,0:T(8,128)(2,1)S(1)}, bf16[512,512]{1,0:T(8,128)(2,1)S(1)}, u32[]{:S(2)}, u32[]{:S(2)}) collective-permute-start(bf16[512,512]{1,0:T(8,128)(2,1)S(1)} %maximum_maximum_fusion.5), channel_id=1, source_target_pairs={{0,12},{1,13},{2,14},{3,15},{4,0},{5,1},{6,2},{7,3},{8,4},{9,5},{1... | collective-permute-start | bytes 1572872 | tf_op jit(solution)/shard_map/while/body/eval_jaxpr/ppermute | solution.py:87
  300.8 16.2 %collective-permute-start = (bf16[128,4096]{1,0:T(8,128)(2,1)S(1)}, bf16[128,4096]{1,0:T(8,128)(2,1)}, u32[]{:S(2)}, u32[]{:S(2)}) collective-permute-start(bf16[128,4096]{1,0:T(8,128)(2,1)S(1)} %broadcast_select_fusion.4), channel_id=1, source_target_pairs={{0,16},{16,32},{32,48},{48,64},{64,80},{80,96},{96,112},{1,17},{17... | collective-permute-start | bytes 3145736 | tf_op jit(solution)/shard_map/while/body/eval_jaxpr/ppermute | solution.py:22
  327.1 13.1 %collective-permute-start.3 = (bf16[128,512]{1,0:T(8,128)(2,1)}, bf16[128,512]{1,0:T(8,128)(2,1)}, u32[]{:S(2)}, u32[]{:S(2)}) collective-permute-start(bf16[128,512]{1,0:T(8,128)(2,1)} %slice.268), channel_id=1, source_target_pairs={{0,4},{1,5},{2,6},{3,7},{4,8},{5,9},{6,10},{7,11},{8,12},{9,13},{1... | collective-permute-start | bytes 393224 | tf_op jit(solution)/shard_map/while/body/eval_jaxpr/ppermute | solution.py:87
  342.0 21.5 %collective-permute-start.13 = (bf16[512,512]{1,0:T(8,128)(2,1)S(1)}, bf16[512,512]{1,0:T(8,128)(2,1)S(1)}, u32[]{:S(2)}, u32[]{:S(2)}) collective-permute-start(bf16[512,512]{1,0:T(8,128)(2,1)S(1)} %maximum_maximum_fusion.5), channel_id=1, source_target_pairs={{0,4},{1,5},{2,6},{3,7},{4,8},{5,9},{6,10},{7,11},{8,12},{9,13},{1... | collective-permute-start | bytes 1572872 | tf_op jit(solution)/shard_map/while/body/eval_jaxpr/ppermute | solution.py:87
  343.5 19.2 %collective-permute-start.14 = (bf16[512,512]{1,0:T(8,128)(2,1)S(1)}, bf16[512,512]{1,0:T(8,128)(2,1)S(1)}, u32[]{:S(2)}, u32[]{:S(2)}) collective-permute-start(bf16[512,512]{1,0:T(8,128)(2,1)S(1)} %maximum_maximum_fusion.5), channel_id=1, source_target_pairs={{0,12},{1,13},{2,14},{3,15},{4,0},{5,1},{6,2},{7,3},{8,4},{9,5},{1... | collective-permute-start | bytes 1572872 | tf_op jit(solution)/shard_map/while/body/eval_jaxpr/ppermute | solution.py:87
  440.0 16.2 %collective-permute-start = (bf16[128,4096]{1,0:T(8,128)(2,1)S(1)}, bf16[128,4096]{1,0:T(8,128)(2,1)}, u32[]{:S(2)}, u32[]{:S(2)}) collective-permute-start(bf16[128,4096]{1,0:T(8,128)(2,1)S(1)} %broadcast_select_fusion.4), channel_id=1, source_target_pairs={{0,16},{16,32},{32,48},{48,64},{64,80},{80,96},{96,112},{1,17},{17... | collective-permute-start | bytes 3145736 | tf_op jit(solution)/shard_map/while/body/eval_jaxpr/ppermute | solution.py:22
  481.2 21.5 %collective-permute-start.13 = (bf16[512,512]{1,0:T(8,128)(2,1)S(1)}, bf16[512,512]{1,0:T(8,128)(2,1)S(1)}, u32[]{:S(2)}, u32[]{:S(2)}) collective-permute-start(bf16[512,512]{1,0:T(8,128)(2,1)S(1)} %maximum_maximum_fusion.5), channel_id=1, source_target_pairs={{0,4},{1,5},{2,6},{3,7},{4,8},{5,9},{6,10},{7,11},{8,12},{9,13},{1... | collective-permute-start | bytes 1572872 | tf_op jit(solution)/shard_map/while/body/eval_jaxpr/ppermute | solution.py:87
  482.7 18.5 %collective-permute-start.14 = (bf16[512,512]{1,0:T(8,128)(2,1)S(1)}, bf16[512,512]{1,0:T(8,128)(2,1)S(1)}, u32[]{:S(2)}, u32[]{:S(2)}) collective-permute-start(bf16[512,512]{1,0:T(8,128)(2,1)S(1)} %maximum_maximum_fusion.5), channel_id=1, source_target_pairs={{0,12},{1,13},{2,14},{3,15},{4,0},{5,1},{6,2},{7,3},{8,4},{9,5},{1... | collective-permute-start | bytes 1572872 | tf_op jit(solution)/shard_map/while/body/eval_jaxpr/ppermute | solution.py:87
  487.3 13.3 %collective-permute-start.7 = (bf16[512,512]{1,0:T(8,128)(2,1)S(1)}, bf16[512,512]{1,0:T(8,128)(2,1)S(1)}, u32[]{:S(2)}, u32[]{:S(2)}) collective-permute-start(bf16[512,512]{1,0:T(8,128)(2,1)S(1)} %maximum_maximum_fusion.4), channel_id=1, source_target_pairs={{0,1},{1,2},{2,3},{3,0},{4,5},{5,6},{6,7},{7,4},{8,9},{9,10},{10,1... | collective-permute-start | bytes 1572872 | tf_op jit(solution)/shard_map/while/body/eval_jaxpr/ppermute | solution.py:87
  567.9 16.2 %collective-permute-start = (bf16[128,4096]{1,0:T(8,128)(2,1)S(1)}, bf16[128,4096]{1,0:T(8,128)(2,1)}, u32[]{:S(2)}, u32[]{:S(2)}) collective-permute-start(bf16[128,4096]{1,0:T(8,128)(2,1)S(1)} %broadcast_select_fusion.4), channel_id=1, source_target_pairs={{0,16},{16,32},{32,48},{48,64},{64,80},{80,96},{96,112},{1,17},{17... | collective-permute-start | bytes 3145736 | tf_op jit(solution)/shard_map/while/body/eval_jaxpr/ppermute | solution.py:22
  589.4 14.9 %collective-permute-start.9 = (bf16[128,512]{1,0:T(8,128)(2,1)}, bf16[128,512]{1,0:T(8,128)(2,1)S(1)}, u32[]{:S(2)}, u32[]{:S(2)}) collective-permute-start(bf16[128,512]{1,0:T(8,128)(2,1)} %bitcast.91), channel_id=1, source_target_pairs={{0,1},{1,2},{2,3},{3,0},{4,5},{5,6},{6,7},{7,4},{8,9},{9,10},{10,1... | collective-permute-start | bytes 393224 | tf_op jit(solution)/shard_map/while/body/eval_jaxpr/ppermute | solution.py:87
  589.4 17.0 %collective-permute-start.10 = (bf16[128,512]{1,0:T(8,128)(2,1)}, bf16[128,512]{1,0:T(8,128)(2,1)S(1)}, u32[]{:S(2)}, u32[]{:S(2)}) collective-permute-start(bf16[128,512]{1,0:T(8,128)(2,1)} %bitcast.91), channel_id=1, source_target_pairs={{0,3},{1,0},{2,1},{3,2},{4,7},{5,4},{6,5},{7,6},{8,11},{9,8},{10,9... | collective-permute-start | bytes 393224 | tf_op jit(solution)/shard_map/while/body/eval_jaxpr/ppermute | solution.py:87
  594.2 14.0 %collective-permute-start.1 = (bf16[128,512]{1,0:T(8,128)(2,1)}, bf16[128,512]{1,0:T(8,128)(2,1)}, u32[]{:S(2)}, u32[]{:S(2)}) collective-permute-start(bf16[128,512]{1,0:T(8,128)(2,1)} %slice.268), channel_id=1, source_target_pairs={{0,12},{1,13},{2,14},{3,15},{4,0},{5,1},{6,2},{7,3},{8,4},{9,5},{1... | collective-permute-start | bytes 393224 | tf_op jit(solution)/shard_map/while/body/eval_jaxpr/ppermute | solution.py:87
  614.1 20.8 %collective-permute-start.13 = (bf16[512,512]{1,0:T(8,128)(2,1)S(1)}, bf16[512,512]{1,0:T(8,128)(2,1)S(1)}, u32[]{:S(2)}, u32[]{:S(2)}) collective-permute-start(bf16[512,512]{1,0:T(8,128)(2,1)S(1)} %maximum_maximum_fusion.5), channel_id=1, source_target_pairs={{0,4},{1,5},{2,6},{3,7},{4,8},{5,9},{6,10},{7,11},{8,12},{9,13},{1... | collective-permute-start | bytes 1572872 | tf_op jit(solution)/shard_map/while/body/eval_jaxpr/ppermute | solution.py:87
  614.2 20.6 %collective-permute-start.14 = (bf16[512,512]{1,0:T(8,128)(2,1)S(1)}, bf16[512,512]{1,0:T(8,128)(2,1)S(1)}, u32[]{:S(2)}, u32[]{:S(2)}) collective-permute-start(bf16[512,512]{1,0:T(8,128)(2,1)S(1)} %maximum_maximum_fusion.5), channel_id=1, source_target_pairs={{0,12},{1,13},{2,14},{3,15},{4,0},{5,1},{6,2},{7,3},{8,4},{9,5},{1... | collective-permute-start | bytes 1572872 | tf_op jit(solution)/shard_map/while/body/eval_jaxpr/ppermute | solution.py:87
  698.8 16.2 %collective-permute-start = (bf16[128,4096]{1,0:T(8,128)(2,1)S(1)}, bf16[128,4096]{1,0:T(8,128)(2,1)}, u32[]{:S(2)}, u32[]{:S(2)}) collective-permute-start(bf16[128,4096]{1,0:T(8,128)(2,1)S(1)} %broadcast_select_fusion.4), channel_id=1, source_target_pairs={{0,16},{16,32},{32,48},{48,64},{64,80},{80,96},{96,112},{1,17},{17... | collective-permute-start | bytes 3145736 | tf_op jit(solution)/shard_map/while/body/eval_jaxpr/ppermute | solution.py:22
  720.3 15.6 %collective-permute-start.9 = (bf16[128,512]{1,0:T(8,128)(2,1)}, bf16[128,512]{1,0:T(8,128)(2,1)S(1)}, u32[]{:S(2)}, u32[]{:S(2)}) collective-permute-start(bf16[128,512]{1,0:T(8,128)(2,1)} %bitcast.91), channel_id=1, source_target_pairs={{0,1},{1,2},{2,3},{3,0},{4,5},{5,6},{6,7},{7,4},{8,9},{9,10},{10,1... | collective-permute-start | bytes 393224 | tf_op jit(solution)/shard_map/while/body/eval_jaxpr/ppermute | solution.py:87
  720.3 17.7 %collective-permute-start.10 = (bf16[128,512]{1,0:T(8,128)(2,1)}, bf16[128,512]{1,0:T(8,128)(2,1)S(1)}, u32[]{:S(2)}, u32[]{:S(2)}) collective-permute-start(bf16[128,512]{1,0:T(8,128)(2,1)} %bitcast.91), channel_id=1, source_target_pairs={{0,3},{1,0},{2,1},{3,2},{4,7},{5,4},{6,5},{7,6},{8,11},{9,8},{10,9... | collective-permute-start | bytes 393224 | tf_op jit(solution)/shard_map/while/body/eval_jaxpr/ppermute | solution.py:87
  725.1 14.7 %collective-permute-start.1 = (bf16[128,512]{1,0:T(8,128)(2,1)}, bf16[128,512]{1,0:T(8,128)(2,1)}, u32[]{:S(2)}, u32[]{:S(2)}) collective-permute-start(bf16[128,512]{1,0:T(8,128)(2,1)} %slice.268), channel_id=1, source_target_pairs={{0,12},{1,13},{2,14},{3,15},{4,0},{5,1},{6,2},{7,3},{8,4},{9,5},{1... | collective-permute-start | bytes 393224 | tf_op jit(solution)/shard_map/while/body/eval_jaxpr/ppermute | solution.py:87
  745.7 22.8 %collective-permute-start.13 = (bf16[512,512]{1,0:T(8,128)(2,1)S(1)}, bf16[512,512]{1,0:T(8,128)(2,1)S(1)}, u32[]{:S(2)}, u32[]{:S(2)}) collective-permute-start(bf16[512,512]{1,0:T(8,128)(2,1)S(1)} %maximum_maximum_fusion.5), channel_id=1, source_target_pairs={{0,4},{1,5},{2,6},{3,7},{4,8},{5,9},{6,10},{7,11},{8,12},{9,13},{1... | collective-permute-start | bytes 1572872 | tf_op jit(solution)/shard_map/while/body/eval_jaxpr/ppermute | solution.py:87
  745.8 21.4 %collective-permute-start.14 = (bf16[512,512]{1,0:T(8,128)(2,1)S(1)}, bf16[512,512]{1,0:T(8,128)(2,1)S(1)}, u32[]{:S(2)}, u32[]{:S(2)}) collective-permute-start(bf16[512,512]{1,0:T(8,128)(2,1)S(1)} %maximum_maximum_fusion.5), channel_id=1, source_target_pairs={{0,12},{1,13},{2,14},{3,15},{4,0},{5,1},{6,2},{7,3},{8,4},{9,5},{1... | collective-permute-start | bytes 1572872 | tf_op jit(solution)/shard_map/while/body/eval_jaxpr/ppermute | solution.py:87
  751.4 14.4 %collective-permute-start.7 = (bf16[512,512]{1,0:T(8,128)(2,1)S(1)}, bf16[512,512]{1,0:T(8,128)(2,1)S(1)}, u32[]{:S(2)}, u32[]{:S(2)}) collective-permute-start(bf16[512,512]{1,0:T(8,128)(2,1)S(1)} %maximum_maximum_fusion.4), channel_id=1, source_target_pairs={{0,1},{1,2},{2,3},{3,0},{4,5},{5,6},{6,7},{7,4},{8,9},{9,10},{10,1... | collective-permute-start | bytes 1572872 | tf_op jit(solution)/shard_map/while/body/eval_jaxpr/ppermute | solution.py:87
  834.4 16.2 %collective-permute-start = (bf16[128,4096]{1,0:T(8,128)(2,1)S(1)}, bf16[128,4096]{1,0:T(8,128)(2,1)}, u32[]{:S(2)}, u32[]{:S(2)}) collective-permute-start(bf16[128,4096]{1,0:T(8,128)(2,1)S(1)} %broadcast_select_fusion.4), channel_id=1, source_target_pairs={{0,16},{16,32},{32,48},{48,64},{64,80},{80,96},{96,112},{1,17},{17... | collective-permute-start | bytes 3145736 | tf_op jit(solution)/shard_map/while/body/eval_jaxpr/ppermute | solution.py:22
  855.8 15.9 %collective-permute-start.9 = (bf16[128,512]{1,0:T(8,128)(2,1)}, bf16[128,512]{1,0:T(8,128)(2,1)S(1)}, u32[]{:S(2)}, u32[]{:S(2)}) collective-permute-start(bf16[128,512]{1,0:T(8,128)(2,1)} %bitcast.91), channel_id=1, source_target_pairs={{0,1},{1,2},{2,3},{3,0},{4,5},{5,6},{6,7},{7,4},{8,9},{9,10},{10,1... | collective-permute-start | bytes 393224 | tf_op jit(solution)/shard_map/while/body/eval_jaxpr/ppermute | solution.py:87
  855.8 18.0 %collective-permute-start.10 = (bf16[128,512]{1,0:T(8,128)(2,1)}, bf16[128,512]{1,0:T(8,128)(2,1)S(1)}, u32[]{:S(2)}, u32[]{:S(2)}) collective-permute-start(bf16[128,512]{1,0:T(8,128)(2,1)} %bitcast.91), channel_id=1, source_target_pairs={{0,3},{1,0},{2,1},{3,2},{4,7},{5,4},{6,5},{7,6},{8,11},{9,8},{10,9... | collective-permute-start | bytes 393224 | tf_op jit(solution)/shard_map/while/body/eval_jaxpr/ppermute | solution.py:87
  860.7 15.0 %collective-permute-start.1 = (bf16[128,512]{1,0:T(8,128)(2,1)}, bf16[128,512]{1,0:T(8,128)(2,1)}, u32[]{:S(2)}, u32[]{:S(2)}) collective-permute-start(bf16[128,512]{1,0:T(8,128)(2,1)} %slice.268), channel_id=1, source_target_pairs={{0,12},{1,13},{2,14},{3,15},{4,0},{5,1},{6,2},{7,3},{8,4},{9,5},{1... | collective-permute-start | bytes 393224 | tf_op jit(solution)/shard_map/while/body/eval_jaxpr/ppermute | solution.py:87
  881.6 20.8 %collective-permute-start.13 = (bf16[512,512]{1,0:T(8,128)(2,1)S(1)}, bf16[512,512]{1,0:T(8,128)(2,1)S(1)}, u32[]{:S(2)}, u32[]{:S(2)}) collective-permute-start(bf16[512,512]{1,0:T(8,128)(2,1)S(1)} %maximum_maximum_fusion.5), channel_id=1, source_target_pairs={{0,4},{1,5},{2,6},{3,7},{4,8},{5,9},{6,10},{7,11},{8,12},{9,13},{1... | collective-permute-start | bytes 1572872 | tf_op jit(solution)/shard_map/while/body/eval_jaxpr/ppermute | solution.py:87
  881.7 20.5 %collective-permute-start.14 = (bf16[512,512]{1,0:T(8,128)(2,1)S(1)}, bf16[512,512]{1,0:T(8,128)(2,1)S(1)}, u32[]{:S(2)}, u32[]{:S(2)}) collective-permute-start(bf16[512,512]{1,0:T(8,128)(2,1)S(1)} %maximum_maximum_fusion.5), channel_id=1, source_target_pairs={{0,12},{1,13},{2,14},{3,15},{4,0},{5,1},{6,2},{7,3},{8,4},{9,5},{1... | collective-permute-start | bytes 1572872 | tf_op jit(solution)/shard_map/while/body/eval_jaxpr/ppermute | solution.py:87
  966.3 16.2 %collective-permute-start = (bf16[128,4096]{1,0:T(8,128)(2,1)S(1)}, bf16[128,4096]{1,0:T(8,128)(2,1)}, u32[]{:S(2)}, u32[]{:S(2)}) collective-permute-start(bf16[128,4096]{1,0:T(8,128)(2,1)S(1)} %broadcast_select_fusion.4), channel_id=1, source_target_pairs={{0,16},{16,32},{32,48},{48,64},{64,80},{80,96},{96,112},{1,17},{17... | collective-permute-start | bytes 3145736 | tf_op jit(solution)/shard_map/while/body/eval_jaxpr/ppermute | solution.py:22
  987.7 15.6 %collective-permute-start.9 = (bf16[128,512]{1,0:T(8,128)(2,1)}, bf16[128,512]{1,0:T(8,128)(2,1)S(1)}, u32[]{:S(2)}, u32[]{:S(2)}) collective-permute-start(bf16[128,512]{1,0:T(8,128)(2,1)} %bitcast.91), channel_id=1, source_target_pairs={{0,1},{1,2},{2,3},{3,0},{4,5},{5,6},{6,7},{7,4},{8,9},{9,10},{10,1... | collective-permute-start | bytes 393224 | tf_op jit(solution)/shard_map/while/body/eval_jaxpr/ppermute | solution.py:87
  987.7 17.7 %collective-permute-start.10 = (bf16[128,512]{1,0:T(8,128)(2,1)}, bf16[128,512]{1,0:T(8,128)(2,1)S(1)}, u32[]{:S(2)}, u32[]{:S(2)}) collective-permute-start(bf16[128,512]{1,0:T(8,128)(2,1)} %bitcast.91), channel_id=1, source_target_pairs={{0,3},{1,0},{2,1},{3,2},{4,7},{5,4},{6,5},{7,6},{8,11},{9,8},{10,9... | collective-permute-start | bytes 393224 | tf_op jit(solution)/shard_map/while/body/eval_jaxpr/ppermute | solution.py:87
  992.6 14.8 %collective-permute-start.1 = (bf16[128,512]{1,0:T(8,128)(2,1)}, bf16[128,512]{1,0:T(8,128)(2,1)}, u32[]{:S(2)}, u32[]{:S(2)}) collective-permute-start(bf16[128,512]{1,0:T(8,128)(2,1)} %slice.268), channel_id=1, source_target_pairs={{0,12},{1,13},{2,14},{3,15},{4,0},{5,1},{6,2},{7,3},{8,4},{9,5},{1... | collective-permute-start | bytes 393224 | tf_op jit(solution)/shard_map/while/body/eval_jaxpr/ppermute | solution.py:87
  1013.2 20.8 %collective-permute-start.13 = (bf16[512,512]{1,0:T(8,128)(2,1)S(1)}, bf16[512,512]{1,0:T(8,128)(2,1)S(1)}, u32[]{:S(2)}, u32[]{:S(2)}) collective-permute-start(bf16[512,512]{1,0:T(8,128)(2,1)S(1)} %maximum_maximum_fusion.5), channel_id=1, source_target_pairs={{0,4},{1,5},{2,6},{3,7},{4,8},{5,9},{6,10},{7,11},{8,12},{9,13},{1... | collective-permute-start | bytes 1572872 | tf_op jit(solution)/shard_map/while/body/eval_jaxpr/ppermute | solution.py:87
  1013.3 20.1 %collective-permute-start.14 = (bf16[512,512]{1,0:T(8,128)(2,1)S(1)}, bf16[512,512]{1,0:T(8,128)(2,1)S(1)}, u32[]{:S(2)}, u32[]{:S(2)}) collective-permute-start(bf16[512,512]{1,0:T(8,128)(2,1)S(1)} %maximum_maximum_fusion.5), channel_id=1, source_target_pairs={{0,12},{1,13},{2,14},{3,15},{4,0},{5,1},{6,2},{7,3},{8,4},{9,5},{1... | collective-permute-start | bytes 1572872 | tf_op jit(solution)/shard_map/while/body/eval_jaxpr/ppermute | solution.py:87
  1019.5 13.3 %collective-permute-start.7 = (bf16[512,512]{1,0:T(8,128)(2,1)S(1)}, bf16[512,512]{1,0:T(8,128)(2,1)S(1)}, u32[]{:S(2)}, u32[]{:S(2)}) collective-permute-start(bf16[512,512]{1,0:T(8,128)(2,1)S(1)} %maximum_maximum_fusion.4), channel_id=1, source_target_pairs={{0,1},{1,2},{2,3},{3,0},{4,5},{5,6},{6,7},{7,4},{8,9},{9,10},{10,1... | collective-permute-start | bytes 1572872 | tf_op jit(solution)/shard_map/while/body/eval_jaxpr/ppermute | solution.py:87
  1098.0 16.2 %collective-permute-start = (bf16[128,4096]{1,0:T(8,128)(2,1)S(1)}, bf16[128,4096]{1,0:T(8,128)(2,1)}, u32[]{:S(2)}, u32[]{:S(2)}) collective-permute-start(bf16[128,4096]{1,0:T(8,128)(2,1)S(1)} %broadcast_select_fusion.4), channel_id=1, source_target_pairs={{0,16},{16,32},{32,48},{48,64},{64,80},{80,96},{96,112},{1,17},{17... | collective-permute-start | bytes 3145736 | tf_op jit(solution)/shard_map/while/body/eval_jaxpr/ppermute | solution.py:22
  1119.4 15.6 %collective-permute-start.9 = (bf16[128,512]{1,0:T(8,128)(2,1)}, bf16[128,512]{1,0:T(8,128)(2,1)S(1)}, u32[]{:S(2)}, u32[]{:S(2)}) collective-permute-start(bf16[128,512]{1,0:T(8,128)(2,1)} %bitcast.91), channel_id=1, source_target_pairs={{0,1},{1,2},{2,3},{3,0},{4,5},{5,6},{6,7},{7,4},{8,9},{9,10},{10,1... | collective-permute-start | bytes 393224 | tf_op jit(solution)/shard_map/while/body/eval_jaxpr/ppermute | solution.py:87
  1119.4 17.7 %collective-permute-start.10 = (bf16[128,512]{1,0:T(8,128)(2,1)}, bf16[128,512]{1,0:T(8,128)(2,1)S(1)}, u32[]{:S(2)}, u32[]{:S(2)}) collective-permute-start(bf16[128,512]{1,0:T(8,128)(2,1)} %bitcast.91), channel_id=1, source_target_pairs={{0,3},{1,0},{2,1},{3,2},{4,7},{5,4},{6,5},{7,6},{8,11},{9,8},{10,9... | collective-permute-start | bytes 393224 | tf_op jit(solution)/shard_map/while/body/eval_jaxpr/ppermute | solution.py:87
  1124.3 14.8 %collective-permute-start.1 = (bf16[128,512]{1,0:T(8,128)(2,1)}, bf16[128,512]{1,0:T(8,128)(2,1)}, u32[]{:S(2)}, u32[]{:S(2)}) collective-permute-start(bf16[128,512]{1,0:T(8,128)(2,1)} %slice.268), channel_id=1, source_target_pairs={{0,12},{1,13},{2,14},{3,15},{4,0},{5,1},{6,2},{7,3},{8,4},{9,5},{1... | collective-permute-start | bytes 393224 | tf_op jit(solution)/shard_map/while/body/eval_jaxpr/ppermute | solution.py:87
  1144.9 20.8 %collective-permute-start.13 = (bf16[512,512]{1,0:T(8,128)(2,1)S(1)}, bf16[512,512]{1,0:T(8,128)(2,1)S(1)}, u32[]{:S(2)}, u32[]{:S(2)}) collective-permute-start(bf16[512,512]{1,0:T(8,128)(2,1)S(1)} %maximum_maximum_fusion.5), channel_id=1, source_target_pairs={{0,4},{1,5},{2,6},{3,7},{4,8},{5,9},{6,10},{7,11},{8,12},{9,13},{1... | collective-permute-start | bytes 1572872 | tf_op jit(solution)/shard_map/while/body/eval_jaxpr/ppermute | solution.py:87
  1145.0 19.8 %collective-permute-start.14 = (bf16[512,512]{1,0:T(8,128)(2,1)S(1)}, bf16[512,512]{1,0:T(8,128)(2,1)S(1)}, u32[]{:S(2)}, u32[]{:S(2)}) collective-permute-start(bf16[512,512]{1,0:T(8,128)(2,1)S(1)} %maximum_maximum_fusion.5), channel_id=1, source_target_pairs={{0,12},{1,13},{2,14},{3,15},{4,0},{5,1},{6,2},{7,3},{8,4},{9,5},{1... | collective-permute-start | bytes 1572872 | tf_op jit(solution)/shard_map/while/body/eval_jaxpr/ppermute | solution.py:87
  1150.6 13.3 %collective-permute-start.7 = (bf16[512,512]{1,0:T(8,128)(2,1)S(1)}, bf16[512,512]{1,0:T(8,128)(2,1)S(1)}, u32[]{:S(2)}, u32[]{:S(2)}) collective-permute-start(bf16[512,512]{1,0:T(8,128)(2,1)S(1)} %maximum_maximum_fusion.4), channel_id=1, source_target_pairs={{0,1},{1,2},{2,3},{3,0},{4,5},{5,6},{6,7},{7,4},{8,9},{9,10},{10,1... | collective-permute-start | bytes 1572872 | tf_op jit(solution)/shard_map/while/body/eval_jaxpr/ppermute | solution.py:87
  (187 other events, 1839.2 us)

commit v6 on v4

--- a/solution.py
+++ b/solution.py
@@ -64,10 +64,7 @@
 def ring_gather(value, shift):
     ahead = shift(value, 1)
     behind = shift(value, -1)
-    width = value.shape[1] // 2
-    far = jnp.concatenate(
-        [shift(ahead[:, :width], 1), shift(behind[:, width:], -1)], axis=1
-    )
+    far = shift(ahead, 1)
     return [value, ahead, behind, far]
 
 

time: 871 us -> 820 us (0.941)
  the two profiles are of different devices: /device:TPU:14 before, /device:TPU:1 now
where the time goes in v6:
time: 820 us; the launch traced here: 817 us
  waiting for transfers between devices  207 us (25%)
  Pallas kernels  179 us (22%)
  starting transfers between devices  161 us (20%)
  other arithmetic  130 us (16%)
  local copies, waits for them, and re-layouts  125 us (15%)
  matrix products  12.2 us (1%)
    pallas_call x9, Pallas kernels, attention(): pl.pallas_call(attention_kernel, grid=(HK,), in_specs=[pl.BlockSpec((rows...  179 us
    ppermute x108, waiting for transfers between devices, shift(): return lax.ppermute(piece, 'seq', pairs)  120 us
    ppermute x9, waiting for transfers between devices, from_behind(): return lax.ppermute(value, axis, pairs)  87.3 us
    while x252, local copies, waits for them, and re-layouts  82.6 us
    ppermute x9, starting transfers between devices, from_behind(): return lax.ppermute(value, axis, pairs)  80.8 us
    ppermute x108, starting transfers between devices, shift(): return lax.ppermute(piece, 'seq', pairs)  80.6 us
    concatenate x9, other arithmetic, torus_gather(): return jnp.concatenate([full_a, full_b], axis=1)  23.4 us
    squeeze x9, local copies, waits for them, and re-layouts, run_layer(): bias = lax.dynamic_index_in_dim(bias_all, mb, 0, keepdims=False)  20.8 us
  transfers between devices with their start and end apart: 117, of which 74 were waited for; matrix products, arithmetic and copies ran while one was open for 20% of the time, Pallas kernels for 0%

profile of v6, /device:TPU:1, one launch (start us, length us, event | category | flops | bytes accessed | tf_op | source)
XLA Modules:
  0.0 817.3 jit_solution(11999080591545614843)
XLA Ops:
  11.3 7.9 pad_maximum_fusion.5
  20.8 796.5 %while.17 = (s32[]{:T(128)}, bf16[128,4096]{1,0:T(8,128)(2,1)S(1)}, bf16[2,128,4096]{2,1,0:T(8,128)(2,1)}, s32[]{:T(128)}, bf16[1,2,128,4096]{3,2,1,0:T(8,128)(2...) while((s32[]{:T(128)}, bf16[128,4096]{1,0:T(8,128)(2,1)S(1)}, ...), condition=%wide.region_9.12_spmd.clone, body=%wide.region_7.11_spmd.clone.sunk | while | flops 1098383488 | bytes 143020560 | solution.py:243
  20.9 4.6 collective-permute-start
  27.5 9.7 %collective-permute-done = bf16[128,4096]{1,0:T(8,128)(2,1)} collective-permute-done((bf16[128,4096]{1,0:T(8,128)(2,1)S(1)}, bf16[128,4096]{1,0:T(8,128)(2,1)}, u32[]{:S(2)}, u32[]{:S(2)}) %collective-permute-start) | collective-permute-done | bytes 1048608 | tf_op jit(solution)/shard_map/while/body/eval_jaxpr/ppermute | solution.py:22
  58.4 2.7 collective-permute-start.11
  67.7 3.4 collective-permute-done.10
  84.4 19.9 %eval_jaxpr.6 = bf16[128,4096]{1,0:T(8,128)(2,1)} custom-call(bf16[128,4096]{1,0:T(8,128)(2,1)} %bitcast.89, bf16[2048,1024]{1,0:T(8,128)(2,1)} %pad_maximum_fusion.15.k_ref.v_ref, bf16[2048,1024]{1,0:T(8,128)(2,1)} %pad_maximum_fusion.15.k_ref.v_ref, f32[128,2048]{1,0:T(8,128)} %dynamic-slice_bitcast_fusion.6.bias_ref, bf16[128,4096]{1,0:T(8,128)(2,1)} %copy-done.1), custom_call_target="tpu_custom_call" | custom-call | tf_op jit(solution)/shard_map/while/body/eval_jaxpr/pallas_call | solution.py:145
  106.2 8.2 %collective-permute-start = (bf16[128,4096]{1,0:T(8,128)(2,1)S(1)}, bf16[128,4096]{1,0:T(8,128)(2,1)}, u32[]{:S(2)}, u32[]{:S(2)}) collective-permute-start(bf16[128,4096]{1,0:T(8,128)(2,1)S(1)} %broadcast_select_fusion.4), channel_id=1, source_target_pairs={{0,16},{16,32},{32,48},{48,64},{64,80},{80,96},{96,112},{1,17},{17... | collective-permute-start | bytes 3145736 | tf_op jit(solution)/shard_map/while/body/eval_jaxpr/ppermute | solution.py:22
  116.5 9.7 %collective-permute-done = bf16[128,4096]{1,0:T(8,128)(2,1)} collective-permute-done((bf16[128,4096]{1,0:T(8,128)(2,1)S(1)}, bf16[128,4096]{1,0:T(8,128)(2,1)}, u32[]{:S(2)}, u32[]{:S(2)}) %collective-permute-start) | collective-permute-done | bytes 1048608 | tf_op jit(solution)/shard_map/while/body/eval_jaxpr/ppermute | solution.py:22
  135.9 2.8 collective-permute-start.8
  146.2 2.7 collective-permute-start.11
  151.6 5.0 collective-permute-done.4
  173.3 19.9 %eval_jaxpr.6 = bf16[128,4096]{1,0:T(8,128)(2,1)} custom-call(bf16[128,4096]{1,0:T(8,128)(2,1)} %bitcast.89, bf16[2048,1024]{1,0:T(8,128)(2,1)} %pad_maximum_fusion.15.k_ref.v_ref, bf16[2048,1024]{1,0:T(8,128)(2,1)} %pad_maximum_fusion.15.k_ref.v_ref, f32[128,2048]{1,0:T(8,128)} %dynamic-slice_bitcast_fusion.6.bias_ref, bf16[128,4096]{1,0:T(8,128)(2,1)} %copy-done.1), custom_call_target="tpu_custom_call" | custom-call | tf_op jit(solution)/shard_map/while/body/eval_jaxpr/pallas_call | solution.py:145
  196.4 4.4 collective-permute-start
  202.8 9.7 %collective-permute-done = bf16[128,4096]{1,0:T(8,128)(2,1)} collective-permute-done((bf16[128,4096]{1,0:T(8,128)(2,1)S(1)}, bf16[128,4096]{1,0:T(8,128)(2,1)}, u32[]{:S(2)}, u32[]{:S(2)}) %collective-permute-start) | collective-permute-done | bytes 1048608 | tf_op jit(solution)/shard_map/while/body/eval_jaxpr/ppermute | solution.py:22
  237.4 3.9 collective-permute-done.4
  244.2 2.7 collective-permute-done.10
  260.1 19.9 %eval_jaxpr.6 = bf16[128,4096]{1,0:T(8,128)(2,1)} custom-call(bf16[128,4096]{1,0:T(8,128)(2,1)} %bitcast.89, bf16[2048,1024]{1,0:T(8,128)(2,1)} %pad_maximum_fusion.15.k_ref.v_ref, bf16[2048,1024]{1,0:T(8,128)(2,1)} %pad_maximum_fusion.15.k_ref.v_ref, f32[128,2048]{1,0:T(8,128)} %dynamic-slice_bitcast_fusion.6.bias_ref, bf16[128,4096]{1,0:T(8,128)(2,1)} %copy-done.1), custom_call_target="tpu_custom_call" | custom-call | tf_op jit(solution)/shard_map/while/body/eval_jaxpr/pallas_call | solution.py:145
  283.2 11.3 %collective-permute-start = (bf16[128,4096]{1,0:T(8,128)(2,1)S(1)}, bf16[128,4096]{1,0:T(8,128)(2,1)}, u32[]{:S(2)}, u32[]{:S(2)}) collective-permute-start(bf16[128,4096]{1,0:T(8,128)(2,1)S(1)} %broadcast_select_fusion.4), channel_id=1, source_target_pairs={{0,16},{16,32},{32,48},{48,64},{64,80},{80,96},{96,112},{1,17},{17... | collective-permute-start | bytes 3145736 | tf_op jit(solution)/shard_map/while/body/eval_jaxpr/ppermute | solution.py:22
  296.6 9.7 %collective-permute-done = bf16[128,4096]{1,0:T(8,128)(2,1)} collective-permute-done((bf16[128,4096]{1,0:T(8,128)(2,1)S(1)}, bf16[128,4096]{1,0:T(8,128)(2,1)}, u32[]{:S(2)}, u32[]{:S(2)}) %collective-permute-start) | collective-permute-done | bytes 1048608 | tf_op jit(solution)/shard_map/while/body/eval_jaxpr/ppermute | solution.py:22
  313.2 3.3 collective-permute-done.1
  350.5 19.9 %eval_jaxpr.6 = bf16[128,4096]{1,0:T(8,128)(2,1)} custom-call(bf16[128,4096]{1,0:T(8,128)(2,1)} %bitcast.89, bf16[2048,1024]{1,0:T(8,128)(2,1)} %pad_maximum_fusion.15.k_ref.v_ref, bf16[2048,1024]{1,0:T(8,128)(2,1)} %pad_maximum_fusion.15.k_ref.v_ref, f32[128,2048]{1,0:T(8,128)} %dynamic-slice_bitcast_fusion.6.bias_ref, bf16[128,4096]{1,0:T(8,128)(2,1)} %copy-done.1), custom_call_target="tpu_custom_call" | custom-call | tf_op jit(solution)/shard_map/while/body/eval_jaxpr/pallas_call | solution.py:145
  372.3 12.2 %collective-permute-start = (bf16[128,4096]{1,0:T(8,128)(2,1)S(1)}, bf16[128,4096]{1,0:T(8,128)(2,1)}, u32[]{:S(2)}, u32[]{:S(2)}) collective-permute-start(bf16[128,4096]{1,0:T(8,128)(2,1)S(1)} %broadcast_select_fusion.4), channel_id=1, source_target_pairs={{0,16},{16,32},{32,48},{48,64},{64,80},{80,96},{96,112},{1,17},{17... | collective-permute-start | bytes 3145736 | tf_op jit(solution)/shard_map/while/body/eval_jaxpr/ppermute | solution.py:22
  386.5 9.7 %collective-permute-done = bf16[128,4096]{1,0:T(8,128)(2,1)} collective-permute-done((bf16[128,4096]{1,0:T(8,128)(2,1)S(1)}, bf16[128,4096]{1,0:T(8,128)(2,1)}, u32[]{:S(2)}, u32[]{:S(2)}) %collective-permute-start) | collective-permute-done | bytes 1048608 | tf_op jit(solution)/shard_map/while/body/eval_jaxpr/ppermute | solution.py:22
  403.1 3.4 collective-permute-done.1
  439.4 19.9 %eval_jaxpr.6 = bf16[128,4096]{1,0:T(8,128)(2,1)} custom-call(bf16[128,4096]{1,0:T(8,128)(2,1)} %bitcast.89, bf16[2048,1024]{1,0:T(8,128)(2,1)} %pad_maximum_fusion.15.k_ref.v_ref, bf16[2048,1024]{1,0:T(8,128)(2,1)} %pad_maximum_fusion.15.k_ref.v_ref, f32[128,2048]{1,0:T(8,128)} %dynamic-slice_bitcast_fusion.6.bias_ref, bf16[128,4096]{1,0:T(8,128)(2,1)} %copy-done.1), custom_call_target="tpu_custom_call" | custom-call | tf_op jit(solution)/shard_map/while/body/eval_jaxpr/pallas_call | solution.py:145
  461.2 13.8 %collective-permute-start = (bf16[128,4096]{1,0:T(8,128)(2,1)S(1)}, bf16[128,4096]{1,0:T(8,128)(2,1)}, u32[]{:S(2)}, u32[]{:S(2)}) collective-permute-start(bf16[128,4096]{1,0:T(8,128)(2,1)S(1)} %broadcast_select_fusion.4), channel_id=1, source_target_pairs={{0,16},{16,32},{32,48},{48,64},{64,80},{80,96},{96,112},{1,17},{17... | collective-permute-start | bytes 3145736 | tf_op jit(solution)/shard_map/while/body/eval_jaxpr/ppermute | solution.py:22
  477.0 9.7 %collective-permute-done = bf16[128,4096]{1,0:T(8,128)(2,1)} collective-permute-done((bf16[128,4096]{1,0:T(8,128)(2,1)S(1)}, bf16[128,4096]{1,0:T(8,128)(2,1)}, u32[]{:S(2)}, u32[]{:S(2)}) %collective-permute-start) | collective-permute-done | bytes 1048608 | tf_op jit(solution)/shard_map/while/body/eval_jaxpr/ppermute | solution.py:22
  493.6 3.5 collective-permute-done.1
  529.5 19.9 %eval_jaxpr.6 = bf16[128,4096]{1,0:T(8,128)(2,1)} custom-call(bf16[128,4096]{1,0:T(8,128)(2,1)} %bitcast.89, bf16[2048,1024]{1,0:T(8,128)(2,1)} %pad_maximum_fusion.15.k_ref.v_ref, bf16[2048,1024]{1,0:T(8,128)(2,1)} %pad_maximum_fusion.15.k_ref.v_ref, f32[128,2048]{1,0:T(8,128)} %dynamic-slice_bitcast_fusion.6.bias_ref, bf16[128,4096]{1,0:T(8,128)(2,1)} %copy-done.1), custom_call_target="tpu_custom_call" | custom-call | tf_op jit(solution)/shard_map/while/body/eval_jaxpr/pallas_call | solution.py:145
  551.3 11.0 %collective-permute-start = (bf16[128,4096]{1,0:T(8,128)(2,1)S(1)}, bf16[128,4096]{1,0:T(8,128)(2,1)}, u32[]{:S(2)}, u32[]{:S(2)}) collective-permute-start(bf16[128,4096]{1,0:T(8,128)(2,1)S(1)} %broadcast_select_fusion.4), channel_id=1, source_target_pairs={{0,16},{16,32},{32,48},{48,64},{64,80},{80,96},{96,112},{1,17},{17... | collective-permute-start | bytes 3145736 | tf_op jit(solution)/shard_map/while/body/eval_jaxpr/ppermute | solution.py:22
  564.3 9.7 %collective-permute-done = bf16[128,4096]{1,0:T(8,128)(2,1)} collective-permute-done((bf16[128,4096]{1,0:T(8,128)(2,1)S(1)}, bf16[128,4096]{1,0:T(8,128)(2,1)}, u32[]{:S(2)}, u32[]{:S(2)}) %collective-permute-start) | collective-permute-done | bytes 1048608 | tf_op jit(solution)/shard_map/while/body/eval_jaxpr/ppermute | solution.py:22
  580.9 3.0 collective-permute-done.1
  584.7 3.5 collective-permute-start.8
  592.0 3.0 collective-permute-done.9
  618.6 19.9 %eval_jaxpr.6 = bf16[128,4096]{1,0:T(8,128)(2,1)} custom-call(bf16[128,4096]{1,0:T(8,128)(2,1)} %bitcast.89, bf16[2048,1024]{1,0:T(8,128)(2,1)} %pad_maximum_fusion.15.k_ref.v_ref, bf16[2048,1024]{1,0:T(8,128)(2,1)} %pad_maximum_fusion.15.k_ref.v_ref, f32[128,2048]{1,0:T(8,128)} %dynamic-slice_bitcast_fusion.6.bias_ref, bf16[128,4096]{1,0:T(8,128)(2,1)} %copy-done.1), custom_call_target="tpu_custom_call" | custom-call | tf_op jit(solution)/shard_map/while/body/eval_jaxpr/pallas_call | solution.py:145
  640.4 8.8 %collective-permute-start = (bf16[128,4096]{1,0:T(8,128)(2,1)S(1)}, bf16[128,4096]{1,0:T(8,128)(2,1)}, u32[]{:S(2)}, u32[]{:S(2)}) collective-permute-start(bf16[128,4096]{1,0:T(8,128)(2,1)S(1)} %broadcast_select_fusion.4), channel_id=1, source_target_pairs={{0,16},{16,32},{32,48},{48,64},{64,80},{80,96},{96,112},{1,17},{17... | collective-permute-start | bytes 3145736 | tf_op jit(solution)/shard_map/while/body/eval_jaxpr/ppermute | solution.py:22
  651.3 9.7 %collective-permute-done = bf16[128,4096]{1,0:T(8,128)(2,1)} collective-permute-done((bf16[128,4096]{1,0:T(8,128)(2,1)S(1)}, bf16[128,4096]{1,0:T(8,128)(2,1)}, u32[]{:S(2)}, u32[]{:S(2)}) %collective-permute-start) | collective-permute-done | bytes 1048608 | tf_op jit(solution)/shard_map/while/body/eval_jaxpr/ppermute | solution.py:22
  670.7 4.0 collective-permute-start.8
  682.1 3.0 collective-permute-start.11
  687.6 3.7 collective-permute-done.4
  707.6 19.9 %eval_jaxpr.6 = bf16[128,4096]{1,0:T(8,128)(2,1)} custom-call(bf16[128,4096]{1,0:T(8,128)(2,1)} %bitcast.89, bf16[2048,1024]{1,0:T(8,128)(2,1)} %pad_maximum_fusion.15.k_ref.v_ref, bf16[2048,1024]{1,0:T(8,128)(2,1)} %pad_maximum_fusion.15.k_ref.v_ref, f32[128,2048]{1,0:T(8,128)} %dynamic-slice_bitcast_fusion.6.bias_ref, bf16[128,4096]{1,0:T(8,128)(2,1)} %copy-done.1), custom_call_target="tpu_custom_call" | custom-call | tf_op jit(solution)/shard_map/while/body/eval_jaxpr/pallas_call | solution.py:145
  729.4 6.4 collective-permute-start
  737.8 9.7 %collective-permute-done = bf16[128,4096]{1,0:T(8,128)(2,1)} collective-permute-done((bf16[128,4096]{1,0:T(8,128)(2,1)S(1)}, bf16[128,4096]{1,0:T(8,128)(2,1)}, u32[]{:S(2)}, u32[]{:S(2)}) %collective-permute-start) | collective-permute-done | bytes 1048608 | tf_op jit(solution)/shard_map/while/body/eval_jaxpr/ppermute | solution.py:22
  758.2 3.1 collective-permute-done.7
  767.4 2.7 collective-permute-start.11
  772.7 6.7 collective-permute-done.4
  795.6 19.9 %eval_jaxpr.6 = bf16[128,4096]{1,0:T(8,128)(2,1)} custom-call(bf16[128,4096]{1,0:T(8,128)(2,1)} %bitcast.89, bf16[2048,1024]{1,0:T(8,128)(2,1)} %pad_maximum_fusion.15.k_ref.v_ref, bf16[2048,1024]{1,0:T(8,128)(2,1)} %pad_maximum_fusion.15.k_ref.v_ref, f32[128,2048]{1,0:T(8,128)} %dynamic-slice_bitcast_fusion.6.bias_ref, bf16[128,4096]{1,0:T(8,128)(2,1)} %copy-done.1), custom_call_target="tpu_custom_call" | custom-call | tf_op jit(solution)/shard_map/while/body/eval_jaxpr/pallas_call | solution.py:145
  (684 shorter events, 394.1 us)
Async XLA Ops:
  20.9 16.3 %collective-permute-start = (bf16[128,4096]{1,0:T(8,128)(2,1)S(1)}, bf16[128,4096]{1,0:T(8,128)(2,1)}, u32[]{:S(2)}, u32[]{:S(2)}) collective-permute-start(bf16[128,4096]{1,0:T(8,128)(2,1)S(1)} %broadcast_select_fusion.4), channel_id=1, source_target_pairs={{0,16},{16,32},{32,48},{48,64},{64,80},{80,96},{96,112},{1,17},{17... | collective-permute-start | bytes 3145736 | tf_op jit(solution)/shard_map/while/body/eval_jaxpr/ppermute | solution.py:22
  42.4 10.2 %collective-permute-start.3 = (bf16[128,512]{1,0:T(8,128)(2,1)S(1)}, bf16[128,512]{1,0:T(8,128)(2,1)S(1)}, u32[]{:S(2)}, u32[]{:S(2)}) collective-permute-start(bf16[128,512]{1,0:T(8,128)(2,1)S(1)} %slice.180), channel_id=1, source_target_pairs={{0,12},{1,13},{2,14},{3,15},{4,0},{5,1},{6,2},{7,3},{8,4},{9,5},{1... | collective-permute-start | bytes 393224 | tf_op jit(solution)/shard_map/while/body/eval_jaxpr/ppermute | solution.py:84
  53.4 12.0 %collective-permute-start.4 = (bf16[512,512]{1,0:T(8,128)(2,1)}, bf16[512,512]{1,0:T(8,128)(2,1)}, u32[]{:S(2)}, u32[]{:S(2)}) collective-permute-start(bf16[512,512]{1,0:T(8,128)(2,1)} %pad_maximum_fusion.12), channel_id=1, source_target_pairs={{0,1},{1,2},{2,3},{3,0},{4,5},{5,6},{6,7},{7,4},{8,9},{9,10},{10,1... | collective-permute-start | bytes 1572872 | tf_op jit(solution)/shard_map/while/body/eval_jaxpr/ppermute | solution.py:84
  58.4 12.7 %collective-permute-start.10 = (bf16[512,512]{1,0:T(8,128)(2,1)}, bf16[512,512]{1,0:T(8,128)(2,1)}, u32[]{:S(2)}, u32[]{:S(2)}) collective-permute-start(bf16[512,512]{1,0:T(8,128)(2,1)} %get-tuple-element.455), channel_id=1, source_target_pairs={{0,4},{1,5},{2,6},{3,7},{4,8},{5,9},{6,10},{7,11},{8,12},{9,13},{1... | collective-permute-start | bytes 1572872 | tf_op jit(solution)/shard_map/while/body/eval_jaxpr/ppermute | solution.py:84
  58.4 16.6 %collective-permute-start.11 = (bf16[512,512]{1,0:T(8,128)(2,1)}, bf16[512,512]{1,0:T(8,128)(2,1)}, u32[]{:S(2)}, u32[]{:S(2)}) collective-permute-start(bf16[512,512]{1,0:T(8,128)(2,1)} %get-tuple-element.455), channel_id=1, source_target_pairs={{0,12},{1,13},{2,14},{3,15},{4,0},{5,1},{6,2},{7,3},{8,4},{9,5},{1... | collective-permute-start | bytes 1572872 | tf_op jit(solution)/shard_map/while/body/eval_jaxpr/ppermute | solution.py:84
  62.9 14.0 %collective-permute-start.6 = (bf16[512,512]{1,0:T(8,128)(2,1)}, bf16[512,512]{1,0:T(8,128)(2,1)}, u32[]{:S(2)}, u32[]{:S(2)}) collective-permute-start(bf16[512,512]{1,0:T(8,128)(2,1)} %pad_maximum_fusion.12), channel_id=1, source_target_pairs={{0,3},{1,0},{2,1},{3,2},{4,7},{5,4},{6,5},{7,6},{8,11},{9,8},{10,9... | collective-permute-start | bytes 1572872 | tf_op jit(solution)/shard_map/while/body/eval_jaxpr/ppermute | solution.py:84
  65.4 11.6 %collective-permute-start.5 = (bf16[512,512]{1,0:T(8,128)(2,1)}, bf16[512,512]{1,0:T(8,128)(2,1)}, u32[]{:S(2)}, u32[]{:S(2)}) collective-permute-start(bf16[512,512]{1,0:T(8,128)(2,1)} %collective-permute-done.4), channel_id=1, source_target_pairs={{0,1},{1,2},{2,3},{3,0},{4,5},{5,6},{6,7},{7,4},{8,9},{9,10},{10,1... | collective-permute-start | bytes 1572872 | tf_op jit(solution)/shard_map/while/body/eval_jaxpr/ppermute | solution.py:84
  106.2 20.0 %collective-permute-start = (bf16[128,4096]{1,0:T(8,128)(2,1)S(1)}, bf16[128,4096]{1,0:T(8,128)(2,1)}, u32[]{:S(2)}, u32[]{:S(2)}) collective-permute-start(bf16[128,4096]{1,0:T(8,128)(2,1)S(1)} %broadcast_select_fusion.4), channel_id=1, source_target_pairs={{0,16},{16,32},{32,48},{48,64},{64,80},{80,96},{96,112},{1,17},{17... | collective-permute-start | bytes 3145736 | tf_op jit(solution)/shard_map/while/body/eval_jaxpr/ppermute | solution.py:22
  129.7 11.0 %collective-permute-start.3 = (bf16[128,512]{1,0:T(8,128)(2,1)S(1)}, bf16[128,512]{1,0:T(8,128)(2,1)S(1)}, u32[]{:S(2)}, u32[]{:S(2)}) collective-permute-start(bf16[128,512]{1,0:T(8,128)(2,1)S(1)} %slice.180), channel_id=1, source_target_pairs={{0,12},{1,13},{2,14},{3,15},{4,0},{5,1},{6,2},{7,3},{8,4},{9,5},{1... | collective-permute-start | bytes 393224 | tf_op jit(solution)/shard_map/while/body/eval_jaxpr/ppermute | solution.py:84
  142.9 13.8 %collective-permute-start.4 = (bf16[512,512]{1,0:T(8,128)(2,1)}, bf16[512,512]{1,0:T(8,128)(2,1)}, u32[]{:S(2)}, u32[]{:S(2)}) collective-permute-start(bf16[512,512]{1,0:T(8,128)(2,1)} %pad_maximum_fusion.12), channel_id=1, source_target_pairs={{0,1},{1,2},{2,3},{3,0},{4,5},{5,6},{6,7},{7,4},{8,9},{9,10},{10,1... | collective-permute-start | bytes 1572872 | tf_op jit(solution)/shard_map/while/body/eval_jaxpr/ppermute | solution.py:84
  146.2 13.9 %collective-permute-start.10 = (bf16[512,512]{1,0:T(8,128)(2,1)}, bf16[512,512]{1,0:T(8,128)(2,1)}, u32[]{:S(2)}, u32[]{:S(2)}) collective-permute-start(bf16[512,512]{1,0:T(8,128)(2,1)} %get-tuple-element.455), channel_id=1, source_target_pairs={{0,4},{1,5},{2,6},{3,7},{4,8},{5,9},{6,10},{7,11},{8,12},{9,13},{1... | collective-permute-start | bytes 1572872 | tf_op jit(solution)/shard_map/while/body/eval_jaxpr/ppermute | solution.py:84
  146.2 17.8 %collective-permute-start.11 = (bf16[512,512]{1,0:T(8,128)(2,1)}, bf16[512,512]{1,0:T(8,128)(2,1)}, u32[]{:S(2)}, u32[]{:S(2)}) collective-permute-start(bf16[512,512]{1,0:T(8,128)(2,1)} %get-tuple-element.455), channel_id=1, source_target_pairs={{0,12},{1,13},{2,14},{3,15},{4,0},{5,1},{6,2},{7,3},{8,4},{9,5},{1... | collective-permute-start | bytes 1572872 | tf_op jit(solution)/shard_map/while/body/eval_jaxpr/ppermute | solution.py:84
  150.6 15.3 %collective-permute-start.6 = (bf16[512,512]{1,0:T(8,128)(2,1)}, bf16[512,512]{1,0:T(8,128)(2,1)}, u32[]{:S(2)}, u32[]{:S(2)}) collective-permute-start(bf16[512,512]{1,0:T(8,128)(2,1)} %pad_maximum_fusion.12), channel_id=1, source_target_pairs={{0,3},{1,0},{2,1},{3,2},{4,7},{5,4},{6,5},{7,6},{8,11},{9,8},{10,9... | collective-permute-start | bytes 1572872 | tf_op jit(solution)/shard_map/while/body/eval_jaxpr/ppermute | solution.py:84
  196.4 16.1 %collective-permute-start = (bf16[128,4096]{1,0:T(8,128)(2,1)S(1)}, bf16[128,4096]{1,0:T(8,128)(2,1)}, u32[]{:S(2)}, u32[]{:S(2)}) collective-permute-start(bf16[128,4096]{1,0:T(8,128)(2,1)S(1)} %broadcast_select_fusion.4), channel_id=1, source_target_pairs={{0,16},{16,32},{32,48},{48,64},{64,80},{80,96},{96,112},{1,17},{17... | collective-permute-start | bytes 3145736 | tf_op jit(solution)/shard_map/while/body/eval_jaxpr/ppermute | solution.py:22
  216.0 10.9 %collective-permute-start.3 = (bf16[128,512]{1,0:T(8,128)(2,1)S(1)}, bf16[128,512]{1,0:T(8,128)(2,1)S(1)}, u32[]{:S(2)}, u32[]{:S(2)}) collective-permute-start(bf16[128,512]{1,0:T(8,128)(2,1)S(1)} %slice.180), channel_id=1, source_target_pairs={{0,12},{1,13},{2,14},{3,15},{4,0},{5,1},{6,2},{7,3},{8,4},{9,5},{1... | collective-permute-start | bytes 393224 | tf_op jit(solution)/shard_map/while/body/eval_jaxpr/ppermute | solution.py:84
  227.8 13.5 %collective-permute-start.4 = (bf16[512,512]{1,0:T(8,128)(2,1)}, bf16[512,512]{1,0:T(8,128)(2,1)}, u32[]{:S(2)}, u32[]{:S(2)}) collective-permute-start(bf16[512,512]{1,0:T(8,128)(2,1)} %pad_maximum_fusion.12), channel_id=1, source_target_pairs={{0,1},{1,2},{2,3},{3,0},{4,5},{5,6},{6,7},{7,4},{8,9},{9,10},{10,1... | collective-permute-start | bytes 1572872 | tf_op jit(solution)/shard_map/while/body/eval_jaxpr/ppermute | solution.py:84
  232.6 14.3 %collective-permute-start.10 = (bf16[512,512]{1,0:T(8,128)(2,1)}, bf16[512,512]{1,0:T(8,128)(2,1)}, u32[]{:S(2)}, u32[]{:S(2)}) collective-permute-start(bf16[512,512]{1,0:T(8,128)(2,1)} %get-tuple-element.455), channel_id=1, source_target_pairs={{0,4},{1,5},{2,6},{3,7},{4,8},{5,9},{6,10},{7,11},{8,12},{9,13},{1... | collective-permute-start | bytes 1572872 | tf_op jit(solution)/shard_map/while/body/eval_jaxpr/ppermute | solution.py:84
  232.6 18.2 %collective-permute-start.11 = (bf16[512,512]{1,0:T(8,128)(2,1)}, bf16[512,512]{1,0:T(8,128)(2,1)}, u32[]{:S(2)}, u32[]{:S(2)}) collective-permute-start(bf16[512,512]{1,0:T(8,128)(2,1)} %get-tuple-element.455), channel_id=1, source_target_pairs={{0,12},{1,13},{2,14},{3,15},{4,0},{5,1},{6,2},{7,3},{8,4},{9,5},{1... | collective-permute-start | bytes 1572872 | tf_op jit(solution)/shard_map/while/body/eval_jaxpr/ppermute | solution.py:84
  237.0 15.7 %collective-permute-start.6 = (bf16[512,512]{1,0:T(8,128)(2,1)}, bf16[512,512]{1,0:T(8,128)(2,1)}, u32[]{:S(2)}, u32[]{:S(2)}) collective-permute-start(bf16[512,512]{1,0:T(8,128)(2,1)} %pad_maximum_fusion.12), channel_id=1, source_target_pairs={{0,3},{1,0},{2,1},{3,2},{4,7},{5,4},{6,5},{7,6},{8,11},{9,8},{10,9... | collective-permute-start | bytes 1572872 | tf_op jit(solution)/shard_map/while/body/eval_jaxpr/ppermute | solution.py:84
  241.3 11.4 %collective-permute-start.5 = (bf16[512,512]{1,0:T(8,128)(2,1)}, bf16[512,512]{1,0:T(8,128)(2,1)}, u32[]{:S(2)}, u32[]{:S(2)}) collective-permute-start(bf16[512,512]{1,0:T(8,128)(2,1)} %collective-permute-done.4), channel_id=1, source_target_pairs={{0,1},{1,2},{2,3},{3,0},{4,5},{5,6},{6,7},{7,4},{8,9},{9,10},{10,1... | collective-permute-start | bytes 1572872 | tf_op jit(solution)/shard_map/while/body/eval_jaxpr/ppermute | solution.py:84
  283.2 23.0 %collective-permute-start = (bf16[128,4096]{1,0:T(8,128)(2,1)S(1)}, bf16[128,4096]{1,0:T(8,128)(2,1)}, u32[]{:S(2)}, u32[]{:S(2)}) collective-permute-start(bf16[128,4096]{1,0:T(8,128)(2,1)S(1)} %broadcast_select_fusion.4), channel_id=1, source_target_pairs={{0,16},{16,32},{32,48},{48,64},{64,80},{80,96},{96,112},{1,17},{17... | collective-permute-start | bytes 3145736 | tf_op jit(solution)/shard_map/while/body/eval_jaxpr/ppermute | solution.py:22
  323.1 10.2 %collective-permute-start.4 = (bf16[512,512]{1,0:T(8,128)(2,1)}, bf16[512,512]{1,0:T(8,128)(2,1)}, u32[]{:S(2)}, u32[]{:S(2)}) collective-permute-start(bf16[512,512]{1,0:T(8,128)(2,1)} %pad_maximum_fusion.12), channel_id=1, source_target_pairs={{0,1},{1,2},{2,3},{3,0},{4,5},{5,6},{6,7},{7,4},{8,9},{9,10},{10,1... | collective-permute-start | bytes 1572872 | tf_op jit(solution)/shard_map/while/body/eval_jaxpr/ppermute | solution.py:84
  326.7 10.5 %collective-permute-start.10 = (bf16[512,512]{1,0:T(8,128)(2,1)}, bf16[512,512]{1,0:T(8,128)(2,1)}, u32[]{:S(2)}, u32[]{:S(2)}) collective-permute-start(bf16[512,512]{1,0:T(8,128)(2,1)} %get-tuple-element.455), channel_id=1, source_target_pairs={{0,4},{1,5},{2,6},{3,7},{4,8},{5,9},{6,10},{7,11},{8,12},{9,13},{1... | collective-permute-start | bytes 1572872 | tf_op jit(solution)/shard_map/while/body/eval_jaxpr/ppermute | solution.py:84
  326.7 14.4 %collective-permute-start.11 = (bf16[512,512]{1,0:T(8,128)(2,1)}, bf16[512,512]{1,0:T(8,128)(2,1)}, u32[]{:S(2)}, u32[]{:S(2)}) collective-permute-start(bf16[512,512]{1,0:T(8,128)(2,1)} %get-tuple-element.455), channel_id=1, source_target_pairs={{0,12},{1,13},{2,14},{3,15},{4,0},{5,1},{6,2},{7,3},{8,4},{9,5},{1... | collective-permute-start | bytes 1572872 | tf_op jit(solution)/shard_map/while/body/eval_jaxpr/ppermute | solution.py:84
  331.2 11.9 %collective-permute-start.6 = (bf16[512,512]{1,0:T(8,128)(2,1)}, bf16[512,512]{1,0:T(8,128)(2,1)}, u32[]{:S(2)}, u32[]{:S(2)}) collective-permute-start(bf16[512,512]{1,0:T(8,128)(2,1)} %pad_maximum_fusion.12), channel_id=1, source_target_pairs={{0,3},{1,0},{2,1},{3,2},{4,7},{5,4},{6,5},{7,6},{8,11},{9,8},{10,9... | collective-permute-start | bytes 1572872 | tf_op jit(solution)/shard_map/while/body/eval_jaxpr/ppermute | solution.py:84
  372.3 24.0 %collective-permute-start = (bf16[128,4096]{1,0:T(8,128)(2,1)S(1)}, bf16[128,4096]{1,0:T(8,128)(2,1)}, u32[]{:S(2)}, u32[]{:S(2)}) collective-permute-start(bf16[128,4096]{1,0:T(8,128)(2,1)S(1)} %broadcast_select_fusion.4), channel_id=1, source_target_pairs={{0,16},{16,32},{32,48},{48,64},{64,80},{80,96},{96,112},{1,17},{17... | collective-permute-start | bytes 3145736 | tf_op jit(solution)/shard_map/while/body/eval_jaxpr/ppermute | solution.py:22
  416.2 13.9 %collective-permute-start.11 = (bf16[512,512]{1,0:T(8,128)(2,1)}, bf16[512,512]{1,0:T(8,128)(2,1)}, u32[]{:S(2)}, u32[]{:S(2)}) collective-permute-start(bf16[512,512]{1,0:T(8,128)(2,1)} %get-tuple-element.455), channel_id=1, source_target_pairs={{0,12},{1,13},{2,14},{3,15},{4,0},{5,1},{6,2},{7,3},{8,4},{9,5},{1... | collective-permute-start | bytes 1572872 | tf_op jit(solution)/shard_map/while/body/eval_jaxpr/ppermute | solution.py:84
  420.7 11.3 %collective-permute-start.6 = (bf16[512,512]{1,0:T(8,128)(2,1)}, bf16[512,512]{1,0:T(8,128)(2,1)}, u32[]{:S(2)}, u32[]{:S(2)}) collective-permute-start(bf16[512,512]{1,0:T(8,128)(2,1)} %pad_maximum_fusion.12), channel_id=1, source_target_pairs={{0,3},{1,0},{2,1},{3,2},{4,7},{5,4},{6,5},{7,6},{8,11},{9,8},{10,9... | collective-permute-start | bytes 1572872 | tf_op jit(solution)/shard_map/while/body/eval_jaxpr/ppermute | solution.py:84
  461.2 25.5 %collective-permute-start = (bf16[128,4096]{1,0:T(8,128)(2,1)S(1)}, bf16[128,4096]{1,0:T(8,128)(2,1)}, u32[]{:S(2)}, u32[]{:S(2)}) collective-permute-start(bf16[128,4096]{1,0:T(8,128)(2,1)S(1)} %broadcast_select_fusion.4), channel_id=1, source_target_pairs={{0,16},{16,32},{32,48},{48,64},{64,80},{80,96},{96,112},{1,17},{17... | collective-permute-start | bytes 3145736 | tf_op jit(solution)/shard_map/while/body/eval_jaxpr/ppermute | solution.py:22
  506.7 13.5 %collective-permute-start.11 = (bf16[512,512]{1,0:T(8,128)(2,1)}, bf16[512,512]{1,0:T(8,128)(2,1)}, u32[]{:S(2)}, u32[]{:S(2)}) collective-permute-start(bf16[512,512]{1,0:T(8,128)(2,1)} %get-tuple-element.455), channel_id=1, source_target_pairs={{0,12},{1,13},{2,14},{3,15},{4,0},{5,1},{6,2},{7,3},{8,4},{9,5},{1... | collective-permute-start | bytes 1572872 | tf_op jit(solution)/shard_map/while/body/eval_jaxpr/ppermute | solution.py:84
  511.1 10.9 %collective-permute-start.6 = (bf16[512,512]{1,0:T(8,128)(2,1)}, bf16[512,512]{1,0:T(8,128)(2,1)}, u32[]{:S(2)}, u32[]{:S(2)}) collective-permute-start(bf16[512,512]{1,0:T(8,128)(2,1)} %pad_maximum_fusion.12), channel_id=1, source_target_pairs={{0,3},{1,0},{2,1},{3,2},{4,7},{5,4},{6,5},{7,6},{8,11},{9,8},{10,9... | collective-permute-start | bytes 1572872 | tf_op jit(solution)/shard_map/while/body/eval_jaxpr/ppermute | solution.py:84
  551.3 22.8 %collective-permute-start = (bf16[128,4096]{1,0:T(8,128)(2,1)S(1)}, bf16[128,4096]{1,0:T(8,128)(2,1)}, u32[]{:S(2)}, u32[]{:S(2)}) collective-permute-start(bf16[128,4096]{1,0:T(8,128)(2,1)S(1)} %broadcast_select_fusion.4), channel_id=1, source_target_pairs={{0,16},{16,32},{32,48},{48,64},{64,80},{80,96},{96,112},{1,17},{17... | collective-permute-start | bytes 3145736 | tf_op jit(solution)/shard_map/while/body/eval_jaxpr/ppermute | solution.py:22
  577.6 11.3 %collective-permute-start.3 = (bf16[128,512]{1,0:T(8,128)(2,1)S(1)}, bf16[128,512]{1,0:T(8,128)(2,1)S(1)}, u32[]{:S(2)}, u32[]{:S(2)}) collective-permute-start(bf16[128,512]{1,0:T(8,128)(2,1)S(1)} %slice.180), channel_id=1, source_target_pairs={{0,12},{1,13},{2,14},{3,15},{4,0},{5,1},{6,2},{7,3},{8,4},{9,5},{1... | collective-permute-start | bytes 393224 | tf_op jit(solution)/shard_map/while/body/eval_jaxpr/ppermute | solution.py:84
  590.9 10.5 %collective-permute-start.4 = (bf16[512,512]{1,0:T(8,128)(2,1)}, bf16[512,512]{1,0:T(8,128)(2,1)}, u32[]{:S(2)}, u32[]{:S(2)}) collective-permute-start(bf16[512,512]{1,0:T(8,128)(2,1)} %pad_maximum_fusion.12), channel_id=1, source_target_pairs={{0,1},{1,2},{2,3},{3,0},{4,5},{5,6},{6,7},{7,4},{8,9},{9,10},{10,1... | collective-permute-start | bytes 1572872 | tf_op jit(solution)/shard_map/while/body/eval_jaxpr/ppermute | solution.py:84
  595.8 13.5 %collective-permute-start.11 = (bf16[512,512]{1,0:T(8,128)(2,1)}, bf16[512,512]{1,0:T(8,128)(2,1)}, u32[]{:S(2)}, u32[]{:S(2)}) collective-permute-start(bf16[512,512]{1,0:T(8,128)(2,1)} %get-tuple-element.455), channel_id=1, source_target_pairs={{0,12},{1,13},{2,14},{3,15},{4,0},{5,1},{6,2},{7,3},{8,4},{9,5},{1... | collective-permute-start | bytes 1572872 | tf_op jit(solution)/shard_map/while/body/eval_jaxpr/ppermute | solution.py:84
  600.3 10.9 %collective-permute-start.6 = (bf16[512,512]{1,0:T(8,128)(2,1)}, bf16[512,512]{1,0:T(8,128)(2,1)}, u32[]{:S(2)}, u32[]{:S(2)}) collective-permute-start(bf16[512,512]{1,0:T(8,128)(2,1)} %pad_maximum_fusion.12), channel_id=1, source_target_pairs={{0,3},{1,0},{2,1},{3,2},{4,7},{5,4},{6,5},{7,6},{8,11},{9,8},{10,9... | collective-permute-start | bytes 1572872 | tf_op jit(solution)/shard_map/while/body/eval_jaxpr/ppermute | solution.py:84
  640.4 20.5 %collective-permute-start = (bf16[128,4096]{1,0:T(8,128)(2,1)S(1)}, bf16[128,4096]{1,0:T(8,128)(2,1)}, u32[]{:S(2)}, u32[]{:S(2)}) collective-permute-start(bf16[128,4096]{1,0:T(8,128)(2,1)S(1)} %broadcast_select_fusion.4), channel_id=1, source_target_pairs={{0,16},{16,32},{32,48},{48,64},{64,80},{80,96},{96,112},{1,17},{17... | collective-permute-start | bytes 3145736 | tf_op jit(solution)/shard_map/while/body/eval_jaxpr/ppermute | solution.py:22
  664.5 10.9 %collective-permute-start.3 = (bf16[128,512]{1,0:T(8,128)(2,1)S(1)}, bf16[128,512]{1,0:T(8,128)(2,1)S(1)}, u32[]{:S(2)}, u32[]{:S(2)}) collective-permute-start(bf16[128,512]{1,0:T(8,128)(2,1)S(1)} %slice.180), channel_id=1, source_target_pairs={{0,12},{1,13},{2,14},{3,15},{4,0},{5,1},{6,2},{7,3},{8,4},{9,5},{1... | collective-permute-start | bytes 393224 | tf_op jit(solution)/shard_map/while/body/eval_jaxpr/ppermute | solution.py:84
  677.7 13.6 %collective-permute-start.4 = (bf16[512,512]{1,0:T(8,128)(2,1)}, bf16[512,512]{1,0:T(8,128)(2,1)}, u32[]{:S(2)}, u32[]{:S(2)}) collective-permute-start(bf16[512,512]{1,0:T(8,128)(2,1)} %pad_maximum_fusion.12), channel_id=1, source_target_pairs={{0,1},{1,2},{2,3},{3,0},{4,5},{5,6},{6,7},{7,4},{8,9},{9,10},{10,1... | collective-permute-start | bytes 1572872 | tf_op jit(solution)/shard_map/while/body/eval_jaxpr/ppermute | solution.py:84
  682.1 12.2 %collective-permute-start.10 = (bf16[512,512]{1,0:T(8,128)(2,1)}, bf16[512,512]{1,0:T(8,128)(2,1)}, u32[]{:S(2)}, u32[]{:S(2)}) collective-permute-start(bf16[512,512]{1,0:T(8,128)(2,1)} %get-tuple-element.455), channel_id=1, source_target_pairs={{0,4},{1,5},{2,6},{3,7},{4,8},{5,9},{6,10},{7,11},{8,12},{9,13},{1... | collective-permute-start | bytes 1572872 | tf_op jit(solution)/shard_map/while/body/eval_jaxpr/ppermute | solution.py:84
  682.1 16.1 %collective-permute-start.11 = (bf16[512,512]{1,0:T(8,128)(2,1)}, bf16[512,512]{1,0:T(8,128)(2,1)}, u32[]{:S(2)}, u32[]{:S(2)}) collective-permute-start(bf16[512,512]{1,0:T(8,128)(2,1)} %get-tuple-element.455), channel_id=1, source_target_pairs={{0,12},{1,13},{2,14},{3,15},{4,0},{5,1},{6,2},{7,3},{8,4},{9,5},{1... | collective-permute-start | bytes 1572872 | tf_op jit(solution)/shard_map/while/body/eval_jaxpr/ppermute | solution.py:84
  686.8 13.3 %collective-permute-start.6 = (bf16[512,512]{1,0:T(8,128)(2,1)}, bf16[512,512]{1,0:T(8,128)(2,1)}, u32[]{:S(2)}, u32[]{:S(2)}) collective-permute-start(bf16[512,512]{1,0:T(8,128)(2,1)} %pad_maximum_fusion.12), channel_id=1, source_target_pairs={{0,3},{1,0},{2,1},{3,2},{4,7},{5,4},{6,5},{7,6},{8,11},{9,8},{10,9... | collective-permute-start | bytes 1572872 | tf_op jit(solution)/shard_map/while/body/eval_jaxpr/ppermute | solution.py:84
  729.4 18.1 %collective-permute-start = (bf16[128,4096]{1,0:T(8,128)(2,1)S(1)}, bf16[128,4096]{1,0:T(8,128)(2,1)}, u32[]{:S(2)}, u32[]{:S(2)}) collective-permute-start(bf16[128,4096]{1,0:T(8,128)(2,1)S(1)} %broadcast_select_fusion.4), channel_id=1, source_target_pairs={{0,16},{16,32},{32,48},{48,64},{64,80},{80,96},{96,112},{1,17},{17... | collective-permute-start | bytes 3145736 | tf_op jit(solution)/shard_map/while/body/eval_jaxpr/ppermute | solution.py:22
  751.0 11.0 %collective-permute-start.3 = (bf16[128,512]{1,0:T(8,128)(2,1)S(1)}, bf16[128,512]{1,0:T(8,128)(2,1)S(1)}, u32[]{:S(2)}, u32[]{:S(2)}) collective-permute-start(bf16[128,512]{1,0:T(8,128)(2,1)S(1)} %slice.180), channel_id=1, source_target_pairs={{0,12},{1,13},{2,14},{3,15},{4,0},{5,1},{6,2},{7,3},{8,4},{9,5},{1... | collective-permute-start | bytes 393224 | tf_op jit(solution)/shard_map/while/body/eval_jaxpr/ppermute | solution.py:84
  764.1 15.3 %collective-permute-start.4 = (bf16[512,512]{1,0:T(8,128)(2,1)}, bf16[512,512]{1,0:T(8,128)(2,1)}, u32[]{:S(2)}, u32[]{:S(2)}) collective-permute-start(bf16[512,512]{1,0:T(8,128)(2,1)} %pad_maximum_fusion.12), channel_id=1, source_target_pairs={{0,1},{1,2},{2,3},{3,0},{4,5},{5,6},{6,7},{7,4},{8,9},{9,10},{10,1... | collective-permute-start | bytes 1572872 | tf_op jit(solution)/shard_map/while/body/eval_jaxpr/ppermute | solution.py:84
  767.4 14.9 %collective-permute-start.10 = (bf16[512,512]{1,0:T(8,128)(2,1)}, bf16[512,512]{1,0:T(8,128)(2,1)}, u32[]{:S(2)}, u32[]{:S(2)}) collective-permute-start(bf16[512,512]{1,0:T(8,128)(2,1)} %get-tuple-element.455), channel_id=1, source_target_pairs={{0,4},{1,5},{2,6},{3,7},{4,8},{5,9},{6,10},{7,11},{8,12},{9,13},{1... | collective-permute-start | bytes 1572872 | tf_op jit(solution)/shard_map/while/body/eval_jaxpr/ppermute | solution.py:84
  767.4 18.8 %collective-permute-start.11 = (bf16[512,512]{1,0:T(8,128)(2,1)}, bf16[512,512]{1,0:T(8,128)(2,1)}, u32[]{:S(2)}, u32[]{:S(2)}) collective-permute-start(bf16[512,512]{1,0:T(8,128)(2,1)} %get-tuple-element.455), channel_id=1, source_target_pairs={{0,12},{1,13},{2,14},{3,15},{4,0},{5,1},{6,2},{7,3},{8,4},{9,5},{1... | collective-permute-start | bytes 1572872 | tf_op jit(solution)/shard_map/while/body/eval_jaxpr/ppermute | solution.py:84
  771.9 16.3 %collective-permute-start.6 = (bf16[512,512]{1,0:T(8,128)(2,1)}, bf16[512,512]{1,0:T(8,128)(2,1)}, u32[]{:S(2)}, u32[]{:S(2)}) collective-permute-start(bf16[512,512]{1,0:T(8,128)(2,1)} %pad_maximum_fusion.12), channel_id=1, source_target_pairs={{0,3},{1,0},{2,1},{3,2},{4,7},{5,4},{6,5},{7,6},{8,11},{9,8},{10,9... | collective-permute-start | bytes 1572872 | tf_op jit(solution)/shard_map/while/body/eval_jaxpr/ppermute | solution.py:84
  (160 other events, 1179.1 us)

commit v7 on v6

--- a/solution.py
+++ b/solution.py
@@ -232,8 +232,12 @@
         start_at = jnp.clip(first_mb, 0, micro_count - 1)
         entering = lax.dynamic_index_in_dim(hidden, start_at, 0, keepdims=False)
         current = jnp.where(section_id == 0, entering, incoming)
-        computed = run_layer(current, start_at)
-        result = jnp.where(active, computed, jnp.zeros_like(computed))
+        result = lax.cond(
+            active,
+            lambda rows: run_layer(rows, start_at),
+            jnp.zeros_like,
+            current,
+        )
         stored = lax.dynamic_update_index_in_dim(outputs, result, start_at, 0)
         outputs = jnp.where(active, stored, outputs)
         return (result, outputs)

time: 820 us -> 708 us (0.86)
  the two profiles are of different devices: /device:TPU:1 before, /device:TPU:25 now
where the time goes in v7:
time: 708 us; the launch traced here: 707 us
  waiting for transfers between devices  577 us (81%)
  Pallas kernels  39.3 us (6%)
  starting transfers between devices  29.8 us (4%)
  other arithmetic  29.3 us (4%)
  local copies, waits for them, and re-layouts  19.7 us (3%)
  matrix products  10.2 us (1%)
    ppermute x9, waiting for transfers between devices, from_behind(): return lax.ppermute(value, axis, pairs)  541 us
    pallas_call x2, Pallas kernels, attention(): pl.pallas_call(attention_kernel, grid=(HK,), in_specs=[pl.BlockSpec((rows...  39.3 us
    ppermute x24, waiting for transfers between devices, shift(): return lax.ppermute(piece, 'seq', pairs)  36.5 us
    ppermute x24, starting transfers between devices, shift(): return lax.ppermute(piece, 'seq', pairs)  18.2 us
  transfers between devices with their start and end apart: 33, of which 25 were waited for; matrix products, arithmetic and copies ran while one was open for 2% of the time, Pallas kernels for 0%

profile of v7, /device:TPU:25, one launch (start us, length us, event | category | flops | bytes accessed | tf_op | source)
XLA Modules:
  0.0 707.3 jit_solution(15937925477799923855)
XLA Ops:
  0.0 7.9 %pad_maximum_fusion.5 = bf16[4096,1024]{1,0:T(8,128)(2,1)} fusion(bf16[4096,512]{1,0:T(8,128)(2,1)} %bitcast.60, bf16[4096,512]{1,0:T(8,128)(2,1)} %bitcast.61), kind=kLoop, calls=%fused_computation.54 | loop fusion | flops 16777216 | bytes 16777216 | tf_op jit(solution)/shard_map/concatenate | solution.py:194
  12.1 693.8 %while.18 = (s32[]{:T(128)}, bf16[128,4096]{1,0:T(8,128)(2,1)}, bf16[2,128,4096]{2,1,0:T(8,128)(2,1)S(1)}, s32[]{:T(128)}, bf16[1,2,128,4096]{3,2,1,0:T(8,128)(2...) while((s32[]{:T(128)}, bf16[128,4096]{1,0:T(8,128)(2,1)}, ...), condition=%wide.region_11.14_spmd.clone.clone, body=%wide.region_7.13_spmd.clone.clone.sunk | while | flops 1099186304 | bytes 87595792 | solution.py:247
  12.3 1.3 collective-permute-start.12
  13.7 3.5 collective-permute-done.12
  18.8 1.3 collective-permute-start.12
  20.2 14.9 %collective-permute-done.12 = bf16[128,4096]{1,0:T(8,128)(2,1)S(1)} collective-permute-done((bf16[128,4096]{1,0:T(8,128)(2,1)}, bf16[128,4096]{1,0:T(8,128)(2,1)S(1)}, u32[]{:S(2)}, u32[]{:S(2)}) %collective-permute-start.12) | collective-permute-done | bytes 1048608 | tf_op jit(solution)/shard_map/while/body/eval_jaxpr/ppermute | solution.py:22
  36.6 1.3 collective-permute-start.12
  38.0 14.9 %collective-permute-done.12 = bf16[128,4096]{1,0:T(8,128)(2,1)S(1)} collective-permute-done((bf16[128,4096]{1,0:T(8,128)(2,1)}, bf16[128,4096]{1,0:T(8,128)(2,1)S(1)}, u32[]{:S(2)}, u32[]{:S(2)}) %collective-permute-start.12) | collective-permute-done | bytes 1048608 | tf_op jit(solution)/shard_map/while/body/eval_jaxpr/ppermute | solution.py:22
  54.5 1.3 collective-permute-start.12
  55.9 14.9 %collective-permute-done.12 = bf16[128,4096]{1,0:T(8,128)(2,1)S(1)} collective-permute-done((bf16[128,4096]{1,0:T(8,128)(2,1)}, bf16[128,4096]{1,0:T(8,128)(2,1)S(1)}, u32[]{:S(2)}, u32[]{:S(2)}) %collective-permute-start.12) | collective-permute-done | bytes 1048608 | tf_op jit(solution)/shard_map/while/body/eval_jaxpr/ppermute | solution.py:22
  73.8 14.9 %collective-permute-done.12 = bf16[128,4096]{1,0:T(8,128)(2,1)S(1)} collective-permute-done((bf16[128,4096]{1,0:T(8,128)(2,1)}, bf16[128,4096]{1,0:T(8,128)(2,1)S(1)}, u32[]{:S(2)}, u32[]{:S(2)}) %collective-permute-start.12) | collective-permute-done | bytes 1048608 | tf_op jit(solution)/shard_map/while/body/eval_jaxpr/ppermute | solution.py:22
  91.6 14.9 %collective-permute-done.12 = bf16[128,4096]{1,0:T(8,128)(2,1)S(1)} collective-permute-done((bf16[128,4096]{1,0:T(8,128)(2,1)}, bf16[128,4096]{1,0:T(8,128)(2,1)S(1)}, u32[]{:S(2)}, u32[]{:S(2)}) %collective-permute-start.12) | collective-permute-done | bytes 1048608 | tf_op jit(solution)/shard_map/while/body/eval_jaxpr/ppermute | solution.py:22
  109.5 14.9 %collective-permute-done.12 = bf16[128,4096]{1,0:T(8,128)(2,1)S(1)} collective-permute-done((bf16[128,4096]{1,0:T(8,128)(2,1)}, bf16[128,4096]{1,0:T(8,128)(2,1)S(1)}, u32[]{:S(2)}, u32[]{:S(2)}) %collective-permute-start.12) | collective-permute-done | bytes 1048608 | tf_op jit(solution)/shard_map/while/body/eval_jaxpr/ppermute | solution.py:22
  127.4 428.5 %collective-permute-done.12 = bf16[128,4096]{1,0:T(8,128)(2,1)S(1)} collective-permute-done((bf16[128,4096]{1,0:T(8,128)(2,1)}, bf16[128,4096]{1,0:T(8,128)(2,1)S(1)}, u32[]{:S(2)}, u32[]{:S(2)}) %collective-permute-start.12) | collective-permute-done | bytes 1048608 | tf_op jit(solution)/shard_map/while/body/eval_jaxpr/ppermute | solution.py:22
  555.8 65.8 %conditional.4 = (bf16[128,4096]{1,0:T(8,128)(2,1)}, bf16[1,128,4096]{2,1,0:T(8,128)(2,1)S(1)}) conditional(s32[]{:T(128)} %convert_element_type.63, () %tuple.104, (s32[]{:T(128)}, bf16[1,2,128,4096]{3,2,1,0:T(8,128)(2,1)}, f32[2,128,64]{2,1,0:T(8,128)S(1)}, f32[2,128,64]{2,1,0:T(8,128)S(1)}, pred[]{:T(512)}, ...), branch_computations={%region_8.10_spmd, %region_9.12_spmd} | conditional | flops 1098645632 | bytes 80188504 | solution.py:235
  555.8 1.7 fusion.6
  557.5 5.1 fusion.9
  562.8 2.7 collective-permute-start.7
  566.6 2.7 collective-permute-start.1
  569.5 2.1 collective-permute-done
  571.7 2.8 collective-permute-done.8
  574.6 2.0 collective-permute-done.2
  576.7 1.4 select_bitcast_fusion.bias_ref
  579.5 2.7 collective-permute-start.4
  582.1 2.5 collective-permute-done.9
  586.6 1.5 copy.26
  588.4 9.4 %collective-permute-done.11 = bf16[512,512]{1,0:T(8,128)(2,1)S(1)} collective-permute-done((bf16[512,512]{1,0:T(8,128)(2,1)S(1)}, bf16[512,512]{1,0:T(8,128)(2,1)S(1)}, u32[]{:S(2)}, u32[]{:S(2)}) %collective-permute-start.11) | collective-permute-done | bytes 524320 | tf_op jit(solution)/shard_map/while/body/eval_jaxpr/cond/branch_1_fun/ppermute | solution.py:84
  598.1 2.6 pad_maximum_fusion.k_ref.v_ref
  600.7 19.7 %branch_1_fun.1 = bf16[128,4096]{1,0:T(8,128)(2,1)} custom-call(bf16[128,4096]{1,0:T(8,128)(2,1)} %bitcast.52, bf16[2048,1024]{1,0:T(8,128)(2,1)} %pad_maximum_fusion.k_ref.v_ref, bf16[2048,1024]{1,0:T(8,128)(2,1)} %pad_maximum_fusion.k_ref.v_ref, f32[128,2048]{1,0:T(8,128)} %select_bitcast_fusion.bias_ref, bf16[128,4096]{1,0:T(8,128)(2,1)} %copy-done), custom_call_target="tpu_custom_call" | custom-call | tf_op jit(solution)/shard_map/while/body/eval_jaxpr/cond/branch_1_fun/pallas_call | solution.py:145
  623.4 19.2 %collective-permute-done.12 = bf16[128,4096]{1,0:T(8,128)(2,1)S(1)} collective-permute-done((bf16[128,4096]{1,0:T(8,128)(2,1)}, bf16[128,4096]{1,0:T(8,128)(2,1)S(1)}, u32[]{:S(2)}, u32[]{:S(2)}) %collective-permute-start.12) | collective-permute-done | bytes 1048608 | tf_op jit(solution)/shard_map/while/body/eval_jaxpr/ppermute | solution.py:22
  642.6 63.0 %conditional.4 = (bf16[128,4096]{1,0:T(8,128)(2,1)}, bf16[1,128,4096]{2,1,0:T(8,128)(2,1)S(1)}) conditional(s32[]{:T(128)} %convert_element_type.63, () %tuple.104, (s32[]{:T(128)}, bf16[1,2,128,4096]{3,2,1,0:T(8,128)(2,1)}, f32[2,128,64]{2,1,0:T(8,128)S(1)}, f32[2,128,64]{2,1,0:T(8,128)S(1)}, pred[]{:T(512)}, ...), branch_computations={%region_8.10_spmd, %region_9.12_spmd} | conditional | flops 1098645632 | bytes 80188504 | solution.py:235
  642.6 1.7 fusion.6
  644.3 5.1 fusion.9
  649.6 2.7 collective-permute-start.7
  653.4 2.7 collective-permute-start.1
  656.3 2.1 collective-permute-done
  658.5 2.8 collective-permute-done.8
  661.4 2.0 collective-permute-done.2
  663.6 1.4 select_bitcast_fusion.bias_ref
  666.3 2.7 collective-permute-start.4
  669.0 1.7 collective-permute-done.9
  671.5 1.3 collective-permute-done.3
  673.4 1.5 copy.26
  675.1 4.8 collective-permute-done.11
  680.2 1.9 collective-permute-done.5
  682.1 2.6 pad_maximum_fusion.k_ref.v_ref
  684.7 19.7 %branch_1_fun.1 = bf16[128,4096]{1,0:T(8,128)(2,1)} custom-call(bf16[128,4096]{1,0:T(8,128)(2,1)} %bitcast.52, bf16[2048,1024]{1,0:T(8,128)(2,1)} %pad_maximum_fusion.k_ref.v_ref, bf16[2048,1024]{1,0:T(8,128)(2,1)} %pad_maximum_fusion.k_ref.v_ref, f32[128,2048]{1,0:T(8,128)} %select_bitcast_fusion.bias_ref, bf16[128,4096]{1,0:T(8,128)(2,1)} %copy-done), custom_call_target="tpu_custom_call" | custom-call | tf_op jit(solution)/shard_map/while/body/eval_jaxpr/cond/branch_1_fun/pallas_call | solution.py:145
  705.9 1.3 copy-done.1
  (196 shorter events, 43.3 us)
Async XLA Ops:
  0.0 7.9 %copy-start.5 = (s32[2,2048]{1,0:T(2,128)S(1)}, s32[2,2048]{1,0:T(2,128)}, u32[]{:S(2)}) copy-start(s32[2,2048]{1,0:T(2,128)} %param.22) | copy-start | bytes 49156
  0.0 8.0 %copy-start.6 = (s32[2,32]{1,0:T(2,128)S(1)}, s32[2,32]{1,0:T(2,128)}, u32[]{:S(2)}) copy-start(s32[2,32]{1,0:T(2,128)} %param.23) | copy-start | bytes 772
  0.0 8.1 %copy-start.4 = (s32[2,2048]{1,0:T(2,128)S(1)}, s32[2,2048]{1,0:T(2,128)}, u32[]{:S(2)}) copy-start(s32[2,2048]{1,0:T(2,128)} %param.21) | copy-start | bytes 49156
  9.8 2.3 copy-start.3
  12.3 4.9 collective-permute-start.12
  18.8 16.3 %collective-permute-start.12 = (bf16[128,4096]{1,0:T(8,128)(2,1)}, bf16[128,4096]{1,0:T(8,128)(2,1)S(1)}, u32[]{:S(2)}, u32[]{:S(2)}) collective-permute-start(bf16[128,4096]{1,0:T(8,128)(2,1)} %get-tuple-element.635), channel_id=1, source_target_pairs={{0,16},{16,32},{32,48},{48,64},{64,80},{80,96},{96,112},{1,17},{17... | collective-permute-start | bytes 3145736 | tf_op jit(solution)/shard_map/while/body/eval_jaxpr/ppermute | solution.py:22
  36.6 16.3 %collective-permute-start.12 = (bf16[128,4096]{1,0:T(8,128)(2,1)}, bf16[128,4096]{1,0:T(8,128)(2,1)S(1)}, u32[]{:S(2)}, u32[]{:S(2)}) collective-permute-start(bf16[128,4096]{1,0:T(8,128)(2,1)} %get-tuple-element.635), channel_id=1, source_target_pairs={{0,16},{16,32},{32,48},{48,64},{64,80},{80,96},{96,112},{1,17},{17... | collective-permute-start | bytes 3145736 | tf_op jit(solution)/shard_map/while/body/eval_jaxpr/ppermute | solution.py:22
  54.5 16.3 %collective-permute-start.12 = (bf16[128,4096]{1,0:T(8,128)(2,1)}, bf16[128,4096]{1,0:T(8,128)(2,1)S(1)}, u32[]{:S(2)}, u32[]{:S(2)}) collective-permute-start(bf16[128,4096]{1,0:T(8,128)(2,1)} %get-tuple-element.635), channel_id=1, source_target_pairs={{0,16},{16,32},{32,48},{48,64},{64,80},{80,96},{96,112},{1,17},{17... | collective-permute-start | bytes 3145736 | tf_op jit(solution)/shard_map/while/body/eval_jaxpr/ppermute | solution.py:22
  72.3 16.3 %collective-permute-start.12 = (bf16[128,4096]{1,0:T(8,128)(2,1)}, bf16[128,4096]{1,0:T(8,128)(2,1)S(1)}, u32[]{:S(2)}, u32[]{:S(2)}) collective-permute-start(bf16[128,4096]{1,0:T(8,128)(2,1)} %get-tuple-element.635), channel_id=1, source_target_pairs={{0,16},{16,32},{32,48},{48,64},{64,80},{80,96},{96,112},{1,17},{17... | collective-permute-start | bytes 3145736 | tf_op jit(solution)/shard_map/while/body/eval_jaxpr/ppermute | solution.py:22
  90.2 16.3 %collective-permute-start.12 = (bf16[128,4096]{1,0:T(8,128)(2,1)}, bf16[128,4096]{1,0:T(8,128)(2,1)S(1)}, u32[]{:S(2)}, u32[]{:S(2)}) collective-permute-start(bf16[128,4096]{1,0:T(8,128)(2,1)} %get-tuple-element.635), channel_id=1, source_target_pairs={{0,16},{16,32},{32,48},{48,64},{64,80},{80,96},{96,112},{1,17},{17... | collective-permute-start | bytes 3145736 | tf_op jit(solution)/shard_map/while/body/eval_jaxpr/ppermute | solution.py:22
  108.1 16.3 %collective-permute-start.12 = (bf16[128,4096]{1,0:T(8,128)(2,1)}, bf16[128,4096]{1,0:T(8,128)(2,1)S(1)}, u32[]{:S(2)}, u32[]{:S(2)}) collective-permute-start(bf16[128,4096]{1,0:T(8,128)(2,1)} %get-tuple-element.635), channel_id=1, source_target_pairs={{0,16},{16,32},{32,48},{48,64},{64,80},{80,96},{96,112},{1,17},{17... | collective-permute-start | bytes 3145736 | tf_op jit(solution)/shard_map/while/body/eval_jaxpr/ppermute | solution.py:22
  125.9 429.9 %collective-permute-start.12 = (bf16[128,4096]{1,0:T(8,128)(2,1)}, bf16[128,4096]{1,0:T(8,128)(2,1)S(1)}, u32[]{:S(2)}, u32[]{:S(2)}) collective-permute-start(bf16[128,4096]{1,0:T(8,128)(2,1)} %get-tuple-element.635), channel_id=1, source_target_pairs={{0,16},{16,32},{32,48},{48,64},{64,80},{80,96},{96,112},{1,17},{17... | collective-permute-start | bytes 3145736 | tf_op jit(solution)/shard_map/while/body/eval_jaxpr/ppermute | solution.py:22
  557.5 5.1 copy-start
  562.7 6.7 collective-permute-start.6
  562.8 8.9 %collective-permute-start.7 = (bf16[128,512]{1,0:T(8,128)(2,1)S(1)}, bf16[128,512]{1,0:T(8,128)(2,1)S(1)}, u32[]{:S(2)}, u32[]{:S(2)}) collective-permute-start(bf16[128,512]{1,0:T(8,128)(2,1)S(1)} %slice.127), channel_id=1, source_target_pairs={{0,12},{1,13},{2,14},{3,15},{4,0},{5,1},{6,2},{7,3},{8,4},{9,5},{1... | collective-permute-start | bytes 393224 | tf_op jit(solution)/shard_map/while/body/eval_jaxpr/cond/branch_1_fun/ppermute | solution.py:84
  566.5 11.7 %copy-start.2 = (bf16[1,2,128,4096]{3,2,1,0:T(8,128)(2,1)S(1)}, bf16[1,2,128,4096]{3,2,1,0:T(8,128)(2,1)}, u32[]{:S(2)}) copy-start(bf16[1,2,128,4096]{3,2,1,0:T(8,128)(2,1)} %get-tuple-element.259) | copy-start | bytes 6291460 | tf_op jit(solution)/shard_map/while/body/eval_jaxpr/cond
  566.5 5.1 collective-permute-start
  566.6 5.0 collective-permute-start.1
  569.4 5.1 collective-permute-start.8
  571.6 5.0 collective-permute-start.2
  574.5 10.1 %collective-permute-start.9 = (bf16[512,512]{1,0:T(8,128)(2,1)S(1)}, bf16[512,512]{1,0:T(8,128)(2,1)S(1)}, u32[]{:S(2)}, u32[]{:S(2)}) collective-permute-start(bf16[512,512]{1,0:T(8,128)(2,1)S(1)} %pad_maximum_fusion.3), channel_id=1, source_target_pairs={{0,1},{1,2},{2,3},{3,0},{4,5},{5,6},{6,7},{7,4},{8,9},{9,10},{10,1... | collective-permute-start | bytes 1572872 | tf_op jit(solution)/shard_map/while/body/eval_jaxpr/cond/branch_1_fun/ppermute | solution.py:84
  576.7 9.3 %collective-permute-start.3 = (bf16[512,512]{1,0:T(8,128)(2,1)S(1)}, bf16[512,512]{1,0:T(8,128)(2,1)S(1)}, u32[]{:S(2)}, u32[]{:S(2)}) collective-permute-start(bf16[512,512]{1,0:T(8,128)(2,1)S(1)} %get-tuple-element.464), channel_id=1, source_target_pairs={{0,4},{1,5},{2,6},{3,7},{4,8},{5,9},{6,10},{7,11},{8,12},{9,13},{1... | collective-permute-start | bytes 1572872 | tf_op jit(solution)/shard_map/while/body/eval_jaxpr/cond/branch_1_fun/ppermute | solution.py:84
  578.7 9.7 %collective-permute-start.10 = (bf16[512,512]{1,0:T(8,128)(2,1)S(1)}, bf16[512,512]{1,0:T(8,128)(2,1)S(1)}, u32[]{:S(2)}, u32[]{:S(2)}) collective-permute-start(bf16[512,512]{1,0:T(8,128)(2,1)S(1)} %pad_maximum_fusion.3), channel_id=1, source_target_pairs={{0,3},{1,0},{2,1},{3,2},{4,7},{5,4},{6,5},{7,6},{8,11},{9,8},{10,9... | collective-permute-start | bytes 1572872 | tf_op jit(solution)/shard_map/while/body/eval_jaxpr/cond/branch_1_fun/ppermute | solution.py:84
  579.5 8.8 %collective-permute-start.4 = (bf16[512,512]{1,0:T(8,128)(2,1)S(1)}, bf16[512,512]{1,0:T(8,128)(2,1)S(1)}, u32[]{:S(2)}, u32[]{:S(2)}) collective-permute-start(bf16[512,512]{1,0:T(8,128)(2,1)S(1)} %get-tuple-element.464), channel_id=1, source_target_pairs={{0,12},{1,13},{2,14},{3,15},{4,0},{5,1},{6,2},{7,3},{8,4},{9,5},{1... | collective-permute-start | bytes 1572872 | tf_op jit(solution)/shard_map/while/body/eval_jaxpr/cond/branch_1_fun/ppermute | solution.py:84
  584.6 13.2 %collective-permute-start.11 = (bf16[512,512]{1,0:T(8,128)(2,1)S(1)}, bf16[512,512]{1,0:T(8,128)(2,1)S(1)}, u32[]{:S(2)}, u32[]{:S(2)}) collective-permute-start(bf16[512,512]{1,0:T(8,128)(2,1)S(1)} %collective-permute-done.9), channel_id=1, source_target_pairs={{0,1},{1,2},{2,3},{3,0},{4,5},{5,6},{6,7},{7,4},{8,9},{9,10},{10,1... | collective-permute-start | bytes 1572872 | tf_op jit(solution)/shard_map/while/body/eval_jaxpr/cond/branch_1_fun/ppermute | solution.py:84
  586.0 12.1 %collective-permute-start.5 = (bf16[512,512]{1,0:T(8,128)(2,1)S(1)}, bf16[512,512]{1,0:T(8,128)(2,1)S(1)}, u32[]{:S(2)}, u32[]{:S(2)}) collective-permute-start(bf16[512,512]{1,0:T(8,128)(2,1)S(1)} %collective-permute-done.3), channel_id=1, source_target_pairs={{0,4},{1,5},{2,6},{3,7},{4,8},{5,9},{6,10},{7,11},{8,12},{9,13},{1... | collective-permute-start | bytes 1572872 | tf_op jit(solution)/shard_map/while/body/eval_jaxpr/cond/branch_1_fun/ppermute | solution.py:84
  622.0 20.7 %collective-permute-start.12 = (bf16[128,4096]{1,0:T(8,128)(2,1)}, bf16[128,4096]{1,0:T(8,128)(2,1)S(1)}, u32[]{:S(2)}, u32[]{:S(2)}) collective-permute-start(bf16[128,4096]{1,0:T(8,128)(2,1)} %get-tuple-element.635), channel_id=1, source_target_pairs={{0,16},{16,32},{32,48},{48,64},{64,80},{80,96},{96,112},{1,17},{17... | collective-permute-start | bytes 3145736 | tf_op jit(solution)/shard_map/while/body/eval_jaxpr/ppermute | solution.py:22
  644.3 5.1 copy-start
  649.5 6.7 collective-permute-start.6
  649.6 8.9 %collective-permute-start.7 = (bf16[128,512]{1,0:T(8,128)(2,1)S(1)}, bf16[128,512]{1,0:T(8,128)(2,1)S(1)}, u32[]{:S(2)}, u32[]{:S(2)}) collective-permute-start(bf16[128,512]{1,0:T(8,128)(2,1)S(1)} %slice.127), channel_id=1, source_target_pairs={{0,12},{1,13},{2,14},{3,15},{4,0},{5,1},{6,2},{7,3},{8,4},{9,5},{1... | collective-permute-start | bytes 393224 | tf_op jit(solution)/shard_map/while/body/eval_jaxpr/cond/branch_1_fun/ppermute | solution.py:84
  653.3 11.7 %copy-start.2 = (bf16[1,2,128,4096]{3,2,1,0:T(8,128)(2,1)S(1)}, bf16[1,2,128,4096]{3,2,1,0:T(8,128)(2,1)}, u32[]{:S(2)}) copy-start(bf16[1,2,128,4096]{3,2,1,0:T(8,128)(2,1)} %get-tuple-element.259) | copy-start | bytes 6291460 | tf_op jit(solution)/shard_map/while/body/eval_jaxpr/cond
  653.3 5.1 collective-permute-start
  653.4 5.0 collective-permute-start.1
  656.2 5.1 collective-permute-start.8
  658.4 5.0 collective-permute-start.2
  661.4 9.3 %collective-permute-start.9 = (bf16[512,512]{1,0:T(8,128)(2,1)S(1)}, bf16[512,512]{1,0:T(8,128)(2,1)S(1)}, u32[]{:S(2)}, u32[]{:S(2)}) collective-permute-start(bf16[512,512]{1,0:T(8,128)(2,1)S(1)} %pad_maximum_fusion.3), channel_id=1, source_target_pairs={{0,1},{1,2},{2,3},{3,0},{4,5},{5,6},{6,7},{7,4},{8,9},{9,10},{10,1... | collective-permute-start | bytes 1572872 | tf_op jit(solution)/shard_map/while/body/eval_jaxpr/cond/branch_1_fun/ppermute | solution.py:84
  663.5 9.3 %collective-permute-start.3 = (bf16[512,512]{1,0:T(8,128)(2,1)S(1)}, bf16[512,512]{1,0:T(8,128)(2,1)S(1)}, u32[]{:S(2)}, u32[]{:S(2)}) collective-permute-start(bf16[512,512]{1,0:T(8,128)(2,1)S(1)} %get-tuple-element.464), channel_id=1, source_target_pairs={{0,4},{1,5},{2,6},{3,7},{4,8},{5,9},{6,10},{7,11},{8,12},{9,13},{1... | collective-permute-start | bytes 1572872 | tf_op jit(solution)/shard_map/while/body/eval_jaxpr/cond/branch_1_fun/ppermute | solution.py:84
  665.6 9.5 %collective-permute-start.10 = (bf16[512,512]{1,0:T(8,128)(2,1)S(1)}, bf16[512,512]{1,0:T(8,128)(2,1)S(1)}, u32[]{:S(2)}, u32[]{:S(2)}) collective-permute-start(bf16[512,512]{1,0:T(8,128)(2,1)S(1)} %pad_maximum_fusion.3), channel_id=1, source_target_pairs={{0,3},{1,0},{2,1},{3,2},{4,7},{5,4},{6,5},{7,6},{8,11},{9,8},{10,9... | collective-permute-start | bytes 1572872 | tf_op jit(solution)/shard_map/while/body/eval_jaxpr/cond/branch_1_fun/ppermute | solution.py:84
  666.3 8.8 %collective-permute-start.4 = (bf16[512,512]{1,0:T(8,128)(2,1)S(1)}, bf16[512,512]{1,0:T(8,128)(2,1)S(1)}, u32[]{:S(2)}, u32[]{:S(2)}) collective-permute-start(bf16[512,512]{1,0:T(8,128)(2,1)S(1)} %get-tuple-element.464), channel_id=1, source_target_pairs={{0,12},{1,13},{2,14},{3,15},{4,0},{5,1},{6,2},{7,3},{8,4},{9,5},{1... | collective-permute-start | bytes 1572872 | tf_op jit(solution)/shard_map/while/body/eval_jaxpr/cond/branch_1_fun/ppermute | solution.py:84
  670.7 9.2 %collective-permute-start.11 = (bf16[512,512]{1,0:T(8,128)(2,1)S(1)}, bf16[512,512]{1,0:T(8,128)(2,1)S(1)}, u32[]{:S(2)}, u32[]{:S(2)}) collective-permute-start(bf16[512,512]{1,0:T(8,128)(2,1)S(1)} %collective-permute-done.9), channel_id=1, source_target_pairs={{0,1},{1,2},{2,3},{3,0},{4,5},{5,6},{6,7},{7,4},{8,9},{9,10},{10,1... | collective-permute-start | bytes 1572872 | tf_op jit(solution)/shard_map/while/body/eval_jaxpr/cond/branch_1_fun/ppermute | solution.py:84
  672.8 9.2 %collective-permute-start.5 = (bf16[512,512]{1,0:T(8,128)(2,1)S(1)}, bf16[512,512]{1,0:T(8,128)(2,1)S(1)}, u32[]{:S(2)}, u32[]{:S(2)}) collective-permute-start(bf16[512,512]{1,0:T(8,128)(2,1)S(1)} %collective-permute-done.3), channel_id=1, source_target_pairs={{0,4},{1,5},{2,6},{3,7},{4,8},{5,9},{6,10},{7,11},{8,12},{9,13},{1... | collective-permute-start | bytes 1572872 | tf_op jit(solution)/shard_map/while/body/eval_jaxpr/cond/branch_1_fun/ppermute | solution.py:84
  705.9 1.3 copy-start.1

commit v8 on v7

--- a/solution.py
+++ b/solution.py
@@ -64,7 +64,7 @@
 def ring_gather(value, shift):
     ahead = shift(value, 1)
     behind = shift(value, -1)
-    far = shift(ahead, 1)
+    far = shift(value, 2)
     return [value, ahead, behind, far]
 
 

time: 708 us -> 728 us (1.028)
  waiting for transfers between devices: 577 us -> 589 us
  starting transfers between devices: 29.8 us -> 37.8 us
    ppermute x9, waiting for transfers between devices: 541 us -> 556 us  [from_behind(): return lax.ppermute(value, axis, pairs)]
    ppermute x24, starting transfers between devices: 18.2 us -> 26.2 us  [shift(): return lax.ppermute(piece, 'seq', pairs)]
  transfers between devices with their start and end apart: 33 -> 33, of which waited for: 25 -> 21; matrix products, arithmetic and copies ran while one was open for 2% -> 2% of each run, Pallas kernels for 0% -> 0%
where the time goes in v8:
time: 728 us; the launch traced here: 727 us
  waiting for transfers between devices  589 us (81%)
  Pallas kernels  39.3 us (5%)
  starting transfers between devices  37.8 us (5%)
  other arithmetic  29.3 us (4%)
  local copies, waits for them, and re-layouts  19.7 us (3%)
  matrix products  10.2 us (1%)
    ppermute x9, waiting for transfers between devices, from_behind(): return lax.ppermute(value, axis, pairs)  556 us
    pallas_call x2, Pallas kernels, attention(): pl.pallas_call(attention_kernel, grid=(HK,), in_specs=[pl.BlockSpec((rows...  39.3 us
    ppermute x24, waiting for transfers between devices, shift(): return lax.ppermute(piece, 'seq', pairs)  32.8 us
    ppermute x24, starting transfers between devices, shift(): return lax.ppermute(piece, 'seq', pairs)  26.2 us
  transfers between devices with their start and end apart: 33, of which 21 were waited for; matrix products, arithmetic and copies ran while one was open for 2% of the time, Pallas kernels for 0%

profile of v8, /device:TPU:25, one launch (start us, length us, event | category | flops | bytes accessed | tf_op | source)
XLA Modules:
  0.0 727.0 jit_solution(3854558712153432012)
XLA Ops:
  0.0 7.9 %pad_maximum_fusion.5 = bf16[4096,1024]{1,0:T(8,128)(2,1)} fusion(bf16[4096,512]{1,0:T(8,128)(2,1)} %bitcast.60, bf16[4096,512]{1,0:T(8,128)(2,1)} %bitcast.61), kind=kLoop, calls=%fused_computation.54 | loop fusion | flops 16777216 | bytes 16777216 | tf_op jit(solution)/shard_map/concatenate | solution.py:194
  12.1 713.6 %while.18 = (s32[]{:T(128)}, bf16[128,4096]{1,0:T(8,128)(2,1)}, bf16[2,128,4096]{2,1,0:T(8,128)(2,1)S(1)}, s32[]{:T(128)}, bf16[1,2,128,4096]{3,2,1,0:T(8,128)(2...) while((s32[]{:T(128)}, bf16[128,4096]{1,0:T(8,128)(2,1)}, ...), condition=%wide.region_11.14_spmd.clone.clone, body=%wide.region_7.13_spmd.clone.clone.sunk | while | flops 1099186304 | bytes 87595792 | solution.py:247
  13.7 3.5 collective-permute-done.12
  18.8 1.3 collective-permute-start.12
  20.2 14.9 %collective-permute-done.12 = bf16[128,4096]{1,0:T(8,128)(2,1)S(1)} collective-permute-done((bf16[128,4096]{1,0:T(8,128)(2,1)}, bf16[128,4096]{1,0:T(8,128)(2,1)S(1)}, u32[]{:S(2)}, u32[]{:S(2)}) %collective-permute-start.12) | collective-permute-done | bytes 1048608 | tf_op jit(solution)/shard_map/while/body/eval_jaxpr/ppermute | solution.py:22
  38.0 14.9 %collective-permute-done.12 = bf16[128,4096]{1,0:T(8,128)(2,1)S(1)} collective-permute-done((bf16[128,4096]{1,0:T(8,128)(2,1)}, bf16[128,4096]{1,0:T(8,128)(2,1)S(1)}, u32[]{:S(2)}, u32[]{:S(2)}) %collective-permute-start.12) | collective-permute-done | bytes 1048608 | tf_op jit(solution)/shard_map/while/body/eval_jaxpr/ppermute | solution.py:22
  54.5 1.3 collective-permute-start.12
  55.9 14.9 %collective-permute-done.12 = bf16[128,4096]{1,0:T(8,128)(2,1)S(1)} collective-permute-done((bf16[128,4096]{1,0:T(8,128)(2,1)}, bf16[128,4096]{1,0:T(8,128)(2,1)S(1)}, u32[]{:S(2)}, u32[]{:S(2)}) %collective-permute-start.12) | collective-permute-done | bytes 1048608 | tf_op jit(solution)/shard_map/while/body/eval_jaxpr/ppermute | solution.py:22
  73.8 14.9 %collective-permute-done.12 = bf16[128,4096]{1,0:T(8,128)(2,1)S(1)} collective-permute-done((bf16[128,4096]{1,0:T(8,128)(2,1)}, bf16[128,4096]{1,0:T(8,128)(2,1)S(1)}, u32[]{:S(2)}, u32[]{:S(2)}) %collective-permute-start.12) | collective-permute-done | bytes 1048608 | tf_op jit(solution)/shard_map/while/body/eval_jaxpr/ppermute | solution.py:22
  90.2 1.3 collective-permute-start.12
  91.6 14.9 %collective-permute-done.12 = bf16[128,4096]{1,0:T(8,128)(2,1)S(1)} collective-permute-done((bf16[128,4096]{1,0:T(8,128)(2,1)}, bf16[128,4096]{1,0:T(8,128)(2,1)S(1)}, u32[]{:S(2)}, u32[]{:S(2)}) %collective-permute-start.12) | collective-permute-done | bytes 1048608 | tf_op jit(solution)/shard_map/while/body/eval_jaxpr/ppermute | solution.py:22
  109.5 14.9 %collective-permute-done.12 = bf16[128,4096]{1,0:T(8,128)(2,1)S(1)} collective-permute-done((bf16[128,4096]{1,0:T(8,128)(2,1)}, bf16[128,4096]{1,0:T(8,128)(2,1)S(1)}, u32[]{:S(2)}, u32[]{:S(2)}) %collective-permute-start.12) | collective-permute-done | bytes 1048608 | tf_op jit(solution)/shard_map/while/body/eval_jaxpr/ppermute | solution.py:22
  125.9 1.3 collective-permute-start.12
  127.4 440.2 %collective-permute-done.12 = bf16[128,4096]{1,0:T(8,128)(2,1)S(1)} collective-permute-done((bf16[128,4096]{1,0:T(8,128)(2,1)}, bf16[128,4096]{1,0:T(8,128)(2,1)S(1)}, u32[]{:S(2)}, u32[]{:S(2)}) %collective-permute-start.12) | collective-permute-done | bytes 1048608 | tf_op jit(solution)/shard_map/while/body/eval_jaxpr/ppermute | solution.py:22
  567.5 67.7 %conditional.4 = (bf16[128,4096]{1,0:T(8,128)(2,1)}, bf16[1,128,4096]{2,1,0:T(8,128)(2,1)S(1)}) conditional(s32[]{:T(128)} %convert_element_type.63, () %tuple.104, (s32[]{:T(128)}, bf16[1,2,128,4096]{3,2,1,0:T(8,128)(2,1)}, f32[2,128,64]{2,1,0:T(8,128)S(1)}, f32[2,128,64]{2,1,0:T(8,128)S(1)}, pred[]{:T(512)}, ...), branch_computations={%region_8.10_spmd, %region_9.12_spmd} | conditional | flops 1098645632 | bytes 80188504 | solution.py:235
  567.5 1.7 fusion.6
  569.2 5.1 fusion.9
  574.9 3.5 collective-permute-start.7
  579.6 2.7 collective-permute-start.1
  582.4 1.4 select_bitcast_fusion.bias_ref
  585.5 4.5 collective-permute-done.2
  590.7 1.5 collective-permute-start.11
  592.3 1.4 collective-permute-start.9
  593.7 2.0 collective-permute-start.4
  596.5 5.6 collective-permute-done.3
  603.4 1.5 copy.26
  605.9 1.4 collective-permute-done.9
  607.6 4.0 collective-permute-done.5
  611.7 2.6 pad_maximum_fusion.k_ref.v_ref
  614.3 19.7 %branch_1_fun.1 = bf16[128,4096]{1,0:T(8,128)(2,1)} custom-call(bf16[128,4096]{1,0:T(8,128)(2,1)} %bitcast.52, bf16[2048,1024]{1,0:T(8,128)(2,1)} %pad_maximum_fusion.k_ref.v_ref, bf16[2048,1024]{1,0:T(8,128)(2,1)} %pad_maximum_fusion.k_ref.v_ref, f32[128,2048]{1,0:T(8,128)} %select_bitcast_fusion.bias_ref, bf16[128,4096]{1,0:T(8,128)(2,1)} %copy-done), custom_call_target="tpu_custom_call" | custom-call | tf_op jit(solution)/shard_map/while/body/eval_jaxpr/cond/branch_1_fun/pallas_call | solution.py:145
  637.0 23.0 %collective-permute-done.12 = bf16[128,4096]{1,0:T(8,128)(2,1)S(1)} collective-permute-done((bf16[128,4096]{1,0:T(8,128)(2,1)}, bf16[128,4096]{1,0:T(8,128)(2,1)S(1)}, u32[]{:S(2)}, u32[]{:S(2)}) %collective-permute-start.12) | collective-permute-done | bytes 1048608 | tf_op jit(solution)/shard_map/while/body/eval_jaxpr/ppermute | solution.py:22
  660.0 65.4 %conditional.4 = (bf16[128,4096]{1,0:T(8,128)(2,1)}, bf16[1,128,4096]{2,1,0:T(8,128)(2,1)S(1)}) conditional(s32[]{:T(128)} %convert_element_type.63, () %tuple.104, (s32[]{:T(128)}, bf16[1,2,128,4096]{3,2,1,0:T(8,128)(2,1)}, f32[2,128,64]{2,1,0:T(8,128)S(1)}, f32[2,128,64]{2,1,0:T(8,128)S(1)}, pred[]{:T(512)}, ...), branch_computations={%region_8.10_spmd, %region_9.12_spmd} | conditional | flops 1098645632 | bytes 80188504 | solution.py:235
  660.0 1.7 fusion.6
  661.7 5.1 fusion.9
  666.8 2.5 collective-permute-start.8
  669.3 2.1 collective-permute-start.7
  672.6 2.7 collective-permute-start.1
  675.4 1.4 select_bitcast_fusion.bias_ref
  677.9 5.0 collective-permute-done.2
  685.7 2.5 collective-permute-start.4
  689.0 3.3 collective-permute-done.3
  693.6 1.5 copy.26
  695.2 2.4 collective-permute-done.10
  697.6 1.7 collective-permute-done.9
  699.6 2.2 collective-permute-done.5
  701.9 2.6 pad_maximum_fusion.k_ref.v_ref
  704.5 19.7 %branch_1_fun.1 = bf16[128,4096]{1,0:T(8,128)(2,1)} custom-call(bf16[128,4096]{1,0:T(8,128)(2,1)} %bitcast.52, bf16[2048,1024]{1,0:T(8,128)(2,1)} %pad_maximum_fusion.k_ref.v_ref, bf16[2048,1024]{1,0:T(8,128)(2,1)} %pad_maximum_fusion.k_ref.v_ref, f32[128,2048]{1,0:T(8,128)} %select_bitcast_fusion.bias_ref, bf16[128,4096]{1,0:T(8,128)(2,1)} %copy-done), custom_call_target="tpu_custom_call" | custom-call | tf_op jit(solution)/shard_map/while/body/eval_jaxpr/cond/branch_1_fun/pallas_call | solution.py:145
  725.7 1.3 copy-done.1
  (196 shorter events, 48.1 us)
Async XLA Ops:
  0.0 7.9 %copy-start.5 = (s32[2,2048]{1,0:T(2,128)S(1)}, s32[2,2048]{1,0:T(2,128)}, u32[]{:S(2)}) copy-start(s32[2,2048]{1,0:T(2,128)} %param.22) | copy-start | bytes 49156
  0.0 8.0 %copy-start.6 = (s32[2,32]{1,0:T(2,128)S(1)}, s32[2,32]{1,0:T(2,128)}, u32[]{:S(2)}) copy-start(s32[2,32]{1,0:T(2,128)} %param.23) | copy-start | bytes 772
  0.0 8.1 %copy-start.4 = (s32[2,2048]{1,0:T(2,128)S(1)}, s32[2,2048]{1,0:T(2,128)}, u32[]{:S(2)}) copy-start(s32[2,2048]{1,0:T(2,128)} %param.21) | copy-start | bytes 49156
  9.8 2.3 copy-start.3
  12.3 4.9 collective-permute-start.12
  18.8 16.3 %collective-permute-start.12 = (bf16[128,4096]{1,0:T(8,128)(2,1)}, bf16[128,4096]{1,0:T(8,128)(2,1)S(1)}, u32[]{:S(2)}, u32[]{:S(2)}) collective-permute-start(bf16[128,4096]{1,0:T(8,128)(2,1)} %get-tuple-element.635), channel_id=1, source_target_pairs={{0,16},{16,32},{32,48},{48,64},{64,80},{80,96},{96,112},{1,17},{17... | collective-permute-start | bytes 3145736 | tf_op jit(solution)/shard_map/while/body/eval_jaxpr/ppermute | solution.py:22
  36.6 16.3 %collective-permute-start.12 = (bf16[128,4096]{1,0:T(8,128)(2,1)}, bf16[128,4096]{1,0:T(8,128)(2,1)S(1)}, u32[]{:S(2)}, u32[]{:S(2)}) collective-permute-start(bf16[128,4096]{1,0:T(8,128)(2,1)} %get-tuple-element.635), channel_id=1, source_target_pairs={{0,16},{16,32},{32,48},{48,64},{64,80},{80,96},{96,112},{1,17},{17... | collective-permute-start | bytes 3145736 | tf_op jit(solution)/shard_map/while/body/eval_jaxpr/ppermute | solution.py:22
  54.5 16.3 %collective-permute-start.12 = (bf16[128,4096]{1,0:T(8,128)(2,1)}, bf16[128,4096]{1,0:T(8,128)(2,1)S(1)}, u32[]{:S(2)}, u32[]{:S(2)}) collective-permute-start(bf16[128,4096]{1,0:T(8,128)(2,1)} %get-tuple-element.635), channel_id=1, source_target_pairs={{0,16},{16,32},{32,48},{48,64},{64,80},{80,96},{96,112},{1,17},{17... | collective-permute-start | bytes 3145736 | tf_op jit(solution)/shard_map/while/body/eval_jaxpr/ppermute | solution.py:22
  72.3 16.3 %collective-permute-start.12 = (bf16[128,4096]{1,0:T(8,128)(2,1)}, bf16[128,4096]{1,0:T(8,128)(2,1)S(1)}, u32[]{:S(2)}, u32[]{:S(2)}) collective-permute-start(bf16[128,4096]{1,0:T(8,128)(2,1)} %get-tuple-element.635), channel_id=1, source_target_pairs={{0,16},{16,32},{32,48},{48,64},{64,80},{80,96},{96,112},{1,17},{17... | collective-permute-start | bytes 3145736 | tf_op jit(solution)/shard_map/while/body/eval_jaxpr/ppermute | solution.py:22
  90.2 16.3 %collective-permute-start.12 = (bf16[128,4096]{1,0:T(8,128)(2,1)}, bf16[128,4096]{1,0:T(8,128)(2,1)S(1)}, u32[]{:S(2)}, u32[]{:S(2)}) collective-permute-start(bf16[128,4096]{1,0:T(8,128)(2,1)} %get-tuple-element.635), channel_id=1, source_target_pairs={{0,16},{16,32},{32,48},{48,64},{64,80},{80,96},{96,112},{1,17},{17... | collective-permute-start | bytes 3145736 | tf_op jit(solution)/shard_map/while/body/eval_jaxpr/ppermute | solution.py:22
  108.1 16.3 %collective-permute-start.12 = (bf16[128,4096]{1,0:T(8,128)(2,1)}, bf16[128,4096]{1,0:T(8,128)(2,1)S(1)}, u32[]{:S(2)}, u32[]{:S(2)}) collective-permute-start(bf16[128,4096]{1,0:T(8,128)(2,1)} %get-tuple-element.635), channel_id=1, source_target_pairs={{0,16},{16,32},{32,48},{48,64},{64,80},{80,96},{96,112},{1,17},{17... | collective-permute-start | bytes 3145736 | tf_op jit(solution)/shard_map/while/body/eval_jaxpr/ppermute | solution.py:22
  125.9 441.6 %collective-permute-start.12 = (bf16[128,4096]{1,0:T(8,128)(2,1)}, bf16[128,4096]{1,0:T(8,128)(2,1)S(1)}, u32[]{:S(2)}, u32[]{:S(2)}) collective-permute-start(bf16[128,4096]{1,0:T(8,128)(2,1)} %get-tuple-element.635), channel_id=1, source_target_pairs={{0,16},{16,32},{32,48},{48,64},{64,80},{80,96},{96,112},{1,17},{17... | collective-permute-start | bytes 3145736 | tf_op jit(solution)/shard_map/while/body/eval_jaxpr/ppermute | solution.py:22
  569.2 5.1 copy-start
  574.4 16.2 %collective-permute-start.8 = (bf16[128,512]{1,0:T(8,128)(2,1)S(1)}, bf16[128,512]{1,0:T(8,128)(2,1)S(1)}, u32[]{:S(2)}, u32[]{:S(2)}) collective-permute-start(bf16[128,512]{1,0:T(8,128)(2,1)S(1)} %slice.127), channel_id=1, source_target_pairs={{0,8},{1,9},{2,10},{3,11},{4,12},{5,13},{6,14},{7,15},{8,0},{9,1},... | collective-permute-start | bytes 393224 | tf_op jit(solution)/shard_map/while/body/eval_jaxpr/cond/branch_1_fun/ppermute | solution.py:84
  574.9 15.7 %collective-permute-start.7 = (bf16[128,512]{1,0:T(8,128)(2,1)S(1)}, bf16[128,512]{1,0:T(8,128)(2,1)S(1)}, u32[]{:S(2)}, u32[]{:S(2)}) collective-permute-start(bf16[128,512]{1,0:T(8,128)(2,1)S(1)} %slice.127), channel_id=1, source_target_pairs={{0,12},{1,13},{2,14},{3,15},{4,0},{5,1},{6,2},{7,3},{8,4},{9,5},{1... | collective-permute-start | bytes 393224 | tf_op jit(solution)/shard_map/while/body/eval_jaxpr/cond/branch_1_fun/ppermute | solution.py:84
  578.4 12.2 %collective-permute-start.6 = (bf16[128,512]{1,0:T(8,128)(2,1)S(1)}, bf16[128,512]{1,0:T(8,128)(2,1)S(1)}, u32[]{:S(2)}, u32[]{:S(2)}) collective-permute-start(bf16[128,512]{1,0:T(8,128)(2,1)S(1)} %slice.127), channel_id=1, source_target_pairs={{0,4},{1,5},{2,6},{3,7},{4,8},{5,9},{6,10},{7,11},{8,12},{9,13},{1... | collective-permute-start | bytes 393224 | tf_op jit(solution)/shard_map/while/body/eval_jaxpr/cond/branch_1_fun/ppermute | solution.py:84
  579.0 11.1 %copy-start.2 = (bf16[1,2,128,4096]{3,2,1,0:T(8,128)(2,1)S(1)}, bf16[1,2,128,4096]{3,2,1,0:T(8,128)(2,1)}, u32[]{:S(2)}) copy-start(bf16[1,2,128,4096]{3,2,1,0:T(8,128)(2,1)} %get-tuple-element.259) | copy-start | bytes 6291460 | tf_op jit(solution)/shard_map/while/body/eval_jaxpr/cond
  579.5 5.1 collective-permute-start
  579.6 5.8 collective-permute-start.1
  584.6 5.3 collective-permute-start.2
  589.9 12.2 %collective-permute-start.3 = (bf16[512,512]{1,0:T(8,128)(2,1)S(1)}, bf16[512,512]{1,0:T(8,128)(2,1)S(1)}, u32[]{:S(2)}, u32[]{:S(2)}) collective-permute-start(bf16[512,512]{1,0:T(8,128)(2,1)S(1)} %get-tuple-element.464), channel_id=1, source_target_pairs={{0,4},{1,5},{2,6},{3,7},{4,8},{5,9},{6,10},{7,11},{8,12},{9,13},{1... | collective-permute-start | bytes 1572872 | tf_op jit(solution)/shard_map/while/body/eval_jaxpr/cond/branch_1_fun/ppermute | solution.py:84
  590.7 14.2 %collective-permute-start.11 = (bf16[512,512]{1,0:T(8,128)(2,1)S(1)}, bf16[512,512]{1,0:T(8,128)(2,1)S(1)}, u32[]{:S(2)}, u32[]{:S(2)}) collective-permute-start(bf16[512,512]{1,0:T(8,128)(2,1)S(1)} %pad_maximum_fusion.3), channel_id=1, source_target_pairs={{0,2},{1,3},{2,0},{3,1},{4,6},{5,7},{6,4},{7,5},{8,10},{9,11},{10,... | collective-permute-start | bytes 1572872 | tf_op jit(solution)/shard_map/while/body/eval_jaxpr/cond/branch_1_fun/ppermute | solution.py:84
  592.2 13.7 %collective-permute-start.10 = (bf16[512,512]{1,0:T(8,128)(2,1)S(1)}, bf16[512,512]{1,0:T(8,128)(2,1)S(1)}, u32[]{:S(2)}, u32[]{:S(2)}) collective-permute-start(bf16[512,512]{1,0:T(8,128)(2,1)S(1)} %pad_maximum_fusion.3), channel_id=1, source_target_pairs={{0,3},{1,0},{2,1},{3,2},{4,7},{5,4},{6,5},{7,6},{8,11},{9,8},{10,9... | collective-permute-start | bytes 1572872 | tf_op jit(solution)/shard_map/while/body/eval_jaxpr/cond/branch_1_fun/ppermute | solution.py:84
  592.3 15.0 %collective-permute-start.9 = (bf16[512,512]{1,0:T(8,128)(2,1)S(1)}, bf16[512,512]{1,0:T(8,128)(2,1)S(1)}, u32[]{:S(2)}, u32[]{:S(2)}) collective-permute-start(bf16[512,512]{1,0:T(8,128)(2,1)S(1)} %pad_maximum_fusion.3), channel_id=1, source_target_pairs={{0,1},{1,2},{2,3},{3,0},{4,5},{5,6},{6,7},{7,4},{8,9},{9,10},{10,1... | collective-permute-start | bytes 1572872 | tf_op jit(solution)/shard_map/while/body/eval_jaxpr/cond/branch_1_fun/ppermute | solution.py:84
  593.7 11.2 %collective-permute-start.4 = (bf16[512,512]{1,0:T(8,128)(2,1)S(1)}, bf16[512,512]{1,0:T(8,128)(2,1)S(1)}, u32[]{:S(2)}, u32[]{:S(2)}) collective-permute-start(bf16[512,512]{1,0:T(8,128)(2,1)S(1)} %get-tuple-element.464), channel_id=1, source_target_pairs={{0,12},{1,13},{2,14},{3,15},{4,0},{5,1},{6,2},{7,3},{8,4},{9,5},{1... | collective-permute-start | bytes 1572872 | tf_op jit(solution)/shard_map/while/body/eval_jaxpr/cond/branch_1_fun/ppermute | solution.py:84
  602.1 9.5 %collective-permute-start.5 = (bf16[512,512]{1,0:T(8,128)(2,1)S(1)}, bf16[512,512]{1,0:T(8,128)(2,1)S(1)}, u32[]{:S(2)}, u32[]{:S(2)}) collective-permute-start(bf16[512,512]{1,0:T(8,128)(2,1)S(1)} %get-tuple-element.464), channel_id=1, source_target_pairs={{0,8},{1,9},{2,10},{3,11},{4,12},{5,13},{6,14},{7,15},{8,0},{9,1},... | collective-permute-start | bytes 1572872 | tf_op jit(solution)/shard_map/while/body/eval_jaxpr/cond/branch_1_fun/ppermute | solution.py:84
  635.6 24.4 %collective-permute-start.12 = (bf16[128,4096]{1,0:T(8,128)(2,1)}, bf16[128,4096]{1,0:T(8,128)(2,1)S(1)}, u32[]{:S(2)}, u32[]{:S(2)}) collective-permute-start(bf16[128,4096]{1,0:T(8,128)(2,1)} %get-tuple-element.635), channel_id=1, source_target_pairs={{0,16},{16,32},{32,48},{48,64},{64,80},{80,96},{96,112},{1,17},{17... | collective-permute-start | bytes 3145736 | tf_op jit(solution)/shard_map/while/body/eval_jaxpr/ppermute | solution.py:22
  661.7 5.1 copy-start
  666.8 17.2 %collective-permute-start.8 = (bf16[128,512]{1,0:T(8,128)(2,1)S(1)}, bf16[128,512]{1,0:T(8,128)(2,1)S(1)}, u32[]{:S(2)}, u32[]{:S(2)}) collective-permute-start(bf16[128,512]{1,0:T(8,128)(2,1)S(1)} %slice.127), channel_id=1, source_target_pairs={{0,8},{1,9},{2,10},{3,11},{4,12},{5,13},{6,14},{7,15},{8,0},{9,1},... | collective-permute-start | bytes 393224 | tf_op jit(solution)/shard_map/while/body/eval_jaxpr/cond/branch_1_fun/ppermute | solution.py:84
  669.3 14.7 %collective-permute-start.7 = (bf16[128,512]{1,0:T(8,128)(2,1)S(1)}, bf16[128,512]{1,0:T(8,128)(2,1)S(1)}, u32[]{:S(2)}, u32[]{:S(2)}) collective-permute-start(bf16[128,512]{1,0:T(8,128)(2,1)S(1)} %slice.127), channel_id=1, source_target_pairs={{0,12},{1,13},{2,14},{3,15},{4,0},{5,1},{6,2},{7,3},{8,4},{9,5},{1... | collective-permute-start | bytes 393224 | tf_op jit(solution)/shard_map/while/body/eval_jaxpr/cond/branch_1_fun/ppermute | solution.py:84
  671.4 12.6 %collective-permute-start.6 = (bf16[128,512]{1,0:T(8,128)(2,1)S(1)}, bf16[128,512]{1,0:T(8,128)(2,1)S(1)}, u32[]{:S(2)}, u32[]{:S(2)}) collective-permute-start(bf16[128,512]{1,0:T(8,128)(2,1)S(1)} %slice.127), channel_id=1, source_target_pairs={{0,4},{1,5},{2,6},{3,7},{4,8},{5,9},{6,10},{7,11},{8,12},{9,13},{1... | collective-permute-start | bytes 393224 | tf_op jit(solution)/shard_map/while/body/eval_jaxpr/cond/branch_1_fun/ppermute | solution.py:84
  672.0 11.4 %copy-start.2 = (bf16[1,2,128,4096]{3,2,1,0:T(8,128)(2,1)S(1)}, bf16[1,2,128,4096]{3,2,1,0:T(8,128)(2,1)}, u32[]{:S(2)}) copy-start(bf16[1,2,128,4096]{3,2,1,0:T(8,128)(2,1)} %get-tuple-element.259) | copy-start | bytes 6291460 | tf_op jit(solution)/shard_map/while/body/eval_jaxpr/cond
  672.5 5.1 collective-permute-start
  672.6 5.3 collective-permute-start.1
  677.6 5.3 collective-permute-start.2
  683.0 9.3 %collective-permute-start.3 = (bf16[512,512]{1,0:T(8,128)(2,1)S(1)}, bf16[512,512]{1,0:T(8,128)(2,1)S(1)}, u32[]{:S(2)}, u32[]{:S(2)}) collective-permute-start(bf16[512,512]{1,0:T(8,128)(2,1)S(1)} %get-tuple-element.464), channel_id=1, source_target_pairs={{0,4},{1,5},{2,6},{3,7},{4,8},{5,9},{6,10},{7,11},{8,12},{9,13},{1... | collective-permute-start | bytes 1572872 | tf_op jit(solution)/shard_map/while/body/eval_jaxpr/cond/branch_1_fun/ppermute | solution.py:84
  684.1 11.1 %collective-permute-start.11 = (bf16[512,512]{1,0:T(8,128)(2,1)S(1)}, bf16[512,512]{1,0:T(8,128)(2,1)S(1)}, u32[]{:S(2)}, u32[]{:S(2)}) collective-permute-start(bf16[512,512]{1,0:T(8,128)(2,1)S(1)} %pad_maximum_fusion.3), channel_id=1, source_target_pairs={{0,2},{1,3},{2,0},{3,1},{4,6},{5,7},{6,4},{7,5},{8,10},{9,11},{10,... | collective-permute-start | bytes 1572872 | tf_op jit(solution)/shard_map/while/body/eval_jaxpr/cond/branch_1_fun/ppermute | solution.py:84
  684.2 13.4 %collective-permute-start.10 = (bf16[512,512]{1,0:T(8,128)(2,1)S(1)}, bf16[512,512]{1,0:T(8,128)(2,1)S(1)}, u32[]{:S(2)}, u32[]{:S(2)}) collective-permute-start(bf16[512,512]{1,0:T(8,128)(2,1)S(1)} %pad_maximum_fusion.3), channel_id=1, source_target_pairs={{0,3},{1,0},{2,1},{3,2},{4,7},{5,4},{6,5},{7,6},{8,11},{9,8},{10,9... | collective-permute-start | bytes 1572872 | tf_op jit(solution)/shard_map/while/body/eval_jaxpr/cond/branch_1_fun/ppermute | solution.py:84
  685.4 14.0 %collective-permute-start.9 = (bf16[512,512]{1,0:T(8,128)(2,1)S(1)}, bf16[512,512]{1,0:T(8,128)(2,1)S(1)}, u32[]{:S(2)}, u32[]{:S(2)}) collective-permute-start(bf16[512,512]{1,0:T(8,128)(2,1)S(1)} %pad_maximum_fusion.3), channel_id=1, source_target_pairs={{0,1},{1,2},{2,3},{3,0},{4,5},{5,6},{6,7},{7,4},{8,9},{9,10},{10,1... | collective-permute-start | bytes 1572872 | tf_op jit(solution)/shard_map/while/body/eval_jaxpr/cond/branch_1_fun/ppermute | solution.py:84
  685.7 9.4 %collective-permute-start.4 = (bf16[512,512]{1,0:T(8,128)(2,1)S(1)}, bf16[512,512]{1,0:T(8,128)(2,1)S(1)}, u32[]{:S(2)}, u32[]{:S(2)}) collective-permute-start(bf16[512,512]{1,0:T(8,128)(2,1)S(1)} %get-tuple-element.464), channel_id=1, source_target_pairs={{0,12},{1,13},{2,14},{3,15},{4,0},{5,1},{6,2},{7,3},{8,4},{9,5},{1... | collective-permute-start | bytes 1572872 | tf_op jit(solution)/shard_map/while/body/eval_jaxpr/cond/branch_1_fun/ppermute | solution.py:84
  692.3 9.5 %collective-permute-start.5 = (bf16[512,512]{1,0:T(8,128)(2,1)S(1)}, bf16[512,512]{1,0:T(8,128)(2,1)S(1)}, u32[]{:S(2)}, u32[]{:S(2)}) collective-permute-start(bf16[512,512]{1,0:T(8,128)(2,1)S(1)} %get-tuple-element.464), channel_id=1, source_target_pairs={{0,8},{1,9},{2,10},{3,11},{4,12},{5,13},{6,14},{7,15},{8,0},{9,1},... | collective-permute-start | bytes 1572872 | tf_op jit(solution)/shard_map/while/body/eval_jaxpr/cond/branch_1_fun/ppermute | solution.py:84
  725.7 1.3 copy-start.1

commit v9 on v7

--- a/solution.py
+++ b/solution.py
@@ -90,12 +90,10 @@
     rows = value.shape[0]
     width = value.shape[1] // 2
     row_a = jnp.concatenate(ring_gather(value[:, :width], shift_x), axis=0)
-    full_a = jnp.concatenate(ring_gather(row_a, shift_z), axis=0)
+    pieces_a = ring_gather(row_a, shift_z)
     col_b = jnp.concatenate(ring_gather(value[:, width:], shift_z), axis=0)
     pieces_b = ring_gather(col_b, shift_x)
-    full_b = jnp.stack(pieces_b, axis=0).reshape(side, side, rows, width)
-    full_b = full_b.transpose(1, 0, 2, 3).reshape(side * side * rows, width)
-    return jnp.concatenate([full_a, full_b], axis=1)
+    return pieces_a, pieces_b
 
 
 def torus_order(values, shard_id, side, rows):
@@ -111,50 +109,66 @@
     return blocks.reshape(micro_count, side * side * rows)
 
 
-def attention_kernel(q_ref, k_ref, v_ref, bias_ref, res_ref, o_ref):
+def attention_kernel(q_ref, *refs):
+    side = len(RING_OFFSETS)
+    key_refs = refs[:side]
+    value_refs = refs[side : 2 * side]
+    bias_ref, res_ref, o_ref = refs[2 * side :]
     ratio = HQ // HK
     scale = 1.0 / math.sqrt(HD)
-    keys = k_ref[...]
-    values = v_ref[...]
-    bias = bias_ref[...]
+    piece = key_refs[0].shape[0]
+    rows = piece // side
     for g in range(ratio):
         cols = slice(g * HD, (g + 1) * HD)
-        scores = lax.dot_general(
-            q_ref[:, cols],
-            keys,
-            (((1,), (1,)), ((), ())),
-            preferred_element_type=jnp.float32,
-        )
-        masked = scores * scale + bias
-        row_top = jnp.max(masked, axis=-1, keepdims=True)
-        weights = jnp.exp(masked - row_top)
-        denominator = jnp.sum(weights, axis=-1, keepdims=True)
-        summed = jnp.dot(
-            weights.astype(jnp.bfloat16), values, preferred_element_type=jnp.float32
-        )
+        query = q_ref[:, cols]
+        masked = []
+        for p in range(side):
+            scores = lax.dot_general(
+                query,
+                key_refs[p][...],
+                (((1,), (1,)), ((), ())),
+                preferred_element_type=jnp.float32,
+            )
+            masked.append(scores * scale + bias_ref[:, p * piece : (p + 1) * piece])
+        row_top = jnp.max(masked[0], axis=-1, keepdims=True)
+        for p in range(1, side):
+            row_top = jnp.maximum(row_top, jnp.max(masked[p], axis=-1, keepdims=True))
+        weights = [jnp.exp(m - row_top) for m in masked]
+        denominator = jnp.sum(weights[0], axis=-1, keepdims=True)
+        for p in range(1, side):
+            denominator = denominator + jnp.sum(weights[p], axis=-1, keepdims=True)
+        rounded = [w.astype(jnp.bfloat16) for w in weights]
+        summed = None
+        for q in range(side):
+            picked = jnp.concatenate(
+                [rounded[p][:, q * rows : (q + 1) * rows] for p in range(side)], axis=1
+            )
+            part = jnp.dot(picked, value_refs[q][...], preferred_element_type=jnp.float32)
+            summed = part if summed is None else summed + part
         attended = (summed / denominator).astype(jnp.bfloat16)
         o_ref[:, cols] = (
             res_ref[:, cols].astype(jnp.float32) + attended.astype(jnp.float32)
         ).astype(o_ref.dtype)
 
 
-def attention(turned, kv_all, bias, residual):
+def attention(turned, pieces_a, pieces_b, bias, residual):
     rows, width = turned.shape
-    keys_len = kv_all.shape[0]
+    piece = pieces_a[0].shape[0]
+    keys_len = bias.shape[1]
     group = width // HK
+    piece_spec = pl.BlockSpec((piece, HD), lambda k: (0, k))
     return pl.pallas_call(
         attention_kernel,
         grid=(HK,),
-        in_specs=[
-            pl.BlockSpec((rows, group), lambda k: (0, k)),
-            pl.BlockSpec((keys_len, HD), lambda k: (0, k)),
-            pl.BlockSpec((keys_len, HD), lambda k: (0, HK + k)),
+        in_specs=[pl.BlockSpec((rows, group), lambda k: (0, k))]
+        + [piece_spec] * (len(pieces_a) + len(pieces_b))
+        + [
             pl.BlockSpec((rows, keys_len), lambda k: (0, 0)),
             pl.BlockSpec((rows, group), lambda k: (0, k)),
         ],
         out_specs=pl.BlockSpec((rows, group), lambda k: (0, k)),
         out_shape=jax.ShapeDtypeStruct((rows, width), jnp.bfloat16),
-    )(turned, kv_all, kv_all, bias, residual)
+    )(turned, *pieces_a, *pieces_b, bias, residual)
 
 
 def local(hidden, queries, gain, key_weight, value_weight, tree_ids, branch_ids, span_order):
@@ -209,7 +223,7 @@
         )
         value_rows = kv_proj[:, HK * HD :].astype(jnp.bfloat16)
         kv_rows = jnp.concatenate([key_rows, value_rows], axis=1)
-        kv_all = torus_gather(kv_rows, side)
+        pieces_a, pieces_b = torus_gather(kv_rows, side)
         query_local = lax.dynamic_index_in_dim(queries[0], mb, 0, keepdims=False)
         turned = (
             rotate(
@@ -220,7 +234,7 @@
             .astype(jnp.bfloat16)
             .reshape(row_count, HQ * HD)
         )
-        return attention(turned, kv_all, bias, current)
+        return attention(turned, pieces_a, pieces_b, bias, current)
 
     tick_count = section_count + micro_count - 1
 

time: 708 us -> 707 us (level)
  waiting for transfers between devices: 577 us -> 569 us
    ppermute x9, waiting for transfers between devices: 541 us -> 533 us  [from_behind(): return lax.ppermute(value, axis, pairs)]
  transfers between devices with their start and end apart: 33 -> 33, of which waited for: 25 -> 21; matrix products, arithmetic and copies ran while one was open for 2% -> 2% of each run, Pallas kernels for 0% -> 0%
where the time goes in v9:
time: 707 us; the launch traced here: 706 us
  waiting for transfers between devices  569 us (80%)
  Pallas kernels  39.4 us (6%)
  starting transfers between devices  33.6 us (5%)
  other arithmetic  27.7 us (4%)
  local copies, waits for them, and re-layouts  23.9 us (3%)
  matrix products  10.2 us (1%)
    ppermute x9, waiting for transfers between devices, from_behind(): return lax.ppermute(value, axis, pairs)  533 us
    pallas_call x2, Pallas kernels, attention(): pl.pallas_call(attention_kernel, grid=(HK,), in_specs=[pl.BlockSpec((rows...  39.4 us
    ppermute x24, waiting for transfers between devices, shift(): return lax.ppermute(piece, 'seq', pairs)  36.1 us
    ppermute x24, starting transfers between devices, shift(): return lax.ppermute(piece, 'seq', pairs)  22 us
  transfers between devices with their start and end apart: 33, of which 21 were waited for; matrix products, arithmetic and copies ran while one was open for 2% of the time, Pallas kernels for 0%

profile of v9, /device:TPU:25, one launch (start us, length us, event | category | flops | bytes accessed | tf_op | source)
XLA Modules:
  0.0 705.6 jit_solution(15636232229913056279)
XLA Ops:
  8.4 7.9 %pad_maximum_fusion.3 = bf16[4096,1024]{1,0:T(8,128)(2,1)} fusion(bf16[4096,512]{1,0:T(8,128)(2,1)} %bitcast.38, bf16[4096,512]{1,0:T(8,128)(2,1)} %bitcast.39), kind=kLoop, calls=%fused_computation.45 | loop fusion | flops 16777216 | bytes 16777216 | tf_op jit(solution)/shard_map/concatenate | solution.py:208
  17.6 686.7 %while.18 = (s32[]{:T(128)}, bf16[128,4096]{1,0:T(8,128)(2,1)}, bf16[2,128,4096]{2,1,0:T(8,128)(2,1)S(1)}, s32[]{:T(128)}, bf16[1,2,128,4096]{3,2,1,0:T(8,128)(2...) while((s32[]{:T(128)}, bf16[128,4096]{1,0:T(8,128)(2,1)}, ...), condition=%wide.region_11.14_spmd.clone.clone, body=%wide.region_7.13_spmd.clone.clone.sunk | while | flops 1087651968 | bytes 88120304 | solution.py:261
  17.6 1.3 collective-permute-start.12
  19.1 3.5 collective-permute-done.12
  24.1 1.3 collective-permute-start.12
  25.5 14.9 %collective-permute-done.12 = bf16[128,4096]{1,0:T(8,128)(2,1)S(1)} collective-permute-done((bf16[128,4096]{1,0:T(8,128)(2,1)}, bf16[128,4096]{1,0:T(8,128)(2,1)S(1)}, u32[]{:S(2)}, u32[]{:S(2)}) %collective-permute-start.12) | collective-permute-done | bytes 1048608 | tf_op jit(solution)/shard_map/while/body/eval_jaxpr/ppermute | solution.py:22
  42.0 1.3 collective-permute-start.12
  43.4 14.9 %collective-permute-done.12 = bf16[128,4096]{1,0:T(8,128)(2,1)S(1)} collective-permute-done((bf16[128,4096]{1,0:T(8,128)(2,1)}, bf16[128,4096]{1,0:T(8,128)(2,1)S(1)}, u32[]{:S(2)}, u32[]{:S(2)}) %collective-permute-start.12) | collective-permute-done | bytes 1048608 | tf_op jit(solution)/shard_map/while/body/eval_jaxpr/ppermute | solution.py:22
  59.8 1.3 collective-permute-start.12
  61.3 14.9 %collective-permute-done.12 = bf16[128,4096]{1,0:T(8,128)(2,1)S(1)} collective-permute-done((bf16[128,4096]{1,0:T(8,128)(2,1)}, bf16[128,4096]{1,0:T(8,128)(2,1)S(1)}, u32[]{:S(2)}, u32[]{:S(2)}) %collective-permute-start.12) | collective-permute-done | bytes 1048608 | tf_op jit(solution)/shard_map/while/body/eval_jaxpr/ppermute | solution.py:22
  77.7 1.3 collective-permute-start.12
  79.1 14.9 %collective-permute-done.12 = bf16[128,4096]{1,0:T(8,128)(2,1)S(1)} collective-permute-done((bf16[128,4096]{1,0:T(8,128)(2,1)}, bf16[128,4096]{1,0:T(8,128)(2,1)S(1)}, u32[]{:S(2)}, u32[]{:S(2)}) %collective-permute-start.12) | collective-permute-done | bytes 1048608 | tf_op jit(solution)/shard_map/while/body/eval_jaxpr/ppermute | solution.py:22
  95.6 1.3 collective-permute-start.12
  97.0 14.9 %collective-permute-done.12 = bf16[128,4096]{1,0:T(8,128)(2,1)S(1)} collective-permute-done((bf16[128,4096]{1,0:T(8,128)(2,1)}, bf16[128,4096]{1,0:T(8,128)(2,1)S(1)}, u32[]{:S(2)}, u32[]{:S(2)}) %collective-permute-start.12) | collective-permute-done | bytes 1048608 | tf_op jit(solution)/shard_map/while/body/eval_jaxpr/ppermute | solution.py:22
  113.4 1.3 collective-permute-start.12
  114.9 14.9 %collective-permute-done.12 = bf16[128,4096]{1,0:T(8,128)(2,1)S(1)} collective-permute-done((bf16[128,4096]{1,0:T(8,128)(2,1)}, bf16[128,4096]{1,0:T(8,128)(2,1)S(1)}, u32[]{:S(2)}, u32[]{:S(2)}) %collective-permute-start.12) | collective-permute-done | bytes 1048608 | tf_op jit(solution)/shard_map/while/body/eval_jaxpr/ppermute | solution.py:22
  131.3 1.3 collective-permute-start.12
  132.7 423.7 %collective-permute-done.12 = bf16[128,4096]{1,0:T(8,128)(2,1)S(1)} collective-permute-done((bf16[128,4096]{1,0:T(8,128)(2,1)}, bf16[128,4096]{1,0:T(8,128)(2,1)S(1)}, u32[]{:S(2)}, u32[]{:S(2)}) %collective-permute-start.12) | collective-permute-done | bytes 1048608 | tf_op jit(solution)/shard_map/while/body/eval_jaxpr/ppermute | solution.py:22
  556.4 67.6 %conditional.4 = (bf16[128,4096]{1,0:T(8,128)(2,1)}, bf16[1,128,4096]{2,1,0:T(8,128)(2,1)S(1)}) conditional(s32[]{:T(128)} %convert_element_type.63, () %tuple.100, (s32[]{:T(128)}, bf16[1,2,128,4096]{3,2,1,0:T(8,128)(2,1)}, f32[2,128,64]{2,1,0:T(8,128)S(1)}, f32[2,128,64]{2,1,0:T(8,128)S(1)}, pred[]{:T(512)}, ...), branch_computations={%region_8.10_spmd, %region_9.12_spmd} | conditional | flops 1087111296 | bytes 80713016 | solution.py:249
  556.4 1.7 fusion.6
  558.1 5.1 fusion.9
  564.4 2.7 collective-permute-start.1
  567.2 2.7 collective-permute-start.7
  572.2 4.8 collective-permute-done.2
  577.4 2.6 collective-permute-start.4
  580.0 2.6 collective-permute-start.10
  582.7 5.0 collective-permute-done.3.refs_1_
  587.8 1.5 copy.16
  589.3 1.4 select_bitcast_fusion.refs_8_
  590.8 10.7 %collective-permute-done.5.refs_3_ = bf16[512,512]{1,0:T(8,128)(2,1)S(1)} collective-permute-done((bf16[512,512]{1,0:T(8,128)(2,1)S(1)}, bf16[512,512]{1,0:T(8,128)(2,1)S(1)}, u32[]{:S(2)}, u32[]{:S(2)}) %collective-permute-start.5) | collective-permute-done | bytes 524320 | tf_op jit(solution)/shard_map/while/body/eval_jaxpr/cond/branch_1_fun/ppermute | solution.py:84
  603.1 19.7 %branch_1_fun.1 = bf16[128,4096]{1,0:T(8,128)(2,1)} custom-call(bf16[128,4096]{1,0:T(8,128)(2,1)} %bitcast.35, bf16[512,512]{1,0:T(8,128)(2,1)} %copy-done.3, bf16[512,512]{1,0:T(8,128)(2,1)} %copy-done.4, bf16[512,512]{1,0:T(8,128)(2,1)} %copy-done.6, bf16[512,512]{1,0:T(8,128)(2,1)} %copy-done.8, bf16[512,512]{1,0:T(8,128)(2,1)} %copy-done.1, ...), custom_call_target="tpu_custom_call" | custom-call | tf_op jit(solution)/shard_map/while/body/eval_jaxpr/cond/branch_1_fun/pallas_call | solution.py:160
  624.4 1.3 collective-permute-start.12
  625.8 16.5 %collective-permute-done.12 = bf16[128,4096]{1,0:T(8,128)(2,1)S(1)} collective-permute-done((bf16[128,4096]{1,0:T(8,128)(2,1)}, bf16[128,4096]{1,0:T(8,128)(2,1)S(1)}, u32[]{:S(2)}, u32[]{:S(2)}) %collective-permute-start.12) | collective-permute-done | bytes 1048608 | tf_op jit(solution)/shard_map/while/body/eval_jaxpr/ppermute | solution.py:22
  642.3 61.7 %conditional.4 = (bf16[128,4096]{1,0:T(8,128)(2,1)}, bf16[1,128,4096]{2,1,0:T(8,128)(2,1)S(1)}) conditional(s32[]{:T(128)} %convert_element_type.63, () %tuple.100, (s32[]{:T(128)}, bf16[1,2,128,4096]{3,2,1,0:T(8,128)(2,1)}, f32[2,128,64]{2,1,0:T(8,128)S(1)}, f32[2,128,64]{2,1,0:T(8,128)S(1)}, pred[]{:T(512)}, ...), branch_computations={%region_8.10_spmd, %region_9.12_spmd} | conditional | flops 1087111296 | bytes 80713016 | solution.py:249
  642.3 1.7 fusion.6
  644.0 5.1 fusion.9
  650.3 2.7 collective-permute-start.1
  653.0 2.7 collective-permute-start.7
  658.1 4.8 collective-permute-done.2
  663.3 2.6 collective-permute-start.4
  665.9 2.6 collective-permute-start.10
  668.5 3.6 collective-permute-done.3.refs_1_
  672.5 1.5 copy.16
  674.0 1.4 select_bitcast_fusion.refs_8_
  675.4 6.0 collective-permute-done.5.refs_3_
  683.0 19.7 %branch_1_fun.1 = bf16[128,4096]{1,0:T(8,128)(2,1)} custom-call(bf16[128,4096]{1,0:T(8,128)(2,1)} %bitcast.35, bf16[512,512]{1,0:T(8,128)(2,1)} %copy-done.3, bf16[512,512]{1,0:T(8,128)(2,1)} %copy-done.4, bf16[512,512]{1,0:T(8,128)(2,1)} %copy-done.6, bf16[512,512]{1,0:T(8,128)(2,1)} %copy-done.8, bf16[512,512]{1,0:T(8,128)(2,1)} %copy-done.1, ...), custom_call_target="tpu_custom_call" | custom-call | tf_op jit(solution)/shard_map/while/body/eval_jaxpr/cond/branch_1_fun/pallas_call | solution.py:160
  702.7 1.2 copy.24
  704.3 1.3 copy-done.2
  (212 shorter events, 42.3 us)
Async XLA Ops:
  17.6 4.9 collective-permute-start.12
  24.1 16.3 %collective-permute-start.12 = (bf16[128,4096]{1,0:T(8,128)(2,1)}, bf16[128,4096]{1,0:T(8,128)(2,1)S(1)}, u32[]{:S(2)}, u32[]{:S(2)}) collective-permute-start(bf16[128,4096]{1,0:T(8,128)(2,1)} %get-tuple-element.627), channel_id=1, source_target_pairs={{0,16},{16,32},{32,48},{48,64},{64,80},{80,96},{96,112},{1,17},{17... | collective-permute-start | bytes 3145736 | tf_op jit(solution)/shard_map/while/body/eval_jaxpr/ppermute | solution.py:22
  42.0 16.3 %collective-permute-start.12 = (bf16[128,4096]{1,0:T(8,128)(2,1)}, bf16[128,4096]{1,0:T(8,128)(2,1)S(1)}, u32[]{:S(2)}, u32[]{:S(2)}) collective-permute-start(bf16[128,4096]{1,0:T(8,128)(2,1)} %get-tuple-element.627), channel_id=1, source_target_pairs={{0,16},{16,32},{32,48},{48,64},{64,80},{80,96},{96,112},{1,17},{17... | collective-permute-start | bytes 3145736 | tf_op jit(solution)/shard_map/while/body/eval_jaxpr/ppermute | solution.py:22
  59.8 16.3 %collective-permute-start.12 = (bf16[128,4096]{1,0:T(8,128)(2,1)}, bf16[128,4096]{1,0:T(8,128)(2,1)S(1)}, u32[]{:S(2)}, u32[]{:S(2)}) collective-permute-start(bf16[128,4096]{1,0:T(8,128)(2,1)} %get-tuple-element.627), channel_id=1, source_target_pairs={{0,16},{16,32},{32,48},{48,64},{64,80},{80,96},{96,112},{1,17},{17... | collective-permute-start | bytes 3145736 | tf_op jit(solution)/shard_map/while/body/eval_jaxpr/ppermute | solution.py:22
  77.7 16.3 %collective-permute-start.12 = (bf16[128,4096]{1,0:T(8,128)(2,1)}, bf16[128,4096]{1,0:T(8,128)(2,1)S(1)}, u32[]{:S(2)}, u32[]{:S(2)}) collective-permute-start(bf16[128,4096]{1,0:T(8,128)(2,1)} %get-tuple-element.627), channel_id=1, source_target_pairs={{0,16},{16,32},{32,48},{48,64},{64,80},{80,96},{96,112},{1,17},{17... | collective-permute-start | bytes 3145736 | tf_op jit(solution)/shard_map/while/body/eval_jaxpr/ppermute | solution.py:22
  95.6 16.3 %collective-permute-start.12 = (bf16[128,4096]{1,0:T(8,128)(2,1)}, bf16[128,4096]{1,0:T(8,128)(2,1)S(1)}, u32[]{:S(2)}, u32[]{:S(2)}) collective-permute-start(bf16[128,4096]{1,0:T(8,128)(2,1)} %get-tuple-element.627), channel_id=1, source_target_pairs={{0,16},{16,32},{32,48},{48,64},{64,80},{80,96},{96,112},{1,17},{17... | collective-permute-start | bytes 3145736 | tf_op jit(solution)/shard_map/while/body/eval_jaxpr/ppermute | solution.py:22
  113.4 16.3 %collective-permute-start.12 = (bf16[128,4096]{1,0:T(8,128)(2,1)}, bf16[128,4096]{1,0:T(8,128)(2,1)S(1)}, u32[]{:S(2)}, u32[]{:S(2)}) collective-permute-start(bf16[128,4096]{1,0:T(8,128)(2,1)} %get-tuple-element.627), channel_id=1, source_target_pairs={{0,16},{16,32},{32,48},{48,64},{64,80},{80,96},{96,112},{1,17},{17... | collective-permute-start | bytes 3145736 | tf_op jit(solution)/shard_map/while/body/eval_jaxpr/ppermute | solution.py:22
  131.3 425.1 %collective-permute-start.12 = (bf16[128,4096]{1,0:T(8,128)(2,1)}, bf16[128,4096]{1,0:T(8,128)(2,1)S(1)}, u32[]{:S(2)}, u32[]{:S(2)}) collective-permute-start(bf16[128,4096]{1,0:T(8,128)(2,1)} %get-tuple-element.627), channel_id=1, source_target_pairs={{0,16},{16,32},{32,48},{48,64},{64,80},{80,96},{96,112},{1,17},{17... | collective-permute-start | bytes 3145736 | tf_op jit(solution)/shard_map/while/body/eval_jaxpr/ppermute | solution.py:22
  558.1 5.1 copy-start
  563.3 6.5 copy-start.10
  564.3 7.6 %collective-permute-start = (bf16[128,512]{1,0:T(8,128)(2,1)S(1)}, bf16[128,512]{1,0:T(8,128)(2,1)S(1)}, u32[]{:S(2)}, u32[]{:S(2)}) collective-permute-start(bf16[128,512]{1,0:T(8,128)(2,1)S(1)} %bitcast.40), channel_id=1, source_target_pairs={{0,1},{1,2},{2,3},{3,0},{4,5},{5,6},{6,7},{7,4},{8,9},{9,10},{10,1... | collective-permute-start | bytes 393224 | tf_op jit(solution)/shard_map/while/body/eval_jaxpr/cond/branch_1_fun/ppermute | solution.py:84
  564.4 7.8 %collective-permute-start.1 = (bf16[128,512]{1,0:T(8,128)(2,1)S(1)}, bf16[128,512]{1,0:T(8,128)(2,1)S(1)}, u32[]{:S(2)}, u32[]{:S(2)}) collective-permute-start(bf16[128,512]{1,0:T(8,128)(2,1)S(1)} %bitcast.41), channel_id=1, source_target_pairs={{0,3},{1,0},{2,1},{3,2},{4,7},{5,4},{6,5},{7,6},{8,11},{9,8},{10,9... | collective-permute-start | bytes 393224 | tf_op jit(solution)/shard_map/while/body/eval_jaxpr/cond/branch_1_fun/ppermute | solution.py:84
  567.1 5.1 collective-permute-start.6
  567.2 9.9 %collective-permute-start.7 = (bf16[128,512]{1,0:T(8,128)(2,1)S(1)}, bf16[128,512]{1,0:T(8,128)(2,1)S(1)}, u32[]{:S(2)}, u32[]{:S(2)}) collective-permute-start(bf16[128,512]{1,0:T(8,128)(2,1)S(1)} %slice.127), channel_id=1, source_target_pairs={{0,12},{1,13},{2,14},{3,15},{4,0},{5,1},{6,2},{7,3},{8,4},{9,5},{1... | collective-permute-start | bytes 393224 | tf_op jit(solution)/shard_map/while/body/eval_jaxpr/cond/branch_1_fun/ppermute | solution.py:84
  571.9 5.1 collective-permute-start.2
  572.2 5.0 collective-permute-start.8
  577.0 13.8 %copy-start.3 = (bf16[512,512]{1,0:T(8,128)(2,1)}, bf16[512,512]{1,0:T(8,128)(2,1)S(1)}, u32[]{:S(2)}) copy-start(bf16[512,512]{1,0:T(8,128)(2,1)S(1)} %constant_dynamic-update-slice_fusion.refs_0_) | copy-start | bytes 1572868 | tf_op jit(solution)/shard_map/while/body/eval_jaxpr/cond
  577.0 10.7 %collective-permute-start.3 = (bf16[512,512]{1,0:T(8,128)(2,1)S(1)}, bf16[512,512]{1,0:T(8,128)(2,1)S(1)}, u32[]{:S(2)}, u32[]{:S(2)}) collective-permute-start(bf16[512,512]{1,0:T(8,128)(2,1)S(1)} %constant_dynamic-update-slice_fusion.refs_0_), channel_id=1, source_target_pairs={{0,4},{1,5},{2,6},{3,7},{4,8},{5,9},{6,10},{7,11},{8,12},{9,13},{1... | collective-permute-start | bytes 1572872 | tf_op jit(solution)/shard_map/while/body/eval_jaxpr/cond/branch_1_fun/ppermute | solution.py:84
  577.2 25.8 %copy-start.1 = (bf16[512,512]{1,0:T(8,128)(2,1)}, bf16[512,512]{1,0:T(8,128)(2,1)S(1)}, u32[]{:S(2)}) copy-start(bf16[512,512]{1,0:T(8,128)(2,1)S(1)} %pad_maximum_fusion.1.refs_4_) | copy-start | bytes 1572868 | tf_op jit(solution)/shard_map/while/body/eval_jaxpr/cond
  577.3 10.5 %collective-permute-start.9 = (bf16[512,512]{1,0:T(8,128)(2,1)S(1)}, bf16[512,512]{1,0:T(8,128)(2,1)S(1)}, u32[]{:S(2)}, u32[]{:S(2)}) collective-permute-start(bf16[512,512]{1,0:T(8,128)(2,1)S(1)} %pad_maximum_fusion.1.refs_4_), channel_id=1, source_target_pairs={{0,1},{1,2},{2,3},{3,0},{4,5},{5,6},{6,7},{7,4},{8,9},{9,10},{10,1... | collective-permute-start | bytes 1572872 | tf_op jit(solution)/shard_map/while/body/eval_jaxpr/cond/branch_1_fun/ppermute | solution.py:84
  577.4 13.3 %collective-permute-start.4 = (bf16[512,512]{1,0:T(8,128)(2,1)S(1)}, bf16[512,512]{1,0:T(8,128)(2,1)S(1)}, u32[]{:S(2)}, u32[]{:S(2)}) collective-permute-start(bf16[512,512]{1,0:T(8,128)(2,1)S(1)} %constant_dynamic-update-slice_fusion.refs_0_), channel_id=1, source_target_pairs={{0,12},{1,13},{2,14},{3,15},{4,0},{5,1},{6,2},{7,3},{8,4},{9,5},{1... | collective-permute-start | bytes 1572872 | tf_op jit(solution)/shard_map/while/body/eval_jaxpr/cond/branch_1_fun/ppermute | solution.py:84
  580.0 10.7 %collective-permute-start.10 = (bf16[512,512]{1,0:T(8,128)(2,1)S(1)}, bf16[512,512]{1,0:T(8,128)(2,1)S(1)}, u32[]{:S(2)}, u32[]{:S(2)}) collective-permute-start(bf16[512,512]{1,0:T(8,128)(2,1)S(1)} %pad_maximum_fusion.1.refs_4_), channel_id=1, source_target_pairs={{0,3},{1,0},{2,1},{3,2},{4,7},{5,4},{6,5},{7,6},{8,11},{9,8},{10,9... | collective-permute-start | bytes 1572872 | tf_op jit(solution)/shard_map/while/body/eval_jaxpr/cond/branch_1_fun/ppermute | solution.py:84
  587.7 13.8 %collective-permute-start.5 = (bf16[512,512]{1,0:T(8,128)(2,1)S(1)}, bf16[512,512]{1,0:T(8,128)(2,1)S(1)}, u32[]{:S(2)}, u32[]{:S(2)}) collective-permute-start(bf16[512,512]{1,0:T(8,128)(2,1)S(1)} %collective-permute-done.3.refs_1_), channel_id=1, source_target_pairs={{0,4},{1,5},{2,6},{3,7},{4,8},{5,9},{6,10},{7,11},{8,12},{9,13},{1... | collective-permute-start | bytes 1572872 | tf_op jit(solution)/shard_map/while/body/eval_jaxpr/cond/branch_1_fun/ppermute | solution.py:84
  587.7 13.7 %copy-start.5 = (bf16[512,512]{1,0:T(8,128)(2,1)}, bf16[512,512]{1,0:T(8,128)(2,1)S(1)}, u32[]{:S(2)}) copy-start(bf16[512,512]{1,0:T(8,128)(2,1)S(1)} %collective-permute-done.9.refs_5_) | copy-start | bytes 1572868 | tf_op jit(solution)/shard_map/while/body/eval_jaxpr/cond
  587.7 13.7 %collective-permute-start.11 = (bf16[512,512]{1,0:T(8,128)(2,1)S(1)}, bf16[512,512]{1,0:T(8,128)(2,1)S(1)}, u32[]{:S(2)}, u32[]{:S(2)}) collective-permute-start(bf16[512,512]{1,0:T(8,128)(2,1)S(1)} %collective-permute-done.9.refs_5_), channel_id=1, source_target_pairs={{0,1},{1,2},{2,3},{3,0},{4,5},{5,6},{6,7},{7,4},{8,9},{9,10},{10,1... | collective-permute-start | bytes 1572872 | tf_op jit(solution)/shard_map/while/body/eval_jaxpr/cond/branch_1_fun/ppermute | solution.py:84
  590.8 10.7 %copy-start.6 = (bf16[512,512]{1,0:T(8,128)(2,1)}, bf16[512,512]{1,0:T(8,128)(2,1)S(1)}, u32[]{:S(2)}) copy-start(bf16[512,512]{1,0:T(8,128)(2,1)S(1)} %collective-permute-done.4.refs_2_) | copy-start | bytes 1572868 | tf_op jit(solution)/shard_map/while/body/eval_jaxpr/cond
  590.8 10.7 %copy-start.7 = (bf16[512,512]{1,0:T(8,128)(2,1)}, bf16[512,512]{1,0:T(8,128)(2,1)S(1)}, u32[]{:S(2)}) copy-start(bf16[512,512]{1,0:T(8,128)(2,1)S(1)} %collective-permute-done.10.refs_6_) | copy-start | bytes 1572868 | tf_op jit(solution)/shard_map/while/body/eval_jaxpr/cond
  624.4 17.9 %collective-permute-start.12 = (bf16[128,4096]{1,0:T(8,128)(2,1)}, bf16[128,4096]{1,0:T(8,128)(2,1)S(1)}, u32[]{:S(2)}, u32[]{:S(2)}) collective-permute-start(bf16[128,4096]{1,0:T(8,128)(2,1)} %get-tuple-element.627), channel_id=1, source_target_pairs={{0,16},{16,32},{32,48},{48,64},{64,80},{80,96},{96,112},{1,17},{17... | collective-permute-start | bytes 3145736 | tf_op jit(solution)/shard_map/while/body/eval_jaxpr/ppermute | solution.py:22
  643.9 5.1 copy-start
  649.2 6.5 copy-start.10
  650.2 7.6 %collective-permute-start = (bf16[128,512]{1,0:T(8,128)(2,1)S(1)}, bf16[128,512]{1,0:T(8,128)(2,1)S(1)}, u32[]{:S(2)}, u32[]{:S(2)}) collective-permute-start(bf16[128,512]{1,0:T(8,128)(2,1)S(1)} %bitcast.40), channel_id=1, source_target_pairs={{0,1},{1,2},{2,3},{3,0},{4,5},{5,6},{6,7},{7,4},{8,9},{9,10},{10,1... | collective-permute-start | bytes 393224 | tf_op jit(solution)/shard_map/while/body/eval_jaxpr/cond/branch_1_fun/ppermute | solution.py:84
  650.3 7.8 %collective-permute-start.1 = (bf16[128,512]{1,0:T(8,128)(2,1)S(1)}, bf16[128,512]{1,0:T(8,128)(2,1)S(1)}, u32[]{:S(2)}, u32[]{:S(2)}) collective-permute-start(bf16[128,512]{1,0:T(8,128)(2,1)S(1)} %bitcast.41), channel_id=1, source_target_pairs={{0,3},{1,0},{2,1},{3,2},{4,7},{5,4},{6,5},{7,6},{8,11},{9,8},{10,9... | collective-permute-start | bytes 393224 | tf_op jit(solution)/shard_map/while/body/eval_jaxpr/cond/branch_1_fun/ppermute | solution.py:84
  653.0 5.1 collective-permute-start.6
  653.0 9.9 %collective-permute-start.7 = (bf16[128,512]{1,0:T(8,128)(2,1)S(1)}, bf16[128,512]{1,0:T(8,128)(2,1)S(1)}, u32[]{:S(2)}, u32[]{:S(2)}) collective-permute-start(bf16[128,512]{1,0:T(8,128)(2,1)S(1)} %slice.127), channel_id=1, source_target_pairs={{0,12},{1,13},{2,14},{3,15},{4,0},{5,1},{6,2},{7,3},{8,4},{9,5},{1... | collective-permute-start | bytes 393224 | tf_op jit(solution)/shard_map/while/body/eval_jaxpr/cond/branch_1_fun/ppermute | solution.py:84
  657.7 5.1 collective-permute-start.2
  658.0 5.0 collective-permute-start.8
  662.9 12.5 %copy-start.3 = (bf16[512,512]{1,0:T(8,128)(2,1)}, bf16[512,512]{1,0:T(8,128)(2,1)S(1)}, u32[]{:S(2)}) copy-start(bf16[512,512]{1,0:T(8,128)(2,1)S(1)} %constant_dynamic-update-slice_fusion.refs_0_) | copy-start | bytes 1572868 | tf_op jit(solution)/shard_map/while/body/eval_jaxpr/cond
  662.9 9.3 %collective-permute-start.3 = (bf16[512,512]{1,0:T(8,128)(2,1)S(1)}, bf16[512,512]{1,0:T(8,128)(2,1)S(1)}, u32[]{:S(2)}, u32[]{:S(2)}) collective-permute-start(bf16[512,512]{1,0:T(8,128)(2,1)S(1)} %constant_dynamic-update-slice_fusion.refs_0_), channel_id=1, source_target_pairs={{0,4},{1,5},{2,6},{3,7},{4,8},{5,9},{6,10},{7,11},{8,12},{9,13},{1... | collective-permute-start | bytes 1572872 | tf_op jit(solution)/shard_map/while/body/eval_jaxpr/cond/branch_1_fun/ppermute | solution.py:84
  663.1 19.9 %copy-start.1 = (bf16[512,512]{1,0:T(8,128)(2,1)}, bf16[512,512]{1,0:T(8,128)(2,1)S(1)}, u32[]{:S(2)}) copy-start(bf16[512,512]{1,0:T(8,128)(2,1)S(1)} %pad_maximum_fusion.1.refs_4_) | copy-start | bytes 1572868 | tf_op jit(solution)/shard_map/while/body/eval_jaxpr/cond
  663.1 9.3 %collective-permute-start.9 = (bf16[512,512]{1,0:T(8,128)(2,1)S(1)}, bf16[512,512]{1,0:T(8,128)(2,1)S(1)}, u32[]{:S(2)}, u32[]{:S(2)}) collective-permute-start(bf16[512,512]{1,0:T(8,128)(2,1)S(1)} %pad_maximum_fusion.1.refs_4_), channel_id=1, source_target_pairs={{0,1},{1,2},{2,3},{3,0},{4,5},{5,6},{6,7},{7,4},{8,9},{9,10},{10,1... | collective-permute-start | bytes 1572872 | tf_op jit(solution)/shard_map/while/body/eval_jaxpr/cond/branch_1_fun/ppermute | solution.py:84
  663.3 12.1 %collective-permute-start.4 = (bf16[512,512]{1,0:T(8,128)(2,1)S(1)}, bf16[512,512]{1,0:T(8,128)(2,1)S(1)}, u32[]{:S(2)}, u32[]{:S(2)}) collective-permute-start(bf16[512,512]{1,0:T(8,128)(2,1)S(1)} %constant_dynamic-update-slice_fusion.refs_0_), channel_id=1, source_target_pairs={{0,12},{1,13},{2,14},{3,15},{4,0},{5,1},{6,2},{7,3},{8,4},{9,5},{1... | collective-permute-start | bytes 1572872 | tf_op jit(solution)/shard_map/while/body/eval_jaxpr/cond/branch_1_fun/ppermute | solution.py:84
  665.9 9.5 %collective-permute-start.10 = (bf16[512,512]{1,0:T(8,128)(2,1)S(1)}, bf16[512,512]{1,0:T(8,128)(2,1)S(1)}, u32[]{:S(2)}, u32[]{:S(2)}) collective-permute-start(bf16[512,512]{1,0:T(8,128)(2,1)S(1)} %pad_maximum_fusion.1.refs_4_), channel_id=1, source_target_pairs={{0,3},{1,0},{2,1},{3,2},{4,7},{5,4},{6,5},{7,6},{8,11},{9,8},{10,9... | collective-permute-start | bytes 1572872 | tf_op jit(solution)/shard_map/while/body/eval_jaxpr/cond/branch_1_fun/ppermute | solution.py:84
  672.2 3.2 copy-start.4
  672.2 9.2 %collective-permute-start.5 = (bf16[512,512]{1,0:T(8,128)(2,1)S(1)}, bf16[512,512]{1,0:T(8,128)(2,1)S(1)}, u32[]{:S(2)}, u32[]{:S(2)}) collective-permute-start(bf16[512,512]{1,0:T(8,128)(2,1)S(1)} %collective-permute-done.3.refs_1_), channel_id=1, source_target_pairs={{0,4},{1,5},{2,6},{3,7},{4,8},{5,9},{6,10},{7,11},{8,12},{9,13},{1... | collective-permute-start | bytes 1572872 | tf_op jit(solution)/shard_map/while/body/eval_jaxpr/cond/branch_1_fun/ppermute | solution.py:84
  672.4 9.0 %copy-start.5 = (bf16[512,512]{1,0:T(8,128)(2,1)}, bf16[512,512]{1,0:T(8,128)(2,1)S(1)}, u32[]{:S(2)}) copy-start(bf16[512,512]{1,0:T(8,128)(2,1)S(1)} %collective-permute-done.9.refs_5_) | copy-start | bytes 1572868 | tf_op jit(solution)/shard_map/while/body/eval_jaxpr/cond
  672.4 9.2 %collective-permute-start.11 = (bf16[512,512]{1,0:T(8,128)(2,1)S(1)}, bf16[512,512]{1,0:T(8,128)(2,1)S(1)}, u32[]{:S(2)}, u32[]{:S(2)}) collective-permute-start(bf16[512,512]{1,0:T(8,128)(2,1)S(1)} %collective-permute-done.9.refs_5_), channel_id=1, source_target_pairs={{0,1},{1,2},{2,3},{3,0},{4,5},{5,6},{6,7},{7,4},{8,9},{9,10},{10,1... | collective-permute-start | bytes 1572872 | tf_op jit(solution)/shard_map/while/body/eval_jaxpr/cond/branch_1_fun/ppermute | solution.py:84
  675.4 6.3 copy-start.6
  675.4 6.3 copy-start.7
  (7 other events, 9.0 us)

commit v10 on v9

--- a/solution.py
+++ b/solution.py
@@ -71,7 +71,7 @@
 RING_OFFSETS = (0, -1, 1, 2)
 
 
-def torus_gather(value, side):
+def torus_gather(key_rows, value_rows, side):
     def shifter(along_z):
         def shift(piece, by):
             pairs = []
@@ -87,11 +87,9 @@
 
     shift_z = shifter(True)
     shift_x = shifter(False)
-    rows = value.shape[0]
-    width = value.shape[1] // 2
-    row_a = jnp.concatenate(ring_gather(value[:, :width], shift_x), axis=0)
+    row_a = jnp.concatenate(ring_gather(key_rows, shift_x), axis=0)
     pieces_a = ring_gather(row_a, shift_z)
-    col_b = jnp.concatenate(ring_gather(value[:, width:], shift_z), axis=0)
+    col_b = jnp.concatenate(ring_gather(value_rows, shift_z), axis=0)
     pieces_b = ring_gather(col_b, shift_x)
     return pieces_a, pieces_b
 
@@ -109,7 +107,7 @@
     return blocks.reshape(micro_count, side * side * rows)
 
 
-def attention_kernel(q_ref, *refs):
+def attention_kernel(mb_ref, q_ref, *refs):
     side = len(RING_OFFSETS)
     key_refs = refs[:side]
     value_refs = refs[side : 2 * side]
@@ -151,24 +149,28 @@
         ).astype(o_ref.dtype)
 
 
-def attention(turned, pieces_a, pieces_b, bias, residual):
+def attention(mb, turned, pieces_a, pieces_b, bias_all, residual):
     rows, width = turned.shape
     piece = pieces_a[0].shape[0]
-    keys_len = bias.shape[1]
+    keys_len = bias_all.shape[2]
     group = width // HK
-    piece_spec = pl.BlockSpec((piece, HD), lambda k: (0, k))
+    piece_spec = pl.BlockSpec((piece, HD), lambda k, m: (0, k))
+    grid_spec = pltpu.PrefetchScalarGridSpec(
+        num_scalar_prefetch=1,
+        grid=(HK,),
+        in_specs=[pl.BlockSpec((rows, group), lambda k, m: (0, k))]
+        + [piece_spec] * (len(pieces_a) + len(pieces_b))
+        + [
+            pl.BlockSpec((None, rows, keys_len), lambda k, m: (m[0], 0, 0)),
+            pl.BlockSpec((rows, group), lambda k, m: (0, k)),
+        ],
+        out_specs=pl.BlockSpec((rows, group), lambda k, m: (0, k)),
+    )
     return pl.pallas_call(
         attention_kernel,
-        grid=(HK,),
-        in_specs=[pl.BlockSpec((rows, group), lambda k: (0, k))]
-        + [piece_spec] * (len(pieces_a) + len(pieces_b))
-        + [
-            pl.BlockSpec((rows, keys_len), lambda k: (0, 0)),
-            pl.BlockSpec((rows, group), lambda k: (0, k)),
-        ],
-        out_specs=pl.BlockSpec((rows, group), lambda k: (0, k)),
+        grid_spec=grid_spec,
         out_shape=jax.ShapeDtypeStruct((rows, width), jnp.bfloat16),
-    )(turned, *pieces_a, *pieces_b, bias, residual)
+    )(mb.reshape(1), turned, *pieces_a, *pieces_b, bias_all, residual)
 
 
 def local(hidden, queries, gain, key_weight, value_weight, tree_ids, branch_ids, span_order):
@@ -205,25 +207,25 @@
     gain_row = gain[0]
     key_mat = key_weight[0]
     value_mat = value_weight[0]
-    kv_mat = jnp.concatenate([key_mat, value_mat], axis=1)
 
     def run_layer(current, mb):
         cosine = lax.dynamic_index_in_dim(cos_all, mb, 0, keepdims=False)
         sine_part = lax.dynamic_index_in_dim(sin_all, mb, 0, keepdims=False)
-        bias = lax.dynamic_index_in_dim(bias_all, mb, 0, keepdims=False)
         widened = current.astype(jnp.float32)
         norm_scale = lax.rsqrt(jnp.mean(widened * widened, axis=-1, keepdims=True) + 1e-05)
         normed = (widened * norm_scale * gain_row).astype(jnp.bfloat16)
-        kv_proj = jnp.dot(normed, kv_mat, preferred_element_type=jnp.float32)
-        key_proj = kv_proj[:, : HK * HD].reshape(row_count, HK, HD)
+        key_proj = jnp.dot(normed, key_mat, preferred_element_type=jnp.float32).reshape(
+            row_count, HK, HD
+        )
         key_rows = (
             rotate(key_proj, cosine[:, None, :], sine_part[:, None, :])
             .astype(jnp.bfloat16)
             .reshape(row_count, HK * HD)
         )
-        value_rows = kv_proj[:, HK * HD :].astype(jnp.bfloat16)
-        kv_rows = jnp.concatenate([key_rows, value_rows], axis=1)
-        pieces_a, pieces_b = torus_gather(kv_rows, side)
+        value_rows = jnp.dot(normed, value_mat, preferred_element_type=jnp.float32).astype(
+            jnp.bfloat16
+        )
+        pieces_a, pieces_b = torus_gather(key_rows, value_rows, side)
         query_local = lax.dynamic_index_in_dim(queries[0], mb, 0, keepdims=False)
         turned = (
             rotate(
@@ -234,7 +236,7 @@
             .astype(jnp.bfloat16)
             .reshape(row_count, HQ * HD)
         )
-        return attention(turned, pieces_a, pieces_b, bias, current)
+        return attention(mb, turned, pieces_a, pieces_b, bias_all, current)
 
     tick_count = section_count + micro_count - 1
 

time: 707 us -> 719 us (1.017)
  other arithmetic: 27.7 us -> 41.2 us
    select_n x9, other arithmetic: 2.94 us -> 22 us  [advance(): outputs = jnp.where(active, stored, outputs)]
    concatenate x3 -> x2, other arithmetic: 7.97 us -> 0.07 us  [torus_gather(): col_b = jnp.concatenate(ring_gather(value_rows, shift_z), axis=0)]
  transfers between devices with their start and end apart: 33 -> 33, of which waited for: 21 -> 22; matrix products, arithmetic and copies ran while one was open for 2% -> 3% of each run, Pallas kernels for 0% -> 0%
where the time goes in v10:
time: 719 us; the launch traced here: 717 us
  waiting for transfers between devices  571 us (79%)
  other arithmetic  41.2 us (6%)
  Pallas kernels  39.3 us (5%)
  starting transfers between devices  29.4 us (4%)
  local copies, waits for them, and re-layouts  22.4 us (3%)
  matrix products  12.7 us (2%)
    ppermute x9, waiting for transfers between devices, from_behind(): return lax.ppermute(value, axis, pairs)  536 us
    pallas_call x2, Pallas kernels, attention(): pl.pallas_call(attention_kernel, grid_spec=grid_spec, out_shape=jax.Shape...  39.3 us
    ppermute x24, waiting for transfers between devices, shift(): return lax.ppermute(piece, 'seq', pairs)  35 us
    select_n x9, other arithmetic, advance(): outputs = jnp.where(active, stored, outputs)  22 us
    ppermute x24, starting transfers between devices, shift(): return lax.ppermute(piece, 'seq', pairs)  17.9 us
  transfers between devices with their start and end apart: 33, of which 22 were waited for; matrix products, arithmetic and copies ran while one was open for 3% of the time, Pallas kernels for 0%

profile of v10, /device:TPU:25, one launch (start us, length us, event | category | flops | bytes accessed | tf_op | source)
XLA Modules:
  0.0 717.4 jit_solution(12251947627638325325)
XLA Ops:
  11.1 706.3 %while.18 = (s32[]{:T(128)}, bf16[128,4096]{1,0:T(8,128)(2,1)}, bf16[2,128,4096]{2,1,0:T(8,128)(2,1)}, s32[]{:T(128)}, bf16[1,2,128,4096]{3,2,1,0:T(8,128)(2,1)}...) while((s32[]{:T(128)}, bf16[128,4096]{1,0:T(8,128)(2,1)}, ...), condition=%wide.region_11.14_spmd.clone.clone, body=%wide.region_7.13_spmd.clone.clone.sunk | while | flops 1091649664 | bytes 89289208 | solution.py:263
  12.5 3.5 collective-permute-done.12
  17.2 2.4 select_dynamic-update-slice_fusion.2
  21.1 14.9 %collective-permute-done.12 = bf16[128,4096]{1,0:T(8,128)(2,1)S(1)} collective-permute-done((bf16[128,4096]{1,0:T(8,128)(2,1)}, bf16[128,4096]{1,0:T(8,128)(2,1)S(1)}, u32[]{:S(2)}, u32[]{:S(2)}) %collective-permute-start.12) | collective-permute-done | bytes 1048608 | tf_op jit(solution)/shard_map/while/body/eval_jaxpr/ppermute | solution.py:22
  37.2 2.4 select_dynamic-update-slice_fusion.2
  41.0 14.9 %collective-permute-done.12 = bf16[128,4096]{1,0:T(8,128)(2,1)S(1)} collective-permute-done((bf16[128,4096]{1,0:T(8,128)(2,1)}, bf16[128,4096]{1,0:T(8,128)(2,1)S(1)}, u32[]{:S(2)}, u32[]{:S(2)}) %collective-permute-start.12) | collective-permute-done | bytes 1048608 | tf_op jit(solution)/shard_map/while/body/eval_jaxpr/ppermute | solution.py:22
  57.1 2.4 select_dynamic-update-slice_fusion.2
  61.0 14.9 %collective-permute-done.12 = bf16[128,4096]{1,0:T(8,128)(2,1)S(1)} collective-permute-done((bf16[128,4096]{1,0:T(8,128)(2,1)}, bf16[128,4096]{1,0:T(8,128)(2,1)S(1)}, u32[]{:S(2)}, u32[]{:S(2)}) %collective-permute-start.12) | collective-permute-done | bytes 1048608 | tf_op jit(solution)/shard_map/while/body/eval_jaxpr/ppermute | solution.py:22
  77.0 2.4 select_dynamic-update-slice_fusion.2
  80.9 14.9 %collective-permute-done.12 = bf16[128,4096]{1,0:T(8,128)(2,1)S(1)} collective-permute-done((bf16[128,4096]{1,0:T(8,128)(2,1)}, bf16[128,4096]{1,0:T(8,128)(2,1)S(1)}, u32[]{:S(2)}, u32[]{:S(2)}) %collective-permute-start.12) | collective-permute-done | bytes 1048608 | tf_op jit(solution)/shard_map/while/body/eval_jaxpr/ppermute | solution.py:22
  97.0 2.4 select_dynamic-update-slice_fusion.2
  100.8 14.9 %collective-permute-done.12 = bf16[128,4096]{1,0:T(8,128)(2,1)S(1)} collective-permute-done((bf16[128,4096]{1,0:T(8,128)(2,1)}, bf16[128,4096]{1,0:T(8,128)(2,1)S(1)}, u32[]{:S(2)}, u32[]{:S(2)}) %collective-permute-start.12) | collective-permute-done | bytes 1048608 | tf_op jit(solution)/shard_map/while/body/eval_jaxpr/ppermute | solution.py:22
  116.9 2.4 select_dynamic-update-slice_fusion.2
  120.8 14.9 %collective-permute-done.12 = bf16[128,4096]{1,0:T(8,128)(2,1)S(1)} collective-permute-done((bf16[128,4096]{1,0:T(8,128)(2,1)}, bf16[128,4096]{1,0:T(8,128)(2,1)S(1)}, u32[]{:S(2)}, u32[]{:S(2)}) %collective-permute-start.12) | collective-permute-done | bytes 1048608 | tf_op jit(solution)/shard_map/while/body/eval_jaxpr/ppermute | solution.py:22
  136.9 2.4 select_dynamic-update-slice_fusion.2
  140.7 423.6 %collective-permute-done.12 = bf16[128,4096]{1,0:T(8,128)(2,1)S(1)} collective-permute-done((bf16[128,4096]{1,0:T(8,128)(2,1)}, bf16[128,4096]{1,0:T(8,128)(2,1)S(1)}, u32[]{:S(2)}, u32[]{:S(2)}) %collective-permute-start.12) | collective-permute-done | bytes 1048608 | tf_op jit(solution)/shard_map/while/body/eval_jaxpr/ppermute | solution.py:22
  564.3 64.7 %conditional.4 = (bf16[128,4096]{1,0:T(8,128)(2,1)}, bf16[1,128,4096]{2,1,0:T(8,128)(2,1)S(1)}) conditional(s32[]{:T(128)} %convert_element_type.68, () %tuple.98, (s32[]{:T(128)}, bf16[1,2,128,4096]{3,2,1,0:T(8,128)(2,1)}, f32[2,128,64]{2,1,0:T(8,128)S(1)}, f32[2,128,64]{2,1,0:T(8,128)S(1)}, pred[]{:T(512)}, ...), branch_computations={%region_8.10_spmd, %region_9.12_spmd} | conditional | flops 1091108992 | bytes 81881400 | solution.py:251
  566.1 3.4 fusion.12
  570.7 2.7 collective-permute-start.1
  573.3 3.0 convolution_convert_fusion
  576.4 2.7 collective-permute-start.7
  579.2 2.2 collective-permute-done.6
  581.5 2.8 collective-permute-done.2
  584.3 2.1 collective-permute-done.8
  588.7 2.7 collective-permute-start.10
  591.4 2.8 collective-permute-done.3.refs_1_
  597.8 2.3 fusion.10.refs_8_
  600.2 7.0 collective-permute-done.5.refs_3_
  608.2 19.6 %branch_1_fun.1 = bf16[128,4096]{1,0:T(8,128)(2,1)} custom-call(s32[1]{0:T(128)} %bitcast.mb_ref, bf16[128,4096]{1,0:T(8,128)(2,1)} %bitcast.34, bf16[512,512]{1,0:T(8,128)(2,1)} %copy-done.2, bf16[512,512]{1,0:T(8,128)(2,1)} %copy-done.3, bf16[512,512]{1,0:T(8,128)(2,1)} %copy-done.5, bf16[512,512]{1,0:T(8,128)(2,1)} %copy-done.7, ...), custom_call_target="tpu_custom_call" | custom-call | tf_op jit(solution)/shard_map/while/body/eval_jaxpr/cond/branch_1_fun/pallas_call | solution.py:169
  629.1 2.4 select_dynamic-update-slice_fusion.2
  632.9 19.7 %collective-permute-done.12 = bf16[128,4096]{1,0:T(8,128)(2,1)S(1)} collective-permute-done((bf16[128,4096]{1,0:T(8,128)(2,1)}, bf16[128,4096]{1,0:T(8,128)(2,1)S(1)}, u32[]{:S(2)}, u32[]{:S(2)}) %collective-permute-start.12) | collective-permute-done | bytes 1048608 | tf_op jit(solution)/shard_map/while/body/eval_jaxpr/ppermute | solution.py:22
  652.6 62.4 %conditional.4 = (bf16[128,4096]{1,0:T(8,128)(2,1)}, bf16[1,128,4096]{2,1,0:T(8,128)(2,1)S(1)}) conditional(s32[]{:T(128)} %convert_element_type.68, () %tuple.98, (s32[]{:T(128)}, bf16[1,2,128,4096]{3,2,1,0:T(8,128)(2,1)}, f32[2,128,64]{2,1,0:T(8,128)S(1)}, f32[2,128,64]{2,1,0:T(8,128)S(1)}, pred[]{:T(512)}, ...), branch_computations={%region_8.10_spmd, %region_9.12_spmd} | conditional | flops 1091108992 | bytes 81881400 | solution.py:251
  652.6 1.8 fusion.6
  654.4 3.4 fusion.12
  658.9 2.7 collective-permute-start.1
  661.6 3.0 convolution_convert_fusion
  664.7 2.7 collective-permute-start.7
  667.4 2.2 collective-permute-done.6
  669.7 2.8 collective-permute-done.2
  672.6 2.1 collective-permute-done.8
  677.0 2.7 collective-permute-start.10
  679.6 2.2 collective-permute-done.3.refs_1_
  681.8 2.3 collective-permute-done.9.refs_5_
  686.1 2.3 fusion.10.refs_8_
  688.4 2.6 collective-permute-done.5.refs_3_
  691.0 2.3 collective-permute-done.11.refs_7_
  694.1 19.6 %branch_1_fun.1 = bf16[128,4096]{1,0:T(8,128)(2,1)} custom-call(s32[1]{0:T(128)} %bitcast.mb_ref, bf16[128,4096]{1,0:T(8,128)(2,1)} %bitcast.34, bf16[512,512]{1,0:T(8,128)(2,1)} %copy-done.2, bf16[512,512]{1,0:T(8,128)(2,1)} %copy-done.3, bf16[512,512]{1,0:T(8,128)(2,1)} %copy-done.5, bf16[512,512]{1,0:T(8,128)(2,1)} %copy-done.7, ...), custom_call_target="tpu_custom_call" | custom-call | tf_op jit(solution)/shard_map/while/body/eval_jaxpr/cond/branch_1_fun/pallas_call | solution.py:169
  715.0 2.4 select_dynamic-update-slice_fusion.2
  (197 shorter events, 58.5 us)
Async XLA Ops:
  7.4 3.7 copy-start.10
  11.1 4.9 collective-permute-start.12
  19.7 16.3 %collective-permute-start.12 = (bf16[128,4096]{1,0:T(8,128)(2,1)}, bf16[128,4096]{1,0:T(8,128)(2,1)S(1)}, u32[]{:S(2)}, u32[]{:S(2)}) collective-permute-start(bf16[128,4096]{1,0:T(8,128)(2,1)} %get-tuple-element.658), channel_id=1, source_target_pairs={{0,16},{16,32},{32,48},{48,64},{64,80},{80,96},{96,112},{1,17},{17... | collective-permute-start | bytes 3145736 | tf_op jit(solution)/shard_map/while/body/eval_jaxpr/ppermute | solution.py:22
  39.6 16.3 %collective-permute-start.12 = (bf16[128,4096]{1,0:T(8,128)(2,1)}, bf16[128,4096]{1,0:T(8,128)(2,1)S(1)}, u32[]{:S(2)}, u32[]{:S(2)}) collective-permute-start(bf16[128,4096]{1,0:T(8,128)(2,1)} %get-tuple-element.658), channel_id=1, source_target_pairs={{0,16},{16,32},{32,48},{48,64},{64,80},{80,96},{96,112},{1,17},{17... | collective-permute-start | bytes 3145736 | tf_op jit(solution)/shard_map/while/body/eval_jaxpr/ppermute | solution.py:22
  59.5 16.3 %collective-permute-start.12 = (bf16[128,4096]{1,0:T(8,128)(2,1)}, bf16[128,4096]{1,0:T(8,128)(2,1)S(1)}, u32[]{:S(2)}, u32[]{:S(2)}) collective-permute-start(bf16[128,4096]{1,0:T(8,128)(2,1)} %get-tuple-element.658), channel_id=1, source_target_pairs={{0,16},{16,32},{32,48},{48,64},{64,80},{80,96},{96,112},{1,17},{17... | collective-permute-start | bytes 3145736 | tf_op jit(solution)/shard_map/while/body/eval_jaxpr/ppermute | solution.py:22
  79.5 16.3 %collective-permute-start.12 = (bf16[128,4096]{1,0:T(8,128)(2,1)}, bf16[128,4096]{1,0:T(8,128)(2,1)S(1)}, u32[]{:S(2)}, u32[]{:S(2)}) collective-permute-start(bf16[128,4096]{1,0:T(8,128)(2,1)} %get-tuple-element.658), channel_id=1, source_target_pairs={{0,16},{16,32},{32,48},{48,64},{64,80},{80,96},{96,112},{1,17},{17... | collective-permute-start | bytes 3145736 | tf_op jit(solution)/shard_map/while/body/eval_jaxpr/ppermute | solution.py:22
  99.4 16.3 %collective-permute-start.12 = (bf16[128,4096]{1,0:T(8,128)(2,1)}, bf16[128,4096]{1,0:T(8,128)(2,1)S(1)}, u32[]{:S(2)}, u32[]{:S(2)}) collective-permute-start(bf16[128,4096]{1,0:T(8,128)(2,1)} %get-tuple-element.658), channel_id=1, source_target_pairs={{0,16},{16,32},{32,48},{48,64},{64,80},{80,96},{96,112},{1,17},{17... | collective-permute-start | bytes 3145736 | tf_op jit(solution)/shard_map/while/body/eval_jaxpr/ppermute | solution.py:22
  119.4 16.3 %collective-permute-start.12 = (bf16[128,4096]{1,0:T(8,128)(2,1)}, bf16[128,4096]{1,0:T(8,128)(2,1)S(1)}, u32[]{:S(2)}, u32[]{:S(2)}) collective-permute-start(bf16[128,4096]{1,0:T(8,128)(2,1)} %get-tuple-element.658), channel_id=1, source_target_pairs={{0,16},{16,32},{32,48},{48,64},{64,80},{80,96},{96,112},{1,17},{17... | collective-permute-start | bytes 3145736 | tf_op jit(solution)/shard_map/while/body/eval_jaxpr/ppermute | solution.py:22
  139.3 425.0 %collective-permute-start.12 = (bf16[128,4096]{1,0:T(8,128)(2,1)}, bf16[128,4096]{1,0:T(8,128)(2,1)S(1)}, u32[]{:S(2)}, u32[]{:S(2)}) collective-permute-start(bf16[128,4096]{1,0:T(8,128)(2,1)} %get-tuple-element.658), channel_id=1, source_target_pairs={{0,16},{16,32},{32,48},{48,64},{64,80},{80,96},{96,112},{1,17},{17... | collective-permute-start | bytes 3145736 | tf_op jit(solution)/shard_map/while/body/eval_jaxpr/ppermute | solution.py:22
  566.1 7.2 %copy-start = (bf16[128,4096]{1,0:T(8,128)(2,1)}, bf16[128,4096]{1,0:T(8,128)(2,1)S(1)}, u32[]{:S(2)}) copy-start(bf16[128,4096]{1,0:T(8,128)(2,1)S(1)} %get-tuple-element.487.refs_9_) | copy-start | bytes 3145732 | tf_op jit(solution)/shard_map/while/body/eval_jaxpr/cond
  570.6 8.5 %collective-permute-start = (bf16[128,512]{1,0:T(8,128)(2,1)S(1)}, bf16[128,512]{1,0:T(8,128)(2,1)S(1)}, u32[]{:S(2)}, u32[]{:S(2)}) collective-permute-start(bf16[128,512]{1,0:T(8,128)(2,1)S(1)} %bitcast.38), channel_id=1, source_target_pairs={{0,1},{1,2},{2,3},{3,0},{4,5},{5,6},{6,7},{7,4},{8,9},{9,10},{10,1... | collective-permute-start | bytes 393224 | tf_op jit(solution)/shard_map/while/body/eval_jaxpr/cond/branch_1_fun/ppermute | solution.py:84
  570.7 10.8 %collective-permute-start.1 = (bf16[128,512]{1,0:T(8,128)(2,1)S(1)}, bf16[128,512]{1,0:T(8,128)(2,1)S(1)}, u32[]{:S(2)}, u32[]{:S(2)}) collective-permute-start(bf16[128,512]{1,0:T(8,128)(2,1)S(1)} %bitcast.39), channel_id=1, source_target_pairs={{0,3},{1,0},{2,1},{3,2},{4,7},{5,4},{6,5},{7,6},{8,11},{9,8},{10,9... | collective-permute-start | bytes 393224 | tf_op jit(solution)/shard_map/while/body/eval_jaxpr/cond/branch_1_fun/ppermute | solution.py:84
  576.3 10.3 %copy-start.9 = (bf16[1,2,128,4096]{3,2,1,0:T(8,128)(2,1)S(1)}, bf16[1,2,128,4096]{3,2,1,0:T(8,128)(2,1)}, u32[]{:S(2)}) copy-start(bf16[1,2,128,4096]{3,2,1,0:T(8,128)(2,1)} %get-tuple-element.280) | copy-start | bytes 6291460 | tf_op jit(solution)/shard_map/while/body/eval_jaxpr/cond
  576.3 5.1 collective-permute-start.6
  576.4 7.9 %collective-permute-start.7 = (bf16[128,512]{1,0:T(8,128)(2,1)S(1)}, bf16[128,512]{1,0:T(8,128)(2,1)S(1)}, u32[]{:S(2)}, u32[]{:S(2)}) collective-permute-start(bf16[128,512]{1,0:T(8,128)(2,1)S(1)} %convolution_convert_fusion), channel_id=1, source_target_pairs={{0,12},{1,13},{2,14},{3,15},{4,0},{5,1},{6,2},{7,3},{8,4},{9,5},{1... | collective-permute-start | bytes 393224 | tf_op jit(solution)/shard_map/while/body/eval_jaxpr/cond/branch_1_fun/ppermute | solution.py:84
  579.1 5.1 collective-permute-start.2
  581.4 5.0 collective-permute-start.8
  584.2 3.9 copy-start.2
  584.2 10.0 %collective-permute-start.3 = (bf16[512,512]{1,0:T(8,128)(2,1)S(1)}, bf16[512,512]{1,0:T(8,128)(2,1)S(1)}, u32[]{:S(2)}, u32[]{:S(2)}) collective-permute-start(bf16[512,512]{1,0:T(8,128)(2,1)S(1)} %constant_dynamic-update-slice_fusion.refs_0_), channel_id=1, source_target_pairs={{0,4},{1,5},{2,6},{3,7},{4,8},{5,9},{6,10},{7,11},{8,12},{9,13},{1... | collective-permute-start | bytes 1572872 | tf_op jit(solution)/shard_map/while/body/eval_jaxpr/cond/branch_1_fun/ppermute | solution.py:84
  586.5 2.2 copy-start.1
  586.5 9.3 %collective-permute-start.9 = (bf16[512,512]{1,0:T(8,128)(2,1)S(1)}, bf16[512,512]{1,0:T(8,128)(2,1)S(1)}, u32[]{:S(2)}, u32[]{:S(2)}) collective-permute-start(bf16[512,512]{1,0:T(8,128)(2,1)S(1)} %pad_maximum_fusion.1.refs_4_), channel_id=1, source_target_pairs={{0,1},{1,2},{2,3},{3,0},{4,5},{5,6},{6,7},{7,4},{8,9},{9,10},{10,1... | collective-permute-start | bytes 1572872 | tf_op jit(solution)/shard_map/while/body/eval_jaxpr/cond/branch_1_fun/ppermute | solution.py:84
  588.1 12.0 %collective-permute-start.4 = (bf16[512,512]{1,0:T(8,128)(2,1)S(1)}, bf16[512,512]{1,0:T(8,128)(2,1)S(1)}, u32[]{:S(2)}, u32[]{:S(2)}) collective-permute-start(bf16[512,512]{1,0:T(8,128)(2,1)S(1)} %constant_dynamic-update-slice_fusion.refs_0_), channel_id=1, source_target_pairs={{0,12},{1,13},{2,14},{3,15},{4,0},{5,1},{6,2},{7,3},{8,4},{9,5},{1... | collective-permute-start | bytes 1572872 | tf_op jit(solution)/shard_map/while/body/eval_jaxpr/cond/branch_1_fun/ppermute | solution.py:84
  588.7 11.5 %collective-permute-start.10 = (bf16[512,512]{1,0:T(8,128)(2,1)S(1)}, bf16[512,512]{1,0:T(8,128)(2,1)S(1)}, u32[]{:S(2)}, u32[]{:S(2)}) collective-permute-start(bf16[512,512]{1,0:T(8,128)(2,1)S(1)} %pad_maximum_fusion.1.refs_4_), channel_id=1, source_target_pairs={{0,3},{1,0},{2,1},{3,2},{4,7},{5,4},{6,5},{7,6},{8,11},{9,8},{10,9... | collective-permute-start | bytes 1572872 | tf_op jit(solution)/shard_map/while/body/eval_jaxpr/cond/branch_1_fun/ppermute | solution.py:84
  594.2 3.6 copy-start.3
  594.2 13.0 %collective-permute-start.5 = (bf16[512,512]{1,0:T(8,128)(2,1)S(1)}, bf16[512,512]{1,0:T(8,128)(2,1)S(1)}, u32[]{:S(2)}, u32[]{:S(2)}) collective-permute-start(bf16[512,512]{1,0:T(8,128)(2,1)S(1)} %collective-permute-done.3.refs_1_), channel_id=1, source_target_pairs={{0,4},{1,5},{2,6},{3,7},{4,8},{5,9},{6,10},{7,11},{8,12},{9,13},{1... | collective-permute-start | bytes 1572872 | tf_op jit(solution)/shard_map/while/body/eval_jaxpr/cond/branch_1_fun/ppermute | solution.py:84
  595.8 11.4 %collective-permute-start.11 = (bf16[512,512]{1,0:T(8,128)(2,1)S(1)}, bf16[512,512]{1,0:T(8,128)(2,1)S(1)}, u32[]{:S(2)}, u32[]{:S(2)}) collective-permute-start(bf16[512,512]{1,0:T(8,128)(2,1)S(1)} %collective-permute-done.9.refs_5_), channel_id=1, source_target_pairs={{0,1},{1,2},{2,3},{3,0},{4,5},{5,6},{6,7},{7,4},{8,9},{9,10},{10,1... | collective-permute-start | bytes 1572872 | tf_op jit(solution)/shard_map/while/body/eval_jaxpr/cond/branch_1_fun/ppermute | solution.py:84
  600.2 7.9 %copy-start.5 = (bf16[512,512]{1,0:T(8,128)(2,1)}, bf16[512,512]{1,0:T(8,128)(2,1)S(1)}, u32[]{:S(2)}) copy-start(bf16[512,512]{1,0:T(8,128)(2,1)S(1)} %collective-permute-done.4.refs_2_) | copy-start | bytes 1572868 | tf_op jit(solution)/shard_map/while/body/eval_jaxpr/cond
  600.2 7.9 %copy-start.6 = (bf16[512,512]{1,0:T(8,128)(2,1)}, bf16[512,512]{1,0:T(8,128)(2,1)S(1)}, u32[]{:S(2)}) copy-start(bf16[512,512]{1,0:T(8,128)(2,1)S(1)} %collective-permute-done.10.refs_6_) | copy-start | bytes 1572868 | tf_op jit(solution)/shard_map/while/body/eval_jaxpr/cond
  631.5 21.1 %collective-permute-start.12 = (bf16[128,4096]{1,0:T(8,128)(2,1)}, bf16[128,4096]{1,0:T(8,128)(2,1)S(1)}, u32[]{:S(2)}, u32[]{:S(2)}) collective-permute-start(bf16[128,4096]{1,0:T(8,128)(2,1)} %get-tuple-element.658), channel_id=1, source_target_pairs={{0,16},{16,32},{32,48},{48,64},{64,80},{80,96},{96,112},{1,17},{17... | collective-permute-start | bytes 3145736 | tf_op jit(solution)/shard_map/while/body/eval_jaxpr/ppermute | solution.py:22
  654.3 7.2 %copy-start = (bf16[128,4096]{1,0:T(8,128)(2,1)}, bf16[128,4096]{1,0:T(8,128)(2,1)S(1)}, u32[]{:S(2)}) copy-start(bf16[128,4096]{1,0:T(8,128)(2,1)S(1)} %get-tuple-element.487.refs_9_) | copy-start | bytes 3145732 | tf_op jit(solution)/shard_map/while/body/eval_jaxpr/cond
  658.8 8.5 %collective-permute-start = (bf16[128,512]{1,0:T(8,128)(2,1)S(1)}, bf16[128,512]{1,0:T(8,128)(2,1)S(1)}, u32[]{:S(2)}, u32[]{:S(2)}) collective-permute-start(bf16[128,512]{1,0:T(8,128)(2,1)S(1)} %bitcast.38), channel_id=1, source_target_pairs={{0,1},{1,2},{2,3},{3,0},{4,5},{5,6},{6,7},{7,4},{8,9},{9,10},{10,1... | collective-permute-start | bytes 393224 | tf_op jit(solution)/shard_map/while/body/eval_jaxpr/cond/branch_1_fun/ppermute | solution.py:84
  658.9 10.8 %collective-permute-start.1 = (bf16[128,512]{1,0:T(8,128)(2,1)S(1)}, bf16[128,512]{1,0:T(8,128)(2,1)S(1)}, u32[]{:S(2)}, u32[]{:S(2)}) collective-permute-start(bf16[128,512]{1,0:T(8,128)(2,1)S(1)} %bitcast.39), channel_id=1, source_target_pairs={{0,3},{1,0},{2,1},{3,2},{4,7},{5,4},{6,5},{7,6},{8,11},{9,8},{10,9... | collective-permute-start | bytes 393224 | tf_op jit(solution)/shard_map/while/body/eval_jaxpr/cond/branch_1_fun/ppermute | solution.py:84
  664.6 10.3 %copy-start.9 = (bf16[1,2,128,4096]{3,2,1,0:T(8,128)(2,1)S(1)}, bf16[1,2,128,4096]{3,2,1,0:T(8,128)(2,1)}, u32[]{:S(2)}) copy-start(bf16[1,2,128,4096]{3,2,1,0:T(8,128)(2,1)} %get-tuple-element.280) | copy-start | bytes 6291460 | tf_op jit(solution)/shard_map/while/body/eval_jaxpr/cond
  664.6 5.1 collective-permute-start.6
  664.7 7.9 %collective-permute-start.7 = (bf16[128,512]{1,0:T(8,128)(2,1)S(1)}, bf16[128,512]{1,0:T(8,128)(2,1)S(1)}, u32[]{:S(2)}, u32[]{:S(2)}) collective-permute-start(bf16[128,512]{1,0:T(8,128)(2,1)S(1)} %convolution_convert_fusion), channel_id=1, source_target_pairs={{0,12},{1,13},{2,14},{3,15},{4,0},{5,1},{6,2},{7,3},{8,4},{9,5},{1... | collective-permute-start | bytes 393224 | tf_op jit(solution)/shard_map/while/body/eval_jaxpr/cond/branch_1_fun/ppermute | solution.py:84
  667.3 5.1 collective-permute-start.2
  669.7 5.0 collective-permute-start.8
  672.5 3.9 copy-start.2
  672.5 9.3 %collective-permute-start.3 = (bf16[512,512]{1,0:T(8,128)(2,1)S(1)}, bf16[512,512]{1,0:T(8,128)(2,1)S(1)}, u32[]{:S(2)}, u32[]{:S(2)}) collective-permute-start(bf16[512,512]{1,0:T(8,128)(2,1)S(1)} %constant_dynamic-update-slice_fusion.refs_0_), channel_id=1, source_target_pairs={{0,4},{1,5},{2,6},{3,7},{4,8},{5,9},{6,10},{7,11},{8,12},{9,13},{1... | collective-permute-start | bytes 1572872 | tf_op jit(solution)/shard_map/while/body/eval_jaxpr/cond/branch_1_fun/ppermute | solution.py:84
  674.7 9.3 %collective-permute-start.9 = (bf16[512,512]{1,0:T(8,128)(2,1)S(1)}, bf16[512,512]{1,0:T(8,128)(2,1)S(1)}, u32[]{:S(2)}, u32[]{:S(2)}) collective-permute-start(bf16[512,512]{1,0:T(8,128)(2,1)S(1)} %pad_maximum_fusion.1.refs_4_), channel_id=1, source_target_pairs={{0,1},{1,2},{2,3},{3,0},{4,5},{5,6},{6,7},{7,4},{8,9},{9,10},{10,1... | collective-permute-start | bytes 1572872 | tf_op jit(solution)/shard_map/while/body/eval_jaxpr/cond/branch_1_fun/ppermute | solution.py:84
  676.4 12.0 %collective-permute-start.4 = (bf16[512,512]{1,0:T(8,128)(2,1)S(1)}, bf16[512,512]{1,0:T(8,128)(2,1)S(1)}, u32[]{:S(2)}, u32[]{:S(2)}) collective-permute-start(bf16[512,512]{1,0:T(8,128)(2,1)S(1)} %constant_dynamic-update-slice_fusion.refs_0_), channel_id=1, source_target_pairs={{0,12},{1,13},{2,14},{3,15},{4,0},{5,1},{6,2},{7,3},{8,4},{9,5},{1... | collective-permute-start | bytes 1572872 | tf_op jit(solution)/shard_map/while/body/eval_jaxpr/cond/branch_1_fun/ppermute | solution.py:84
  677.0 11.4 %collective-permute-start.10 = (bf16[512,512]{1,0:T(8,128)(2,1)S(1)}, bf16[512,512]{1,0:T(8,128)(2,1)S(1)}, u32[]{:S(2)}, u32[]{:S(2)}) collective-permute-start(bf16[512,512]{1,0:T(8,128)(2,1)S(1)} %pad_maximum_fusion.1.refs_4_), channel_id=1, source_target_pairs={{0,3},{1,0},{2,1},{3,2},{4,7},{5,4},{6,5},{7,6},{8,11},{9,8},{10,9... | collective-permute-start | bytes 1572872 | tf_op jit(solution)/shard_map/while/body/eval_jaxpr/cond/branch_1_fun/ppermute | solution.py:84
  681.8 4.3 copy-start.3
  681.8 9.2 %collective-permute-start.5 = (bf16[512,512]{1,0:T(8,128)(2,1)S(1)}, bf16[512,512]{1,0:T(8,128)(2,1)S(1)}, u32[]{:S(2)}, u32[]{:S(2)}) collective-permute-start(bf16[512,512]{1,0:T(8,128)(2,1)S(1)} %collective-permute-done.3.refs_1_), channel_id=1, source_target_pairs={{0,4},{1,5},{2,6},{3,7},{4,8},{5,9},{6,10},{7,11},{8,12},{9,13},{1... | collective-permute-start | bytes 1572872 | tf_op jit(solution)/shard_map/while/body/eval_jaxpr/cond/branch_1_fun/ppermute | solution.py:84
  684.1 9.2 %collective-permute-start.11 = (bf16[512,512]{1,0:T(8,128)(2,1)S(1)}, bf16[512,512]{1,0:T(8,128)(2,1)S(1)}, u32[]{:S(2)}, u32[]{:S(2)}) collective-permute-start(bf16[512,512]{1,0:T(8,128)(2,1)S(1)} %collective-permute-done.9.refs_5_), channel_id=1, source_target_pairs={{0,1},{1,2},{2,3},{3,0},{4,5},{5,6},{6,7},{7,4},{8,9},{9,10},{10,1... | collective-permute-start | bytes 1572872 | tf_op jit(solution)/shard_map/while/body/eval_jaxpr/cond/branch_1_fun/ppermute | solution.py:84
  688.4 5.7 copy-start.5
  688.4 5.7 copy-start.6
  691.0 3.1 copy-start.7
  (6 other events, 8.9 us)

commit v11 on v10

--- a/solution.py
+++ b/solution.py
@@ -71,7 +71,7 @@
 RING_OFFSETS = (0, -1, 1, 2)
 
 
-def torus_gather(key_rows, value_rows, side):
+def torus_gather(value, side):
     def shifter(along_z):
         def shift(piece, by):
             pairs = []
@@ -87,9 +87,11 @@
 
     shift_z = shifter(True)
     shift_x = shifter(False)
-    row_a = jnp.concatenate(ring_gather(key_rows, shift_x), axis=0)
+    rows = value.shape[0]
+    width = value.shape[1] // 2
+    row_a = jnp.concatenate(ring_gather(value[:, :width], shift_x), axis=0)
     pieces_a = ring_gather(row_a, shift_z)
-    col_b = jnp.concatenate(ring_gather(value_rows, shift_z), axis=0)
+    col_b = jnp.concatenate(ring_gather(value[:, width:], shift_z), axis=0)
     pieces_b = ring_gather(col_b, shift_x)
     return pieces_a, pieces_b
 
@@ -207,6 +209,7 @@
     gain_row = gain[0]
     key_mat = key_weight[0]
     value_mat = value_weight[0]
+    kv_mat = jnp.concatenate([key_mat, value_mat], axis=1)
 
     def run_layer(current, mb):
         cosine = lax.dynamic_index_in_dim(cos_all, mb, 0, keepdims=False)
@@ -214,18 +217,16 @@
         widened = current.astype(jnp.float32)
         norm_scale = lax.rsqrt(jnp.mean(widened * widened, axis=-1, keepdims=True) + 1e-05)
         normed = (widened * norm_scale * gain_row).astype(jnp.bfloat16)
-        key_proj = jnp.dot(normed, key_mat, preferred_element_type=jnp.float32).reshape(
-            row_count, HK, HD
-        )
+        kv_proj = jnp.dot(normed, kv_mat, preferred_element_type=jnp.float32)
+        key_proj = kv_proj[:, : HK * HD].reshape(row_count, HK, HD)
         key_rows = (
             rotate(key_proj, cosine[:, None, :], sine_part[:, None, :])
             .astype(jnp.bfloat16)
             .reshape(row_count, HK * HD)
         )
-        value_rows = jnp.dot(normed, value_mat, preferred_element_type=jnp.float32).astype(
-            jnp.bfloat16
-        )
-        pieces_a, pieces_b = torus_gather(key_rows, value_rows, side)
+        value_rows = kv_proj[:, HK * HD :].astype(jnp.bfloat16)
+        kv_rows = jnp.concatenate([key_rows, value_rows], axis=1)
+        pieces_a, pieces_b = torus_gather(kv_rows, side)
         query_local = lax.dynamic_index_in_dim(queries[0], mb, 0, keepdims=False)
         turned = (
             rotate(

time: 719 us -> 694 us (0.965)
  other arithmetic: 41.2 us -> 29.5 us
  waiting for transfers between devices: 571 us -> 560 us
    select_n x9, other arithmetic: 22 us -> 2.94 us  [advance(): outputs = jnp.where(active, stored, outputs)]
    ppermute x9, waiting for transfers between devices: 536 us -> 526 us  [from_behind(): return lax.ppermute(value, axis, pairs)]
    concatenate x2 -> x3, other arithmetic: 0.07 us -> 7.94 us  [the longest x1 7.87 us: local(): kv_mat = jnp.concatenate([key_mat, value_mat], axis=1)]
  transfers between devices with their start and end apart: 33 -> 33, of which waited for: 22 -> 23; matrix products, arithmetic and copies ran while one was open for 3% -> 2% of each run, Pallas kernels for 0% -> 0%
where the time goes in v11:
time: 694 us; the launch traced here: 693 us
  waiting for transfers between devices  560 us (81%)
  Pallas kernels  39.3 us (6%)
  other arithmetic  29.5 us (4%)
  starting transfers between devices  29.5 us (4%)
  local copies, waits for them, and re-layouts  22.6 us (3%)
  matrix products  10.2 us (1%)
    ppermute x9, waiting for transfers between devices, from_behind(): return lax.ppermute(value, axis, pairs)  526 us
    pallas_call x2, Pallas kernels, attention(): pl.pallas_call(attention_kernel, grid_spec=grid_spec, out_shape=jax.Shape...  39.3 us
    ppermute x24, waiting for transfers between devices, shift(): return lax.ppermute(piece, 'seq', pairs)  34.7 us
    ppermute x24, starting transfers between devices, shift(): return lax.ppermute(piece, 'seq', pairs)  17.9 us
  transfers between devices with their start and end apart: 33, of which 23 were waited for; matrix products, arithmetic and copies ran while one was open for 2% of the time, Pallas kernels for 0%

profile of v11, /device:TPU:25, one launch (start us, length us, event | category | flops | bytes accessed | tf_op | source)
XLA Modules:
  0.0 692.8 jit_solution(17484786608163042720)
XLA Ops:
  8.4 7.9 %pad_maximum_fusion.3 = bf16[4096,1024]{1,0:T(8,128)(2,1)} fusion(bf16[4096,512]{1,0:T(8,128)(2,1)} %bitcast.37, bf16[4096,512]{1,0:T(8,128)(2,1)} %bitcast.38), kind=kLoop, calls=%fused_computation.38 | loop fusion | flops 16777216 | bytes 16777216 | tf_op jit(solution)/shard_map/concatenate | solution.py:212
  17.6 673.9 %while.18 = (s32[]{:T(128)}, bf16[128,4096]{1,0:T(8,128)(2,1)}, bf16[2,128,4096]{2,1,0:T(8,128)(2,1)S(1)}, s32[]{:T(128)}, bf16[1,2,128,4096]{3,2,1,0:T(8,128)(2...) while((s32[]{:T(128)}, bf16[128,4096]{1,0:T(8,128)(2,1)}, ...), condition=%wide.region_11.14_spmd.clone.clone, body=%wide.region_7.13_spmd.clone.clone.sunk | while | flops 1089486976 | bytes 89140720 | solution.py:264
  19.0 3.5 collective-permute-done.12
  24.1 1.3 collective-permute-start.12
  25.5 14.9 %collective-permute-done.12 = bf16[128,4096]{1,0:T(8,128)(2,1)S(1)} collective-permute-done((bf16[128,4096]{1,0:T(8,128)(2,1)}, bf16[128,4096]{1,0:T(8,128)(2,1)S(1)}, u32[]{:S(2)}, u32[]{:S(2)}) %collective-permute-start.12) | collective-permute-done | bytes 1048608 | tf_op jit(solution)/shard_map/while/body/eval_jaxpr/ppermute | solution.py:22
  42.0 1.3 collective-permute-start.12
  43.4 14.9 %collective-permute-done.12 = bf16[128,4096]{1,0:T(8,128)(2,1)S(1)} collective-permute-done((bf16[128,4096]{1,0:T(8,128)(2,1)}, bf16[128,4096]{1,0:T(8,128)(2,1)S(1)}, u32[]{:S(2)}, u32[]{:S(2)}) %collective-permute-start.12) | collective-permute-done | bytes 1048608 | tf_op jit(solution)/shard_map/while/body/eval_jaxpr/ppermute | solution.py:22
  61.3 14.9 %collective-permute-done.12 = bf16[128,4096]{1,0:T(8,128)(2,1)S(1)} collective-permute-done((bf16[128,4096]{1,0:T(8,128)(2,1)}, bf16[128,4096]{1,0:T(8,128)(2,1)S(1)}, u32[]{:S(2)}, u32[]{:S(2)}) %collective-permute-start.12) | collective-permute-done | bytes 1048608 | tf_op jit(solution)/shard_map/while/body/eval_jaxpr/ppermute | solution.py:22
  77.7 1.3 collective-permute-start.12
  79.2 14.9 %collective-permute-done.12 = bf16[128,4096]{1,0:T(8,128)(2,1)S(1)} collective-permute-done((bf16[128,4096]{1,0:T(8,128)(2,1)}, bf16[128,4096]{1,0:T(8,128)(2,1)S(1)}, u32[]{:S(2)}, u32[]{:S(2)}) %collective-permute-start.12) | collective-permute-done | bytes 1048608 | tf_op jit(solution)/shard_map/while/body/eval_jaxpr/ppermute | solution.py:22
  97.0 14.9 %collective-permute-done.12 = bf16[128,4096]{1,0:T(8,128)(2,1)S(1)} collective-permute-done((bf16[128,4096]{1,0:T(8,128)(2,1)}, bf16[128,4096]{1,0:T(8,128)(2,1)S(1)}, u32[]{:S(2)}, u32[]{:S(2)}) %collective-permute-start.12) | collective-permute-done | bytes 1048608 | tf_op jit(solution)/shard_map/while/body/eval_jaxpr/ppermute | solution.py:22
  114.9 14.9 %collective-permute-done.12 = bf16[128,4096]{1,0:T(8,128)(2,1)S(1)} collective-permute-done((bf16[128,4096]{1,0:T(8,128)(2,1)}, bf16[128,4096]{1,0:T(8,128)(2,1)S(1)}, u32[]{:S(2)}, u32[]{:S(2)}) %collective-permute-start.12) | collective-permute-done | bytes 1048608 | tf_op jit(solution)/shard_map/while/body/eval_jaxpr/ppermute | solution.py:22
  132.8 412.4 %collective-permute-done.12 = bf16[128,4096]{1,0:T(8,128)(2,1)S(1)} collective-permute-done((bf16[128,4096]{1,0:T(8,128)(2,1)}, bf16[128,4096]{1,0:T(8,128)(2,1)S(1)}, u32[]{:S(2)}, u32[]{:S(2)}) %collective-permute-start.12) | collective-permute-done | bytes 1048608 | tf_op jit(solution)/shard_map/while/body/eval_jaxpr/ppermute | solution.py:22
  545.1 62.8 %conditional.4 = (bf16[128,4096]{1,0:T(8,128)(2,1)}, bf16[1,128,4096]{2,1,0:T(8,128)(2,1)S(1)}) conditional(s32[]{:T(128)} %convert_element_type.63, () %tuple.98, (s32[]{:T(128)}, bf16[1,2,128,4096]{3,2,1,0:T(8,128)(2,1)}, f32[2,128,64]{2,1,0:T(8,128)S(1)}, f32[2,128,64]{2,1,0:T(8,128)S(1)}, pred[]{:T(512)}, ...), branch_computations={%region_8.10_spmd, %region_9.12_spmd} | conditional | flops 1088946304 | bytes 81733432 | solution.py:252
  545.1 1.7 fusion.6
  546.9 5.1 fusion.11
  553.1 2.7 collective-permute-start.1
  555.9 2.7 collective-permute-start.7
  558.7 2.2 collective-permute-done.6
  560.9 2.8 collective-permute-done.2
  563.8 2.1 collective-permute-done.8
  568.1 2.6 collective-permute-start.10
  570.7 2.3 collective-permute-done.3.refs_1_
  573.0 3.7 collective-permute-done.9.refs_5_
  577.3 1.5 copy.16
  578.8 2.3 fusion.10.refs_8_
  581.2 2.5 collective-permute-done.5.refs_3_
  583.7 2.6 collective-permute-done.11.refs_7_
  587.1 19.7 %branch_1_fun.1 = bf16[128,4096]{1,0:T(8,128)(2,1)} custom-call(s32[1]{0:T(128)} %bitcast.mb_ref, bf16[128,4096]{1,0:T(8,128)(2,1)} %bitcast.33, bf16[512,512]{1,0:T(8,128)(2,1)} %copy-done.3, bf16[512,512]{1,0:T(8,128)(2,1)} %copy-done.4, bf16[512,512]{1,0:T(8,128)(2,1)} %copy-done.6, bf16[512,512]{1,0:T(8,128)(2,1)} %copy-done.8, ...), custom_call_target="tpu_custom_call" | custom-call | tf_op jit(solution)/shard_map/while/body/eval_jaxpr/cond/branch_1_fun/pallas_call | solution.py:171
  608.3 1.3 collective-permute-start.12
  609.7 20.3 %collective-permute-done.12 = bf16[128,4096]{1,0:T(8,128)(2,1)S(1)} collective-permute-done((bf16[128,4096]{1,0:T(8,128)(2,1)}, bf16[128,4096]{1,0:T(8,128)(2,1)S(1)}, u32[]{:S(2)}, u32[]{:S(2)}) %collective-permute-start.12) | collective-permute-done | bytes 1048608 | tf_op jit(solution)/shard_map/while/body/eval_jaxpr/ppermute | solution.py:22
  630.1 61.1 %conditional.4 = (bf16[128,4096]{1,0:T(8,128)(2,1)}, bf16[1,128,4096]{2,1,0:T(8,128)(2,1)S(1)}) conditional(s32[]{:T(128)} %convert_element_type.63, () %tuple.98, (s32[]{:T(128)}, bf16[1,2,128,4096]{3,2,1,0:T(8,128)(2,1)}, f32[2,128,64]{2,1,0:T(8,128)S(1)}, f32[2,128,64]{2,1,0:T(8,128)S(1)}, pred[]{:T(512)}, ...), branch_computations={%region_8.10_spmd, %region_9.12_spmd} | conditional | flops 1088946304 | bytes 81733432 | solution.py:252
  630.1 1.7 fusion.6
  631.8 5.1 fusion.11
  638.1 2.7 collective-permute-start.1
  640.8 2.7 collective-permute-start.7
  643.6 2.2 collective-permute-done.6
  645.9 2.8 collective-permute-done.2
  648.7 2.1 collective-permute-done.8
  653.0 2.6 collective-permute-start.10
  655.7 2.3 collective-permute-done.3.refs_1_
  658.0 2.3 collective-permute-done.9.refs_5_
  660.8 1.5 copy.16
  662.3 2.3 fusion.10.refs_8_
  664.7 2.5 collective-permute-done.5.refs_3_
  667.2 2.3 collective-permute-done.11.refs_7_
  670.3 19.7 %branch_1_fun.1 = bf16[128,4096]{1,0:T(8,128)(2,1)} custom-call(s32[1]{0:T(128)} %bitcast.mb_ref, bf16[128,4096]{1,0:T(8,128)(2,1)} %bitcast.33, bf16[512,512]{1,0:T(8,128)(2,1)} %copy-done.3, bf16[512,512]{1,0:T(8,128)(2,1)} %copy-done.4, bf16[512,512]{1,0:T(8,128)(2,1)} %copy-done.6, bf16[512,512]{1,0:T(8,128)(2,1)} %copy-done.8, ...), custom_call_target="tpu_custom_call" | custom-call | tf_op jit(solution)/shard_map/while/body/eval_jaxpr/cond/branch_1_fun/pallas_call | solution.py:171
  691.5 1.3 copy-done.2
  (202 shorter events, 48.6 us)
Async XLA Ops:
  17.6 4.9 collective-permute-start.12
  24.1 16.3 %collective-permute-start.12 = (bf16[128,4096]{1,0:T(8,128)(2,1)}, bf16[128,4096]{1,0:T(8,128)(2,1)S(1)}, u32[]{:S(2)}, u32[]{:S(2)}) collective-permute-start(bf16[128,4096]{1,0:T(8,128)(2,1)} %get-tuple-element.623), channel_id=1, source_target_pairs={{0,16},{16,32},{32,48},{48,64},{64,80},{80,96},{96,112},{1,17},{17... | collective-permute-start | bytes 3145736 | tf_op jit(solution)/shard_map/while/body/eval_jaxpr/ppermute | solution.py:22
  42.0 16.3 %collective-permute-start.12 = (bf16[128,4096]{1,0:T(8,128)(2,1)}, bf16[128,4096]{1,0:T(8,128)(2,1)S(1)}, u32[]{:S(2)}, u32[]{:S(2)}) collective-permute-start(bf16[128,4096]{1,0:T(8,128)(2,1)} %get-tuple-element.623), channel_id=1, source_target_pairs={{0,16},{16,32},{32,48},{48,64},{64,80},{80,96},{96,112},{1,17},{17... | collective-permute-start | bytes 3145736 | tf_op jit(solution)/shard_map/while/body/eval_jaxpr/ppermute | solution.py:22
  59.9 16.3 %collective-permute-start.12 = (bf16[128,4096]{1,0:T(8,128)(2,1)}, bf16[128,4096]{1,0:T(8,128)(2,1)S(1)}, u32[]{:S(2)}, u32[]{:S(2)}) collective-permute-start(bf16[128,4096]{1,0:T(8,128)(2,1)} %get-tuple-element.623), channel_id=1, source_target_pairs={{0,16},{16,32},{32,48},{48,64},{64,80},{80,96},{96,112},{1,17},{17... | collective-permute-start | bytes 3145736 | tf_op jit(solution)/shard_map/while/body/eval_jaxpr/ppermute | solution.py:22
  77.7 16.3 %collective-permute-start.12 = (bf16[128,4096]{1,0:T(8,128)(2,1)}, bf16[128,4096]{1,0:T(8,128)(2,1)S(1)}, u32[]{:S(2)}, u32[]{:S(2)}) collective-permute-start(bf16[128,4096]{1,0:T(8,128)(2,1)} %get-tuple-element.623), channel_id=1, source_target_pairs={{0,16},{16,32},{32,48},{48,64},{64,80},{80,96},{96,112},{1,17},{17... | collective-permute-start | bytes 3145736 | tf_op jit(solution)/shard_map/while/body/eval_jaxpr/ppermute | solution.py:22
  95.6 16.3 %collective-permute-start.12 = (bf16[128,4096]{1,0:T(8,128)(2,1)}, bf16[128,4096]{1,0:T(8,128)(2,1)S(1)}, u32[]{:S(2)}, u32[]{:S(2)}) collective-permute-start(bf16[128,4096]{1,0:T(8,128)(2,1)} %get-tuple-element.623), channel_id=1, source_target_pairs={{0,16},{16,32},{32,48},{48,64},{64,80},{80,96},{96,112},{1,17},{17... | collective-permute-start | bytes 3145736 | tf_op jit(solution)/shard_map/while/body/eval_jaxpr/ppermute | solution.py:22
  113.5 16.3 %collective-permute-start.12 = (bf16[128,4096]{1,0:T(8,128)(2,1)}, bf16[128,4096]{1,0:T(8,128)(2,1)S(1)}, u32[]{:S(2)}, u32[]{:S(2)}) collective-permute-start(bf16[128,4096]{1,0:T(8,128)(2,1)} %get-tuple-element.623), channel_id=1, source_target_pairs={{0,16},{16,32},{32,48},{48,64},{64,80},{80,96},{96,112},{1,17},{17... | collective-permute-start | bytes 3145736 | tf_op jit(solution)/shard_map/while/body/eval_jaxpr/ppermute | solution.py:22
  131.4 413.8 %collective-permute-start.12 = (bf16[128,4096]{1,0:T(8,128)(2,1)}, bf16[128,4096]{1,0:T(8,128)(2,1)S(1)}, u32[]{:S(2)}, u32[]{:S(2)}) collective-permute-start(bf16[128,4096]{1,0:T(8,128)(2,1)} %get-tuple-element.623), channel_id=1, source_target_pairs={{0,16},{16,32},{32,48},{48,64},{64,80},{80,96},{96,112},{1,17},{17... | collective-permute-start | bytes 3145736 | tf_op jit(solution)/shard_map/while/body/eval_jaxpr/ppermute | solution.py:22
  546.8 5.1 copy-start
  552.1 14.0 %copy-start.10 = (bf16[1,2,128,4096]{3,2,1,0:T(8,128)(2,1)S(1)}, bf16[1,2,128,4096]{3,2,1,0:T(8,128)(2,1)}, u32[]{:S(2)}) copy-start(bf16[1,2,128,4096]{3,2,1,0:T(8,128)(2,1)} %get-tuple-element.260) | copy-start | bytes 6291460 | tf_op jit(solution)/shard_map/while/body/eval_jaxpr/cond
  553.1 5.5 collective-permute-start
  553.1 7.8 %collective-permute-start.1 = (bf16[128,512]{1,0:T(8,128)(2,1)S(1)}, bf16[128,512]{1,0:T(8,128)(2,1)S(1)}, u32[]{:S(2)}, u32[]{:S(2)}) collective-permute-start(bf16[128,512]{1,0:T(8,128)(2,1)S(1)} %bitcast.40), channel_id=1, source_target_pairs={{0,3},{1,0},{2,1},{3,2},{4,7},{5,4},{6,5},{7,6},{8,11},{9,8},{10,9... | collective-permute-start | bytes 393224 | tf_op jit(solution)/shard_map/while/body/eval_jaxpr/cond/branch_1_fun/ppermute | solution.py:84
  555.8 5.1 collective-permute-start.6
  555.9 7.9 %collective-permute-start.7 = (bf16[128,512]{1,0:T(8,128)(2,1)S(1)}, bf16[128,512]{1,0:T(8,128)(2,1)S(1)}, u32[]{:S(2)}, u32[]{:S(2)}) collective-permute-start(bf16[128,512]{1,0:T(8,128)(2,1)S(1)} %slice.127), channel_id=1, source_target_pairs={{0,12},{1,13},{2,14},{3,15},{4,0},{5,1},{6,2},{7,3},{8,4},{9,5},{1... | collective-permute-start | bytes 393224 | tf_op jit(solution)/shard_map/while/body/eval_jaxpr/cond/branch_1_fun/ppermute | solution.py:84
  558.6 5.1 collective-permute-start.2
  560.9 5.0 collective-permute-start.8
  563.7 3.8 copy-start.3
  563.7 9.3 %collective-permute-start.3 = (bf16[512,512]{1,0:T(8,128)(2,1)S(1)}, bf16[512,512]{1,0:T(8,128)(2,1)S(1)}, u32[]{:S(2)}, u32[]{:S(2)}) collective-permute-start(bf16[512,512]{1,0:T(8,128)(2,1)S(1)} %constant_dynamic-update-slice_fusion.refs_0_), channel_id=1, source_target_pairs={{0,4},{1,5},{2,6},{3,7},{4,8},{5,9},{6,10},{7,11},{8,12},{9,13},{1... | collective-permute-start | bytes 1572872 | tf_op jit(solution)/shard_map/while/body/eval_jaxpr/cond/branch_1_fun/ppermute | solution.py:84
  566.0 10.7 %collective-permute-start.9 = (bf16[512,512]{1,0:T(8,128)(2,1)S(1)}, bf16[512,512]{1,0:T(8,128)(2,1)S(1)}, u32[]{:S(2)}, u32[]{:S(2)}) collective-permute-start(bf16[512,512]{1,0:T(8,128)(2,1)S(1)} %pad_maximum_fusion.1.refs_4_), channel_id=1, source_target_pairs={{0,1},{1,2},{2,3},{3,0},{4,5},{5,6},{6,7},{7,4},{8,9},{9,10},{10,1... | collective-permute-start | bytes 1572872 | tf_op jit(solution)/shard_map/while/body/eval_jaxpr/cond/branch_1_fun/ppermute | solution.py:84
  567.5 13.6 %collective-permute-start.4 = (bf16[512,512]{1,0:T(8,128)(2,1)S(1)}, bf16[512,512]{1,0:T(8,128)(2,1)S(1)}, u32[]{:S(2)}, u32[]{:S(2)}) collective-permute-start(bf16[512,512]{1,0:T(8,128)(2,1)S(1)} %constant_dynamic-update-slice_fusion.refs_0_), channel_id=1, source_target_pairs={{0,12},{1,13},{2,14},{3,15},{4,0},{5,1},{6,2},{7,3},{8,4},{9,5},{1... | collective-permute-start | bytes 1572872 | tf_op jit(solution)/shard_map/while/body/eval_jaxpr/cond/branch_1_fun/ppermute | solution.py:84
  568.1 13.0 %collective-permute-start.10 = (bf16[512,512]{1,0:T(8,128)(2,1)S(1)}, bf16[512,512]{1,0:T(8,128)(2,1)S(1)}, u32[]{:S(2)}, u32[]{:S(2)}) collective-permute-start(bf16[512,512]{1,0:T(8,128)(2,1)S(1)} %pad_maximum_fusion.1.refs_4_), channel_id=1, source_target_pairs={{0,3},{1,0},{2,1},{3,2},{4,7},{5,4},{6,5},{7,6},{8,11},{9,8},{10,9... | collective-permute-start | bytes 1572872 | tf_op jit(solution)/shard_map/while/body/eval_jaxpr/cond/branch_1_fun/ppermute | solution.py:84
  573.0 5.8 copy-start.4
  573.0 10.6 %collective-permute-start.5 = (bf16[512,512]{1,0:T(8,128)(2,1)S(1)}, bf16[512,512]{1,0:T(8,128)(2,1)S(1)}, u32[]{:S(2)}, u32[]{:S(2)}) collective-permute-start(bf16[512,512]{1,0:T(8,128)(2,1)S(1)} %collective-permute-done.3.refs_1_), channel_id=1, source_target_pairs={{0,4},{1,5},{2,6},{3,7},{4,8},{5,9},{6,10},{7,11},{8,12},{9,13},{1... | collective-permute-start | bytes 1572872 | tf_op jit(solution)/shard_map/while/body/eval_jaxpr/cond/branch_1_fun/ppermute | solution.py:84
  576.7 2.1 copy-start.5
  576.7 9.5 %collective-permute-start.11 = (bf16[512,512]{1,0:T(8,128)(2,1)S(1)}, bf16[512,512]{1,0:T(8,128)(2,1)S(1)}, u32[]{:S(2)}, u32[]{:S(2)}) collective-permute-start(bf16[512,512]{1,0:T(8,128)(2,1)S(1)} %collective-permute-done.9.refs_5_), channel_id=1, source_target_pairs={{0,1},{1,2},{2,3},{3,0},{4,5},{5,6},{6,7},{7,4},{8,9},{9,10},{10,1... | collective-permute-start | bytes 1572872 | tf_op jit(solution)/shard_map/while/body/eval_jaxpr/cond/branch_1_fun/ppermute | solution.py:84
  581.1 5.9 copy-start.6
  581.1 5.1 copy-start.7
  583.7 2.6 copy-start.8
  608.3 21.8 %collective-permute-start.12 = (bf16[128,4096]{1,0:T(8,128)(2,1)}, bf16[128,4096]{1,0:T(8,128)(2,1)S(1)}, u32[]{:S(2)}, u32[]{:S(2)}) collective-permute-start(bf16[128,4096]{1,0:T(8,128)(2,1)} %get-tuple-element.623), channel_id=1, source_target_pairs={{0,16},{16,32},{32,48},{48,64},{64,80},{80,96},{96,112},{1,17},{17... | collective-permute-start | bytes 3145736 | tf_op jit(solution)/shard_map/while/body/eval_jaxpr/ppermute | solution.py:22
  631.7 5.1 copy-start
  637.0 14.0 %copy-start.10 = (bf16[1,2,128,4096]{3,2,1,0:T(8,128)(2,1)S(1)}, bf16[1,2,128,4096]{3,2,1,0:T(8,128)(2,1)}, u32[]{:S(2)}) copy-start(bf16[1,2,128,4096]{3,2,1,0:T(8,128)(2,1)} %get-tuple-element.260) | copy-start | bytes 6291460 | tf_op jit(solution)/shard_map/while/body/eval_jaxpr/cond
  638.0 5.5 collective-permute-start
  638.1 7.8 %collective-permute-start.1 = (bf16[128,512]{1,0:T(8,128)(2,1)S(1)}, bf16[128,512]{1,0:T(8,128)(2,1)S(1)}, u32[]{:S(2)}, u32[]{:S(2)}) collective-permute-start(bf16[128,512]{1,0:T(8,128)(2,1)S(1)} %bitcast.40), channel_id=1, source_target_pairs={{0,3},{1,0},{2,1},{3,2},{4,7},{5,4},{6,5},{7,6},{8,11},{9,8},{10,9... | collective-permute-start | bytes 393224 | tf_op jit(solution)/shard_map/while/body/eval_jaxpr/cond/branch_1_fun/ppermute | solution.py:84
  640.7 5.1 collective-permute-start.6
  640.8 7.9 %collective-permute-start.7 = (bf16[128,512]{1,0:T(8,128)(2,1)S(1)}, bf16[128,512]{1,0:T(8,128)(2,1)S(1)}, u32[]{:S(2)}, u32[]{:S(2)}) collective-permute-start(bf16[128,512]{1,0:T(8,128)(2,1)S(1)} %slice.127), channel_id=1, source_target_pairs={{0,12},{1,13},{2,14},{3,15},{4,0},{5,1},{6,2},{7,3},{8,4},{9,5},{1... | collective-permute-start | bytes 393224 | tf_op jit(solution)/shard_map/while/body/eval_jaxpr/cond/branch_1_fun/ppermute | solution.py:84
  643.5 5.1 collective-permute-start.2
  645.8 5.0 collective-permute-start.8
  648.6 3.8 copy-start.3
  648.6 9.3 %collective-permute-start.3 = (bf16[512,512]{1,0:T(8,128)(2,1)S(1)}, bf16[512,512]{1,0:T(8,128)(2,1)S(1)}, u32[]{:S(2)}, u32[]{:S(2)}) collective-permute-start(bf16[512,512]{1,0:T(8,128)(2,1)S(1)} %constant_dynamic-update-slice_fusion.refs_0_), channel_id=1, source_target_pairs={{0,4},{1,5},{2,6},{3,7},{4,8},{5,9},{6,10},{7,11},{8,12},{9,13},{1... | collective-permute-start | bytes 1572872 | tf_op jit(solution)/shard_map/while/body/eval_jaxpr/cond/branch_1_fun/ppermute | solution.py:84
  650.9 9.3 %collective-permute-start.9 = (bf16[512,512]{1,0:T(8,128)(2,1)S(1)}, bf16[512,512]{1,0:T(8,128)(2,1)S(1)}, u32[]{:S(2)}, u32[]{:S(2)}) collective-permute-start(bf16[512,512]{1,0:T(8,128)(2,1)S(1)} %pad_maximum_fusion.1.refs_4_), channel_id=1, source_target_pairs={{0,1},{1,2},{2,3},{3,0},{4,5},{5,6},{6,7},{7,4},{8,9},{9,10},{10,1... | collective-permute-start | bytes 1572872 | tf_op jit(solution)/shard_map/while/body/eval_jaxpr/cond/branch_1_fun/ppermute | solution.py:84
  652.4 12.2 %collective-permute-start.4 = (bf16[512,512]{1,0:T(8,128)(2,1)S(1)}, bf16[512,512]{1,0:T(8,128)(2,1)S(1)}, u32[]{:S(2)}, u32[]{:S(2)}) collective-permute-start(bf16[512,512]{1,0:T(8,128)(2,1)S(1)} %constant_dynamic-update-slice_fusion.refs_0_), channel_id=1, source_target_pairs={{0,12},{1,13},{2,14},{3,15},{4,0},{5,1},{6,2},{7,3},{8,4},{9,5},{1... | collective-permute-start | bytes 1572872 | tf_op jit(solution)/shard_map/while/body/eval_jaxpr/cond/branch_1_fun/ppermute | solution.py:84
  653.0 11.6 %collective-permute-start.10 = (bf16[512,512]{1,0:T(8,128)(2,1)S(1)}, bf16[512,512]{1,0:T(8,128)(2,1)S(1)}, u32[]{:S(2)}, u32[]{:S(2)}) collective-permute-start(bf16[512,512]{1,0:T(8,128)(2,1)S(1)} %pad_maximum_fusion.1.refs_4_), channel_id=1, source_target_pairs={{0,3},{1,0},{2,1},{3,2},{4,7},{5,4},{6,5},{7,6},{8,11},{9,8},{10,9... | collective-permute-start | bytes 1572872 | tf_op jit(solution)/shard_map/while/body/eval_jaxpr/cond/branch_1_fun/ppermute | solution.py:84
  658.0 4.4 copy-start.4
  658.0 9.2 %collective-permute-start.5 = (bf16[512,512]{1,0:T(8,128)(2,1)S(1)}, bf16[512,512]{1,0:T(8,128)(2,1)S(1)}, u32[]{:S(2)}, u32[]{:S(2)}) collective-permute-start(bf16[512,512]{1,0:T(8,128)(2,1)S(1)} %collective-permute-done.3.refs_1_), channel_id=1, source_target_pairs={{0,4},{1,5},{2,6},{3,7},{4,8},{5,9},{6,10},{7,11},{8,12},{9,13},{1... | collective-permute-start | bytes 1572872 | tf_op jit(solution)/shard_map/while/body/eval_jaxpr/cond/branch_1_fun/ppermute | solution.py:84
  660.2 9.2 %collective-permute-start.11 = (bf16[512,512]{1,0:T(8,128)(2,1)S(1)}, bf16[512,512]{1,0:T(8,128)(2,1)S(1)}, u32[]{:S(2)}, u32[]{:S(2)}) collective-permute-start(bf16[512,512]{1,0:T(8,128)(2,1)S(1)} %collective-permute-done.9.refs_5_), channel_id=1, source_target_pairs={{0,1},{1,2},{2,3},{3,0},{4,5},{5,6},{6,7},{7,4},{8,9},{9,10},{10,1... | collective-permute-start | bytes 1572872 | tf_op jit(solution)/shard_map/while/body/eval_jaxpr/cond/branch_1_fun/ppermute | solution.py:84
  664.7 5.6 copy-start.6
  664.7 4.8 copy-start.7
  667.2 2.3 copy-start.8
  (7 other events, 10.6 us)

commit v12 on v11

--- a/solution.py
+++ b/solution.py
@@ -249,15 +249,16 @@
         start_at = jnp.clip(first_mb, 0, micro_count - 1)
         entering = lax.dynamic_index_in_dim(hidden, start_at, 0, keepdims=False)
         current = jnp.where(section_id == 0, entering, incoming)
-        result = lax.cond(
-            active,
-            lambda rows: run_layer(rows, start_at),
-            jnp.zeros_like,
-            current,
-        )
-        stored = lax.dynamic_update_index_in_dim(outputs, result, start_at, 0)
-        outputs = jnp.where(active, stored, outputs)
-        return (result, outputs)
+        def busy(operands):
+            rows, kept = operands
+            computed = run_layer(rows, start_at)
+            return computed, lax.dynamic_update_index_in_dim(kept, computed, start_at, 0)
+
+        def idle(operands):
+            rows, kept = operands
+            return jnp.zeros_like(rows), kept
+
+        return lax.cond(active, busy, idle, (current, outputs))
 
     empty_pass = jnp.zeros((row_count, model_width), jnp.bfloat16)
     empty_out = jnp.zeros((micro_count, row_count, model_width), jnp.bfloat16)

time: 694 us -> 696 us (level)
  waiting for transfers between devices: 560 us -> 569 us
  other arithmetic: 29.5 us -> 22.5 us
    ppermute x9, waiting for transfers between devices: 526 us -> 535 us  [from_behind(): return lax.ppermute(value, axis, pairs)]
  transfers between devices with their start and end apart: 33 -> 33, of which waited for: 23 -> 22; matrix products, arithmetic and copies ran while one was open for 2% -> 2% of each run, Pallas kernels for 0% -> 0%
where the time goes in v12:
time: 696 us
  waiting for transfers between devices  569 us (82%)
  Pallas kernels  39.3 us (6%)
  starting transfers between devices  29.4 us (4%)
  local copies, waits for them, and re-layouts  23.7 us (3%)
  other arithmetic  22.5 us (3%)
  matrix products  10.2 us (1%)
    ppermute x9, waiting for transfers between devices, from_behind(): return lax.ppermute(value, axis, pairs)  535 us
    pallas_call x2, Pallas kernels, attention(): pl.pallas_call(attention_kernel, grid_spec=grid_spec, out_shape=jax.Shape...  39.3 us
    ppermute x24, waiting for transfers between devices, shift(): return lax.ppermute(piece, 'seq', pairs)  34.6 us
    ppermute x24, starting transfers between devices, shift(): return lax.ppermute(piece, 'seq', pairs)  17.9 us
  transfers between devices with their start and end apart: 33, of which 22 were waited for; matrix products, arithmetic and copies ran while one was open for 2% of the time, Pallas kernels for 0%

profile of v12, /device:TPU:25, one launch (start us, length us, event | category | flops | bytes accessed | tf_op | source)
XLA Modules:
  0.0 695.5 jit_solution(7774559362857644126)
XLA Ops:
  0.0 7.9 %pad_maximum_fusion.3 = bf16[4096,1024]{1,0:T(8,128)(2,1)} fusion(bf16[4096,512]{1,0:T(8,128)(2,1)} %bitcast.38, bf16[4096,512]{1,0:T(8,128)(2,1)} %bitcast.39), kind=kLoop, calls=%fused_computation.38 | loop fusion | flops 16777216 | bytes 16777216 | tf_op jit(solution)/shard_map/concatenate | solution.py:212
  11.9 1.6 broadcast_in_dim.114
  13.5 682.0 %while.21 = (s32[]{:T(128)}, bf16[128,4096]{1,0:T(8,128)(2,1)}, bf16[2,128,4096]{2,1,0:T(8,128)(2,1)}, s32[]{:T(128)}, bf16[1,2,128,4096]{3,2,1,0:T(8,128)(2,1)S...) while((s32[]{:T(128)}, bf16[128,4096]{1,0:T(8,128)(2,1)}, ...), condition=%wide.region_11.14_spmd.clone.clone, body=%wide.region_7.13_spmd.clone.clone.sunk | while | flops 1088962688 | bytes 77606840 | solution.py:265
  13.5 1.3 collective-permute-start.12
  14.9 3.5 collective-permute-done.12
  19.6 1.3 collective-permute-start.12
  21.0 14.9 %collective-permute-done.12 = bf16[128,4096]{1,0:T(8,128)(2,1)S(1)} collective-permute-done((bf16[128,4096]{1,0:T(8,128)(2,1)}, bf16[128,4096]{1,0:T(8,128)(2,1)S(1)}, u32[]{:S(2)}, u32[]{:S(2)}) %collective-permute-start.12) | collective-permute-done | bytes 1048608 | tf_op jit(solution)/shard_map/while/body/eval_jaxpr/ppermute | solution.py:22
  37.0 1.3 collective-permute-start.12
  38.4 14.9 %collective-permute-done.12 = bf16[128,4096]{1,0:T(8,128)(2,1)S(1)} collective-permute-done((bf16[128,4096]{1,0:T(8,128)(2,1)}, bf16[128,4096]{1,0:T(8,128)(2,1)S(1)}, u32[]{:S(2)}, u32[]{:S(2)}) %collective-permute-start.12) | collective-permute-done | bytes 1048608 | tf_op jit(solution)/shard_map/while/body/eval_jaxpr/ppermute | solution.py:22
  55.9 14.9 %collective-permute-done.12 = bf16[128,4096]{1,0:T(8,128)(2,1)S(1)} collective-permute-done((bf16[128,4096]{1,0:T(8,128)(2,1)}, bf16[128,4096]{1,0:T(8,128)(2,1)S(1)}, u32[]{:S(2)}, u32[]{:S(2)}) %collective-permute-start.12) | collective-permute-done | bytes 1048608 | tf_op jit(solution)/shard_map/while/body/eval_jaxpr/ppermute | solution.py:22
  73.3 14.9 %collective-permute-done.12 = bf16[128,4096]{1,0:T(8,128)(2,1)S(1)} collective-permute-done((bf16[128,4096]{1,0:T(8,128)(2,1)}, bf16[128,4096]{1,0:T(8,128)(2,1)S(1)}, u32[]{:S(2)}, u32[]{:S(2)}) %collective-permute-start.12) | collective-permute-done | bytes 1048608 | tf_op jit(solution)/shard_map/while/body/eval_jaxpr/ppermute | solution.py:22
  90.8 14.9 %collective-permute-done.12 = bf16[128,4096]{1,0:T(8,128)(2,1)S(1)} collective-permute-done((bf16[128,4096]{1,0:T(8,128)(2,1)}, bf16[128,4096]{1,0:T(8,128)(2,1)S(1)}, u32[]{:S(2)}, u32[]{:S(2)}) %collective-permute-start.12) | collective-permute-done | bytes 1048608 | tf_op jit(solution)/shard_map/while/body/eval_jaxpr/ppermute | solution.py:22
  108.2 14.9 %collective-permute-done.12 = bf16[128,4096]{1,0:T(8,128)(2,1)S(1)} collective-permute-done((bf16[128,4096]{1,0:T(8,128)(2,1)}, bf16[128,4096]{1,0:T(8,128)(2,1)S(1)}, u32[]{:S(2)}, u32[]{:S(2)}) %collective-permute-start.12) | collective-permute-done | bytes 1048608 | tf_op jit(solution)/shard_map/while/body/eval_jaxpr/ppermute | solution.py:22
  125.7 422.2 %collective-permute-done.12 = bf16[128,4096]{1,0:T(8,128)(2,1)S(1)} collective-permute-done((bf16[128,4096]{1,0:T(8,128)(2,1)}, bf16[128,4096]{1,0:T(8,128)(2,1)S(1)}, u32[]{:S(2)}, u32[]{:S(2)}) %collective-permute-start.12) | collective-permute-done | bytes 1048608 | tf_op jit(solution)/shard_map/while/body/eval_jaxpr/ppermute | solution.py:22
  547.8 64.5 %conditional.4 = (bf16[128,4096]{1,0:T(8,128)(2,1)}, bf16[2,128,4096]{2,1,0:T(8,128)(2,1)}) conditional(s32[]{:T(128)} %convert_element_type.63, bf16[2,128,4096]{2,1,0:T(8,128)(2,1)} %get-tuple-element.631, (s32[]{:T(128)}, bf16[1,2,128,4096]{3,2,1,0:T(8,128)(2,1)S(1)}, f32[2,128,64]{2,1,0:T(8,128)S(1)}, f32[2,128,64]{2,1,0:T(8,128)S(1)}, ...), branch_computations={%region_8.10_spmd, %region_9.12_spmd} | conditional | flops 1088946304 | bytes 73345296 | solution.py:261
  547.8 1.7 fusion.6
  549.6 5.1 fusion.11
  555.8 2.7 collective-permute-start.1
  558.6 2.7 collective-permute-start.7
  561.4 2.2 collective-permute-done.6
  563.6 2.8 collective-permute-done.2
  566.5 2.1 collective-permute-done.8
  570.8 2.7 collective-permute-start.10
  573.4 2.9 collective-permute-done.3.refs_1_
  576.4 2.6 collective-permute-done.9.refs_5_
  579.6 1.4 copy.16
  581.0 2.4 fusion.10.refs_8_
  583.4 5.4 collective-permute-done.5.refs_3_
  590.4 19.6 %branch_1_fun.1 = bf16[128,4096]{1,0:T(8,128)(2,1)} custom-call(s32[1]{0:T(128)} %bitcast.mb_ref, bf16[128,4096]{1,0:T(8,128)(2,1)} %bitcast.34, bf16[512,512]{1,0:T(8,128)(2,1)} %copy-done.2, bf16[512,512]{1,0:T(8,128)(2,1)} %copy-done.3, bf16[512,512]{1,0:T(8,128)(2,1)} %copy-done.5, bf16[512,512]{1,0:T(8,128)(2,1)} %copy-done.7, ...), custom_call_target="tpu_custom_call" | custom-call | tf_op jit(solution)/shard_map/while/body/eval_jaxpr/cond/branch_1_fun/pallas_call | solution.py:171
  610.0 2.3 bitcast_dynamic-update-slice_fusion
  613.7 19.6 %collective-permute-done.12 = bf16[128,4096]{1,0:T(8,128)(2,1)S(1)} collective-permute-done((bf16[128,4096]{1,0:T(8,128)(2,1)}, bf16[128,4096]{1,0:T(8,128)(2,1)S(1)}, u32[]{:S(2)}, u32[]{:S(2)}) %collective-permute-start.12) | collective-permute-done | bytes 1048608 | tf_op jit(solution)/shard_map/while/body/eval_jaxpr/ppermute | solution.py:22
  633.4 62.1 %conditional.4 = (bf16[128,4096]{1,0:T(8,128)(2,1)}, bf16[2,128,4096]{2,1,0:T(8,128)(2,1)}) conditional(s32[]{:T(128)} %convert_element_type.63, bf16[2,128,4096]{2,1,0:T(8,128)(2,1)} %get-tuple-element.631, (s32[]{:T(128)}, bf16[1,2,128,4096]{3,2,1,0:T(8,128)(2,1)S(1)}, f32[2,128,64]{2,1,0:T(8,128)S(1)}, f32[2,128,64]{2,1,0:T(8,128)S(1)}, ...), branch_computations={%region_8.10_spmd, %region_9.12_spmd} | conditional | flops 1088946304 | bytes 73345296 | solution.py:261
  633.4 1.7 fusion.6
  635.1 5.1 fusion.11
  641.3 2.7 collective-permute-start.1
  644.1 2.7 collective-permute-start.7
  646.9 2.2 collective-permute-done.6
  649.2 2.8 collective-permute-done.2
  652.0 2.1 collective-permute-done.8
  656.3 2.7 collective-permute-start.10
  658.9 2.3 collective-permute-done.3.refs_1_
  661.2 2.3 collective-permute-done.9.refs_5_
  664.1 1.4 copy.16
  665.5 2.4 fusion.10.refs_8_
  667.9 2.6 collective-permute-done.5.refs_3_
  670.5 2.3 collective-permute-done.11.refs_7_
  673.6 19.6 %branch_1_fun.1 = bf16[128,4096]{1,0:T(8,128)(2,1)} custom-call(s32[1]{0:T(128)} %bitcast.mb_ref, bf16[128,4096]{1,0:T(8,128)(2,1)} %bitcast.34, bf16[512,512]{1,0:T(8,128)(2,1)} %copy-done.2, bf16[512,512]{1,0:T(8,128)(2,1)} %copy-done.3, bf16[512,512]{1,0:T(8,128)(2,1)} %copy-done.5, bf16[512,512]{1,0:T(8,128)(2,1)} %copy-done.7, ...), custom_call_target="tpu_custom_call" | custom-call | tf_op jit(solution)/shard_map/while/body/eval_jaxpr/cond/branch_1_fun/pallas_call | solution.py:171
  693.2 2.3 bitcast_dynamic-update-slice_fusion
  (188 shorter events, 38.8 us)
Async XLA Ops:
  0.0 7.9 %copy-start.12 = (s32[2,2048]{1,0:T(2,128)S(1)}, s32[2,2048]{1,0:T(2,128)}, u32[]{:S(2)}) copy-start(s32[2,2048]{1,0:T(2,128)} %param.22) | copy-start | bytes 49156
  0.0 8.0 %copy-start.13 = (s32[2,32]{1,0:T(2,128)S(1)}, s32[2,32]{1,0:T(2,128)}, u32[]{:S(2)}) copy-start(s32[2,32]{1,0:T(2,128)} %param.23) | copy-start | bytes 772
  0.0 8.1 %copy-start.11 = (s32[2,2048]{1,0:T(2,128)S(1)}, s32[2,2048]{1,0:T(2,128)}, u32[]{:S(2)}) copy-start(s32[2,2048]{1,0:T(2,128)} %param.21) | copy-start | bytes 49156
  9.8 3.7 copy-start.9
  9.8 3.7 copy-start.10
  13.5 4.9 collective-permute-start.12
  19.6 16.3 %collective-permute-start.12 = (bf16[128,4096]{1,0:T(8,128)(2,1)}, bf16[128,4096]{1,0:T(8,128)(2,1)S(1)}, u32[]{:S(2)}, u32[]{:S(2)}) collective-permute-start(bf16[128,4096]{1,0:T(8,128)(2,1)} %get-tuple-element.630), channel_id=1, source_target_pairs={{0,16},{16,32},{32,48},{48,64},{64,80},{80,96},{96,112},{1,17},{17... | collective-permute-start | bytes 3145736 | tf_op jit(solution)/shard_map/while/body/eval_jaxpr/ppermute | solution.py:22
  37.0 16.3 %collective-permute-start.12 = (bf16[128,4096]{1,0:T(8,128)(2,1)}, bf16[128,4096]{1,0:T(8,128)(2,1)S(1)}, u32[]{:S(2)}, u32[]{:S(2)}) collective-permute-start(bf16[128,4096]{1,0:T(8,128)(2,1)} %get-tuple-element.630), channel_id=1, source_target_pairs={{0,16},{16,32},{32,48},{48,64},{64,80},{80,96},{96,112},{1,17},{17... | collective-permute-start | bytes 3145736 | tf_op jit(solution)/shard_map/while/body/eval_jaxpr/ppermute | solution.py:22
  54.5 16.3 %collective-permute-start.12 = (bf16[128,4096]{1,0:T(8,128)(2,1)}, bf16[128,4096]{1,0:T(8,128)(2,1)S(1)}, u32[]{:S(2)}, u32[]{:S(2)}) collective-permute-start(bf16[128,4096]{1,0:T(8,128)(2,1)} %get-tuple-element.630), channel_id=1, source_target_pairs={{0,16},{16,32},{32,48},{48,64},{64,80},{80,96},{96,112},{1,17},{17... | collective-permute-start | bytes 3145736 | tf_op jit(solution)/shard_map/while/body/eval_jaxpr/ppermute | solution.py:22
  71.9 16.3 %collective-permute-start.12 = (bf16[128,4096]{1,0:T(8,128)(2,1)}, bf16[128,4096]{1,0:T(8,128)(2,1)S(1)}, u32[]{:S(2)}, u32[]{:S(2)}) collective-permute-start(bf16[128,4096]{1,0:T(8,128)(2,1)} %get-tuple-element.630), channel_id=1, source_target_pairs={{0,16},{16,32},{32,48},{48,64},{64,80},{80,96},{96,112},{1,17},{17... | collective-permute-start | bytes 3145736 | tf_op jit(solution)/shard_map/while/body/eval_jaxpr/ppermute | solution.py:22
  89.4 16.3 %collective-permute-start.12 = (bf16[128,4096]{1,0:T(8,128)(2,1)}, bf16[128,4096]{1,0:T(8,128)(2,1)S(1)}, u32[]{:S(2)}, u32[]{:S(2)}) collective-permute-start(bf16[128,4096]{1,0:T(8,128)(2,1)} %get-tuple-element.630), channel_id=1, source_target_pairs={{0,16},{16,32},{32,48},{48,64},{64,80},{80,96},{96,112},{1,17},{17... | collective-permute-start | bytes 3145736 | tf_op jit(solution)/shard_map/while/body/eval_jaxpr/ppermute | solution.py:22
  106.8 16.3 %collective-permute-start.12 = (bf16[128,4096]{1,0:T(8,128)(2,1)}, bf16[128,4096]{1,0:T(8,128)(2,1)S(1)}, u32[]{:S(2)}, u32[]{:S(2)}) collective-permute-start(bf16[128,4096]{1,0:T(8,128)(2,1)} %get-tuple-element.630), channel_id=1, source_target_pairs={{0,16},{16,32},{32,48},{48,64},{64,80},{80,96},{96,112},{1,17},{17... | collective-permute-start | bytes 3145736 | tf_op jit(solution)/shard_map/while/body/eval_jaxpr/ppermute | solution.py:22
  124.3 423.6 %collective-permute-start.12 = (bf16[128,4096]{1,0:T(8,128)(2,1)}, bf16[128,4096]{1,0:T(8,128)(2,1)S(1)}, u32[]{:S(2)}, u32[]{:S(2)}) collective-permute-start(bf16[128,4096]{1,0:T(8,128)(2,1)} %get-tuple-element.630), channel_id=1, source_target_pairs={{0,16},{16,32},{32,48},{48,64},{64,80},{80,96},{96,112},{1,17},{17... | collective-permute-start | bytes 3145736 | tf_op jit(solution)/shard_map/while/body/eval_jaxpr/ppermute | solution.py:22
  549.5 5.1 copy-start
  555.7 5.5 collective-permute-start
  555.8 7.8 %collective-permute-start.1 = (bf16[128,512]{1,0:T(8,128)(2,1)S(1)}, bf16[128,512]{1,0:T(8,128)(2,1)S(1)}, u32[]{:S(2)}, u32[]{:S(2)}) collective-permute-start(bf16[128,512]{1,0:T(8,128)(2,1)S(1)} %bitcast.41), channel_id=1, source_target_pairs={{0,3},{1,0},{2,1},{3,2},{4,7},{5,4},{6,5},{7,6},{8,11},{9,8},{10,9... | collective-permute-start | bytes 393224 | tf_op jit(solution)/shard_map/while/body/eval_jaxpr/cond/branch_1_fun/ppermute | solution.py:84
  558.5 5.1 collective-permute-start.6
  558.6 7.9 %collective-permute-start.7 = (bf16[128,512]{1,0:T(8,128)(2,1)S(1)}, bf16[128,512]{1,0:T(8,128)(2,1)S(1)}, u32[]{:S(2)}, u32[]{:S(2)}) collective-permute-start(bf16[128,512]{1,0:T(8,128)(2,1)S(1)} %slice.127), channel_id=1, source_target_pairs={{0,12},{1,13},{2,14},{3,15},{4,0},{5,1},{6,2},{7,3},{8,4},{9,5},{1... | collective-permute-start | bytes 393224 | tf_op jit(solution)/shard_map/while/body/eval_jaxpr/cond/branch_1_fun/ppermute | solution.py:84
  561.3 5.1 collective-permute-start.2
  563.6 5.0 collective-permute-start.8
  566.4 3.8 copy-start.2
  566.4 10.0 %collective-permute-start.3 = (bf16[512,512]{1,0:T(8,128)(2,1)S(1)}, bf16[512,512]{1,0:T(8,128)(2,1)S(1)}, u32[]{:S(2)}, u32[]{:S(2)}) collective-permute-start(bf16[512,512]{1,0:T(8,128)(2,1)S(1)} %constant_dynamic-update-slice_fusion.refs_0_), channel_id=1, source_target_pairs={{0,4},{1,5},{2,6},{3,7},{4,8},{5,9},{6,10},{7,11},{8,12},{9,13},{1... | collective-permute-start | bytes 1572872 | tf_op jit(solution)/shard_map/while/body/eval_jaxpr/cond/branch_1_fun/ppermute | solution.py:84
  568.7 10.3 %collective-permute-start.9 = (bf16[512,512]{1,0:T(8,128)(2,1)S(1)}, bf16[512,512]{1,0:T(8,128)(2,1)S(1)}, u32[]{:S(2)}, u32[]{:S(2)}) collective-permute-start(bf16[512,512]{1,0:T(8,128)(2,1)S(1)} %pad_maximum_fusion.1.refs_4_), channel_id=1, source_target_pairs={{0,1},{1,2},{2,3},{3,0},{4,5},{5,6},{6,7},{7,4},{8,9},{9,10},{10,1... | collective-permute-start | bytes 1572872 | tf_op jit(solution)/shard_map/while/body/eval_jaxpr/cond/branch_1_fun/ppermute | solution.py:84
  570.2 13.2 %collective-permute-start.4 = (bf16[512,512]{1,0:T(8,128)(2,1)S(1)}, bf16[512,512]{1,0:T(8,128)(2,1)S(1)}, u32[]{:S(2)}, u32[]{:S(2)}) collective-permute-start(bf16[512,512]{1,0:T(8,128)(2,1)S(1)} %constant_dynamic-update-slice_fusion.refs_0_), channel_id=1, source_target_pairs={{0,12},{1,13},{2,14},{3,15},{4,0},{5,1},{6,2},{7,3},{8,4},{9,5},{1... | collective-permute-start | bytes 1572872 | tf_op jit(solution)/shard_map/while/body/eval_jaxpr/cond/branch_1_fun/ppermute | solution.py:84
  570.8 12.6 %collective-permute-start.10 = (bf16[512,512]{1,0:T(8,128)(2,1)S(1)}, bf16[512,512]{1,0:T(8,128)(2,1)S(1)}, u32[]{:S(2)}, u32[]{:S(2)}) collective-permute-start(bf16[512,512]{1,0:T(8,128)(2,1)S(1)} %pad_maximum_fusion.1.refs_4_), channel_id=1, source_target_pairs={{0,3},{1,0},{2,1},{3,2},{4,7},{5,4},{6,5},{7,6},{8,11},{9,8},{10,9... | collective-permute-start | bytes 1572872 | tf_op jit(solution)/shard_map/while/body/eval_jaxpr/cond/branch_1_fun/ppermute | solution.py:84
  576.4 4.6 copy-start.3
  576.4 12.4 %collective-permute-start.5 = (bf16[512,512]{1,0:T(8,128)(2,1)S(1)}, bf16[512,512]{1,0:T(8,128)(2,1)S(1)}, u32[]{:S(2)}, u32[]{:S(2)}) collective-permute-start(bf16[512,512]{1,0:T(8,128)(2,1)S(1)} %collective-permute-done.3.refs_1_), channel_id=1, source_target_pairs={{0,4},{1,5},{2,6},{3,7},{4,8},{5,9},{6,10},{7,11},{8,12},{9,13},{1... | collective-permute-start | bytes 1572872 | tf_op jit(solution)/shard_map/while/body/eval_jaxpr/cond/branch_1_fun/ppermute | solution.py:84
  579.0 9.8 %collective-permute-start.11 = (bf16[512,512]{1,0:T(8,128)(2,1)S(1)}, bf16[512,512]{1,0:T(8,128)(2,1)S(1)}, u32[]{:S(2)}, u32[]{:S(2)}) collective-permute-start(bf16[512,512]{1,0:T(8,128)(2,1)S(1)} %collective-permute-done.9.refs_5_), channel_id=1, source_target_pairs={{0,1},{1,2},{2,3},{3,0},{4,5},{5,6},{6,7},{7,4},{8,9},{9,10},{10,1... | collective-permute-start | bytes 1572872 | tf_op jit(solution)/shard_map/while/body/eval_jaxpr/cond/branch_1_fun/ppermute | solution.py:84
  583.4 7.0 %copy-start.5 = (bf16[512,512]{1,0:T(8,128)(2,1)}, bf16[512,512]{1,0:T(8,128)(2,1)S(1)}, u32[]{:S(2)}) copy-start(bf16[512,512]{1,0:T(8,128)(2,1)S(1)} %collective-permute-done.4.refs_2_) | copy-start | bytes 1572868 | tf_op jit(solution)/shard_map/while/body/eval_jaxpr/cond
  583.4 7.0 %copy-start.6 = (bf16[512,512]{1,0:T(8,128)(2,1)}, bf16[512,512]{1,0:T(8,128)(2,1)S(1)}, u32[]{:S(2)}) copy-start(bf16[512,512]{1,0:T(8,128)(2,1)S(1)} %collective-permute-done.10.refs_6_) | copy-start | bytes 1572868 | tf_op jit(solution)/shard_map/while/body/eval_jaxpr/cond
  612.3 21.0 %collective-permute-start.12 = (bf16[128,4096]{1,0:T(8,128)(2,1)}, bf16[128,4096]{1,0:T(8,128)(2,1)S(1)}, u32[]{:S(2)}, u32[]{:S(2)}) collective-permute-start(bf16[128,4096]{1,0:T(8,128)(2,1)} %get-tuple-element.630), channel_id=1, source_target_pairs={{0,16},{16,32},{32,48},{48,64},{64,80},{80,96},{96,112},{1,17},{17... | collective-permute-start | bytes 3145736 | tf_op jit(solution)/shard_map/while/body/eval_jaxpr/ppermute | solution.py:22
  635.0 5.1 copy-start
  641.3 5.5 collective-permute-start
  641.3 7.8 %collective-permute-start.1 = (bf16[128,512]{1,0:T(8,128)(2,1)S(1)}, bf16[128,512]{1,0:T(8,128)(2,1)S(1)}, u32[]{:S(2)}, u32[]{:S(2)}) collective-permute-start(bf16[128,512]{1,0:T(8,128)(2,1)S(1)} %bitcast.41), channel_id=1, source_target_pairs={{0,3},{1,0},{2,1},{3,2},{4,7},{5,4},{6,5},{7,6},{8,11},{9,8},{10,9... | collective-permute-start | bytes 393224 | tf_op jit(solution)/shard_map/while/body/eval_jaxpr/cond/branch_1_fun/ppermute | solution.py:84
  644.0 5.1 collective-permute-start.6
  644.1 7.9 %collective-permute-start.7 = (bf16[128,512]{1,0:T(8,128)(2,1)S(1)}, bf16[128,512]{1,0:T(8,128)(2,1)S(1)}, u32[]{:S(2)}, u32[]{:S(2)}) collective-permute-start(bf16[128,512]{1,0:T(8,128)(2,1)S(1)} %slice.127), channel_id=1, source_target_pairs={{0,12},{1,13},{2,14},{3,15},{4,0},{5,1},{6,2},{7,3},{8,4},{9,5},{1... | collective-permute-start | bytes 393224 | tf_op jit(solution)/shard_map/while/body/eval_jaxpr/cond/branch_1_fun/ppermute | solution.py:84
  646.8 5.1 collective-permute-start.2
  649.1 5.0 collective-permute-start.8
  651.9 3.8 copy-start.2
  651.9 9.3 %collective-permute-start.3 = (bf16[512,512]{1,0:T(8,128)(2,1)S(1)}, bf16[512,512]{1,0:T(8,128)(2,1)S(1)}, u32[]{:S(2)}, u32[]{:S(2)}) collective-permute-start(bf16[512,512]{1,0:T(8,128)(2,1)S(1)} %constant_dynamic-update-slice_fusion.refs_0_), channel_id=1, source_target_pairs={{0,4},{1,5},{2,6},{3,7},{4,8},{5,9},{6,10},{7,11},{8,12},{9,13},{1... | collective-permute-start | bytes 1572872 | tf_op jit(solution)/shard_map/while/body/eval_jaxpr/cond/branch_1_fun/ppermute | solution.py:84
  654.2 9.3 %collective-permute-start.9 = (bf16[512,512]{1,0:T(8,128)(2,1)S(1)}, bf16[512,512]{1,0:T(8,128)(2,1)S(1)}, u32[]{:S(2)}, u32[]{:S(2)}) collective-permute-start(bf16[512,512]{1,0:T(8,128)(2,1)S(1)} %pad_maximum_fusion.1.refs_4_), channel_id=1, source_target_pairs={{0,1},{1,2},{2,3},{3,0},{4,5},{5,6},{6,7},{7,4},{8,9},{9,10},{10,1... | collective-permute-start | bytes 1572872 | tf_op jit(solution)/shard_map/while/body/eval_jaxpr/cond/branch_1_fun/ppermute | solution.py:84
  655.7 12.2 %collective-permute-start.4 = (bf16[512,512]{1,0:T(8,128)(2,1)S(1)}, bf16[512,512]{1,0:T(8,128)(2,1)S(1)}, u32[]{:S(2)}, u32[]{:S(2)}) collective-permute-start(bf16[512,512]{1,0:T(8,128)(2,1)S(1)} %constant_dynamic-update-slice_fusion.refs_0_), channel_id=1, source_target_pairs={{0,12},{1,13},{2,14},{3,15},{4,0},{5,1},{6,2},{7,3},{8,4},{9,5},{1... | collective-permute-start | bytes 1572872 | tf_op jit(solution)/shard_map/while/body/eval_jaxpr/cond/branch_1_fun/ppermute | solution.py:84
  656.3 11.6 %collective-permute-start.10 = (bf16[512,512]{1,0:T(8,128)(2,1)S(1)}, bf16[512,512]{1,0:T(8,128)(2,1)S(1)}, u32[]{:S(2)}, u32[]{:S(2)}) collective-permute-start(bf16[512,512]{1,0:T(8,128)(2,1)S(1)} %pad_maximum_fusion.1.refs_4_), channel_id=1, source_target_pairs={{0,3},{1,0},{2,1},{3,2},{4,7},{5,4},{6,5},{7,6},{8,11},{9,8},{10,9... | collective-permute-start | bytes 1572872 | tf_op jit(solution)/shard_map/while/body/eval_jaxpr/cond/branch_1_fun/ppermute | solution.py:84
  661.2 4.3 copy-start.3
  661.2 9.2 %collective-permute-start.5 = (bf16[512,512]{1,0:T(8,128)(2,1)S(1)}, bf16[512,512]{1,0:T(8,128)(2,1)S(1)}, u32[]{:S(2)}, u32[]{:S(2)}) collective-permute-start(bf16[512,512]{1,0:T(8,128)(2,1)S(1)} %collective-permute-done.3.refs_1_), channel_id=1, source_target_pairs={{0,4},{1,5},{2,6},{3,7},{4,8},{5,9},{6,10},{7,11},{8,12},{9,13},{1... | collective-permute-start | bytes 1572872 | tf_op jit(solution)/shard_map/while/body/eval_jaxpr/cond/branch_1_fun/ppermute | solution.py:84
  663.5 9.2 %collective-permute-start.11 = (bf16[512,512]{1,0:T(8,128)(2,1)S(1)}, bf16[512,512]{1,0:T(8,128)(2,1)S(1)}, u32[]{:S(2)}, u32[]{:S(2)}) collective-permute-start(bf16[512,512]{1,0:T(8,128)(2,1)S(1)} %collective-permute-done.9.refs_5_), channel_id=1, source_target_pairs={{0,1},{1,2},{2,3},{3,0},{4,5},{5,6},{6,7},{7,4},{8,9},{9,10},{10,1... | collective-permute-start | bytes 1572872 | tf_op jit(solution)/shard_map/while/body/eval_jaxpr/cond/branch_1_fun/ppermute | solution.py:84
  667.9 5.7 copy-start.5
  667.9 5.6 copy-start.6
  (8 other events, 12.9 us)

commit v13 on v11

--- a/solution.py
+++ b/solution.py
@@ -252,7 +252,7 @@
         result = lax.cond(
             active,
             lambda rows: run_layer(rows, start_at),
-            jnp.zeros_like,
+            lambda rows: rows,
             current,
         )
         stored = lax.dynamic_update_index_in_dim(outputs, result, start_at, 0)

time: 694 us -> 689 us (level)
  waiting for transfers between devices: 560 us -> 535 us
  local copies, waits for them, and re-layouts: 22.6 us -> 33.7 us
  other arithmetic: 29.5 us -> 38.9 us
    ppermute x9, waiting for transfers between devices: 526 us -> 500 us  [from_behind(): return lax.ppermute(value, axis, pairs)]
    while x0 -> x36, local copies, waits for them, and re-layouts: none -> 22.8 us
    select_n x0 -> x9, other arithmetic: none -> 12 us  [advance(): current = jnp.where(section_id == 0, entering, incoming)]
    another operation x8 -> x0, local copies, waits for them, and re-layouts: 8.67 us -> none
where the time goes in v13:
time: 689 us; the launch traced here: 687 us
  waiting for transfers between devices  535 us (78%)
  other arithmetic  38.9 us (6%)
  Pallas kernels  38 us (6%)
  local copies, waits for them, and re-layouts  33.7 us (5%)
  starting transfers between devices  29.4 us (4%)
  matrix products  10.6 us (2%)
    ppermute x9, waiting for transfers between devices, from_behind(): return lax.ppermute(value, axis, pairs)  500 us
    pallas_call x2, Pallas kernels, attention(): pl.pallas_call(attention_kernel, grid_spec=grid_spec, out_shape=jax.Shape...  38 us
    ppermute x24, waiting for transfers between devices, shift(): return lax.ppermute(piece, 'seq', pairs)  34.7 us
    while x36, local copies, waits for them, and re-layouts  22.8 us
    ppermute x24, starting transfers between devices, shift(): return lax.ppermute(piece, 'seq', pairs)  17.9 us
  transfers between devices with their start and end apart: 33, of which 23 were waited for; matrix products, arithmetic and copies ran while one was open for 2% of the time, Pallas kernels for 0%

profile of v13, /device:TPU:25, one launch (start us, length us, event | category | flops | bytes accessed | tf_op | source)
XLA Modules:
  0.0 687.5 jit_solution(6322572947172698116)
XLA Ops:
  8.4 7.9 %pad_maximum_fusion.3 = bf16[4096,1024]{1,0:T(8,128)(2,1)} fusion(bf16[4096,512]{1,0:T(8,128)(2,1)} %bitcast.43, bf16[4096,512]{1,0:T(8,128)(2,1)} %bitcast.44), kind=kLoop, calls=%fused_computation.39 | loop fusion | flops 16777216 | bytes 16777216 | tf_op jit(solution)/shard_map/concatenate | solution.py:212
  16.3 1.6 broadcast_in_dim.129
  18.0 669.5 %while.18 = (s32[]{:T(128)}, bf16[128,4096]{1,0:T(8,128)(2,1)S(1)}, bf16[2,128,4096]{2,1,0:T(8,128)(2,1)}, s32[]{:T(128)}, pred[]{:T(512)}, /*index=5*/bf16[2,12...) while((s32[]{:T(128)}, bf16[128,4096]{1,0:T(8,128)(2,1)S(1)}, ...), condition=%wide.region_11.14_spmd.clone.clone, body=%wide.region_7.13_spmd.clone.clone.sunk | while | flops 1089486976 | bytes 106966552 | solution.py:264
  19.6 3.3 collective-permute-done.12
  24.3 1.6 copy-done.2
  28.9 14.7 %collective-permute-done.12 = bf16[128,4096]{1,0:T(8,128)(2,1)S(1)} collective-permute-done((bf16[128,4096]{1,0:T(8,128)(2,1)S(1)}, bf16[128,4096]{1,0:T(8,128)(2,1)S(1)}, u32[]{:S(2)}, u32[]{:S(2)}) %collective-permute-start.12) | collective-permute-done | bytes 1048608 | tf_op jit(solution)/shard_map/while/body/eval_jaxpr/ppermute | solution.py:22
  45.0 1.6 copy-done.2
  49.6 14.7 %collective-permute-done.12 = bf16[128,4096]{1,0:T(8,128)(2,1)S(1)} collective-permute-done((bf16[128,4096]{1,0:T(8,128)(2,1)S(1)}, bf16[128,4096]{1,0:T(8,128)(2,1)S(1)}, u32[]{:S(2)}, u32[]{:S(2)}) %collective-permute-start.12) | collective-permute-done | bytes 1048608 | tf_op jit(solution)/shard_map/while/body/eval_jaxpr/ppermute | solution.py:22
  65.7 1.6 copy-done.2
  70.3 14.7 %collective-permute-done.12 = bf16[128,4096]{1,0:T(8,128)(2,1)S(1)} collective-permute-done((bf16[128,4096]{1,0:T(8,128)(2,1)S(1)}, bf16[128,4096]{1,0:T(8,128)(2,1)S(1)}, u32[]{:S(2)}, u32[]{:S(2)}) %collective-permute-start.12) | collective-permute-done | bytes 1048608 | tf_op jit(solution)/shard_map/while/body/eval_jaxpr/ppermute | solution.py:22
  86.4 1.6 copy-done.2
  91.0 14.7 %collective-permute-done.12 = bf16[128,4096]{1,0:T(8,128)(2,1)S(1)} collective-permute-done((bf16[128,4096]{1,0:T(8,128)(2,1)S(1)}, bf16[128,4096]{1,0:T(8,128)(2,1)S(1)}, u32[]{:S(2)}, u32[]{:S(2)}) %collective-permute-start.12) | collective-permute-done | bytes 1048608 | tf_op jit(solution)/shard_map/while/body/eval_jaxpr/ppermute | solution.py:22
  107.1 1.6 copy-done.2
  111.7 14.7 %collective-permute-done.12 = bf16[128,4096]{1,0:T(8,128)(2,1)S(1)} collective-permute-done((bf16[128,4096]{1,0:T(8,128)(2,1)S(1)}, bf16[128,4096]{1,0:T(8,128)(2,1)S(1)}, u32[]{:S(2)}, u32[]{:S(2)}) %collective-permute-start.12) | collective-permute-done | bytes 1048608 | tf_op jit(solution)/shard_map/while/body/eval_jaxpr/ppermute | solution.py:22
  127.8 1.6 copy-done.2
  132.4 14.7 %collective-permute-done.12 = bf16[128,4096]{1,0:T(8,128)(2,1)S(1)} collective-permute-done((bf16[128,4096]{1,0:T(8,128)(2,1)S(1)}, bf16[128,4096]{1,0:T(8,128)(2,1)S(1)}, u32[]{:S(2)}, u32[]{:S(2)}) %collective-permute-start.12) | collective-permute-done | bytes 1048608 | tf_op jit(solution)/shard_map/while/body/eval_jaxpr/ppermute | solution.py:22
  148.5 1.6 copy-done.2
  153.1 388.9 %collective-permute-done.12 = bf16[128,4096]{1,0:T(8,128)(2,1)S(1)} collective-permute-done((bf16[128,4096]{1,0:T(8,128)(2,1)S(1)}, bf16[128,4096]{1,0:T(8,128)(2,1)S(1)}, u32[]{:S(2)}, u32[]{:S(2)}) %collective-permute-start.12) | collective-permute-done | bytes 1048608 | tf_op jit(solution)/shard_map/while/body/eval_jaxpr/ppermute | solution.py:22
  543.3 59.8 %conditional.4 = (bf16[128,4096]{1,0:T(8,128)(2,1)S(1)}) conditional(s32[]{:T(128)} %convert_element_type.63, bf16[128,4096]{1,0:T(8,128)(2,1)S(1)} %bitcast_select_fusion.3, (s32[]{:T(128)}, bf16[1,2,128,4096]{3,2,1,0:T(8,128)(2,1)}, f32[2,128,64]{2,1,0:T(8,128)S(1)}, f32[2,128,64]{2,1,0:T(8,128)S(1)}, bf16[128,4096]{1,0:T(8,128)(2,1)S(1)}, ...), branch_computations={%region_8.10_spmd, %region_9.12_spmd} | conditional | flops 1088422016 | bytes 79636272 | solution.py:252
  543.7 5.3 fusion.11
  550.2 2.7 collective-permute-start.1
  553.0 2.7 collective-permute-start.7
  555.8 2.2 collective-permute-done.6
  558.0 2.8 collective-permute-done.2
  560.9 2.1 collective-permute-done.8
  565.2 2.6 collective-permute-start.10
  567.8 2.3 collective-permute-done.3.refs_1_
  570.1 3.7 collective-permute-done.9.refs_5_
  574.4 1.4 copy.16
  575.8 2.4 fusion.10.refs_8_
  578.2 2.9 collective-permute-done.5.refs_3_
  581.1 2.2 collective-permute-done.11.refs_7_
  584.1 19.0 %branch_1_fun.1 = bf16[128,4096]{1,0:T(8,128)(2,1)S(1)} custom-call(s32[1]{0:T(128)} %bitcast.mb_ref, bf16[128,4096]{1,0:T(8,128)(2,1)} %bitcast.39, bf16[512,512]{1,0:T(8,128)(2,1)} %copy-done.4, bf16[512,512]{1,0:T(8,128)(2,1)} %copy-done.5, bf16[512,512]{1,0:T(8,128)(2,1)} %copy-done.7, bf16[512,512]{1,0:T(8,128)(2,1)} %copy-done.9, ...), custom_call_target="tpu_custom_call" | custom-call | tf_op jit(solution)/shard_map/while/body/eval_jaxpr/cond/branch_1_fun/pallas_call | solution.py:171
  606.2 20.1 %collective-permute-done.12 = bf16[128,4096]{1,0:T(8,128)(2,1)S(1)} collective-permute-done((bf16[128,4096]{1,0:T(8,128)(2,1)S(1)}, bf16[128,4096]{1,0:T(8,128)(2,1)S(1)}, u32[]{:S(2)}, u32[]{:S(2)}) %collective-permute-start.12) | collective-permute-done | bytes 1048608 | tf_op jit(solution)/shard_map/while/body/eval_jaxpr/ppermute | solution.py:22
  627.7 58.1 %conditional.4 = (bf16[128,4096]{1,0:T(8,128)(2,1)S(1)}) conditional(s32[]{:T(128)} %convert_element_type.63, bf16[128,4096]{1,0:T(8,128)(2,1)S(1)} %bitcast_select_fusion.3, (s32[]{:T(128)}, bf16[1,2,128,4096]{3,2,1,0:T(8,128)(2,1)}, f32[2,128,64]{2,1,0:T(8,128)S(1)}, f32[2,128,64]{2,1,0:T(8,128)S(1)}, bf16[128,4096]{1,0:T(8,128)(2,1)S(1)}, ...), branch_computations={%region_8.10_spmd, %region_9.12_spmd} | conditional | flops 1088422016 | bytes 79636272 | solution.py:252
  628.1 5.3 fusion.11
  634.6 2.7 collective-permute-start.1
  637.3 2.7 collective-permute-start.7
  640.1 2.2 collective-permute-done.6
  642.4 2.8 collective-permute-done.2
  645.2 2.1 collective-permute-done.8
  649.5 2.6 collective-permute-start.10
  652.2 2.3 collective-permute-done.3.refs_1_
  654.5 2.3 collective-permute-done.9.refs_5_
  658.8 2.4 fusion.10.refs_8_
  661.2 2.6 collective-permute-done.5.refs_3_
  663.7 2.3 collective-permute-done.11.refs_7_
  666.8 19.0 %branch_1_fun.1 = bf16[128,4096]{1,0:T(8,128)(2,1)S(1)} custom-call(s32[1]{0:T(128)} %bitcast.mb_ref, bf16[128,4096]{1,0:T(8,128)(2,1)} %bitcast.39, bf16[512,512]{1,0:T(8,128)(2,1)} %copy-done.4, bf16[512,512]{1,0:T(8,128)(2,1)} %copy-done.5, bf16[512,512]{1,0:T(8,128)(2,1)} %copy-done.7, bf16[512,512]{1,0:T(8,128)(2,1)} %copy-done.9, ...), custom_call_target="tpu_custom_call" | custom-call | tf_op jit(solution)/shard_map/while/body/eval_jaxpr/cond/branch_1_fun/pallas_call | solution.py:171
  (231 shorter events, 59.6 us)
Async XLA Ops:
  18.2 4.7 collective-permute-start.12
  27.5 16.1 %collective-permute-start.12 = (bf16[128,4096]{1,0:T(8,128)(2,1)S(1)}, bf16[128,4096]{1,0:T(8,128)(2,1)S(1)}, u32[]{:S(2)}, u32[]{:S(2)}) collective-permute-start(bf16[128,4096]{1,0:T(8,128)(2,1)S(1)} %get-tuple-element.603), channel_id=1, source_target_pairs={{0,16},{16,32},{32,48},{48,64},{64,80},{80,96},{96,112},{1,17},{17... | collective-permute-start | bytes 3145736 | tf_op jit(solution)/shard_map/while/body/eval_jaxpr/ppermute | solution.py:22
  48.2 16.1 %collective-permute-start.12 = (bf16[128,4096]{1,0:T(8,128)(2,1)S(1)}, bf16[128,4096]{1,0:T(8,128)(2,1)S(1)}, u32[]{:S(2)}, u32[]{:S(2)}) collective-permute-start(bf16[128,4096]{1,0:T(8,128)(2,1)S(1)} %get-tuple-element.603), channel_id=1, source_target_pairs={{0,16},{16,32},{32,48},{48,64},{64,80},{80,96},{96,112},{1,17},{17... | collective-permute-start | bytes 3145736 | tf_op jit(solution)/shard_map/while/body/eval_jaxpr/ppermute | solution.py:22
  68.9 16.1 %collective-permute-start.12 = (bf16[128,4096]{1,0:T(8,128)(2,1)S(1)}, bf16[128,4096]{1,0:T(8,128)(2,1)S(1)}, u32[]{:S(2)}, u32[]{:S(2)}) collective-permute-start(bf16[128,4096]{1,0:T(8,128)(2,1)S(1)} %get-tuple-element.603), channel_id=1, source_target_pairs={{0,16},{16,32},{32,48},{48,64},{64,80},{80,96},{96,112},{1,17},{17... | collective-permute-start | bytes 3145736 | tf_op jit(solution)/shard_map/while/body/eval_jaxpr/ppermute | solution.py:22
  89.6 16.1 %collective-permute-start.12 = (bf16[128,4096]{1,0:T(8,128)(2,1)S(1)}, bf16[128,4096]{1,0:T(8,128)(2,1)S(1)}, u32[]{:S(2)}, u32[]{:S(2)}) collective-permute-start(bf16[128,4096]{1,0:T(8,128)(2,1)S(1)} %get-tuple-element.603), channel_id=1, source_target_pairs={{0,16},{16,32},{32,48},{48,64},{64,80},{80,96},{96,112},{1,17},{17... | collective-permute-start | bytes 3145736 | tf_op jit(solution)/shard_map/while/body/eval_jaxpr/ppermute | solution.py:22
  110.3 16.1 %collective-permute-start.12 = (bf16[128,4096]{1,0:T(8,128)(2,1)S(1)}, bf16[128,4096]{1,0:T(8,128)(2,1)S(1)}, u32[]{:S(2)}, u32[]{:S(2)}) collective-permute-start(bf16[128,4096]{1,0:T(8,128)(2,1)S(1)} %get-tuple-element.603), channel_id=1, source_target_pairs={{0,16},{16,32},{32,48},{48,64},{64,80},{80,96},{96,112},{1,17},{17... | collective-permute-start | bytes 3145736 | tf_op jit(solution)/shard_map/while/body/eval_jaxpr/ppermute | solution.py:22
  131.0 16.1 %collective-permute-start.12 = (bf16[128,4096]{1,0:T(8,128)(2,1)S(1)}, bf16[128,4096]{1,0:T(8,128)(2,1)S(1)}, u32[]{:S(2)}, u32[]{:S(2)}) collective-permute-start(bf16[128,4096]{1,0:T(8,128)(2,1)S(1)} %get-tuple-element.603), channel_id=1, source_target_pairs={{0,16},{16,32},{32,48},{48,64},{64,80},{80,96},{96,112},{1,17},{17... | collective-permute-start | bytes 3145736 | tf_op jit(solution)/shard_map/while/body/eval_jaxpr/ppermute | solution.py:22
  151.7 390.3 %collective-permute-start.12 = (bf16[128,4096]{1,0:T(8,128)(2,1)S(1)}, bf16[128,4096]{1,0:T(8,128)(2,1)S(1)}, u32[]{:S(2)}, u32[]{:S(2)}) collective-permute-start(bf16[128,4096]{1,0:T(8,128)(2,1)S(1)} %get-tuple-element.603), channel_id=1, source_target_pairs={{0,16},{16,32},{32,48},{48,64},{64,80},{80,96},{96,112},{1,17},{17... | collective-permute-start | bytes 3145736 | tf_op jit(solution)/shard_map/while/body/eval_jaxpr/ppermute | solution.py:22
  543.3 59.9 %copy-start.2 = (bf16[2,128,4096]{2,1,0:T(8,128)(2,1)S(1)}, bf16[2,128,4096]{2,1,0:T(8,128)(2,1)}, u32[]{:S(2)}) copy-start(bf16[2,128,4096]{2,1,0:T(8,128)(2,1)} %get-tuple-element.604) | copy-start | bytes 6291460 | tf_op jit(solution)/shard_map/while
  543.4 5.6 copy-start
  549.2 14.0 %copy-start.11 = (bf16[1,2,128,4096]{3,2,1,0:T(8,128)(2,1)S(1)}, bf16[1,2,128,4096]{3,2,1,0:T(8,128)(2,1)}, u32[]{:S(2)}) copy-start(bf16[1,2,128,4096]{3,2,1,0:T(8,128)(2,1)} %get-tuple-element.258) | copy-start | bytes 6291460 | tf_op jit(solution)/shard_map/while/body/eval_jaxpr/cond
  550.1 5.5 collective-permute-start
  550.2 7.8 %collective-permute-start.1 = (bf16[128,512]{1,0:T(8,128)(2,1)S(1)}, bf16[128,512]{1,0:T(8,128)(2,1)S(1)}, u32[]{:S(2)}, u32[]{:S(2)}) collective-permute-start(bf16[128,512]{1,0:T(8,128)(2,1)S(1)} %bitcast.46), channel_id=1, source_target_pairs={{0,3},{1,0},{2,1},{3,2},{4,7},{5,4},{6,5},{7,6},{8,11},{9,8},{10,9... | collective-permute-start | bytes 393224 | tf_op jit(solution)/shard_map/while/body/eval_jaxpr/cond/branch_1_fun/ppermute | solution.py:84
  552.9 5.1 collective-permute-start.6
  553.0 7.9 %collective-permute-start.7 = (bf16[128,512]{1,0:T(8,128)(2,1)S(1)}, bf16[128,512]{1,0:T(8,128)(2,1)S(1)}, u32[]{:S(2)}, u32[]{:S(2)}) collective-permute-start(bf16[128,512]{1,0:T(8,128)(2,1)S(1)} %slice.127), channel_id=1, source_target_pairs={{0,12},{1,13},{2,14},{3,15},{4,0},{5,1},{6,2},{7,3},{8,4},{9,5},{1... | collective-permute-start | bytes 393224 | tf_op jit(solution)/shard_map/while/body/eval_jaxpr/cond/branch_1_fun/ppermute | solution.py:84
  555.7 5.1 collective-permute-start.2
  558.0 5.0 collective-permute-start.8
  560.8 3.8 copy-start.4
  560.8 9.3 %collective-permute-start.3 = (bf16[512,512]{1,0:T(8,128)(2,1)S(1)}, bf16[512,512]{1,0:T(8,128)(2,1)S(1)}, u32[]{:S(2)}, u32[]{:S(2)}) collective-permute-start(bf16[512,512]{1,0:T(8,128)(2,1)S(1)} %constant_dynamic-update-slice_fusion.refs_0_), channel_id=1, source_target_pairs={{0,4},{1,5},{2,6},{3,7},{4,8},{5,9},{6,10},{7,11},{8,12},{9,13},{1... | collective-permute-start | bytes 1572872 | tf_op jit(solution)/shard_map/while/body/eval_jaxpr/cond/branch_1_fun/ppermute | solution.py:84
  563.1 10.7 %collective-permute-start.9 = (bf16[512,512]{1,0:T(8,128)(2,1)S(1)}, bf16[512,512]{1,0:T(8,128)(2,1)S(1)}, u32[]{:S(2)}, u32[]{:S(2)}) collective-permute-start(bf16[512,512]{1,0:T(8,128)(2,1)S(1)} %pad_maximum_fusion.1.refs_4_), channel_id=1, source_target_pairs={{0,1},{1,2},{2,3},{3,0},{4,5},{5,6},{6,7},{7,4},{8,9},{9,10},{10,1... | collective-permute-start | bytes 1572872 | tf_op jit(solution)/shard_map/while/body/eval_jaxpr/cond/branch_1_fun/ppermute | solution.py:84
  564.6 13.6 %collective-permute-start.4 = (bf16[512,512]{1,0:T(8,128)(2,1)S(1)}, bf16[512,512]{1,0:T(8,128)(2,1)S(1)}, u32[]{:S(2)}, u32[]{:S(2)}) collective-permute-start(bf16[512,512]{1,0:T(8,128)(2,1)S(1)} %constant_dynamic-update-slice_fusion.refs_0_), channel_id=1, source_target_pairs={{0,12},{1,13},{2,14},{3,15},{4,0},{5,1},{6,2},{7,3},{8,4},{9,5},{1... | collective-permute-start | bytes 1572872 | tf_op jit(solution)/shard_map/while/body/eval_jaxpr/cond/branch_1_fun/ppermute | solution.py:84
  565.2 13.0 %collective-permute-start.10 = (bf16[512,512]{1,0:T(8,128)(2,1)S(1)}, bf16[512,512]{1,0:T(8,128)(2,1)S(1)}, u32[]{:S(2)}, u32[]{:S(2)}) collective-permute-start(bf16[512,512]{1,0:T(8,128)(2,1)S(1)} %pad_maximum_fusion.1.refs_4_), channel_id=1, source_target_pairs={{0,3},{1,0},{2,1},{3,2},{4,7},{5,4},{6,5},{7,6},{8,11},{9,8},{10,9... | collective-permute-start | bytes 1572872 | tf_op jit(solution)/shard_map/while/body/eval_jaxpr/cond/branch_1_fun/ppermute | solution.py:84
  570.1 5.7 copy-start.5
  570.1 11.0 %collective-permute-start.5 = (bf16[512,512]{1,0:T(8,128)(2,1)S(1)}, bf16[512,512]{1,0:T(8,128)(2,1)S(1)}, u32[]{:S(2)}, u32[]{:S(2)}) collective-permute-start(bf16[512,512]{1,0:T(8,128)(2,1)S(1)} %collective-permute-done.3.refs_1_), channel_id=1, source_target_pairs={{0,4},{1,5},{2,6},{3,7},{4,8},{5,9},{6,10},{7,11},{8,12},{9,13},{1... | collective-permute-start | bytes 1572872 | tf_op jit(solution)/shard_map/while/body/eval_jaxpr/cond/branch_1_fun/ppermute | solution.py:84
  573.8 9.5 %collective-permute-start.11 = (bf16[512,512]{1,0:T(8,128)(2,1)S(1)}, bf16[512,512]{1,0:T(8,128)(2,1)S(1)}, u32[]{:S(2)}, u32[]{:S(2)}) collective-permute-start(bf16[512,512]{1,0:T(8,128)(2,1)S(1)} %collective-permute-done.9.refs_5_), channel_id=1, source_target_pairs={{0,1},{1,2},{2,3},{3,0},{4,5},{5,6},{6,7},{7,4},{8,9},{9,10},{10,1... | collective-permute-start | bytes 1572872 | tf_op jit(solution)/shard_map/while/body/eval_jaxpr/cond/branch_1_fun/ppermute | solution.py:84
  578.2 5.2 copy-start.7
  578.2 5.2 copy-start.8
  604.8 21.5 %collective-permute-start.12 = (bf16[128,4096]{1,0:T(8,128)(2,1)S(1)}, bf16[128,4096]{1,0:T(8,128)(2,1)S(1)}, u32[]{:S(2)}, u32[]{:S(2)}) collective-permute-start(bf16[128,4096]{1,0:T(8,128)(2,1)S(1)} %get-tuple-element.603), channel_id=1, source_target_pairs={{0,16},{16,32},{32,48},{48,64},{64,80},{80,96},{96,112},{1,17},{17... | collective-permute-start | bytes 3145736 | tf_op jit(solution)/shard_map/while/body/eval_jaxpr/ppermute | solution.py:22
  627.7 58.2 %copy-start.2 = (bf16[2,128,4096]{2,1,0:T(8,128)(2,1)S(1)}, bf16[2,128,4096]{2,1,0:T(8,128)(2,1)}, u32[]{:S(2)}) copy-start(bf16[2,128,4096]{2,1,0:T(8,128)(2,1)} %get-tuple-element.604) | copy-start | bytes 6291460 | tf_op jit(solution)/shard_map/while
  627.8 5.6 copy-start
  633.5 14.0 %copy-start.11 = (bf16[1,2,128,4096]{3,2,1,0:T(8,128)(2,1)S(1)}, bf16[1,2,128,4096]{3,2,1,0:T(8,128)(2,1)}, u32[]{:S(2)}) copy-start(bf16[1,2,128,4096]{3,2,1,0:T(8,128)(2,1)} %get-tuple-element.258) | copy-start | bytes 6291460 | tf_op jit(solution)/shard_map/while/body/eval_jaxpr/cond
  634.5 5.5 collective-permute-start
  634.6 7.8 %collective-permute-start.1 = (bf16[128,512]{1,0:T(8,128)(2,1)S(1)}, bf16[128,512]{1,0:T(8,128)(2,1)S(1)}, u32[]{:S(2)}, u32[]{:S(2)}) collective-permute-start(bf16[128,512]{1,0:T(8,128)(2,1)S(1)} %bitcast.46), channel_id=1, source_target_pairs={{0,3},{1,0},{2,1},{3,2},{4,7},{5,4},{6,5},{7,6},{8,11},{9,8},{10,9... | collective-permute-start | bytes 393224 | tf_op jit(solution)/shard_map/while/body/eval_jaxpr/cond/branch_1_fun/ppermute | solution.py:84
  637.3 5.1 collective-permute-start.6
  637.3 7.9 %collective-permute-start.7 = (bf16[128,512]{1,0:T(8,128)(2,1)S(1)}, bf16[128,512]{1,0:T(8,128)(2,1)S(1)}, u32[]{:S(2)}, u32[]{:S(2)}) collective-permute-start(bf16[128,512]{1,0:T(8,128)(2,1)S(1)} %slice.127), channel_id=1, source_target_pairs={{0,12},{1,13},{2,14},{3,15},{4,0},{5,1},{6,2},{7,3},{8,4},{9,5},{1... | collective-permute-start | bytes 393224 | tf_op jit(solution)/shard_map/while/body/eval_jaxpr/cond/branch_1_fun/ppermute | solution.py:84
  640.0 5.1 collective-permute-start.2
  642.4 5.0 collective-permute-start.8
  645.1 3.8 copy-start.4
  645.2 9.3 %collective-permute-start.3 = (bf16[512,512]{1,0:T(8,128)(2,1)S(1)}, bf16[512,512]{1,0:T(8,128)(2,1)S(1)}, u32[]{:S(2)}, u32[]{:S(2)}) collective-permute-start(bf16[512,512]{1,0:T(8,128)(2,1)S(1)} %constant_dynamic-update-slice_fusion.refs_0_), channel_id=1, source_target_pairs={{0,4},{1,5},{2,6},{3,7},{4,8},{5,9},{6,10},{7,11},{8,12},{9,13},{1... | collective-permute-start | bytes 1572872 | tf_op jit(solution)/shard_map/while/body/eval_jaxpr/cond/branch_1_fun/ppermute | solution.py:84
  647.4 9.3 %collective-permute-start.9 = (bf16[512,512]{1,0:T(8,128)(2,1)S(1)}, bf16[512,512]{1,0:T(8,128)(2,1)S(1)}, u32[]{:S(2)}, u32[]{:S(2)}) collective-permute-start(bf16[512,512]{1,0:T(8,128)(2,1)S(1)} %pad_maximum_fusion.1.refs_4_), channel_id=1, source_target_pairs={{0,1},{1,2},{2,3},{3,0},{4,5},{5,6},{6,7},{7,4},{8,9},{9,10},{10,1... | collective-permute-start | bytes 1572872 | tf_op jit(solution)/shard_map/while/body/eval_jaxpr/cond/branch_1_fun/ppermute | solution.py:84
  648.9 12.2 %collective-permute-start.4 = (bf16[512,512]{1,0:T(8,128)(2,1)S(1)}, bf16[512,512]{1,0:T(8,128)(2,1)S(1)}, u32[]{:S(2)}, u32[]{:S(2)}) collective-permute-start(bf16[512,512]{1,0:T(8,128)(2,1)S(1)} %constant_dynamic-update-slice_fusion.refs_0_), channel_id=1, source_target_pairs={{0,12},{1,13},{2,14},{3,15},{4,0},{5,1},{6,2},{7,3},{8,4},{9,5},{1... | collective-permute-start | bytes 1572872 | tf_op jit(solution)/shard_map/while/body/eval_jaxpr/cond/branch_1_fun/ppermute | solution.py:84
  649.5 11.6 %collective-permute-start.10 = (bf16[512,512]{1,0:T(8,128)(2,1)S(1)}, bf16[512,512]{1,0:T(8,128)(2,1)S(1)}, u32[]{:S(2)}, u32[]{:S(2)}) collective-permute-start(bf16[512,512]{1,0:T(8,128)(2,1)S(1)} %pad_maximum_fusion.1.refs_4_), channel_id=1, source_target_pairs={{0,3},{1,0},{2,1},{3,2},{4,7},{5,4},{6,5},{7,6},{8,11},{9,8},{10,9... | collective-permute-start | bytes 1572872 | tf_op jit(solution)/shard_map/while/body/eval_jaxpr/cond/branch_1_fun/ppermute | solution.py:84
  654.5 4.3 copy-start.5
  654.5 9.2 %collective-permute-start.5 = (bf16[512,512]{1,0:T(8,128)(2,1)S(1)}, bf16[512,512]{1,0:T(8,128)(2,1)S(1)}, u32[]{:S(2)}, u32[]{:S(2)}) collective-permute-start(bf16[512,512]{1,0:T(8,128)(2,1)S(1)} %collective-permute-done.3.refs_1_), channel_id=1, source_target_pairs={{0,4},{1,5},{2,6},{3,7},{4,8},{5,9},{6,10},{7,11},{8,12},{9,13},{1... | collective-permute-start | bytes 1572872 | tf_op jit(solution)/shard_map/while/body/eval_jaxpr/cond/branch_1_fun/ppermute | solution.py:84
  656.7 9.2 %collective-permute-start.11 = (bf16[512,512]{1,0:T(8,128)(2,1)S(1)}, bf16[512,512]{1,0:T(8,128)(2,1)S(1)}, u32[]{:S(2)}, u32[]{:S(2)}) collective-permute-start(bf16[512,512]{1,0:T(8,128)(2,1)S(1)} %collective-permute-done.9.refs_5_), channel_id=1, source_target_pairs={{0,1},{1,2},{2,3},{3,0},{4,5},{5,6},{6,7},{7,4},{8,9},{9,10},{10,1... | collective-permute-start | bytes 1572872 | tf_op jit(solution)/shard_map/while/body/eval_jaxpr/cond/branch_1_fun/ppermute | solution.py:84
  661.1 4.9 copy-start.7
  661.1 4.9 copy-start.8
  663.7 2.3 copy-start.9
  (24 other events, 36.8 us)

commit v14 on v12

--- a/solution.py
+++ b/solution.py
@@ -254,11 +254,7 @@
             computed = run_layer(rows, start_at)
             return computed, lax.dynamic_update_index_in_dim(kept, computed, start_at, 0)
 
-        def idle(operands):
-            rows, kept = operands
-            return jnp.zeros_like(rows), kept
-
-        return lax.cond(active, busy, idle, (current, outputs))
+        return lax.cond(active, busy, lambda operands: operands, (current, outputs))
 
     empty_pass = jnp.zeros((row_count, model_width), jnp.bfloat16)
     empty_out = jnp.zeros((micro_count, row_count, model_width), jnp.bfloat16)

time: 696 us -> 719 us (1.033)
  other arithmetic: 22.5 us -> 45.1 us
    select_n x0 -> x9, other arithmetic: none -> 21.3 us  [advance(): current = jnp.where(section_id == 0, entering, incoming)]
    another operation x8 -> x0, local copies, waits for them, and re-layouts: 9.1 us -> none
where the time goes in v14:
time: 719 us; the launch traced here: 718 us
  waiting for transfers between devices  574 us (80%)
  other arithmetic  45.1 us (6%)
  Pallas kernels  39.3 us (5%)
  starting transfers between devices  29.4 us (4%)
  local copies, waits for them, and re-layouts  19.5 us (3%)
  matrix products  9.61 us (1%)
    ppermute x9, waiting for transfers between devices, from_behind(): return lax.ppermute(value, axis, pairs)  539 us
    pallas_call x2, Pallas kernels, attention(): pl.pallas_call(attention_kernel, grid_spec=grid_spec, out_shape=jax.Shape...  39.3 us
    ppermute x24, waiting for transfers between devices, shift(): return lax.ppermute(piece, 'seq', pairs)  34.7 us
    select_n x9, other arithmetic, advance(): current = jnp.where(section_id == 0, entering, incoming)  21.3 us
    ppermute x24, starting transfers between devices, shift(): return lax.ppermute(piece, 'seq', pairs)  17.9 us
  transfers between devices with their start and end apart: 33, of which 22 were waited for; matrix products, arithmetic and copies ran while one was open for 2% of the time, Pallas kernels for 0%

profile of v14, /device:TPU:25, one launch (start us, length us, event | category | flops | bytes accessed | tf_op | source)
XLA Modules:
  0.0 717.9 jit_solution(6527351690405156882)
XLA Ops:
  8.4 7.9 %pad_maximum_fusion.3 = bf16[4096,1024]{1,0:T(8,128)(2,1)} fusion(bf16[4096,512]{1,0:T(8,128)(2,1)} %bitcast.39, bf16[4096,512]{1,0:T(8,128)(2,1)} %bitcast.40), kind=kLoop, calls=%fused_computation.38 | loop fusion | flops 16777216 | bytes 16777216 | tf_op jit(solution)/shard_map/concatenate | solution.py:212
  19.0 698.9 %while.18 = (s32[]{:T(128)}, bf16[128,4096]{1,0:T(8,128)(2,1)}, bf16[2,128,4096]{2,1,0:T(8,128)(2,1)}, s32[]{:T(128)}, pred[]{:T(512)}, /*index=5*/bf16[2,128,40...) while((s32[]{:T(128)}, bf16[128,4096]{1,0:T(8,128)(2,1)}, ...), condition=%wide.region_11.14_spmd.clone.clone, body=%wide.region_7.13_spmd.clone.clone.sunk | while | flops 1088962688 | bytes 80752104 | solution.py:261
  20.4 3.5 collective-permute-done.12
  23.9 2.4 bitcast_select_fusion.2
  27.7 14.9 %collective-permute-done.12 = bf16[128,4096]{1,0:T(8,128)(2,1)S(1)} collective-permute-done((bf16[128,4096]{1,0:T(8,128)(2,1)}, bf16[128,4096]{1,0:T(8,128)(2,1)S(1)}, u32[]{:S(2)}, u32[]{:S(2)}) %collective-permute-start.12) | collective-permute-done | bytes 1048608 | tf_op jit(solution)/shard_map/while/body/eval_jaxpr/ppermute | solution.py:22
  42.6 2.4 bitcast_select_fusion.2
  46.4 14.9 %collective-permute-done.12 = bf16[128,4096]{1,0:T(8,128)(2,1)S(1)} collective-permute-done((bf16[128,4096]{1,0:T(8,128)(2,1)}, bf16[128,4096]{1,0:T(8,128)(2,1)S(1)}, u32[]{:S(2)}, u32[]{:S(2)}) %collective-permute-start.12) | collective-permute-done | bytes 1048608 | tf_op jit(solution)/shard_map/while/body/eval_jaxpr/ppermute | solution.py:22
  61.3 2.4 bitcast_select_fusion.2
  65.1 14.9 %collective-permute-done.12 = bf16[128,4096]{1,0:T(8,128)(2,1)S(1)} collective-permute-done((bf16[128,4096]{1,0:T(8,128)(2,1)}, bf16[128,4096]{1,0:T(8,128)(2,1)S(1)}, u32[]{:S(2)}, u32[]{:S(2)}) %collective-permute-start.12) | collective-permute-done | bytes 1048608 | tf_op jit(solution)/shard_map/while/body/eval_jaxpr/ppermute | solution.py:22
  80.0 2.4 bitcast_select_fusion.2
  83.7 14.9 %collective-permute-done.12 = bf16[128,4096]{1,0:T(8,128)(2,1)S(1)} collective-permute-done((bf16[128,4096]{1,0:T(8,128)(2,1)}, bf16[128,4096]{1,0:T(8,128)(2,1)S(1)}, u32[]{:S(2)}, u32[]{:S(2)}) %collective-permute-start.12) | collective-permute-done | bytes 1048608 | tf_op jit(solution)/shard_map/while/body/eval_jaxpr/ppermute | solution.py:22
  98.7 2.4 bitcast_select_fusion.2
  102.4 14.9 %collective-permute-done.12 = bf16[128,4096]{1,0:T(8,128)(2,1)S(1)} collective-permute-done((bf16[128,4096]{1,0:T(8,128)(2,1)}, bf16[128,4096]{1,0:T(8,128)(2,1)S(1)}, u32[]{:S(2)}, u32[]{:S(2)}) %collective-permute-start.12) | collective-permute-done | bytes 1048608 | tf_op jit(solution)/shard_map/while/body/eval_jaxpr/ppermute | solution.py:22
  117.3 2.4 bitcast_select_fusion.2
  121.1 14.9 %collective-permute-done.12 = bf16[128,4096]{1,0:T(8,128)(2,1)S(1)} collective-permute-done((bf16[128,4096]{1,0:T(8,128)(2,1)}, bf16[128,4096]{1,0:T(8,128)(2,1)S(1)}, u32[]{:S(2)}, u32[]{:S(2)}) %collective-permute-start.12) | collective-permute-done | bytes 1048608 | tf_op jit(solution)/shard_map/while/body/eval_jaxpr/ppermute | solution.py:22
  136.0 2.4 bitcast_select_fusion.2
  139.8 426.7 %collective-permute-done.12 = bf16[128,4096]{1,0:T(8,128)(2,1)S(1)} collective-permute-done((bf16[128,4096]{1,0:T(8,128)(2,1)}, bf16[128,4096]{1,0:T(8,128)(2,1)S(1)}, u32[]{:S(2)}, u32[]{:S(2)}) %collective-permute-start.12) | collective-permute-done | bytes 1048608 | tf_op jit(solution)/shard_map/while/body/eval_jaxpr/ppermute | solution.py:22
  566.5 2.4 bitcast_select_fusion.2
  568.8 64.0 %conditional.4 = ((bf16[128,4096]{1,0:T(8,128)(2,1)}, bf16[2,128,4096]{2,1,0:T(8,128)(2,1)})) conditional(s32[]{:T(128)} %convert_element_type.63, (bf16[128,4096]{1,0:T(8,128)(2,1)}, bf16[2,128,4096]{2,1,0:T(8,128)(2,1)}) %tuple.94, (s32[]{:T(128)}, bf16[1,2,128,4096]{3,2,1,0:T(8,128)(2,1)S(1)}, f32[2,128,64]{2,1,0:T(8,128)S(1)}, ...), branch_computations={%region_8.10_spmd, %region_9.12_spmd} | conditional | flops 1088422016 | bytes 73344808 | solution.py:257
  570.4 4.8 fusion.11
  576.3 2.7 collective-permute-start.1
  579.1 2.7 collective-permute-start.7
  581.9 2.2 collective-permute-done.6
  584.1 2.8 collective-permute-done.2
  587.0 2.1 collective-permute-done.8
  591.3 2.7 collective-permute-start.10
  593.9 3.0 collective-permute-done.3.refs_1_
  596.9 2.6 collective-permute-done.9.refs_5_
  601.5 2.4 fusion.10.refs_8_
  603.9 5.5 collective-permute-done.5.refs_3_
  611.0 19.6 %branch_1_fun.1 = bf16[128,4096]{1,0:T(8,128)(2,1)} custom-call(s32[1]{0:T(128)} %bitcast.mb_ref, bf16[128,4096]{1,0:T(8,128)(2,1)} %bitcast.35, bf16[512,512]{1,0:T(8,128)(2,1)} %copy-done.2, bf16[512,512]{1,0:T(8,128)(2,1)} %copy-done.3, bf16[512,512]{1,0:T(8,128)(2,1)} %copy-done.5, bf16[512,512]{1,0:T(8,128)(2,1)} %copy-done.7, ...), custom_call_target="tpu_custom_call" | custom-call | tf_op jit(solution)/shard_map/while/body/eval_jaxpr/cond/branch_1_fun/pallas_call | solution.py:171
  630.6 2.3 bitcast_dynamic-update-slice_fusion
  634.3 19.6 %collective-permute-done.12 = bf16[128,4096]{1,0:T(8,128)(2,1)S(1)} collective-permute-done((bf16[128,4096]{1,0:T(8,128)(2,1)}, bf16[128,4096]{1,0:T(8,128)(2,1)S(1)}, u32[]{:S(2)}, u32[]{:S(2)}) %collective-permute-start.12) | collective-permute-done | bytes 1048608 | tf_op jit(solution)/shard_map/while/body/eval_jaxpr/ppermute | solution.py:22
  653.9 2.4 bitcast_select_fusion.2
  656.2 61.6 %conditional.4 = ((bf16[128,4096]{1,0:T(8,128)(2,1)}, bf16[2,128,4096]{2,1,0:T(8,128)(2,1)})) conditional(s32[]{:T(128)} %convert_element_type.63, (bf16[128,4096]{1,0:T(8,128)(2,1)}, bf16[2,128,4096]{2,1,0:T(8,128)(2,1)}) %tuple.94, (s32[]{:T(128)}, bf16[1,2,128,4096]{3,2,1,0:T(8,128)(2,1)S(1)}, f32[2,128,64]{2,1,0:T(8,128)S(1)}, ...), branch_computations={%region_8.10_spmd, %region_9.12_spmd} | conditional | flops 1088422016 | bytes 73344808 | solution.py:257
  657.7 4.8 fusion.11
  663.7 2.7 collective-permute-start.1
  666.5 2.7 collective-permute-start.7
  669.3 2.2 collective-permute-done.6
  671.5 2.8 collective-permute-done.2
  678.7 2.7 collective-permute-start.10
  681.3 2.3 collective-permute-done.3.refs_1_
  683.6 2.3 collective-permute-done.9.refs_5_
  687.9 2.4 fusion.10.refs_8_
  690.3 2.6 collective-permute-done.5.refs_3_
  692.9 2.3 collective-permute-done.11.refs_7_
  696.0 19.6 %branch_1_fun.1 = bf16[128,4096]{1,0:T(8,128)(2,1)} custom-call(s32[1]{0:T(128)} %bitcast.mb_ref, bf16[128,4096]{1,0:T(8,128)(2,1)} %bitcast.35, bf16[512,512]{1,0:T(8,128)(2,1)} %copy-done.2, bf16[512,512]{1,0:T(8,128)(2,1)} %copy-done.3, bf16[512,512]{1,0:T(8,128)(2,1)} %copy-done.5, bf16[512,512]{1,0:T(8,128)(2,1)} %copy-done.7, ...), custom_call_target="tpu_custom_call" | custom-call | tf_op jit(solution)/shard_map/while/body/eval_jaxpr/cond/branch_1_fun/pallas_call | solution.py:171
  715.6 2.3 bitcast_dynamic-update-slice_fusion
  (186 shorter events, 41.8 us)
Async XLA Ops:
  16.3 2.7 copy-start.9
  16.3 2.7 copy-start.10
  19.0 4.9 collective-permute-start.12
  26.3 16.3 %collective-permute-start.12 = (bf16[128,4096]{1,0:T(8,128)(2,1)}, bf16[128,4096]{1,0:T(8,128)(2,1)S(1)}, u32[]{:S(2)}, u32[]{:S(2)}) collective-permute-start(bf16[128,4096]{1,0:T(8,128)(2,1)} %get-tuple-element.615), channel_id=1, source_target_pairs={{0,16},{16,32},{32,48},{48,64},{64,80},{80,96},{96,112},{1,17},{17... | collective-permute-start | bytes 3145736 | tf_op jit(solution)/shard_map/while/body/eval_jaxpr/ppermute | solution.py:22
  45.0 16.3 %collective-permute-start.12 = (bf16[128,4096]{1,0:T(8,128)(2,1)}, bf16[128,4096]{1,0:T(8,128)(2,1)S(1)}, u32[]{:S(2)}, u32[]{:S(2)}) collective-permute-start(bf16[128,4096]{1,0:T(8,128)(2,1)} %get-tuple-element.615), channel_id=1, source_target_pairs={{0,16},{16,32},{32,48},{48,64},{64,80},{80,96},{96,112},{1,17},{17... | collective-permute-start | bytes 3145736 | tf_op jit(solution)/shard_map/while/body/eval_jaxpr/ppermute | solution.py:22
  63.7 16.3 %collective-permute-start.12 = (bf16[128,4096]{1,0:T(8,128)(2,1)}, bf16[128,4096]{1,0:T(8,128)(2,1)S(1)}, u32[]{:S(2)}, u32[]{:S(2)}) collective-permute-start(bf16[128,4096]{1,0:T(8,128)(2,1)} %get-tuple-element.615), channel_id=1, source_target_pairs={{0,16},{16,32},{32,48},{48,64},{64,80},{80,96},{96,112},{1,17},{17... | collective-permute-start | bytes 3145736 | tf_op jit(solution)/shard_map/while/body/eval_jaxpr/ppermute | solution.py:22
  82.3 16.3 %collective-permute-start.12 = (bf16[128,4096]{1,0:T(8,128)(2,1)}, bf16[128,4096]{1,0:T(8,128)(2,1)S(1)}, u32[]{:S(2)}, u32[]{:S(2)}) collective-permute-start(bf16[128,4096]{1,0:T(8,128)(2,1)} %get-tuple-element.615), channel_id=1, source_target_pairs={{0,16},{16,32},{32,48},{48,64},{64,80},{80,96},{96,112},{1,17},{17... | collective-permute-start | bytes 3145736 | tf_op jit(solution)/shard_map/while/body/eval_jaxpr/ppermute | solution.py:22
  101.0 16.3 %collective-permute-start.12 = (bf16[128,4096]{1,0:T(8,128)(2,1)}, bf16[128,4096]{1,0:T(8,128)(2,1)S(1)}, u32[]{:S(2)}, u32[]{:S(2)}) collective-permute-start(bf16[128,4096]{1,0:T(8,128)(2,1)} %get-tuple-element.615), channel_id=1, source_target_pairs={{0,16},{16,32},{32,48},{48,64},{64,80},{80,96},{96,112},{1,17},{17... | collective-permute-start | bytes 3145736 | tf_op jit(solution)/shard_map/while/body/eval_jaxpr/ppermute | solution.py:22
  119.7 16.3 %collective-permute-start.12 = (bf16[128,4096]{1,0:T(8,128)(2,1)}, bf16[128,4096]{1,0:T(8,128)(2,1)S(1)}, u32[]{:S(2)}, u32[]{:S(2)}) collective-permute-start(bf16[128,4096]{1,0:T(8,128)(2,1)} %get-tuple-element.615), channel_id=1, source_target_pairs={{0,16},{16,32},{32,48},{48,64},{64,80},{80,96},{96,112},{1,17},{17... | collective-permute-start | bytes 3145736 | tf_op jit(solution)/shard_map/while/body/eval_jaxpr/ppermute | solution.py:22
  138.4 428.1 %collective-permute-start.12 = (bf16[128,4096]{1,0:T(8,128)(2,1)}, bf16[128,4096]{1,0:T(8,128)(2,1)S(1)}, u32[]{:S(2)}, u32[]{:S(2)}) collective-permute-start(bf16[128,4096]{1,0:T(8,128)(2,1)} %get-tuple-element.615), channel_id=1, source_target_pairs={{0,16},{16,32},{32,48},{48,64},{64,80},{80,96},{96,112},{1,17},{17... | collective-permute-start | bytes 3145736 | tf_op jit(solution)/shard_map/while/body/eval_jaxpr/ppermute | solution.py:22
  570.1 5.1 copy-start
  576.3 5.5 collective-permute-start
  576.3 7.8 %collective-permute-start.1 = (bf16[128,512]{1,0:T(8,128)(2,1)S(1)}, bf16[128,512]{1,0:T(8,128)(2,1)S(1)}, u32[]{:S(2)}, u32[]{:S(2)}) collective-permute-start(bf16[128,512]{1,0:T(8,128)(2,1)S(1)} %bitcast.42), channel_id=1, source_target_pairs={{0,3},{1,0},{2,1},{3,2},{4,7},{5,4},{6,5},{7,6},{8,11},{9,8},{10,9... | collective-permute-start | bytes 393224 | tf_op jit(solution)/shard_map/while/body/eval_jaxpr/cond/branch_1_fun/ppermute | solution.py:84
  579.0 5.1 collective-permute-start.6
  579.1 7.9 %collective-permute-start.7 = (bf16[128,512]{1,0:T(8,128)(2,1)S(1)}, bf16[128,512]{1,0:T(8,128)(2,1)S(1)}, u32[]{:S(2)}, u32[]{:S(2)}) collective-permute-start(bf16[128,512]{1,0:T(8,128)(2,1)S(1)} %slice.127), channel_id=1, source_target_pairs={{0,12},{1,13},{2,14},{3,15},{4,0},{5,1},{6,2},{7,3},{8,4},{9,5},{1... | collective-permute-start | bytes 393224 | tf_op jit(solution)/shard_map/while/body/eval_jaxpr/cond/branch_1_fun/ppermute | solution.py:84
  581.8 5.1 collective-permute-start.2
  584.1 5.0 collective-permute-start.8
  586.9 3.8 copy-start.2
  586.9 10.0 %collective-permute-start.3 = (bf16[512,512]{1,0:T(8,128)(2,1)S(1)}, bf16[512,512]{1,0:T(8,128)(2,1)S(1)}, u32[]{:S(2)}, u32[]{:S(2)}) collective-permute-start(bf16[512,512]{1,0:T(8,128)(2,1)S(1)} %constant_dynamic-update-slice_fusion.refs_0_), channel_id=1, source_target_pairs={{0,4},{1,5},{2,6},{3,7},{4,8},{5,9},{6,10},{7,11},{8,12},{9,13},{1... | collective-permute-start | bytes 1572872 | tf_op jit(solution)/shard_map/while/body/eval_jaxpr/cond/branch_1_fun/ppermute | solution.py:84
  589.2 2.1 copy-start.1
  589.2 10.3 %collective-permute-start.9 = (bf16[512,512]{1,0:T(8,128)(2,1)S(1)}, bf16[512,512]{1,0:T(8,128)(2,1)S(1)}, u32[]{:S(2)}, u32[]{:S(2)}) collective-permute-start(bf16[512,512]{1,0:T(8,128)(2,1)S(1)} %pad_maximum_fusion.1.refs_4_), channel_id=1, source_target_pairs={{0,1},{1,2},{2,3},{3,0},{4,5},{5,6},{6,7},{7,4},{8,9},{9,10},{10,1... | collective-permute-start | bytes 1572872 | tf_op jit(solution)/shard_map/while/body/eval_jaxpr/cond/branch_1_fun/ppermute | solution.py:84
  590.7 13.2 %collective-permute-start.4 = (bf16[512,512]{1,0:T(8,128)(2,1)S(1)}, bf16[512,512]{1,0:T(8,128)(2,1)S(1)}, u32[]{:S(2)}, u32[]{:S(2)}) collective-permute-start(bf16[512,512]{1,0:T(8,128)(2,1)S(1)} %constant_dynamic-update-slice_fusion.refs_0_), channel_id=1, source_target_pairs={{0,12},{1,13},{2,14},{3,15},{4,0},{5,1},{6,2},{7,3},{8,4},{9,5},{1... | collective-permute-start | bytes 1572872 | tf_op jit(solution)/shard_map/while/body/eval_jaxpr/cond/branch_1_fun/ppermute | solution.py:84
  591.3 12.6 %collective-permute-start.10 = (bf16[512,512]{1,0:T(8,128)(2,1)S(1)}, bf16[512,512]{1,0:T(8,128)(2,1)S(1)}, u32[]{:S(2)}, u32[]{:S(2)}) collective-permute-start(bf16[512,512]{1,0:T(8,128)(2,1)S(1)} %pad_maximum_fusion.1.refs_4_), channel_id=1, source_target_pairs={{0,3},{1,0},{2,1},{3,2},{4,7},{5,4},{6,5},{7,6},{8,11},{9,8},{10,9... | collective-permute-start | bytes 1572872 | tf_op jit(solution)/shard_map/while/body/eval_jaxpr/cond/branch_1_fun/ppermute | solution.py:84
  596.9 4.6 copy-start.3
  596.9 12.4 %collective-permute-start.5 = (bf16[512,512]{1,0:T(8,128)(2,1)S(1)}, bf16[512,512]{1,0:T(8,128)(2,1)S(1)}, u32[]{:S(2)}, u32[]{:S(2)}) collective-permute-start(bf16[512,512]{1,0:T(8,128)(2,1)S(1)} %collective-permute-done.3.refs_1_), channel_id=1, source_target_pairs={{0,4},{1,5},{2,6},{3,7},{4,8},{5,9},{6,10},{7,11},{8,12},{9,13},{1... | collective-permute-start | bytes 1572872 | tf_op jit(solution)/shard_map/while/body/eval_jaxpr/cond/branch_1_fun/ppermute | solution.py:84
  599.5 9.8 %collective-permute-start.11 = (bf16[512,512]{1,0:T(8,128)(2,1)S(1)}, bf16[512,512]{1,0:T(8,128)(2,1)S(1)}, u32[]{:S(2)}, u32[]{:S(2)}) collective-permute-start(bf16[512,512]{1,0:T(8,128)(2,1)S(1)} %collective-permute-done.9.refs_5_), channel_id=1, source_target_pairs={{0,1},{1,2},{2,3},{3,0},{4,5},{5,6},{6,7},{7,4},{8,9},{9,10},{10,1... | collective-permute-start | bytes 1572872 | tf_op jit(solution)/shard_map/while/body/eval_jaxpr/cond/branch_1_fun/ppermute | solution.py:84
  603.9 7.1 copy-start.5
  603.9 7.1 copy-start.6
  632.9 21.0 %collective-permute-start.12 = (bf16[128,4096]{1,0:T(8,128)(2,1)}, bf16[128,4096]{1,0:T(8,128)(2,1)S(1)}, u32[]{:S(2)}, u32[]{:S(2)}) collective-permute-start(bf16[128,4096]{1,0:T(8,128)(2,1)} %get-tuple-element.615), channel_id=1, source_target_pairs={{0,16},{16,32},{32,48},{48,64},{64,80},{80,96},{96,112},{1,17},{17... | collective-permute-start | bytes 3145736 | tf_op jit(solution)/shard_map/while/body/eval_jaxpr/ppermute | solution.py:22
  657.5 5.1 copy-start
  663.6 5.5 collective-permute-start
  663.7 7.8 %collective-permute-start.1 = (bf16[128,512]{1,0:T(8,128)(2,1)S(1)}, bf16[128,512]{1,0:T(8,128)(2,1)S(1)}, u32[]{:S(2)}, u32[]{:S(2)}) collective-permute-start(bf16[128,512]{1,0:T(8,128)(2,1)S(1)} %bitcast.42), channel_id=1, source_target_pairs={{0,3},{1,0},{2,1},{3,2},{4,7},{5,4},{6,5},{7,6},{8,11},{9,8},{10,9... | collective-permute-start | bytes 393224 | tf_op jit(solution)/shard_map/while/body/eval_jaxpr/cond/branch_1_fun/ppermute | solution.py:84
  666.4 5.1 collective-permute-start.6
  666.5 7.9 %collective-permute-start.7 = (bf16[128,512]{1,0:T(8,128)(2,1)S(1)}, bf16[128,512]{1,0:T(8,128)(2,1)S(1)}, u32[]{:S(2)}, u32[]{:S(2)}) collective-permute-start(bf16[128,512]{1,0:T(8,128)(2,1)S(1)} %slice.127), channel_id=1, source_target_pairs={{0,12},{1,13},{2,14},{3,15},{4,0},{5,1},{6,2},{7,3},{8,4},{9,5},{1... | collective-permute-start | bytes 393224 | tf_op jit(solution)/shard_map/while/body/eval_jaxpr/cond/branch_1_fun/ppermute | solution.py:84
  669.2 5.1 collective-permute-start.2
  671.5 5.0 collective-permute-start.8
  674.3 3.8 copy-start.2
  674.3 9.3 %collective-permute-start.3 = (bf16[512,512]{1,0:T(8,128)(2,1)S(1)}, bf16[512,512]{1,0:T(8,128)(2,1)S(1)}, u32[]{:S(2)}, u32[]{:S(2)}) collective-permute-start(bf16[512,512]{1,0:T(8,128)(2,1)S(1)} %constant_dynamic-update-slice_fusion.refs_0_), channel_id=1, source_target_pairs={{0,4},{1,5},{2,6},{3,7},{4,8},{5,9},{6,10},{7,11},{8,12},{9,13},{1... | collective-permute-start | bytes 1572872 | tf_op jit(solution)/shard_map/while/body/eval_jaxpr/cond/branch_1_fun/ppermute | solution.py:84
  676.6 2.1 copy-start.1
  676.6 9.3 %collective-permute-start.9 = (bf16[512,512]{1,0:T(8,128)(2,1)S(1)}, bf16[512,512]{1,0:T(8,128)(2,1)S(1)}, u32[]{:S(2)}, u32[]{:S(2)}) collective-permute-start(bf16[512,512]{1,0:T(8,128)(2,1)S(1)} %pad_maximum_fusion.1.refs_4_), channel_id=1, source_target_pairs={{0,1},{1,2},{2,3},{3,0},{4,5},{5,6},{6,7},{7,4},{8,9},{9,10},{10,1... | collective-permute-start | bytes 1572872 | tf_op jit(solution)/shard_map/while/body/eval_jaxpr/cond/branch_1_fun/ppermute | solution.py:84
  678.1 12.2 %collective-permute-start.4 = (bf16[512,512]{1,0:T(8,128)(2,1)S(1)}, bf16[512,512]{1,0:T(8,128)(2,1)S(1)}, u32[]{:S(2)}, u32[]{:S(2)}) collective-permute-start(bf16[512,512]{1,0:T(8,128)(2,1)S(1)} %constant_dynamic-update-slice_fusion.refs_0_), channel_id=1, source_target_pairs={{0,12},{1,13},{2,14},{3,15},{4,0},{5,1},{6,2},{7,3},{8,4},{9,5},{1... | collective-permute-start | bytes 1572872 | tf_op jit(solution)/shard_map/while/body/eval_jaxpr/cond/branch_1_fun/ppermute | solution.py:84
  678.7 11.6 %collective-permute-start.10 = (bf16[512,512]{1,0:T(8,128)(2,1)S(1)}, bf16[512,512]{1,0:T(8,128)(2,1)S(1)}, u32[]{:S(2)}, u32[]{:S(2)}) collective-permute-start(bf16[512,512]{1,0:T(8,128)(2,1)S(1)} %pad_maximum_fusion.1.refs_4_), channel_id=1, source_target_pairs={{0,3},{1,0},{2,1},{3,2},{4,7},{5,4},{6,5},{7,6},{8,11},{9,8},{10,9... | collective-permute-start | bytes 1572872 | tf_op jit(solution)/shard_map/while/body/eval_jaxpr/cond/branch_1_fun/ppermute | solution.py:84
  683.6 4.3 copy-start.3
  683.6 9.2 %collective-permute-start.5 = (bf16[512,512]{1,0:T(8,128)(2,1)S(1)}, bf16[512,512]{1,0:T(8,128)(2,1)S(1)}, u32[]{:S(2)}, u32[]{:S(2)}) collective-permute-start(bf16[512,512]{1,0:T(8,128)(2,1)S(1)} %collective-permute-done.3.refs_1_), channel_id=1, source_target_pairs={{0,4},{1,5},{2,6},{3,7},{4,8},{5,9},{6,10},{7,11},{8,12},{9,13},{1... | collective-permute-start | bytes 1572872 | tf_op jit(solution)/shard_map/while/body/eval_jaxpr/cond/branch_1_fun/ppermute | solution.py:84
  685.9 9.2 %collective-permute-start.11 = (bf16[512,512]{1,0:T(8,128)(2,1)S(1)}, bf16[512,512]{1,0:T(8,128)(2,1)S(1)}, u32[]{:S(2)}, u32[]{:S(2)}) collective-permute-start(bf16[512,512]{1,0:T(8,128)(2,1)S(1)} %collective-permute-done.9.refs_5_), channel_id=1, source_target_pairs={{0,1},{1,2},{2,3},{3,0},{4,5},{5,6},{6,7},{7,4},{8,9},{9,10},{10,1... | collective-permute-start | bytes 1572872 | tf_op jit(solution)/shard_map/while/body/eval_jaxpr/cond/branch_1_fun/ppermute | solution.py:84
  690.3 5.7 copy-start.5
  690.3 5.7 copy-start.6
  692.9 2.3 copy-start.7
  (5 other events, 6.4 us)
